TPU v7x, 256 devices: a whole 4x4x8 slice. The times are simulated.
256 devices in a mesh: seq: 32 (over x, z), tensor: 8 (over y, core).
Axes of the slice: x: 4, y: 4, z: 8, core: 2. Of those that a mesh axis runs over, the one named last changes fastest.
Arguments:
- features: bfloat16 [16, 7168], P(None, 'seq'), may hold values from -300 to 300
- input_norm_scale: float32 [7168], P('seq'), may hold values from 0.25 to 1.75
- query_key_value_weight: bfloat16 [7168, 3, 7168], P('seq', None, 'tensor'), may hold values from -0.0625 to 0.0625
- adapter_down_weight: bfloat16 [7168, 128], P('seq'), may hold values from -0.0625 to 0.0625
- adapter_up_weight: bfloat16 [128, 7168], P(None, 'tensor'), may hold values from -0.5 to 0.5
- output_weight: bfloat16 [7168, 3584], P('tensor', 'seq'), may hold values from -0.0625 to 0.0625
- cached_key_rows: bfloat16 [4, 16384, 7168], P(None, 'seq', 'tensor'), may hold values from -400 to 400
- cached_value_rows: bfloat16 [4, 16384, 7168], P(None, 'seq', 'tensor'), may hold values from -6 to 6
- lengths: int32 [4], replicated, may hold values from 16 to 16380, as said below
- sinks: int32 [4], replicated, may hold values from 1 to 4, as said below
- windows: int32 [4], replicated, may hold values from 2048 to 4096, as said below
Outputs:
- mixed: float32 [16, 3584], P(None, 'seq')
- new_kv: float32 [2, 16, 7168], P(None, None, 'tensor')
Inputs may be any that keep to these rules, and one draw needn't show every extreme that they name: `lengths`: heavy-tailed; at least one request has 16380. `sinks`: at least one request has 4. `windows`: at least one request has 4096.
All inputs are finite; a program needn't handle non-finite values.
Results may differ from a plain program's by a relative error of at most 0.022.
Values sent between devices are 32-bit elements; how exact they have to be, the bound alone decides.
No kernel may reach another device: no remote copies, remote signals or barrier semaphores. Data moves between devices by JAX's collectives and lax.ppermute only.
A program may use at most 64 MiB of HBM per device.

v0:
```python
import jax
import jax.numpy as jnp
from jax import lax
from jax.sharding import PartitionSpec as P

HD = 224
NEW = 4
INPUT_WIDTH = 7168


NEG = -1e30
CUT = -1e29


def row_stats(partial_low_rank, partial_sq):
    return lax.psum((partial_low_rank, partial_sq), "seq")


def live_block(base, span, length, sink, window):
    return (base < length) & ((base < sink) | (base + span - 1 > length - window))


def cache_scores(query_all, cached_key_rows, lengths, sinks, windows, base):
    count, span = (cached_key_rows.shape[0], cached_key_rows.shape[1])
    heads = query_all.shape[2]
    position = base + jnp.arange(span, dtype=jnp.int32)
    order = jnp.arange(NEW, dtype=jnp.int32)

    def score_one(index):
        length = lengths[index]
        sink = sinks[index]
        window = windows[index]

        def score_compute():
            keys = cached_key_rows[index].reshape(span, heads, HD)
            raw = jnp.einsum(
                "thd,phd->htp", query_all[index], keys, preferred_element_type=jnp.float32
            ) * HD ** (-0.5)
            seen = (position[None, :] < length) & (
                (position[None, :] < sink) | (length + order[:, None] - position[None, :] < window)
            )
            return jnp.where(seen[None], raw, NEG)

        def score_skipped():
            return jnp.full((heads, NEW, span), NEG, jnp.float32)

        return lax.cond(live_block(base, span, length, sink, window), score_compute, score_skipped)

    return lax.map(score_one, jnp.arange(count, dtype=jnp.int32))


def cache_terms(scores, cached_value_rows, top, lengths, sinks, windows, base):
    count, span = (cached_value_rows.shape[0], cached_value_rows.shape[1])
    heads = scores.shape[1]

    def weigh_one(index):

        def weigh_compute():
            expo = jnp.where(
                scores[index] > CUT, jnp.exp(scores[index] - top[index][..., None]), 0.0
            )
            values = cached_value_rows[index].reshape(span, heads, HD)
            output = jnp.einsum(
                "htp,phd->htd",
                expo.astype(jnp.bfloat16),
                values,
                preferred_element_type=jnp.float32,
            )
            return (jnp.sum(expo, axis=-1), output)

        def weigh_skipped():
            return (jnp.zeros((heads, NEW), jnp.float32), jnp.zeros((heads, NEW, HD), jnp.float32))

        return lax.cond(
            live_block(base, span, lengths[index], sinks[index], windows[index]),
            weigh_compute,
            weigh_skipped,
        )

    return lax.map(weigh_one, jnp.arange(count, dtype=jnp.int32))


def own_scores(query_all, key_all):
    raw = jnp.einsum(
        "rthd,ruhd->rhtu", query_all, key_all, preferred_element_type=jnp.float32
    ) * HD ** (-0.5)
    order = jnp.arange(NEW, dtype=jnp.int32)
    causal = order[:, None] >= order[None, :]
    return jnp.where(causal[None, None], raw, NEG)


def own_terms(fresh, value_all, top):
    expo = jnp.where(fresh > CUT, jnp.exp(fresh - top[..., None]), 0.0)
    output = jnp.einsum(
        "rhtu,ruhd->rhtd", expo.astype(jnp.bfloat16), value_all, preferred_element_type=jnp.float32
    )
    return (jnp.sum(expo, axis=-1), output)


def shards(
    features,
    input_norm_scale,
    query_key_value_weight,
    adapter_down_weight,
    adapter_up_weight,
    output_weight,
    cached_key_rows,
    cached_value_rows,
    lengths,
    sinks,
    windows,
):
    rows = features.shape[0]
    count = cached_key_rows.shape[0]
    local_attention = adapter_up_weight.shape[1]
    heads = local_attention // HD
    feat = features.astype(jnp.float32)
    scaled_scores = (feat * input_norm_scale).astype(jnp.bfloat16)
    weights = query_key_value_weight.reshape(query_key_value_weight.shape[0], 3 * local_attention)
    partial_low_rank = jnp.dot(
        scaled_scores, adapter_down_weight, preferred_element_type=jnp.float32
    )
    partial_sq = jnp.sum(feat * feat, axis=1)
    partial_proj = jnp.dot(scaled_scores, weights, preferred_element_type=jnp.float32)
    low_rank_query, total_sq = row_stats(partial_low_rank, partial_sq)
    scale_rows = lax.rsqrt(total_sq / INPUT_WIDTH + 1e-05)[:, None]
    lowrank = (low_rank_query * scale_rows).astype(jnp.bfloat16)
    query_adapter = jnp.dot(lowrank, adapter_up_weight, preferred_element_type=jnp.float32)
    projected = lax.psum(partial_proj, "seq")
    queries = (projected[:, :local_attention] * scale_rows + query_adapter).astype(jnp.bfloat16)
    keys_full = projected[:, local_attention : 2 * local_attention] * scale_rows
    values_full = projected[:, 2 * local_attention :] * scale_rows
    new_keys = keys_full.astype(jnp.bfloat16)
    new_values = values_full.astype(jnp.bfloat16)
    base = lax.axis_index("seq") * cached_key_rows.shape[1]
    query_all = queries.reshape(count, NEW, heads, HD)
    key_all = new_keys.reshape(count, NEW, heads, HD)
    value_all = new_values.reshape(count, NEW, heads, HD)
    scores = cache_scores(query_all, cached_key_rows, lengths, sinks, windows, base)
    fresh = own_scores(query_all, key_all)
    local_top = jnp.maximum(jnp.max(scores, axis=-1), jnp.max(fresh, axis=-1))
    top = lax.pmax(local_top, "seq")
    total, output = cache_terms(scores, cached_value_rows, top, lengths, sinks, windows, base)
    total, output = lax.psum((total, output), "seq")
    own_total, own_output = own_terms(fresh, value_all, top)
    total = total + own_total
    output = output + own_output
    attn = (
        (output / total[..., None])
        .transpose(0, 2, 1, 3)
        .reshape(rows, local_attention)
        .astype(jnp.bfloat16)
    )
    partial_out = jnp.dot(attn, output_weight, preferred_element_type=jnp.float32)
    mixed = lax.psum(partial_out, "tensor")
    return (mixed, jnp.stack([keys_full, values_full]))


def solution(mesh):
    in_specs = (
        P(None, "seq"),
        P("seq"),
        P("seq", None, "tensor"),
        P("seq", None),
        P(None, "tensor"),
        P("tensor", "seq"),
        P(None, "seq", "tensor"),
        P(None, "seq", "tensor"),
        P(),
        P(),
        P(),
    )
    out_specs = (P(None, "seq"), P(None, None, "tensor"))
    return jax.shard_map(shards, mesh=mesh, in_specs=in_specs, out_specs=out_specs, check_vma=False)
```

profile of v0, /device:TPU:1, one launch (start us, length us, event | category | flops | bytes accessed | tf_op | source)
XLA Modules:
  0.0 486.1 jit_solution(430829376250287808)
XLA Ops:
  7.3 1.8 copy.20
  9.1 1.9 fusion.35
  11.3 5.9 %copy.22 = bf16[4,512,896]{1,2,0:T(8,128)(2,1)} copy(bf16[4,512,896]{2,1,0:T(8,128)(2,1)} %param.25) | data formatting | bytes 7340032
  17.3 6.0 %copy.25 = bf16[4,512,896]{1,2,0:T(8,128)(2,1)} copy(bf16[4,512,896]{2,1,0:T(8,128)(2,1)} %param.26) | data formatting | bytes 7340032 | tf_op jit(solution)/shard_map/while | solution.py:80
  23.2 66.3 %all-reduce.1 = (f32[16]{0:T(128)S(1)}, f32[16,128]{1,0:T(8,128)S(1)}) all-reduce(f32[16]{0:T(128)S(1)} %fusion.29, f32[16,128]{1,0:T(8,128)S(1)} %fusion.33), channel_id=1, replica_groups=mesh['seq'=32,'tensor'=8] {'seq'}, use_global_device_ids=true, to_apply=%region_2.0 | all-reduce | flops 2064 | bytes 16512 | tf_op jit(solution)/shard_map/psum | solution.py:16
  89.6 63.3 %all-reduce.4.cloned.1.call-done = f32[16,2688]{1,0:T(8,128)} async-done(((f32[16,2688]{1,0:T(8,128)}), f32[16,2688]{1,0:T(8,128)}) %all-reduce.4.cloned.1.call-update) | async-done | bytes 172048 | tf_op jit(solution)/shard_map/psum | solution.py:129
  152.9 0.9 fusion.22
  153.9 1.0 fusion.19
  155.1 52.7 %while.31 = (s32[]{:T(128)}, f32[4,4,4,512]{3,2,1,0:T(4,128)S(1)}, s32[4]{0:T(128)S(1)}, s32[4]{0:T(128)S(1)}, s32[]{:T(128)}, /*index=5*/s32[4]{0:T(128)S(1)}, ...) while((s32[]{:T(128)}, f32[4,4,4,512]{3,2,1,0:T(4,128)S(1)}, ...), condition=%wide.region_7.8_spmd.clone.clone.clone, body=%wide.region_4.7_spmd.clone.clone.clone.sunk | while | flops 3696147 | bytes 2875843 | solution.py:49
  155.1 0.7 dynamic_slice.98
  157.8 0.6 dynamic_slice.99
  158.4 0.6 dynamic_slice.100
  159.1 0.6 dynamic_slice.101
  162.2 6.1 %conditional.8 = (f32[1,4,4,512]{3,2,1,0:T(4,128)S(1)}) conditional(s32[]{:T(128)} %convert_element_type.83, () %tuple.102, (s32[]{:T(128)}, s32[]{:T(128)}, s32[]{:T(128)}, s32[4]{0:T(128)S(1)}, s32[]{:T(128)}, /*index=5*/s32[]{:T(128)}, bf16[4,4,4,224]{3,1,2,0:T(4,128)(2,1)S(1)}, bf16[4,512,896]{1,2,0:T(8,128)(2,1)}, s32[512]{0:T(512)S(1)}) %tuple.103), branch_computations={%region_5.5_spmd, %region_6.6_spmd} | conditional | flops 3696135 | bytes 2807926 | solution.py:47
  162.8 0.6 broadcast_compare_fusion
  164.0 0.7 fusion.7
  166.8 1.2 constant_dynamic-slice_fusion
  168.3 0.7 dynamic_slice.98
  171.0 0.6 dynamic_slice.99
  171.6 0.6 dynamic_slice.100
  172.2 0.6 dynamic_slice.101
  175.3 6.1 %conditional.8 = (f32[1,4,4,512]{3,2,1,0:T(4,128)S(1)}) conditional(s32[]{:T(128)} %convert_element_type.83, () %tuple.102, (s32[]{:T(128)}, s32[]{:T(128)}, s32[]{:T(128)}, s32[4]{0:T(128)S(1)}, s32[]{:T(128)}, /*index=5*/s32[]{:T(128)}, bf16[4,4,4,224]{3,1,2,0:T(4,128)(2,1)S(1)}, bf16[4,512,896]{1,2,0:T(8,128)(2,1)}, s32[512]{0:T(512)S(1)}) %tuple.103), branch_computations={%region_5.5_spmd, %region_6.6_spmd} | conditional | flops 3696135 | bytes 2807926 | solution.py:47
  175.9 0.6 broadcast_compare_fusion
  177.1 0.7 fusion.7
  180.0 1.2 constant_dynamic-slice_fusion
  181.5 0.7 dynamic_slice.98
  184.2 0.6 dynamic_slice.99
  184.8 0.6 dynamic_slice.100
  185.4 0.6 dynamic_slice.101
  188.5 6.1 %conditional.8 = (f32[1,4,4,512]{3,2,1,0:T(4,128)S(1)}) conditional(s32[]{:T(128)} %convert_element_type.83, () %tuple.102, (s32[]{:T(128)}, s32[]{:T(128)}, s32[]{:T(128)}, s32[4]{0:T(128)S(1)}, s32[]{:T(128)}, /*index=5*/s32[]{:T(128)}, bf16[4,4,4,224]{3,1,2,0:T(4,128)(2,1)S(1)}, bf16[4,512,896]{1,2,0:T(8,128)(2,1)}, s32[512]{0:T(512)S(1)}) %tuple.103), branch_computations={%region_5.5_spmd, %region_6.6_spmd} | conditional | flops 3696135 | bytes 2807926 | solution.py:47
  189.1 0.6 broadcast_compare_fusion
  190.3 0.7 fusion.7
  193.1 1.2 constant_dynamic-slice_fusion
  194.7 0.7 dynamic_slice.98
  197.4 0.6 dynamic_slice.99
  198.0 0.6 dynamic_slice.100
  198.6 0.6 dynamic_slice.101
  201.7 6.1 %conditional.8 = (f32[1,4,4,512]{3,2,1,0:T(4,128)S(1)}) conditional(s32[]{:T(128)} %convert_element_type.83, () %tuple.102, (s32[]{:T(128)}, s32[]{:T(128)}, s32[]{:T(128)}, s32[4]{0:T(128)S(1)}, s32[]{:T(128)}, /*index=5*/s32[]{:T(128)}, bf16[4,4,4,224]{3,1,2,0:T(4,128)(2,1)S(1)}, bf16[4,512,896]{1,2,0:T(8,128)(2,1)}, s32[512]{0:T(512)S(1)}) %tuple.103), branch_computations={%region_5.5_spmd, %region_6.6_spmd} | conditional | flops 3696135 | bytes 2807926 | solution.py:47
  202.3 0.6 broadcast_compare_fusion
  203.5 0.7 fusion.7
  206.3 1.2 constant_dynamic-slice_fusion
  208.1 57.0 %pmax.7 = f32[4,4,4]{2,1,0:T(4,128)S(1)} all-reduce(f32[4,4,4]{2,1,0:T(4,128)S(1)} %max.5), channel_id=1, replica_groups=mesh['seq'=32,'tensor'=8] {'seq'}, use_global_device_ids=true, to_apply=%region_10.11 | all-reduce | flops 64 | bytes 512 | tf_op jit(solution)/shard_map/pmax | solution.py:142
  265.2 43.1 %while.30 = (s32[]{:T(128)}, f32[4,4,4]{2,1,0:T(4,128)S(1)}, f32[4,4,4,224]{3,2,1,0:T(4,128)S(1)}, s32[4]{0:T(128)S(1)}, s32[4]{0:T(128)S(1)}, /*index=5*/s32[]{...) while((s32[]{:T(128)}, f32[4,4,4]{2,1,0:T(4,128)S(1)}, ...), condition=%wide.region_15.16_spmd, body=%wide.region_11.15_spmd.sunk | while | flops 3735551 | bytes 2871931 | solution.py:80
  267.7 0.6 dynamic_slice.95
  268.3 0.7 dynamic_slice.97
  270.2 0.7 dynamic_slice.96
  272.2 3.8 conditional.7
  274.2 1.2 constant_dynamic-slice_fusion.1
  278.5 0.6 dynamic_slice.95
  279.1 0.7 dynamic_slice.97
  281.0 0.7 dynamic_slice.96
  283.0 3.8 conditional.7
  284.9 1.2 constant_dynamic-slice_fusion.1
  289.9 0.7 dynamic_slice.97
  291.8 0.7 dynamic_slice.96
  293.7 3.8 conditional.7
  295.7 1.2 constant_dynamic-slice_fusion.1
  300.6 0.7 dynamic_slice.97
  302.6 0.7 dynamic_slice.96
  304.5 3.8 conditional.7
  306.5 1.2 constant_dynamic-slice_fusion.1
  308.5 110.7 %all-reduce = (f32[4,4,4,224]{3,2,1,0:T(4,128)S(1)}, f32[4,4,4]{2,1,0:T(4,128)S(1)}) all-reduce(f32[4,4,4,224]{3,2,1,0:T(4,128)S(1)} %get-tuple-element.337, f32[4,4,4]{2,1,0:T(4,128)S(1)} %get-tuple-element.338), channel_id=1, replica_groups=mesh['seq'=32,'tensor'=8] {'seq'}, use_global_device_ids=true, to_apply=%region_16.17 | all-reduce | flops 14400 | bytes 115200 | tf_op jit(solution)/shard_map/psum | solution.py:144
  419.6 59.0 %psum.47 = f32[16,112]{1,0:T(8,128)} all-reduce(f32[16,112]{1,0:T(8,128)S(1)} %fusion.43), channel_id=1, replica_groups=mesh['seq'=32,'tensor'=8] {'tensor'}, use_global_device_ids=true, to_apply=%region_19.20 | all-reduce | flops 1792 | bytes 14336 | tf_op jit(solution)/shard_map/psum | solution.py:155
  478.6 0.7 pad_maximum_fusion
  (87 shorter events, 12.9 us)
Async XLA Ops:
  7.2 146.7 %copy-start = (bf16[128,896]{1,0:T(8,128)(2,1)S(1)}, bf16[128,896]{1,0:T(8,128)(2,1)}, u32[]{:S(2)}) copy-start(bf16[128,896]{1,0:T(8,128)(2,1)} %param.23) | copy-start | bytes 688132
  7.2 3.8 copy-start.2
  7.2 4.0 copy-start.4
  7.2 4.0 copy-start.3
  7.2 145.6 %all-reduce.4.cloned.1.call-start = ((), (), s32[]{:S(2)}) async-start(), calls=%async_computation | async-start | bytes 344064 | tf_op jit(solution)/shard_map/psum | solution.py:129
  17.3 137.8 %copy-start.5 = (s32[4]{0:T(128)S(1)}, s32[4]{0:T(128)}, u32[]{:S(2)}) copy-start(s32[4]{0:T(128)} %param.27) | copy-start | bytes 52
  17.3 137.8 %copy-start.6 = (s32[4]{0:T(128)S(1)}, s32[4]{0:T(128)}, u32[]{:S(2)}) copy-start(s32[4]{0:T(128)} %param.28) | copy-start | bytes 52
  17.3 137.8 %copy-start.7 = (s32[4]{0:T(128)S(1)}, s32[4]{0:T(128)}, u32[]{:S(2)}) copy-start(s32[4]{0:T(128)} %param.29) | copy-start | bytes 52
  265.2 154.3 %copy-start.1 = (bf16[896,112]{0,1:T(8,128)(2,1)S(1)}, bf16[896,112]{0,1:T(8,128)(2,1)}, u32[]{:S(2)}) copy-start(bf16[896,112]{0,1:T(8,128)(2,1)} %param.24) | copy-start | bytes 602116
Sparse Core Ops, SparseCore 0:
  11.5 141.3 all-reduce.3
where the time goes:
time: 488 us; the launch traced here: 486 us
  blocking collectives  293 us (60%)
  waiting for transfers between devices  63.3 us (13%)
  loops' own time  52.4 us (11%)
  local copies, waits for them, and re-layouts  44.5 us (9%)
  between operations  14.3 us (3%)
  other arithmetic  12.7 us (3%)
  matrix products  5.88 us (1%)
    psum x1, blocking collectives, shards(): total, output = lax.psum((total, output), 'seq')  111 us
    psum x1, blocking collectives, row_stats(): return lax.psum((partial_low_rank, partial_sq), 'seq')  66.3 us
    psum x1, waiting for transfers between devices, shards(): projected = lax.psum(partial_proj, 'seq')  63.3 us
    psum x1, blocking collectives, shards(): mixed = lax.psum(partial_out, 'tensor')  59 us
    pmax x1, blocking collectives, shards(): top = lax.pmax(local_top, 'seq')  57 us
    another operation x1, loops' own time, cache_scores(): return lax.map(score_one, jnp.arange(count, dtype=jnp.int32))  18.2 us
    another operation x1, loops' own time, cache_terms(): return lax.map(weigh_one, jnp.arange(count, dtype=jnp.int32))  17.9 us
  transfers between devices with their start and end apart: 1, of which 1 were waited for; matrix products, arithmetic and copies ran while one was open for 3% of the time, Pallas kernels for 0%

commit v1 on v0

v1 whole, which is shorter than its diff:
```python
import jax
import jax.numpy as jnp
from jax import lax
from jax.sharding import PartitionSpec as P

HD = 224
NEW = 4
INPUT_WIDTH = 7168


NEG = -1e30
CUT = -1e29


def butterfly_sum(x, axis, size):
    step = 1
    while step < size:
        x = x + lax.ppermute(x, axis, [(i, i ^ step) for i in range(size)])
        step *= 2
    return x


def merge_softmax(a, b, width, heads):
    top = jnp.maximum(a[:, width + heads : width + 2 * heads], b[:, width + heads : width + 2 * heads])
    sa = jnp.exp(a[:, width + heads : width + 2 * heads] - top)
    sb = jnp.exp(b[:, width + heads : width + 2 * heads] - top)
    values = a[:, :width] * jnp.repeat(sa, HD, axis=1) + b[:, :width] * jnp.repeat(sb, HD, axis=1)
    totals = a[:, width : width + heads] * sa + b[:, width : width + heads] * sb
    pad = a.shape[1] - width - 2 * heads
    return jnp.concatenate([values, totals, top, jnp.zeros((a.shape[0], pad), jnp.float32)], axis=1)


def butterfly_softmax(x, axis, size, width, heads):
    step = 1
    while step < size:
        other = lax.ppermute(x, axis, [(i, i ^ step) for i in range(size)])
        x = merge_softmax(x, other, width, heads)
        step *= 2
    return x


def shards(
    features,
    input_norm_scale,
    query_key_value_weight,
    adapter_down_weight,
    adapter_up_weight,
    output_weight,
    cached_key_rows,
    cached_value_rows,
    lengths,
    sinks,
    windows,
    seq_size,
):
    rows = features.shape[0]
    count, span = cached_key_rows.shape[0], cached_key_rows.shape[1]
    local = adapter_up_weight.shape[1]
    heads = local // HD
    rank = adapter_down_weight.shape[1]
    f32, bf16 = jnp.float32, jnp.bfloat16

    feat = features.astype(f32)
    scaled = (feat * input_norm_scale).astype(bf16)
    weights = query_key_value_weight.reshape(query_key_value_weight.shape[0], 3 * local)
    partial_proj = jnp.dot(scaled, weights, preferred_element_type=f32)
    partial_low = jnp.dot(scaled, adapter_down_weight, preferred_element_type=f32)
    partial_sq = jnp.sum(feat * feat, axis=1, keepdims=True)
    packed = jnp.concatenate(
        [partial_proj, partial_low, partial_sq, jnp.zeros((rows, 127), f32)], axis=1
    )
    summed = butterfly_sum(packed, "seq", seq_size)
    projected = summed[:, : 3 * local]
    low = summed[:, 3 * local : 3 * local + rank]
    total_sq = summed[:, 3 * local + rank]
    scale_rows = lax.rsqrt(total_sq / INPUT_WIDTH + 1e-05)[:, None]
    lowrank = (low * scale_rows).astype(bf16)
    query_adapter = jnp.dot(lowrank, adapter_up_weight, preferred_element_type=f32)
    queries = (projected[:, :local] * scale_rows + query_adapter).astype(bf16)
    keys_full = projected[:, local : 2 * local] * scale_rows
    values_full = projected[:, 2 * local :] * scale_rows
    new_keys = keys_full.astype(bf16)
    new_values = values_full.astype(bf16)

    col_head = jnp.arange(local, dtype=jnp.int32) // HD
    head_mask = col_head[None, :] == jnp.arange(heads, dtype=jnp.int32)[:, None]
    q_rows = queries.reshape(count, NEW, local)
    q_block = jnp.where(head_mask[None, :, None, :], q_rows[:, None, :, :], jnp.zeros((), bf16))
    q_block = q_block.reshape(count, heads * NEW, local)
    raw = jnp.einsum(
        "rnc,rpc->rnp", q_block, cached_key_rows, preferred_element_type=f32
    ) * HD ** (-0.5)
    base = lax.axis_index("seq") * span
    position = base + jnp.arange(span, dtype=jnp.int32)
    order = jnp.arange(NEW, dtype=jnp.int32)
    length = lengths[:, None, None]
    sink = sinks[:, None, None]
    window = windows[:, None, None]
    pos = position[None, None, :]
    seen = (pos < length) & ((pos < sink) | (length + order[None, :, None] - pos < window))
    seen = jnp.broadcast_to(seen[:, None], (count, heads, NEW, span)).reshape(count, heads * NEW, span)
    scores = jnp.where(seen, raw, NEG)
    local_top = jnp.max(scores, axis=-1)
    expo = jnp.where(scores > CUT, jnp.exp(scores - local_top[..., None]), 0.0)
    local_total = jnp.sum(expo, axis=-1)
    weighted = jnp.einsum(
        "rnp,rpc->rnc", expo.astype(bf16), cached_value_rows, preferred_element_type=f32
    )
    weighted = jnp.sum(
        jnp.where(head_mask[None, :, None, :], weighted.reshape(count, heads, NEW, local), 0.0),
        axis=1,
    )

    def by_row(x):
        return x.reshape(count, heads, NEW).transpose(0, 2, 1).reshape(rows, heads)

    packed = jnp.concatenate(
        [
            weighted.reshape(rows, local),
            by_row(local_total),
            by_row(local_top),
            jnp.zeros((rows, 128 - 2 * heads), f32),
        ],
        axis=1,
    )
    merged = butterfly_softmax(packed, "seq", seq_size, local, heads)
    cache_out = merged[:, :local]
    cache_total = merged[:, local : local + heads]
    cache_top = merged[:, local + heads : local + 2 * heads]

    query_all = queries.reshape(count, NEW, heads, HD)
    key_all = new_keys.reshape(count, NEW, heads, HD)
    value_all = new_values.reshape(count, NEW, heads, HD)
    fresh = jnp.einsum(
        "rthd,ruhd->rhtu", query_all, key_all, preferred_element_type=f32
    ) * HD ** (-0.5)
    causal = order[:, None] >= order[None, :]
    fresh = jnp.where(causal[None, None], fresh, NEG)
    own_top = by_row(jnp.max(fresh, axis=-1))
    top = jnp.maximum(cache_top, own_top)
    top_rht = top.reshape(count, NEW, heads).transpose(0, 2, 1)
    own_e = jnp.where(fresh > CUT, jnp.exp(fresh - top_rht[..., None]), 0.0)
    own_total = by_row(jnp.sum(own_e, axis=-1))
    own_out = jnp.einsum(
        "rhtu,ruhd->rthd", own_e.astype(bf16), value_all, preferred_element_type=f32
    ).reshape(rows, local)
    cache_scale = jnp.exp(cache_top - top)
    output = cache_out * jnp.repeat(cache_scale, HD, axis=1) + own_out
    total = cache_total * cache_scale + own_total
    attn = (output / jnp.repeat(total, HD, axis=1)).astype(bf16)
    partial_out = jnp.dot(attn, output_weight, preferred_element_type=f32)
    mixed = lax.psum(partial_out, "tensor")
    return (mixed, jnp.stack([keys_full, values_full]))


def solution(mesh):
    in_specs = (
        P(None, "seq"),
        P("seq"),
        P("seq", None, "tensor"),
        P("seq", None),
        P(None, "tensor"),
        P("tensor", "seq"),
        P(None, "seq", "tensor"),
        P(None, "seq", "tensor"),
        P(),
        P(),
        P(),
    )
    out_specs = (P(None, "seq"), P(None, None, "tensor"))
    seq_size = mesh.shape["seq"]

    def body(*args):
        return shards(*args, seq_size)

    return jax.shard_map(body, mesh=mesh, in_specs=in_specs, out_specs=out_specs, check_vma=False)
```

time: 488 us -> 104 us (0.21)
  blocking collectives: 293 us -> 20.6 us
  loops' own time: 52.4 us -> 0 us
  local copies, waits for them, and re-layouts: 44.5 us -> 5.78 us
  starting transfers between devices: 0.04 us -> 29.3 us
  waiting for transfers between devices: 63.3 us -> 35.8 us
  between operations: 14.3 us -> 1.01 us
  other arithmetic: 12.7 us -> 3.37 us
    psum x2 -> x0, blocking collectives: 177 us -> none  [the longest x1 111 us: shards(): total, output = lax.psum((total, output), 'seq')]
    psum x1 -> x0, waiting for transfers between devices: 63.3 us -> none  [shards(): projected = lax.psum(partial_proj, 'seq')]
    pmax x1 -> x0, blocking collectives: 57 us -> none  [shards(): top = lax.pmax(local_top, 'seq')]
    another operation x10 -> x0, loops' own time: 52.4 us -> none  [the longest x1 18.2 us: cache_scores(): return lax.map(score_one, jnp.arange(count, dtype=jnp.int32))]
    psum x1, blocking collectives: 59 us -> 20.6 us  [shards(): mixed = lax.psum(partial_out, 'tensor')]
    ppermute x0 -> x10, waiting for transfers between devices: none -> 35.8 us  [the longest x5 24.8 us: butterfly_sum(): x = x + lax.ppermute(x, axis, [(i, i ^ step) for i in range(size)])]
    dynamic_slice x40 -> x0, local copies, waits for them, and re-layouts: 30.1 us -> none  [the longest x8 5.01 us: cache_scores(): return lax.map(score_one, jnp.arange(count, dtype=jnp.int32))]
    ppermute x0 -> x10, starting transfers between devices: none -> 29.3 us  [the longest x5 17.2 us: butterfly_sum(): x = x + lax.ppermute(x, axis, [(i, i ^ step) for i in range(size)])]
  transfers between devices with their start and end apart: 1 -> 10, of which waited for: 1 -> 10; matrix products, arithmetic and copies ran while one was open for 3% -> 2% of each run, Pallas kernels for 0% -> 0%
where the time goes in v1:
time: 104 us
  waiting for transfers between devices  35.8 us (34%)
  starting transfers between devices  29.3 us (28%)
  blocking collectives  20.6 us (20%)
  matrix products  7.9 us (8%)
  local copies, waits for them, and re-layouts  5.78 us (6%)
  other arithmetic  3.37 us (3%)
    ppermute x5, waiting for transfers between devices, butterfly_sum(): x = x + lax.ppermute(x, axis, [(i, i ^ step) for i in range(size)])  24.8 us
    psum x1, blocking collectives, shards(): mixed = lax.psum(partial_out, 'tensor')  20.6 us
    ppermute x5, starting transfers between devices, butterfly_sum(): x = x + lax.ppermute(x, axis, [(i, i ^ step) for i in range(size)])  17.2 us
    ppermute x5, starting transfers between devices, butterfly_softmax(): other = lax.ppermute(x, axis, [(i, i ^ step) for i in range(size)])  12.2 us
    ppermute x5, waiting for transfers between devices, butterfly_softmax(): other = lax.ppermute(x, axis, [(i, i ^ step) for i in range(size)])  11.1 us
    dot_general x1, matrix products, shards(): jnp.einsum('rnc,rpc->rnp', q_block, cached_key_rows, preferred_element_ty...  3.17 us
    dot_general x1, matrix products, shards(): jnp.einsum('rnp,rpc->rnc', expo.astype(bf16), cached_value_rows, preferre...  2.68 us
  transfers between devices with their start and end apart: 10, of which 10 were waited for; matrix products, arithmetic and copies ran while one was open for 2% of the time, Pallas kernels for 0%

profile of v1, /device:TPU:1, one launch (start us, length us, event | category | flops | bytes accessed | tf_op | source)
XLA Modules:
  0.0 103.8 jit_solution(5638813589371884692)
XLA Ops:
  0.7 1.9 %copy.39 = bf16[224,3,896]{0,2,1:T(8,128)(2,1)S(1)} copy(bf16[224,3,896]{2,0,1:T(8,128)(2,1)} %param.13) | data formatting | bytes 2408448 | tf_op args[2]
  2.6 0.8 fusion.36
  3.4 0.1 copy.40
  3.5 1.2 %fusion.54 = f32[16,2688]{1,0:T(8,128)S(1)} fusion(bf16[224,2688]{0,1:T(8,128)(2,1)S(1)} %bitcast.26, bf16[16,224]{1,0:T(8,128)(2,1)} %param.11, f32[224]{0:T(256)} %param.12), kind=kOutput, calls=%fused_computation.105 | convolution fusion | flops 19278336 | bytes 1384320 | tf_op jit(solution)/shard_map/dot_general | solution.py:66
  4.7 0.1 fusion.52
  4.8 0.1 concatenate.18
  4.9 2.5 %collective-permute-start = (f32[16,2944]{1,0:T(8,128)S(1)}, f32[16,2944]{1,0:T(8,128)S(1)}, u32[]{:S(2)}, u32[]{:S(2)}) collective-permute-start(f32[16,2944]{1,0:T(8,128)S(1)} %concatenate.18), channel_id=1, source_target_pairs={{0,8},{8,0},{16,24},{24,16},{32,40},{40,32},{48,56},{56,48},{64,72... | collective-permute-start | bytes 565256 | tf_op jit(solution)/shard_map/ppermute | solution.py:18
  7.4 3.4 %collective-permute-done = f32[16,2944]{1,0:T(8,128)S(1)} collective-permute-done((f32[16,2944]{1,0:T(8,128)S(1)}, f32[16,2944]{1,0:T(8,128)S(1)}, u32[]{:S(2)}, u32[]{:S(2)}) %collective-permute-start) | collective-permute-done | bytes 188448 | tf_op jit(solution)/shard_map/ppermute | solution.py:18
  10.9 4.0 %collective-permute-start.1 = (f32[16,2944]{1,0:T(8,128)S(1)}, f32[16,2944]{1,0:T(8,128)S(1)}, u32[]{:S(2)}, u32[]{:S(2)}) collective-permute-start(f32[16,2944]{1,0:T(8,128)S(1)} %add.96), channel_id=1, source_target_pairs={{0,16},{8,24},{16,0},{24,8},{32,48},{40,56},{48,32},{56,40},{64,80... | collective-permute-start | bytes 565256 | tf_op jit(solution)/shard_map/ppermute | solution.py:18
  15.0 8.1 %collective-permute-done.1 = f32[16,2944]{1,0:T(8,128)S(1)} collective-permute-done((f32[16,2944]{1,0:T(8,128)S(1)}, f32[16,2944]{1,0:T(8,128)S(1)}, u32[]{:S(2)}, u32[]{:S(2)}) %collective-permute-start.1) | collective-permute-done | bytes 188448 | tf_op jit(solution)/shard_map/ppermute | solution.py:18
  23.1 6.5 %collective-permute-start.2 = (f32[16,2944]{1,0:T(8,128)S(1)}, f32[16,2944]{1,0:T(8,128)S(1)}, u32[]{:S(2)}, u32[]{:S(2)}) collective-permute-start(f32[16,2944]{1,0:T(8,128)S(1)} %add.97), channel_id=1, source_target_pairs={{0,32},{8,40},{16,48},{24,56},{32,0},{40,8},{48,16},{56,24},{64,96... | collective-permute-start | bytes 565256 | tf_op jit(solution)/shard_map/ppermute | solution.py:18
  29.7 6.9 %collective-permute-done.2 = f32[16,2944]{1,0:T(8,128)S(1)} collective-permute-done((f32[16,2944]{1,0:T(8,128)S(1)}, f32[16,2944]{1,0:T(8,128)S(1)}, u32[]{:S(2)}, u32[]{:S(2)}) %collective-permute-start.2) | collective-permute-done | bytes 188448 | tf_op jit(solution)/shard_map/ppermute | solution.py:18
  36.6 1.3 %collective-permute-start.3 = (f32[16,2944]{1,0:T(8,128)S(1)}, f32[16,2944]{1,0:T(8,128)S(1)}, u32[]{:S(2)}, u32[]{:S(2)}) collective-permute-start(f32[16,2944]{1,0:T(8,128)S(1)} %add.98), channel_id=1, source_target_pairs={{0,64},{8,72},{16,80},{24,88},{32,96},{40,104},{48,112},{56,120},{... | collective-permute-start | bytes 565256 | tf_op jit(solution)/shard_map/ppermute | solution.py:18
  37.9 0.1 fusion.32
  38.1 3.0 %collective-permute-done.3 = f32[16,2944]{1,0:T(8,128)S(1)} collective-permute-done((f32[16,2944]{1,0:T(8,128)S(1)}, f32[16,2944]{1,0:T(8,128)S(1)}, u32[]{:S(2)}, u32[]{:S(2)}) %collective-permute-start.3) | collective-permute-done | bytes 188448 | tf_op jit(solution)/shard_map/ppermute | solution.py:18
  41.1 2.8 %collective-permute-start.4 = (f32[16,2944]{1,0:T(8,128)S(1)}, f32[16,2944]{1,0:T(8,128)S(1)}, u32[]{:S(2)}, u32[]{:S(2)}) collective-permute-start(f32[16,2944]{1,0:T(8,128)S(1)} %add.99), channel_id=1, source_target_pairs={{0,128},{8,136},{16,144},{24,152},{32,160},{40,168},{48,176},{56,1... | collective-permute-start | bytes 565256 | tf_op jit(solution)/shard_map/ppermute | solution.py:18
  44.1 3.3 %collective-permute-done.4 = f32[16,2944]{1,0:T(8,128)S(1)} collective-permute-done((f32[16,2944]{1,0:T(8,128)S(1)}, f32[16,2944]{1,0:T(8,128)S(1)}, u32[]{:S(2)}, u32[]{:S(2)}) %collective-permute-start.4) | collective-permute-done | bytes 188448 | tf_op jit(solution)/shard_map/ppermute | solution.py:18
  47.5 0.1 fusion.50
  47.6 0.2 fusion.20
  47.9 3.2 %fusion.72 = (f32[4,16]{1,0:T(4,128)S(1)}, f32[4,16,512]{2,1,0:T(8,128)S(1)}) fusion(pred[4,16,512]{2,1,0:T(8,128)(4,1)S(1)} %reshape.218, bf16[4,512,896]{2,1,0:T(8,128)(2,1)} %param.17, bf16[4,16,896]{2,1,0:T(8,128)(2,1)S(1)} %broadcast_in_dim.136, pred[16,896]{1,0:T(8,128)(4,1)S(1)} %broadcast_in_dim.130), kind=kOutput, calls=%fused_computation.125 | convolution fusion | flops 58875840 | bytes 3963136 | tf_op jit(solution)/shard_map/rnc,rpc->rnp/dot_general | solution.py:90
  51.1 0.1 reshape.222
  51.2 0.2 fusion.4
  51.4 2.7 %fusion.6 = f32[4,16,896]{2,1,0:T(8,128)S(1)} fusion(bf16[4,512,896]{2,1,0:T(8,128)(2,1)} %param.18, f32[4,16,512]{2,1,0:T(8,128)S(1)} %get-tuple-element.31, f32[4,16]{1,0:T(4,128)S(1)} %get-tuple-element.30, u8[16,512]{1,0:T(8,128)(4,1)S(1)} %fusion.27), kind=kOutput, calls=%fused_computation.14 | convolution fusion | flops 58949632 | bytes 4038912 | tf_op jit(solution)/shard_map/rnp,rpc->rnc/dot_general | solution.py:106
  54.2 0.1 reshape.224
  54.3 0.1 copy.66
  54.4 0.1 copy.64
  54.7 3.1 %collective-permute-done.5 = f32[16,1024]{1,0:T(8,128)S(1)} collective-permute-done((f32[16,1024]{1,0:T(8,128)S(1)}, f32[16,1024]{1,0:T(8,128)S(1)}, u32[]{:S(2)}, u32[]{:S(2)}) %collective-permute-start.5) | collective-permute-done | bytes 65568 | tf_op jit(solution)/shard_map/ppermute | solution.py:36
  57.8 0.1 fusion.46
  58.0 0.1 reshape.226
  58.1 0.1 reshape.227
  58.3 4.0 %collective-permute-start.6 = (f32[16,1024]{1,0:T(8,128)S(1)}, f32[16,1024]{1,0:T(8,128)S(1)}, u32[]{:S(2)}, u32[]{:S(2)}) collective-permute-start(f32[16,1024]{1,0:T(8,128)S(1)} %maximum_maximum_fusion.1), channel_id=1, source_target_pairs={{0,16},{8,24},{16,0},{24,8},{32,48},{40,56},{48,32},{56,40},{64,80... | collective-permute-start | bytes 196616 | tf_op jit(solution)/shard_map/ppermute | solution.py:36
  62.4 0.1 fusion.23
  62.4 0.1 reshape.236
  62.5 0.1 reshape.237
  62.6 1.4 %collective-permute-done.6 = f32[16,1024]{1,0:T(8,128)S(1)} collective-permute-done((f32[16,1024]{1,0:T(8,128)S(1)}, f32[16,1024]{1,0:T(8,128)S(1)}, u32[]{:S(2)}, u32[]{:S(2)}) %collective-permute-start.6) | collective-permute-done | bytes 65568 | tf_op jit(solution)/shard_map/ppermute | solution.py:36
  64.0 0.1 fusion.45
  64.2 0.1 reshape.228
  64.4 0.1 reshape.229
  64.6 4.1 %collective-permute-start.7 = (f32[16,1024]{1,0:T(8,128)S(1)}, f32[16,1024]{1,0:T(8,128)S(1)}, u32[]{:S(2)}, u32[]{:S(2)}) collective-permute-start(f32[16,1024]{1,0:T(8,128)S(1)} %maximum_maximum_fusion.2), channel_id=1, source_target_pairs={{0,32},{8,40},{16,48},{24,56},{32,0},{40,8},{48,16},{56,24},{64,96... | collective-permute-start | bytes 196616 | tf_op jit(solution)/shard_map/ppermute | solution.py:36
  68.7 0.2 fusion.71
  68.9 0.1 copy.60
  69.0 0.1 reshape.240
  69.1 3.2 %collective-permute-done.7 = f32[16,1024]{1,0:T(8,128)S(1)} collective-permute-done((f32[16,1024]{1,0:T(8,128)S(1)}, f32[16,1024]{1,0:T(8,128)S(1)}, u32[]{:S(2)}, u32[]{:S(2)}) %collective-permute-start.7) | collective-permute-done | bytes 65568 | tf_op jit(solution)/shard_map/ppermute | solution.py:36
  72.3 0.1 fusion.44
  72.5 0.1 reshape.230
  72.7 0.1 reshape.231
  72.9 1.2 %collective-permute-start.8 = (f32[16,1024]{1,0:T(8,128)S(1)}, f32[16,1024]{1,0:T(8,128)S(1)}, u32[]{:S(2)}, u32[]{:S(2)}) collective-permute-start(f32[16,1024]{1,0:T(8,128)S(1)} %maximum_maximum_fusion.3), channel_id=1, source_target_pairs={{0,64},{8,72},{16,80},{24,88},{32,96},{40,104},{48,112},{56,120},{... | collective-permute-start | bytes 196616 | tf_op jit(solution)/shard_map/ppermute | solution.py:36
  74.1 0.7 pad_maximum_fusion
  74.8 1.5 %collective-permute-done.8 = f32[16,1024]{1,0:T(8,128)S(1)} collective-permute-done((f32[16,1024]{1,0:T(8,128)S(1)}, f32[16,1024]{1,0:T(8,128)S(1)}, u32[]{:S(2)}, u32[]{:S(2)}) %collective-permute-start.8) | collective-permute-done | bytes 65568 | tf_op jit(solution)/shard_map/ppermute | solution.py:36
  76.5 0.1 reshape.232
  76.7 0.1 reshape.233
  76.9 2.8 %collective-permute-start.9 = (f32[16,1024]{1,0:T(8,128)S(1)}, f32[16,1024]{1,0:T(8,128)S(1)}, u32[]{:S(2)}, u32[]{:S(2)}) collective-permute-start(f32[16,1024]{1,0:T(8,128)S(1)} %maximum_maximum_fusion.4), channel_id=1, source_target_pairs={{0,128},{8,136},{16,144},{24,152},{32,160},{40,168},{48,176},{56,1... | collective-permute-start | bytes 196616 | tf_op jit(solution)/shard_map/ppermute | solution.py:36
  79.7 1.8 %collective-permute-done.9 = f32[16,1024]{1,0:T(8,128)S(1)} collective-permute-done((f32[16,1024]{1,0:T(8,128)S(1)}, f32[16,1024]{1,0:T(8,128)S(1)}, u32[]{:S(2)}, u32[]{:S(2)}) %collective-permute-start.9) | collective-permute-done | bytes 65568 | tf_op jit(solution)/shard_map/ppermute | solution.py:36
  81.6 0.1 copy.53
  81.8 0.2 convolution_bitcast_fusion
  82.0 0.1 reshape.242
  82.1 0.1 copy.63
  82.2 0.1 fusion.42
  82.4 0.1 reshape.234
  82.6 0.1 reshape.235
  82.8 0.1 reshape.239
  83.0 0.1 reshape.244
  83.1 0.2 fusion.33
  83.2 20.6 %psum.7 = f32[16,112]{1,0:T(8,128)} all-reduce(f32[16,112]{1,0:T(8,128)S(1)} %fusion.33), channel_id=1, replica_groups=mesh['seq'=32,'tensor'=8] {'tensor'}, use_global_device_ids=true, to_apply=%region_6.7 | all-reduce | flops 1792 | bytes 14336 | tf_op jit(solution)/shard_map/psum | solution.py:152
  (68 shorter events, 2.5 us)
Async XLA Ops:
  0.6 47.0 %copy-start = (bf16[128,896]{1,0:T(8,128)(2,1)S(1)}, bf16[128,896]{1,0:T(8,128)(2,1)}, u32[]{:S(2)}) copy-start(bf16[128,896]{1,0:T(8,128)(2,1)} %param.15) | copy-start | bytes 688132
  0.6 4.0 %copy-start.2 = (bf16[16,224]{1,0:T(8,128)(2,1)S(1)}, bf16[16,224]{1,0:T(8,128)(2,1)}, u32[]{:S(2)}) copy-start(bf16[16,224]{1,0:T(8,128)(2,1)} %param.11) | copy-start | bytes 21508
  0.7 4.0 %copy-start.4 = (f32[224]{0:T(256)S(1)}, f32[224]{0:T(256)}, u32[]{:S(2)}) copy-start(f32[224]{0:T(256)} %param.12) | copy-start | bytes 2692
  0.7 4.0 %copy-start.3 = (bf16[224,128]{1,0:T(8,128)(2,1)S(1)}, bf16[224,128]{1,0:T(8,128)(2,1)}, u32[]{:S(2)}) copy-start(bf16[224,128]{1,0:T(8,128)(2,1)} %param.14) | copy-start | bytes 172036
  0.7 14.2 %copy-start.5 = (s32[4]{0:T(128)S(1)}, s32[4]{0:T(128)}, u32[]{:S(2)}) copy-start(s32[4]{0:T(128)} %param.19) | copy-start | bytes 52
  0.7 14.2 %copy-start.6 = (s32[4]{0:T(128)S(1)}, s32[4]{0:T(128)}, u32[]{:S(2)}) copy-start(s32[4]{0:T(128)} %param.20) | copy-start | bytes 52
  0.7 37.2 %copy-start.7 = (s32[4]{0:T(128)S(1)}, s32[4]{0:T(128)}, u32[]{:S(2)}) copy-start(s32[4]{0:T(128)} %param.21) | copy-start | bytes 52
  4.9 5.9 %collective-permute-start = (f32[16,2944]{1,0:T(8,128)S(1)}, f32[16,2944]{1,0:T(8,128)S(1)}, u32[]{:S(2)}, u32[]{:S(2)}) collective-permute-start(f32[16,2944]{1,0:T(8,128)S(1)} %concatenate.18), channel_id=1, source_target_pairs={{0,8},{8,0},{16,24},{24,16},{32,40},{40,32},{48,56},{56,48},{64,72... | collective-permute-start | bytes 565256 | tf_op jit(solution)/shard_map/ppermute | solution.py:18
  10.9 12.2 %collective-permute-start.1 = (f32[16,2944]{1,0:T(8,128)S(1)}, f32[16,2944]{1,0:T(8,128)S(1)}, u32[]{:S(2)}, u32[]{:S(2)}) collective-permute-start(f32[16,2944]{1,0:T(8,128)S(1)} %add.96), channel_id=1, source_target_pairs={{0,16},{8,24},{16,0},{24,8},{32,48},{40,56},{48,32},{56,40},{64,80... | collective-permute-start | bytes 565256 | tf_op jit(solution)/shard_map/ppermute | solution.py:18
  23.1 13.5 %collective-permute-start.2 = (f32[16,2944]{1,0:T(8,128)S(1)}, f32[16,2944]{1,0:T(8,128)S(1)}, u32[]{:S(2)}, u32[]{:S(2)}) collective-permute-start(f32[16,2944]{1,0:T(8,128)S(1)} %add.97), channel_id=1, source_target_pairs={{0,32},{8,40},{16,48},{24,56},{32,0},{40,8},{48,16},{56,24},{64,96... | collective-permute-start | bytes 565256 | tf_op jit(solution)/shard_map/ppermute | solution.py:18
  36.6 4.5 %collective-permute-start.3 = (f32[16,2944]{1,0:T(8,128)S(1)}, f32[16,2944]{1,0:T(8,128)S(1)}, u32[]{:S(2)}, u32[]{:S(2)}) collective-permute-start(f32[16,2944]{1,0:T(8,128)S(1)} %add.98), channel_id=1, source_target_pairs={{0,64},{8,72},{16,80},{24,88},{32,96},{40,104},{48,112},{56,120},{... | collective-permute-start | bytes 565256 | tf_op jit(solution)/shard_map/ppermute | solution.py:18
  41.1 6.3 %collective-permute-start.4 = (f32[16,2944]{1,0:T(8,128)S(1)}, f32[16,2944]{1,0:T(8,128)S(1)}, u32[]{:S(2)}, u32[]{:S(2)}) collective-permute-start(f32[16,2944]{1,0:T(8,128)S(1)} %add.99), channel_id=1, source_target_pairs={{0,128},{8,136},{16,144},{24,152},{32,160},{40,168},{48,176},{56,1... | collective-permute-start | bytes 565256 | tf_op jit(solution)/shard_map/ppermute | solution.py:18
  54.1 29.0 %copy-start.1 = (bf16[896,112]{0,1:T(8,128)(2,1)S(1)}, bf16[896,112]{0,1:T(8,128)(2,1)}, u32[]{:S(2)}) copy-start(bf16[896,112]{0,1:T(8,128)(2,1)} %param.16) | copy-start | bytes 602116
  54.6 3.1 %collective-permute-start.5 = (f32[16,1024]{1,0:T(8,128)S(1)}, f32[16,1024]{1,0:T(8,128)S(1)}, u32[]{:S(2)}, u32[]{:S(2)}) collective-permute-start(f32[16,1024]{1,0:T(8,128)S(1)} %maximum_maximum_fusion), channel_id=1, source_target_pairs={{0,8},{8,0},{16,24},{24,16},{32,40},{40,32},{48,56},{56,48},{64,72... | collective-permute-start | bytes 196616 | tf_op jit(solution)/shard_map/ppermute | solution.py:36
  58.3 5.7 %collective-permute-start.6 = (f32[16,1024]{1,0:T(8,128)S(1)}, f32[16,1024]{1,0:T(8,128)S(1)}, u32[]{:S(2)}, u32[]{:S(2)}) collective-permute-start(f32[16,1024]{1,0:T(8,128)S(1)} %maximum_maximum_fusion.1), channel_id=1, source_target_pairs={{0,16},{8,24},{16,0},{24,8},{32,48},{40,56},{48,32},{56,40},{64,80... | collective-permute-start | bytes 196616 | tf_op jit(solution)/shard_map/ppermute | solution.py:36
  64.6 7.7 %collective-permute-start.7 = (f32[16,1024]{1,0:T(8,128)S(1)}, f32[16,1024]{1,0:T(8,128)S(1)}, u32[]{:S(2)}, u32[]{:S(2)}) collective-permute-start(f32[16,1024]{1,0:T(8,128)S(1)} %maximum_maximum_fusion.2), channel_id=1, source_target_pairs={{0,32},{8,40},{16,48},{24,56},{32,0},{40,8},{48,16},{56,24},{64,96... | collective-permute-start | bytes 196616 | tf_op jit(solution)/shard_map/ppermute | solution.py:36
  72.9 3.4 %collective-permute-start.8 = (f32[16,1024]{1,0:T(8,128)S(1)}, f32[16,1024]{1,0:T(8,128)S(1)}, u32[]{:S(2)}, u32[]{:S(2)}) collective-permute-start(f32[16,1024]{1,0:T(8,128)S(1)} %maximum_maximum_fusion.3), channel_id=1, source_target_pairs={{0,64},{8,72},{16,80},{24,88},{32,96},{40,104},{48,112},{56,120},{... | collective-permute-start | bytes 196616 | tf_op jit(solution)/shard_map/ppermute | solution.py:36
  76.9 4.6 %collective-permute-start.9 = (f32[16,1024]{1,0:T(8,128)S(1)}, f32[16,1024]{1,0:T(8,128)S(1)}, u32[]{:S(2)}, u32[]{:S(2)}) collective-permute-start(f32[16,1024]{1,0:T(8,128)S(1)} %maximum_maximum_fusion.4), channel_id=1, source_target_pairs={{0,128},{8,136},{16,144},{24,152},{32,160},{40,168},{48,176},{56,1... | collective-permute-start | bytes 196616 | tf_op jit(solution)/shard_map/ppermute | solution.py:36

commit v2 on v1

--- a/solution.py
+++ b/solution.py
@@ -52,6 +52,7 @@
     sinks,
     windows,
     seq_size,
+    tensor_size,
 ):
     rows = features.shape[0]
     count, span = cached_key_rows.shape[0], cached_key_rows.shape[1]
@@ -62,23 +63,25 @@
 
     feat = features.astype(f32)
     scaled = (feat * input_norm_scale).astype(bf16)
-    weights = query_key_value_weight.reshape(query_key_value_weight.shape[0], 3 * local)
-    partial_proj = jnp.dot(scaled, weights, preferred_element_type=f32)
+
+    def project(j):
+        return jnp.dot(scaled, query_key_value_weight[:, j, :], preferred_element_type=f32)
+
     partial_low = jnp.dot(scaled, adapter_down_weight, preferred_element_type=f32)
     partial_sq = jnp.sum(feat * feat, axis=1, keepdims=True)
     packed = jnp.concatenate(
-        [partial_proj, partial_low, partial_sq, jnp.zeros((rows, 127), f32)], axis=1
+        [project(0), partial_low, partial_sq, jnp.zeros((rows, 127), f32)], axis=1
     )
     summed = butterfly_sum(packed, "seq", seq_size)
-    projected = summed[:, : 3 * local]
-    low = summed[:, 3 * local : 3 * local + rank]
-    total_sq = summed[:, 3 * local + rank]
+    kv_summed = butterfly_sum(jnp.concatenate([project(1), project(2)], axis=1), "seq", seq_size)
+    low = summed[:, local : local + rank]
+    total_sq = summed[:, local + rank]
     scale_rows = lax.rsqrt(total_sq / INPUT_WIDTH + 1e-05)[:, None]
     lowrank = (low * scale_rows).astype(bf16)
     query_adapter = jnp.dot(lowrank, adapter_up_weight, preferred_element_type=f32)
-    queries = (projected[:, :local] * scale_rows + query_adapter).astype(bf16)
-    keys_full = projected[:, local : 2 * local] * scale_rows
-    values_full = projected[:, 2 * local :] * scale_rows
+    queries = (summed[:, :local] * scale_rows + query_adapter).astype(bf16)
+    keys_full = kv_summed[:, :local] * scale_rows
+    values_full = kv_summed[:, local:] * scale_rows
     new_keys = keys_full.astype(bf16)
     new_values = values_full.astype(bf16)
 
@@ -149,7 +152,7 @@
     total = cache_total * cache_scale + own_total
     attn = (output / jnp.repeat(total, HD, axis=1)).astype(bf16)
     partial_out = jnp.dot(attn, output_weight, preferred_element_type=f32)
-    mixed = lax.psum(partial_out, "tensor")
+    mixed = butterfly_sum(partial_out, "tensor", tensor_size)
     return (mixed, jnp.stack([keys_full, values_full]))
 
 
@@ -168,9 +171,9 @@
         P(),
     )
     out_specs = (P(None, "seq"), P(None, None, "tensor"))
-    seq_size = mesh.shape["seq"]
+    seq_size, tensor_size = mesh.shape["seq"], mesh.shape["tensor"]
 
     def body(*args):
-        return shards(*args, seq_size)
+        return shards(*args, seq_size, tensor_size)
 
     return jax.shard_map(body, mesh=mesh, in_specs=in_specs, out_specs=out_specs, check_vma=False)

time: 104 us -> 91.7 us (0.88)
  the two profiles are of different devices: /device:TPU:1 before, /device:TPU:4 now
where the time goes in v2:
time: 91.7 us; the launch traced here: 91.4 us
  waiting for transfers between devices  35.8 us (39%)
  starting transfers between devices  33.6 us (37%)
  matrix products  11.2 us (12%)
  other arithmetic  6.04 us (7%)
  local copies, waits for them, and re-layouts  3.84 us (4%)
  between operations  0.99 us (1%)
    ppermute x13, starting transfers between devices, butterfly_sum(): x = x + lax.ppermute(x, axis, [(i, i ^ step) for i in range(size)])  26.6 us
    ppermute x13, waiting for transfers between devices, butterfly_sum(): x = x + lax.ppermute(x, axis, [(i, i ^ step) for i in range(size)])  18.7 us
    ppermute x5, waiting for transfers between devices, butterfly_softmax(): other = lax.ppermute(x, axis, [(i, i ^ step) for i in range(size)])  17.1 us
    ppermute x5, starting transfers between devices, butterfly_softmax(): other = lax.ppermute(x, axis, [(i, i ^ step) for i in range(size)])  6.98 us
    dot_general x3, matrix products, project(): jnp.dot(scaled, query_key_value_weight[:, j, :], preferred_element_type=f32)  3.6 us
    dot_general x1, matrix products, shards(): jnp.einsum('rnc,rpc->rnp', q_block, cached_key_rows, preferred_element_ty...  3.17 us
    dot_general x1, matrix products, shards(): jnp.einsum('rnp,rpc->rnc', expo.astype(bf16), cached_value_rows, preferre...  2.68 us
  transfers between devices with their start and end apart: 18, of which 13 were waited for; matrix products, arithmetic and copies ran while one was open for 16% of the time, Pallas kernels for 0%

profile of v2, /device:TPU:4, one launch (start us, length us, event | category | flops | bytes accessed | tf_op | source)
XLA Modules:
  0.0 91.4 jit_solution(15388809390665166221)
XLA Ops:
  0.6 0.9 fusion.45
  1.6 1.0 %fusion.72 = f32[16,128]{1,0:T(8,128)S(1)} fusion(bf16[224,128]{1,0:T(8,128)(2,1)} %param.14, bf16[16,224]{1,0:T(8,128)(2,1)} %param.11, f32[224]{0:T(256)} %param.12), kind=kOutput, calls=%fused_computation.123 | convolution fusion | flops 928256 | bytes 73600 | tf_op jit(solution)/shard_map/dot_general | solution.py:70
  2.6 1.2 %fusion.6 = f32[16,896]{1,0:T(8,128)S(1)} fusion(bf16[224,3,896]{2,0,1:T(8,128)(2,1)} %param.13, bf16[16,224]{1,0:T(8,128)(2,1)} %param.11, f32[224]{0:T(256)} %param.12), kind=kOutput, calls=%fused_computation.9 | convolution fusion | flops 6433280 | bytes 467968 | tf_op jit(solution)/shard_map/dot_general | solution.py:68
  3.9 1.9 %collective-permute-start = (f32[16,1152]{1,0:T(8,128)S(1)}, f32[16,1152]{1,0:T(8,128)S(1)}, u32[]{:S(2)}, u32[]{:S(2)}) collective-permute-start(f32[16,1152]{1,0:T(8,128)S(1)} %concatenate.21), channel_id=1, source_target_pairs={{0,8},{8,0},{16,24},{24,16},{32,40},{40,32},{48,56},{56,48},{64,72... | collective-permute-start | bytes 221192 | tf_op jit(solution)/shard_map/ppermute | solution.py:18
  5.8 1.2 %fusion.2 = f32[16,896]{1,0:T(8,128)S(1)} fusion(bf16[224,3,896]{2,0,1:T(8,128)(2,1)} %param.13, bf16[16,224]{1,0:T(8,128)(2,1)} %param.11, f32[224]{0:T(256)} %param.12), kind=kOutput, calls=%fused_computation.5 | convolution fusion | flops 6433280 | bytes 467968 | tf_op jit(solution)/shard_map/dot_general | solution.py:68
  7.0 1.2 %fusion.4 = f32[16,896]{1,0:T(8,128)S(1)} fusion(bf16[224,3,896]{2,0,1:T(8,128)(2,1)} %param.13, bf16[16,224]{1,0:T(8,128)(2,1)} %param.11, f32[224]{0:T(256)} %param.12), kind=kOutput, calls=%fused_computation.7 | convolution fusion | flops 6433280 | bytes 467968 | tf_op jit(solution)/shard_map/dot_general | solution.py:68
  8.2 0.2 collective-permute-start.10
  8.4 0.7 broadcast_compare_fusion.1
  9.2 0.7 iota_add_fusion
  9.9 3.4 %collective-permute-start.1 = (f32[16,1152]{1,0:T(8,128)S(1)}, f32[16,1152]{1,0:T(8,128)S(1)}, u32[]{:S(2)}, u32[]{:S(2)}) collective-permute-start(f32[16,1152]{1,0:T(8,128)S(1)} %add.118), channel_id=1, source_target_pairs={{0,16},{8,24},{16,0},{24,8},{32,48},{40,56},{48,32},{56,40},{64,80... | collective-permute-start | bytes 221192 | tf_op jit(solution)/shard_map/ppermute | solution.py:18
  13.3 0.7 fusion.41
  14.0 2.3 %collective-permute-done.1 = f32[16,1152]{1,0:T(8,128)S(1)} collective-permute-done((f32[16,1152]{1,0:T(8,128)S(1)}, f32[16,1152]{1,0:T(8,128)S(1)}, u32[]{:S(2)}, u32[]{:S(2)}) %collective-permute-start.1) | collective-permute-done | bytes 73760 | tf_op jit(solution)/shard_map/ppermute | solution.py:18
  16.4 7.0 %collective-permute-start.2 = (f32[16,1152]{1,0:T(8,128)S(1)}, f32[16,1152]{1,0:T(8,128)S(1)}, u32[]{:S(2)}, u32[]{:S(2)}) collective-permute-start(f32[16,1152]{1,0:T(8,128)S(1)} %add.119), channel_id=1, source_target_pairs={{0,32},{8,40},{16,48},{24,56},{32,0},{40,8},{48,16},{56,24},{64,96... | collective-permute-start | bytes 221192 | tf_op jit(solution)/shard_map/ppermute | solution.py:18
  23.4 2.3 %collective-permute-done.2 = f32[16,1152]{1,0:T(8,128)S(1)} collective-permute-done((f32[16,1152]{1,0:T(8,128)S(1)}, f32[16,1152]{1,0:T(8,128)S(1)}, u32[]{:S(2)}, u32[]{:S(2)}) %collective-permute-start.2) | collective-permute-done | bytes 73760 | tf_op jit(solution)/shard_map/ppermute | solution.py:18
  25.7 1.3 %collective-permute-start.3 = (f32[16,1152]{1,0:T(8,128)S(1)}, f32[16,1152]{1,0:T(8,128)S(1)}, u32[]{:S(2)}, u32[]{:S(2)}) collective-permute-start(f32[16,1152]{1,0:T(8,128)S(1)} %add.120), channel_id=1, source_target_pairs={{0,64},{8,72},{16,80},{24,88},{32,96},{40,104},{48,112},{56,120},{... | collective-permute-start | bytes 221192 | tf_op jit(solution)/shard_map/ppermute | solution.py:18
  27.2 3.6 %collective-permute-done.3 = f32[16,1152]{1,0:T(8,128)S(1)} collective-permute-done((f32[16,1152]{1,0:T(8,128)S(1)}, f32[16,1152]{1,0:T(8,128)S(1)}, u32[]{:S(2)}, u32[]{:S(2)}) %collective-permute-start.3) | collective-permute-done | bytes 73760 | tf_op jit(solution)/shard_map/ppermute | solution.py:18
  30.8 1.9 %collective-permute-start.4 = (f32[16,1152]{1,0:T(8,128)S(1)}, f32[16,1152]{1,0:T(8,128)S(1)}, u32[]{:S(2)}, u32[]{:S(2)}) collective-permute-start(f32[16,1152]{1,0:T(8,128)S(1)} %add.121), channel_id=1, source_target_pairs={{0,128},{8,136},{16,144},{24,152},{32,160},{40,168},{48,176},{56,1... | collective-permute-start | bytes 221192 | tf_op jit(solution)/shard_map/ppermute | solution.py:18
  32.8 3.9 %collective-permute-done.4 = f32[16,1152]{1,0:T(8,128)S(1)} collective-permute-done((f32[16,1152]{1,0:T(8,128)S(1)}, f32[16,1152]{1,0:T(8,128)S(1)}, u32[]{:S(2)}, u32[]{:S(2)}) %collective-permute-start.4) | collective-permute-done | bytes 73760 | tf_op jit(solution)/shard_map/ppermute | solution.py:18
  36.7 0.1 fusion.59
  36.9 0.2 fusion.29
  37.2 3.2 %fusion.83 = (f32[4,16]{1,0:T(4,128)S(1)}, f32[4,16,512]{2,1,0:T(8,128)S(1)}) fusion(pred[4,16,512]{2,1,0:T(8,128)(4,1)S(1)} %reshape.215, bf16[4,512,896]{2,1,0:T(8,128)(2,1)} %param.17, bf16[4,16,896]{2,1,0:T(8,128)(2,1)S(1)} %broadcast_in_dim.136, pred[16,896]{1,0:T(8,128)(4,1)S(1)} %broadcast_in_dim.130), kind=kOutput, calls=%fused_computation.135 | convolution fusion | flops 58875840 | bytes 3963136 | tf_op jit(solution)/shard_map/rnc,rpc->rnp/dot_general | solution.py:93
  40.5 0.2 fusion.13
  40.7 0.1 copy.64
  40.8 0.1 copy.62
  40.9 2.7 %fusion.15 = f32[4,16,896]{2,1,0:T(8,128)S(1)} fusion(bf16[4,512,896]{2,1,0:T(8,128)(2,1)} %param.18, f32[4,16,512]{2,1,0:T(8,128)S(1)} %get-tuple-element.31, f32[4,16]{1,0:T(4,128)S(1)} %get-tuple-element.30, u8[16,512]{1,0:T(8,128)(4,1)S(1)} %fusion.36), kind=kOutput, calls=%fused_computation.24 | convolution fusion | flops 58949632 | bytes 4038912 | tf_op jit(solution)/shard_map/rnp,rpc->rnc/dot_general | solution.py:109
  43.9 1.2 %collective-permute-start.5 = (f32[16,1024]{1,0:T(8,128)S(1)}, f32[16,1024]{1,0:T(8,128)S(1)}, u32[]{:S(2)}, u32[]{:S(2)}) collective-permute-start(f32[16,1024]{1,0:T(8,128)S(1)} %maximum_maximum_fusion), channel_id=1, source_target_pairs={{0,8},{8,0},{16,24},{24,16},{32,40},{40,32},{48,56},{56,48},{64,72... | collective-permute-start | bytes 196616 | tf_op jit(solution)/shard_map/ppermute | solution.py:36
  45.1 5.3 %collective-permute-start.12 = (f32[16,1792]{1,0:T(8,128)S(1)}, f32[16,1792]{1,0:T(8,128)S(1)}, u32[]{:S(2)}, u32[]{:S(2)}) collective-permute-start(f32[16,1792]{1,0:T(8,128)S(1)} %add.135), channel_id=1, source_target_pairs={{0,32},{8,40},{16,48},{24,56},{32,0},{40,8},{48,16},{56,24},{64,96... | collective-permute-start | bytes 344072 | tf_op jit(solution)/shard_map/ppermute | solution.py:18
  50.6 0.1 reshape.222
  50.8 0.1 reshape.223
  51.0 2.1 %collective-permute-start.6 = (f32[16,1024]{1,0:T(8,128)S(1)}, f32[16,1024]{1,0:T(8,128)S(1)}, u32[]{:S(2)}, u32[]{:S(2)}) collective-permute-start(f32[16,1024]{1,0:T(8,128)S(1)} %maximum_maximum_fusion.1), channel_id=1, source_target_pairs={{0,16},{8,24},{16,0},{24,8},{32,48},{40,56},{48,32},{56,40},{64,80... | collective-permute-start | bytes 196616 | tf_op jit(solution)/shard_map/ppermute | solution.py:36
  53.1 1.5 %collective-permute-done.12 = f32[16,1792]{1,0:T(8,128)S(1)} collective-permute-done((f32[16,1792]{1,0:T(8,128)S(1)}, f32[16,1792]{1,0:T(8,128)S(1)}, u32[]{:S(2)}, u32[]{:S(2)}) %collective-permute-start.12) | collective-permute-done | bytes 114720 | tf_op jit(solution)/shard_map/ppermute | solution.py:18
  54.6 0.6 collective-permute-start.13
  55.2 3.9 %collective-permute-done.6 = f32[16,1024]{1,0:T(8,128)S(1)} collective-permute-done((f32[16,1024]{1,0:T(8,128)S(1)}, f32[16,1024]{1,0:T(8,128)S(1)}, u32[]{:S(2)}, u32[]{:S(2)}) %collective-permute-start.6) | collective-permute-done | bytes 65568 | tf_op jit(solution)/shard_map/ppermute | solution.py:36
  59.3 0.1 reshape.224
  59.5 0.1 reshape.225
  59.7 3.2 %collective-permute-start.7 = (f32[16,1024]{1,0:T(8,128)S(1)}, f32[16,1024]{1,0:T(8,128)S(1)}, u32[]{:S(2)}, u32[]{:S(2)}) collective-permute-start(f32[16,1024]{1,0:T(8,128)S(1)} %maximum_maximum_fusion.2), channel_id=1, source_target_pairs={{0,32},{8,40},{16,48},{24,56},{32,0},{40,8},{48,16},{56,24},{64,96... | collective-permute-start | bytes 196616 | tf_op jit(solution)/shard_map/ppermute | solution.py:36
  63.1 4.7 %collective-permute-done.7 = f32[16,1024]{1,0:T(8,128)S(1)} collective-permute-done((f32[16,1024]{1,0:T(8,128)S(1)}, f32[16,1024]{1,0:T(8,128)S(1)}, u32[]{:S(2)}, u32[]{:S(2)}) %collective-permute-start.7) | collective-permute-done | bytes 65568 | tf_op jit(solution)/shard_map/ppermute | solution.py:36
  68.0 0.1 reshape.226
  68.2 0.1 reshape.227
  68.4 0.5 collective-permute-start.8
  68.9 0.5 collective-permute-done.14
  69.5 0.1 reshape.233
  69.6 0.2 fusion.82
  69.9 0.1 copy.58
  70.0 2.7 %collective-permute-done.8 = f32[16,1024]{1,0:T(8,128)S(1)} collective-permute-done((f32[16,1024]{1,0:T(8,128)S(1)}, f32[16,1024]{1,0:T(8,128)S(1)}, u32[]{:S(2)}, u32[]{:S(2)}) %collective-permute-start.8) | collective-permute-done | bytes 65568 | tf_op jit(solution)/shard_map/ppermute | solution.py:36
  72.9 0.1 reshape.228
  73.1 0.1 reshape.229
  73.4 5.7 %collective-permute-done.9 = f32[16,1024]{1,0:T(8,128)S(1)} collective-permute-done((f32[16,1024]{1,0:T(8,128)S(1)}, f32[16,1024]{1,0:T(8,128)S(1)}, u32[]{:S(2)}, u32[]{:S(2)}) %collective-permute-start.9) | collective-permute-done | bytes 65568 | tf_op jit(solution)/shard_map/ppermute | solution.py:36
  79.2 0.1 copy.51
  79.3 0.2 convolution_bitcast_fusion
  79.6 0.1 reshape.238
  79.7 0.1 copy.61
  80.0 0.1 reshape.240
  80.2 0.1 reshape.230
  80.3 0.1 reshape.231
  80.5 0.1 reshape.235
  80.6 0.2 fusion.42
  80.8 1.2 %collective-permute-done.15 = f32[16,112]{1,0:T(8,128)S(1)} collective-permute-done((f32[16,112]{1,0:T(8,128)S(1)}, f32[16,112]{1,0:T(8,128)S(1)}, u32[]{:S(2)}, u32[]{:S(2)}) %collective-permute-start.15) | collective-permute-done | bytes 7200 | tf_op jit(solution)/shard_map/ppermute | solution.py:18
  82.0 1.6 %collective-permute-start.16 = (f32[16,112]{1,0:T(8,128)S(1)}, f32[16,112]{1,0:T(8,128)S(1)}, u32[]{:S(2)}, u32[]{:S(2)}) collective-permute-start(f32[16,112]{1,0:T(8,128)S(1)} %add.142), channel_id=1, source_target_pairs={{0,2},{1,3},{2,0},{3,1},{4,6},{5,7},{6,4},{7,5},{8,10},{9,11},{10,... | collective-permute-start | bytes 21512 | tf_op jit(solution)/shard_map/ppermute | solution.py:18
  83.6 2.1 %collective-permute-done.16 = f32[16,112]{1,0:T(8,128)S(1)} collective-permute-done((f32[16,112]{1,0:T(8,128)S(1)}, f32[16,112]{1,0:T(8,128)S(1)}, u32[]{:S(2)}, u32[]{:S(2)}) %collective-permute-start.16) | collective-permute-done | bytes 7200 | tf_op jit(solution)/shard_map/ppermute | solution.py:18
  85.7 3.2 %collective-permute-start.17 = (f32[16,112]{1,0:T(8,128)S(1)}, f32[16,112]{1,0:T(8,128)S(1)}, u32[]{:S(2)}, u32[]{:S(2)}) collective-permute-start(f32[16,112]{1,0:T(8,128)S(1)} %add.143), channel_id=1, source_target_pairs={{0,4},{1,5},{2,6},{3,7},{4,0},{5,1},{6,2},{7,3},{8,12},{9,13},{10,... | collective-permute-start | bytes 21512 | tf_op jit(solution)/shard_map/ppermute | solution.py:18
  88.9 0.7 pad_maximum_fusion.1
  89.5 1.3 %collective-permute-done.17 = f32[16,112]{1,0:T(8,128)S(1)} collective-permute-done((f32[16,112]{1,0:T(8,128)S(1)}, f32[16,112]{1,0:T(8,128)S(1)}, u32[]{:S(2)}, u32[]{:S(2)}) %collective-permute-start.17) | collective-permute-done | bytes 7200 | tf_op jit(solution)/shard_map/ppermute | solution.py:18
  90.8 0.6 add.144
  (81 shorter events, 3.5 us)
Async XLA Ops:
  0.6 36.2 %copy-start = (bf16[128,896]{1,0:T(8,128)(2,1)S(1)}, bf16[128,896]{1,0:T(8,128)(2,1)}, u32[]{:S(2)}) copy-start(bf16[128,896]{1,0:T(8,128)(2,1)} %param.15) | copy-start | bytes 688132
  3.9 6.0 %collective-permute-start = (f32[16,1152]{1,0:T(8,128)S(1)}, f32[16,1152]{1,0:T(8,128)S(1)}, u32[]{:S(2)}, u32[]{:S(2)}) collective-permute-start(f32[16,1152]{1,0:T(8,128)S(1)} %concatenate.21), channel_id=1, source_target_pairs={{0,8},{8,0},{16,24},{24,16},{32,40},{40,32},{48,56},{56,48},{64,72... | collective-permute-start | bytes 221192 | tf_op jit(solution)/shard_map/ppermute | solution.py:18
  8.2 24.5 %collective-permute-start.10 = (f32[16,1792]{1,0:T(8,128)S(1)}, f32[16,1792]{1,0:T(8,128)S(1)}, u32[]{:S(2)}, u32[]{:S(2)}) collective-permute-start(f32[16,1792]{1,0:T(8,128)S(1)} %pad_maximum_fusion), channel_id=1, source_target_pairs={{0,8},{8,0},{16,24},{24,16},{32,40},{40,32},{48,56},{56,48},{64,72... | collective-permute-start | bytes 344072 | tf_op jit(solution)/shard_map/ppermute | solution.py:18
  9.9 6.4 %collective-permute-start.1 = (f32[16,1152]{1,0:T(8,128)S(1)}, f32[16,1152]{1,0:T(8,128)S(1)}, u32[]{:S(2)}, u32[]{:S(2)}) collective-permute-start(f32[16,1152]{1,0:T(8,128)S(1)} %add.118), channel_id=1, source_target_pairs={{0,16},{8,24},{16,0},{24,8},{32,48},{40,56},{48,32},{56,40},{64,80... | collective-permute-start | bytes 221192 | tf_op jit(solution)/shard_map/ppermute | solution.py:18
  16.4 9.3 %collective-permute-start.2 = (f32[16,1152]{1,0:T(8,128)S(1)}, f32[16,1152]{1,0:T(8,128)S(1)}, u32[]{:S(2)}, u32[]{:S(2)}) collective-permute-start(f32[16,1152]{1,0:T(8,128)S(1)} %add.119), channel_id=1, source_target_pairs={{0,32},{8,40},{16,48},{24,56},{32,0},{40,8},{48,16},{56,24},{64,96... | collective-permute-start | bytes 221192 | tf_op jit(solution)/shard_map/ppermute | solution.py:18
  25.7 5.1 %collective-permute-start.3 = (f32[16,1152]{1,0:T(8,128)S(1)}, f32[16,1152]{1,0:T(8,128)S(1)}, u32[]{:S(2)}, u32[]{:S(2)}) collective-permute-start(f32[16,1152]{1,0:T(8,128)S(1)} %add.120), channel_id=1, source_target_pairs={{0,64},{8,72},{16,80},{24,88},{32,96},{40,104},{48,112},{56,120},{... | collective-permute-start | bytes 221192 | tf_op jit(solution)/shard_map/ppermute | solution.py:18
  30.8 5.9 %collective-permute-start.4 = (f32[16,1152]{1,0:T(8,128)S(1)}, f32[16,1152]{1,0:T(8,128)S(1)}, u32[]{:S(2)}, u32[]{:S(2)}) collective-permute-start(f32[16,1152]{1,0:T(8,128)S(1)} %add.121), channel_id=1, source_target_pairs={{0,128},{8,136},{16,144},{24,152},{32,160},{40,168},{48,176},{56,1... | collective-permute-start | bytes 221192 | tf_op jit(solution)/shard_map/ppermute | solution.py:18
  32.7 12.3 %collective-permute-start.11 = (f32[16,1792]{1,0:T(8,128)S(1)}, f32[16,1792]{1,0:T(8,128)S(1)}, u32[]{:S(2)}, u32[]{:S(2)}) collective-permute-start(f32[16,1792]{1,0:T(8,128)S(1)} %fusion.81), channel_id=1, source_target_pairs={{0,16},{8,24},{16,0},{24,8},{32,48},{40,56},{48,32},{56,40},{64,80... | collective-permute-start | bytes 344072 | tf_op jit(solution)/shard_map/ppermute | solution.py:18
  43.8 36.8 %copy-start.1 = (bf16[896,112]{0,1:T(8,128)(2,1)S(1)}, bf16[896,112]{0,1:T(8,128)(2,1)}, u32[]{:S(2)}) copy-start(bf16[896,112]{0,1:T(8,128)(2,1)} %param.16) | copy-start | bytes 602116
  43.9 6.5 %collective-permute-start.5 = (f32[16,1024]{1,0:T(8,128)S(1)}, f32[16,1024]{1,0:T(8,128)S(1)}, u32[]{:S(2)}, u32[]{:S(2)}) collective-permute-start(f32[16,1024]{1,0:T(8,128)S(1)} %maximum_maximum_fusion), channel_id=1, source_target_pairs={{0,8},{8,0},{16,24},{24,16},{32,40},{40,32},{48,56},{56,48},{64,72... | collective-permute-start | bytes 196616 | tf_op jit(solution)/shard_map/ppermute | solution.py:36
  45.1 9.5 %collective-permute-start.12 = (f32[16,1792]{1,0:T(8,128)S(1)}, f32[16,1792]{1,0:T(8,128)S(1)}, u32[]{:S(2)}, u32[]{:S(2)}) collective-permute-start(f32[16,1792]{1,0:T(8,128)S(1)} %add.135), channel_id=1, source_target_pairs={{0,32},{8,40},{16,48},{24,56},{32,0},{40,8},{48,16},{56,24},{64,96... | collective-permute-start | bytes 344072 | tf_op jit(solution)/shard_map/ppermute | solution.py:18
  51.0 8.1 %collective-permute-start.6 = (f32[16,1024]{1,0:T(8,128)S(1)}, f32[16,1024]{1,0:T(8,128)S(1)}, u32[]{:S(2)}, u32[]{:S(2)}) collective-permute-start(f32[16,1024]{1,0:T(8,128)S(1)} %maximum_maximum_fusion.1), channel_id=1, source_target_pairs={{0,16},{8,24},{16,0},{24,8},{32,48},{40,56},{48,32},{56,40},{64,80... | collective-permute-start | bytes 196616 | tf_op jit(solution)/shard_map/ppermute | solution.py:36
  54.6 8.4 %collective-permute-start.13 = (f32[16,1792]{1,0:T(8,128)S(1)}, f32[16,1792]{1,0:T(8,128)S(1)}, u32[]{:S(2)}, u32[]{:S(2)}) collective-permute-start(f32[16,1792]{1,0:T(8,128)S(1)} %add.136), channel_id=1, source_target_pairs={{0,64},{8,72},{16,80},{24,88},{32,96},{40,104},{48,112},{56,120},{... | collective-permute-start | bytes 344072 | tf_op jit(solution)/shard_map/ppermute | solution.py:18
  59.7 8.2 %collective-permute-start.7 = (f32[16,1024]{1,0:T(8,128)S(1)}, f32[16,1024]{1,0:T(8,128)S(1)}, u32[]{:S(2)}, u32[]{:S(2)}) collective-permute-start(f32[16,1024]{1,0:T(8,128)S(1)} %maximum_maximum_fusion.2), channel_id=1, source_target_pairs={{0,32},{8,40},{16,48},{24,56},{32,0},{40,8},{48,16},{56,24},{64,96... | collective-permute-start | bytes 196616 | tf_op jit(solution)/shard_map/ppermute | solution.py:36
  63.0 6.4 %collective-permute-start.14 = (f32[16,1792]{1,0:T(8,128)S(1)}, f32[16,1792]{1,0:T(8,128)S(1)}, u32[]{:S(2)}, u32[]{:S(2)}) collective-permute-start(f32[16,1792]{1,0:T(8,128)S(1)} %add.137), channel_id=1, source_target_pairs={{0,128},{8,136},{16,144},{24,152},{32,160},{40,168},{48,176},{56,1... | collective-permute-start | bytes 344072 | tf_op jit(solution)/shard_map/ppermute | solution.py:18
  68.4 4.3 %collective-permute-start.8 = (f32[16,1024]{1,0:T(8,128)S(1)}, f32[16,1024]{1,0:T(8,128)S(1)}, u32[]{:S(2)}, u32[]{:S(2)}) collective-permute-start(f32[16,1024]{1,0:T(8,128)S(1)} %maximum_maximum_fusion.3), channel_id=1, source_target_pairs={{0,64},{8,72},{16,80},{24,88},{32,96},{40,104},{48,112},{56,120},{... | collective-permute-start | bytes 196616 | tf_op jit(solution)/shard_map/ppermute | solution.py:36
  73.3 5.8 %collective-permute-start.9 = (f32[16,1024]{1,0:T(8,128)S(1)}, f32[16,1024]{1,0:T(8,128)S(1)}, u32[]{:S(2)}, u32[]{:S(2)}) collective-permute-start(f32[16,1024]{1,0:T(8,128)S(1)} %maximum_maximum_fusion.4), channel_id=1, source_target_pairs={{0,128},{8,136},{16,144},{24,152},{32,160},{40,168},{48,176},{56,1... | collective-permute-start | bytes 196616 | tf_op jit(solution)/shard_map/ppermute | solution.py:36
  80.8 1.2 %collective-permute-start.15 = (f32[16,112]{1,0:T(8,128)S(1)}, f32[16,112]{1,0:T(8,128)S(1)}, u32[]{:S(2)}, u32[]{:S(2)}) collective-permute-start(f32[16,112]{1,0:T(8,128)S(1)} %fusion.42), channel_id=1, source_target_pairs={{0,1},{1,0},{2,3},{3,2},{4,5},{5,4},{6,7},{7,6},{8,9},{9,8},{10,11... | collective-permute-start | bytes 21512 | tf_op jit(solution)/shard_map/ppermute | solution.py:18
  82.0 3.7 %collective-permute-start.16 = (f32[16,112]{1,0:T(8,128)S(1)}, f32[16,112]{1,0:T(8,128)S(1)}, u32[]{:S(2)}, u32[]{:S(2)}) collective-permute-start(f32[16,112]{1,0:T(8,128)S(1)} %add.142), channel_id=1, source_target_pairs={{0,2},{1,3},{2,0},{3,1},{4,6},{5,7},{6,4},{7,5},{8,10},{9,11},{10,... | collective-permute-start | bytes 21512 | tf_op jit(solution)/shard_map/ppermute | solution.py:18
  85.7 5.2 %collective-permute-start.17 = (f32[16,112]{1,0:T(8,128)S(1)}, f32[16,112]{1,0:T(8,128)S(1)}, u32[]{:S(2)}, u32[]{:S(2)}) collective-permute-start(f32[16,112]{1,0:T(8,128)S(1)} %add.143), channel_id=1, source_target_pairs={{0,4},{1,5},{2,6},{3,7},{4,0},{5,1},{6,2},{7,3},{8,12},{9,13},{10,... | collective-permute-start | bytes 21512 | tf_op jit(solution)/shard_map/ppermute | solution.py:18

commit v3 on v2

--- a/solution.py
+++ b/solution.py
@@ -12,11 +12,21 @@
 CUT = -1e29
 
 
-def butterfly_sum(x, axis, size):
-    step = 1
-    while step < size:
-        x = x + lax.ppermute(x, axis, [(i, i ^ step) for i in range(size)])
-        step *= 2
+def butterfly_masks(axes):
+    masks, shift = [], 0
+    for size in reversed(axes):
+        bit = 1
+        while bit < size:
+            masks.append((bit if 2 * bit < size or size <= 2 else size - 2 if size > 4 else size - 1) << shift)
+            bit *= 2
+        shift += size.bit_length() - 1
+    return masks
+
+
+def butterfly_sum(x, axis, masks):
+    size = 1 << len(masks)
+    for mask in masks:
+        x = x + lax.ppermute(x, axis, [(i, i ^ mask) for i in range(size)])
     return x
 
 
@@ -30,13 +40,20 @@
     return jnp.concatenate([values, totals, top, jnp.zeros((a.shape[0], pad), jnp.float32)], axis=1)
 
 
-def butterfly_softmax(x, axis, size, width, heads):
-    step = 1
-    while step < size:
-        other = lax.ppermute(x, axis, [(i, i ^ step) for i in range(size)])
+def butterfly_softmax(x, axis, masks, width, heads):
+    size = 1 << len(masks)
+    for mask in masks:
+        other = lax.ppermute(x, axis, [(i, i ^ mask) for i in range(size)])
         x = merge_softmax(x, other, width, heads)
-        step *= 2
     return x
+
+
+RINGS = {"seq": {32: (4, 8)}, "tensor": {8: (4, 2)}}
+
+
+def axis_masks(axis, size):
+    rings = RINGS[axis].get(size, (size,))
+    return butterfly_masks(rings)
 
 
 def shards(
@@ -51,8 +68,8 @@
     lengths,
     sinks,
     windows,
-    seq_size,
-    tensor_size,
+    seq_masks,
+    tensor_masks,
 ):
     rows = features.shape[0]
     count, span = cached_key_rows.shape[0], cached_key_rows.shape[1]
@@ -72,8 +89,8 @@
     packed = jnp.concatenate(
         [project(0), partial_low, partial_sq, jnp.zeros((rows, 127), f32)], axis=1
     )
-    summed = butterfly_sum(packed, "seq", seq_size)
-    kv_summed = butterfly_sum(jnp.concatenate([project(1), project(2)], axis=1), "seq", seq_size)
+    summed = butterfly_sum(packed, "seq", seq_masks)
+    kv_summed = butterfly_sum(jnp.concatenate([project(1), project(2)], axis=1), "seq", seq_masks)
     low = summed[:, local : local + rank]
     total_sq = summed[:, local + rank]
     scale_rows = lax.rsqrt(total_sq / INPUT_WIDTH + 1e-05)[:, None]
@@ -126,7 +143,7 @@
         ],
         axis=1,
     )
-    merged = butterfly_softmax(packed, "seq", seq_size, local, heads)
+    merged = butterfly_softmax(packed, "seq", seq_masks, local, heads)
     cache_out = merged[:, :local]
     cache_total = merged[:, local : local + heads]
     cache_top = merged[:, local + heads : local + 2 * heads]
@@ -152,7 +169,7 @@
     total = cache_total * cache_scale + own_total
     attn = (output / jnp.repeat(total, HD, axis=1)).astype(bf16)
     partial_out = jnp.dot(attn, output_weight, preferred_element_type=f32)
-    mixed = butterfly_sum(partial_out, "tensor", tensor_size)
+    mixed = butterfly_sum(partial_out, "tensor", tensor_masks)
     return (mixed, jnp.stack([keys_full, values_full]))
 
 
@@ -171,9 +188,10 @@
         P(),
     )
     out_specs = (P(None, "seq"), P(None, None, "tensor"))
-    seq_size, tensor_size = mesh.shape["seq"], mesh.shape["tensor"]
+    seq_masks = axis_masks("seq", mesh.shape["seq"])
+    tensor_masks = axis_masks("tensor", mesh.shape["tensor"])
 
     def body(*args):
-        return shards(*args, seq_size, tensor_size)
+        return shards(*args, seq_masks, tensor_masks)
 
     return jax.shard_map(body, mesh=mesh, in_specs=in_specs, out_specs=out_specs, check_vma=False)

time: 91.7 us -> 83.7 us (0.913)
  the two profiles are of different devices: /device:TPU:4 before, /device:TPU:1 now
where the time goes in v3:
time: 83.7 us; the launch traced here: 82.3 us
  starting transfers between devices  43.6 us (52%)
  waiting for transfers between devices  16.6 us (20%)
  matrix products  11.2 us (13%)
  other arithmetic  6.04 us (7%)
  local copies, waits for them, and re-layouts  3.84 us (5%)
  between operations  0.98 us (1%)
    ppermute x13, starting transfers between devices, butterfly_sum(): x = x + lax.ppermute(x, axis, [(i, i ^ mask) for i in range(size)])  37.1 us
    ppermute x13, waiting for transfers between devices, butterfly_sum(): x = x + lax.ppermute(x, axis, [(i, i ^ mask) for i in range(size)])  10 us
    ppermute x5, starting transfers between devices, butterfly_softmax(): other = lax.ppermute(x, axis, [(i, i ^ mask) for i in range(size)])  6.55 us
    ppermute x5, waiting for transfers between devices, butterfly_softmax(): other = lax.ppermute(x, axis, [(i, i ^ mask) for i in range(size)])  6.53 us
    dot_general x3, matrix products, project(): jnp.dot(scaled, query_key_value_weight[:, j, :], preferred_element_type=f32)  3.6 us
    dot_general x1, matrix products, shards(): jnp.einsum('rnc,rpc->rnp', q_block, cached_key_rows, preferred_element_ty...  3.17 us
    dot_general x1, matrix products, shards(): jnp.einsum('rnp,rpc->rnc', expo.astype(bf16), cached_value_rows, preferre...  2.68 us
  transfers between devices with their start and end apart: 18, of which 12 were waited for; matrix products, arithmetic and copies ran while one was open for 18% of the time, Pallas kernels for 0%

profile of v3, /device:TPU:1, one launch (start us, length us, event | category | flops | bytes accessed | tf_op | source)
XLA Modules:
  0.0 82.3 jit_solution(7186739237668357336)
XLA Ops:
  0.6 0.9 %fusion.45 = f32[16]{0:T(128)S(1)} fusion(bf16[16,224]{1,0:T(8,128)(2,1)} %param.11), kind=kLoop, calls=%fused_computation.71 | loop fusion | flops 10736 | bytes 7232 | tf_op jit(solution)/shard_map/reduce_sum | solution.py:88
  1.6 1.0 %fusion.72 = f32[16,128]{1,0:T(8,128)S(1)} fusion(bf16[224,128]{1,0:T(8,128)(2,1)} %param.14, bf16[16,224]{1,0:T(8,128)(2,1)} %param.11, f32[224]{0:T(256)} %param.12), kind=kOutput, calls=%fused_computation.123 | convolution fusion | flops 928256 | bytes 73600 | tf_op jit(solution)/shard_map/dot_general | solution.py:87
  2.6 1.2 %fusion.6 = f32[16,896]{1,0:T(8,128)S(1)} fusion(bf16[224,3,896]{2,0,1:T(8,128)(2,1)} %param.13, bf16[16,224]{1,0:T(8,128)(2,1)} %param.11, f32[224]{0:T(256)} %param.12), kind=kOutput, calls=%fused_computation.9 | convolution fusion | flops 6433280 | bytes 467968 | tf_op jit(solution)/shard_map/dot_general | solution.py:85
  3.9 2.5 %collective-permute-start = (f32[16,1152]{1,0:T(8,128)S(1)}, f32[16,1152]{1,0:T(8,128)S(1)}, u32[]{:S(2)}, u32[]{:S(2)}) collective-permute-start(f32[16,1152]{1,0:T(8,128)S(1)} %concatenate.21), channel_id=1, source_target_pairs={{0,8},{8,0},{16,24},{24,16},{32,40},{40,32},{48,56},{56,48},{64,72... | collective-permute-start | bytes 221192 | tf_op jit(solution)/shard_map/ppermute | solution.py:29
  6.4 1.2 %fusion.2 = f32[16,896]{1,0:T(8,128)S(1)} fusion(bf16[224,3,896]{2,0,1:T(8,128)(2,1)} %param.13, bf16[16,224]{1,0:T(8,128)(2,1)} %param.11, f32[224]{0:T(256)} %param.12), kind=kOutput, calls=%fused_computation.5 | convolution fusion | flops 6433280 | bytes 467968 | tf_op jit(solution)/shard_map/dot_general | solution.py:85
  7.6 1.2 %fusion.4 = f32[16,896]{1,0:T(8,128)S(1)} fusion(bf16[224,3,896]{2,0,1:T(8,128)(2,1)} %param.13, bf16[16,224]{1,0:T(8,128)(2,1)} %param.11, f32[224]{0:T(256)} %param.12), kind=kOutput, calls=%fused_computation.7 | convolution fusion | flops 6433280 | bytes 467968 | tf_op jit(solution)/shard_map/dot_general | solution.py:85
  8.8 0.1 collective-permute-start.10
  8.9 0.7 broadcast_compare_fusion.1
  9.7 0.7 iota_add_fusion
  10.4 3.1 %collective-permute-start.1 = (f32[16,1152]{1,0:T(8,128)S(1)}, f32[16,1152]{1,0:T(8,128)S(1)}, u32[]{:S(2)}, u32[]{:S(2)}) collective-permute-start(f32[16,1152]{1,0:T(8,128)S(1)} %add.118), channel_id=1, source_target_pairs={{0,16},{8,24},{16,0},{24,8},{32,48},{40,56},{48,32},{56,40},{64,80... | collective-permute-start | bytes 221192 | tf_op jit(solution)/shard_map/ppermute | solution.py:29
  13.5 0.7 fusion.41
  14.2 1.0 %collective-permute-done.1 = f32[16,1152]{1,0:T(8,128)S(1)} collective-permute-done((f32[16,1152]{1,0:T(8,128)S(1)}, f32[16,1152]{1,0:T(8,128)S(1)}, u32[]{:S(2)}, u32[]{:S(2)}) %collective-permute-start.1) | collective-permute-done | bytes 73760 | tf_op jit(solution)/shard_map/ppermute | solution.py:29
  15.2 5.4 %collective-permute-start.2 = (f32[16,1152]{1,0:T(8,128)S(1)}, f32[16,1152]{1,0:T(8,128)S(1)}, u32[]{:S(2)}, u32[]{:S(2)}) collective-permute-start(f32[16,1152]{1,0:T(8,128)S(1)} %add.119), channel_id=1, source_target_pairs={{0,48},{8,56},{16,32},{24,40},{32,16},{40,24},{48,0},{56,8},{64,11... | collective-permute-start | bytes 221192 | tf_op jit(solution)/shard_map/ppermute | solution.py:29
  20.6 2.0 %collective-permute-done.2 = f32[16,1152]{1,0:T(8,128)S(1)} collective-permute-done((f32[16,1152]{1,0:T(8,128)S(1)}, f32[16,1152]{1,0:T(8,128)S(1)}, u32[]{:S(2)}, u32[]{:S(2)}) %collective-permute-start.2) | collective-permute-done | bytes 73760 | tf_op jit(solution)/shard_map/ppermute | solution.py:29
  22.6 1.3 %collective-permute-start.3 = (f32[16,1152]{1,0:T(8,128)S(1)}, f32[16,1152]{1,0:T(8,128)S(1)}, u32[]{:S(2)}, u32[]{:S(2)}) collective-permute-start(f32[16,1152]{1,0:T(8,128)S(1)} %add.120), channel_id=1, source_target_pairs={{0,64},{8,72},{16,80},{24,88},{32,96},{40,104},{48,112},{56,120},{... | collective-permute-start | bytes 221192 | tf_op jit(solution)/shard_map/ppermute | solution.py:29
  24.1 1.8 %collective-permute-done.3 = f32[16,1152]{1,0:T(8,128)S(1)} collective-permute-done((f32[16,1152]{1,0:T(8,128)S(1)}, f32[16,1152]{1,0:T(8,128)S(1)}, u32[]{:S(2)}, u32[]{:S(2)}) %collective-permute-start.3) | collective-permute-done | bytes 73760 | tf_op jit(solution)/shard_map/ppermute | solution.py:29
  25.9 2.6 %collective-permute-start.4 = (f32[16,1152]{1,0:T(8,128)S(1)}, f32[16,1152]{1,0:T(8,128)S(1)}, u32[]{:S(2)}, u32[]{:S(2)}) collective-permute-start(f32[16,1152]{1,0:T(8,128)S(1)} %add.121), channel_id=1, source_target_pairs={{0,192},{8,200},{16,208},{24,216},{32,224},{40,232},{48,240},{56,2... | collective-permute-start | bytes 221192 | tf_op jit(solution)/shard_map/ppermute | solution.py:29
  28.5 2.5 %collective-permute-start.11 = (f32[16,1792]{1,0:T(8,128)S(1)}, f32[16,1792]{1,0:T(8,128)S(1)}, u32[]{:S(2)}, u32[]{:S(2)}) collective-permute-start(f32[16,1792]{1,0:T(8,128)S(1)} %fusion.81), channel_id=1, source_target_pairs={{0,16},{8,24},{16,0},{24,8},{32,48},{40,56},{48,32},{56,40},{64,80... | collective-permute-start | bytes 344072 | tf_op jit(solution)/shard_map/ppermute | solution.py:29
  31.0 0.1 fusion.59
  31.1 0.2 fusion.29
  31.4 3.2 %fusion.83 = (f32[4,16]{1,0:T(4,128)S(1)}, f32[4,16,512]{2,1,0:T(8,128)S(1)}) fusion(pred[4,16,512]{2,1,0:T(8,128)(4,1)S(1)} %reshape.215, bf16[4,512,896]{2,1,0:T(8,128)(2,1)} %param.17, bf16[4,16,896]{2,1,0:T(8,128)(2,1)S(1)} %broadcast_in_dim.136, pred[16,896]{1,0:T(8,128)(4,1)S(1)} %broadcast_in_dim.130), kind=kOutput, calls=%fused_computation.135 | convolution fusion | flops 58875840 | bytes 3963136 | tf_op jit(solution)/shard_map/rnc,rpc->rnp/dot_general | solution.py:110
  34.7 0.2 fusion.13
  35.0 0.1 copy.64
  35.1 0.1 copy.62
  35.2 2.7 %fusion.15 = f32[4,16,896]{2,1,0:T(8,128)S(1)} fusion(bf16[4,512,896]{2,1,0:T(8,128)(2,1)} %param.18, f32[4,16,512]{2,1,0:T(8,128)S(1)} %get-tuple-element.31, f32[4,16]{1,0:T(4,128)S(1)} %get-tuple-element.30, u8[16,512]{1,0:T(8,128)(4,1)S(1)} %fusion.36), kind=kOutput, calls=%fused_computation.24 | convolution fusion | flops 58949632 | bytes 4038912 | tf_op jit(solution)/shard_map/rnp,rpc->rnc/dot_general | solution.py:126
  38.2 1.2 %collective-permute-start.5 = (f32[16,1024]{1,0:T(8,128)S(1)}, f32[16,1024]{1,0:T(8,128)S(1)}, u32[]{:S(2)}, u32[]{:S(2)}) collective-permute-start(f32[16,1024]{1,0:T(8,128)S(1)} %maximum_maximum_fusion), channel_id=1, source_target_pairs={{0,8},{8,0},{16,24},{24,16},{32,40},{40,32},{48,56},{56,48},{64,72... | collective-permute-start | bytes 196616 | tf_op jit(solution)/shard_map/ppermute | solution.py:46
  39.4 3.1 %collective-permute-start.12 = (f32[16,1792]{1,0:T(8,128)S(1)}, f32[16,1792]{1,0:T(8,128)S(1)}, u32[]{:S(2)}, u32[]{:S(2)}) collective-permute-start(f32[16,1792]{1,0:T(8,128)S(1)} %add.135), channel_id=1, source_target_pairs={{0,48},{8,56},{16,32},{24,40},{32,16},{40,24},{48,0},{56,8},{64,11... | collective-permute-start | bytes 344072 | tf_op jit(solution)/shard_map/ppermute | solution.py:29
  42.7 0.1 reshape.222
  42.8 0.1 reshape.223
  43.1 0.7 collective-permute-start.6
  43.7 1.6 %collective-permute-done.12 = f32[16,1792]{1,0:T(8,128)S(1)} collective-permute-done((f32[16,1792]{1,0:T(8,128)S(1)}, f32[16,1792]{1,0:T(8,128)S(1)}, u32[]{:S(2)}, u32[]{:S(2)}) %collective-permute-start.12) | collective-permute-done | bytes 114720 | tf_op jit(solution)/shard_map/ppermute | solution.py:29
  45.4 0.3 collective-permute-start.13
  45.7 2.0 %collective-permute-done.6 = f32[16,1024]{1,0:T(8,128)S(1)} collective-permute-done((f32[16,1024]{1,0:T(8,128)S(1)}, f32[16,1024]{1,0:T(8,128)S(1)}, u32[]{:S(2)}, u32[]{:S(2)}) %collective-permute-start.6) | collective-permute-done | bytes 65568 | tf_op jit(solution)/shard_map/ppermute | solution.py:46
  47.9 0.1 reshape.224
  48.1 0.1 reshape.225
  48.3 2.2 %collective-permute-start.7 = (f32[16,1024]{1,0:T(8,128)S(1)}, f32[16,1024]{1,0:T(8,128)S(1)}, u32[]{:S(2)}, u32[]{:S(2)}) collective-permute-start(f32[16,1024]{1,0:T(8,128)S(1)} %maximum_maximum_fusion.2), channel_id=1, source_target_pairs={{0,48},{8,56},{16,32},{24,40},{32,16},{40,24},{48,0},{56,8},{64,11... | collective-permute-start | bytes 196616 | tf_op jit(solution)/shard_map/ppermute | solution.py:46
  50.6 2.5 %collective-permute-start.14 = (f32[16,1792]{1,0:T(8,128)S(1)}, f32[16,1792]{1,0:T(8,128)S(1)}, u32[]{:S(2)}, u32[]{:S(2)}) collective-permute-start(f32[16,1792]{1,0:T(8,128)S(1)} %add.137), channel_id=1, source_target_pairs={{0,192},{8,200},{16,208},{24,216},{32,224},{40,232},{48,240},{56,2... | collective-permute-start | bytes 344072 | tf_op jit(solution)/shard_map/ppermute | solution.py:29
  53.2 0.4 collective-permute-done.7
  53.7 0.1 reshape.226
  53.9 0.1 reshape.227
  54.1 0.2 collective-permute-start.8
  54.3 1.3 %collective-permute-done.14 = f32[16,1792]{1,0:T(8,128)S(1)} collective-permute-done((f32[16,1792]{1,0:T(8,128)S(1)}, f32[16,1792]{1,0:T(8,128)S(1)}, u32[]{:S(2)}, u32[]{:S(2)}) %collective-permute-start.14) | collective-permute-done | bytes 114720 | tf_op jit(solution)/shard_map/ppermute | solution.py:29
  55.8 0.2 fusion.82
  56.0 0.1 copy.58
  56.1 2.1 %collective-permute-done.8 = f32[16,1024]{1,0:T(8,128)S(1)} collective-permute-done((f32[16,1024]{1,0:T(8,128)S(1)}, f32[16,1024]{1,0:T(8,128)S(1)}, u32[]{:S(2)}, u32[]{:S(2)}) %collective-permute-start.8) | collective-permute-done | bytes 65568 | tf_op jit(solution)/shard_map/ppermute | solution.py:46
  58.4 0.1 reshape.228
  58.6 0.1 reshape.229
  58.8 2.2 %collective-permute-start.9 = (f32[16,1024]{1,0:T(8,128)S(1)}, f32[16,1024]{1,0:T(8,128)S(1)}, u32[]{:S(2)}, u32[]{:S(2)}) collective-permute-start(f32[16,1024]{1,0:T(8,128)S(1)} %maximum_maximum_fusion.4), channel_id=1, source_target_pairs={{0,192},{8,200},{16,208},{24,216},{32,224},{40,232},{48,240},{56,2... | collective-permute-start | bytes 196616 | tf_op jit(solution)/shard_map/ppermute | solution.py:46
  61.1 2.1 %collective-permute-done.9 = f32[16,1024]{1,0:T(8,128)S(1)} collective-permute-done((f32[16,1024]{1,0:T(8,128)S(1)}, f32[16,1024]{1,0:T(8,128)S(1)}, u32[]{:S(2)}, u32[]{:S(2)}) %collective-permute-start.9) | collective-permute-done | bytes 65568 | tf_op jit(solution)/shard_map/ppermute | solution.py:46
  63.2 0.1 copy.51
  63.4 0.2 convolution_bitcast_fusion
  63.6 0.1 reshape.238
  63.7 0.1 copy.61
  64.0 0.1 reshape.240
  64.2 0.1 reshape.230
  64.7 0.2 fusion.42
  64.9 9.7 %collective-permute-start.15 = (f32[16,112]{1,0:T(8,128)S(1)}, f32[16,112]{1,0:T(8,128)S(1)}, u32[]{:S(2)}, u32[]{:S(2)}) collective-permute-start(f32[16,112]{1,0:T(8,128)S(1)} %fusion.42), channel_id=1, source_target_pairs={{0,1},{1,0},{2,3},{3,2},{4,5},{5,4},{6,7},{7,6},{8,9},{9,8},{10,11... | collective-permute-start | bytes 21512 | tf_op jit(solution)/shard_map/ppermute | solution.py:29
  74.6 0.8 %collective-permute-done.15 = f32[16,112]{1,0:T(8,128)S(1)} collective-permute-done((f32[16,112]{1,0:T(8,128)S(1)}, f32[16,112]{1,0:T(8,128)S(1)}, u32[]{:S(2)}, u32[]{:S(2)}) %collective-permute-start.15) | collective-permute-done | bytes 7200 | tf_op jit(solution)/shard_map/ppermute | solution.py:29
  75.4 1.3 %collective-permute-start.16 = (f32[16,112]{1,0:T(8,128)S(1)}, f32[16,112]{1,0:T(8,128)S(1)}, u32[]{:S(2)}, u32[]{:S(2)}) collective-permute-start(f32[16,112]{1,0:T(8,128)S(1)} %add.142), channel_id=1, source_target_pairs={{0,2},{1,3},{2,0},{3,1},{4,6},{5,7},{6,4},{7,5},{8,10},{9,11},{10,... | collective-permute-start | bytes 21512 | tf_op jit(solution)/shard_map/ppermute | solution.py:29
  76.7 1.2 %collective-permute-done.16 = f32[16,112]{1,0:T(8,128)S(1)} collective-permute-done((f32[16,112]{1,0:T(8,128)S(1)}, f32[16,112]{1,0:T(8,128)S(1)}, u32[]{:S(2)}, u32[]{:S(2)}) %collective-permute-start.16) | collective-permute-done | bytes 7200 | tf_op jit(solution)/shard_map/ppermute | solution.py:29
  77.9 2.7 %collective-permute-start.17 = (f32[16,112]{1,0:T(8,128)S(1)}, f32[16,112]{1,0:T(8,128)S(1)}, u32[]{:S(2)}, u32[]{:S(2)}) collective-permute-start(f32[16,112]{1,0:T(8,128)S(1)} %add.143), channel_id=1, source_target_pairs={{0,6},{1,7},{2,4},{3,5},{4,2},{5,3},{6,0},{7,1},{8,14},{9,15},{10,... | collective-permute-start | bytes 21512 | tf_op jit(solution)/shard_map/ppermute | solution.py:29
  80.6 0.7 pad_maximum_fusion.1
  81.3 0.4 collective-permute-done.17
  81.7 0.6 add.144
  (81 shorter events, 3.6 us)
Async XLA Ops:
  0.6 30.5 %copy-start = (bf16[128,896]{1,0:T(8,128)(2,1)S(1)}, bf16[128,896]{1,0:T(8,128)(2,1)}, u32[]{:S(2)}) copy-start(bf16[128,896]{1,0:T(8,128)(2,1)} %param.15) | copy-start | bytes 688132
  3.9 6.5 %collective-permute-start = (f32[16,1152]{1,0:T(8,128)S(1)}, f32[16,1152]{1,0:T(8,128)S(1)}, u32[]{:S(2)}, u32[]{:S(2)}) collective-permute-start(f32[16,1152]{1,0:T(8,128)S(1)} %concatenate.21), channel_id=1, source_target_pairs={{0,8},{8,0},{16,24},{24,16},{32,40},{40,32},{48,56},{56,48},{64,72... | collective-permute-start | bytes 221192 | tf_op jit(solution)/shard_map/ppermute | solution.py:29
  8.8 19.7 %collective-permute-start.10 = (f32[16,1792]{1,0:T(8,128)S(1)}, f32[16,1792]{1,0:T(8,128)S(1)}, u32[]{:S(2)}, u32[]{:S(2)}) collective-permute-start(f32[16,1792]{1,0:T(8,128)S(1)} %pad_maximum_fusion), channel_id=1, source_target_pairs={{0,8},{8,0},{16,24},{24,16},{32,40},{40,32},{48,56},{56,48},{64,72... | collective-permute-start | bytes 344072 | tf_op jit(solution)/shard_map/ppermute | solution.py:29
  10.4 4.8 %collective-permute-start.1 = (f32[16,1152]{1,0:T(8,128)S(1)}, f32[16,1152]{1,0:T(8,128)S(1)}, u32[]{:S(2)}, u32[]{:S(2)}) collective-permute-start(f32[16,1152]{1,0:T(8,128)S(1)} %add.118), channel_id=1, source_target_pairs={{0,16},{8,24},{16,0},{24,8},{32,48},{40,56},{48,32},{56,40},{64,80... | collective-permute-start | bytes 221192 | tf_op jit(solution)/shard_map/ppermute | solution.py:29
  15.2 7.4 %collective-permute-start.2 = (f32[16,1152]{1,0:T(8,128)S(1)}, f32[16,1152]{1,0:T(8,128)S(1)}, u32[]{:S(2)}, u32[]{:S(2)}) collective-permute-start(f32[16,1152]{1,0:T(8,128)S(1)} %add.119), channel_id=1, source_target_pairs={{0,48},{8,56},{16,32},{24,40},{32,16},{40,24},{48,0},{56,8},{64,11... | collective-permute-start | bytes 221192 | tf_op jit(solution)/shard_map/ppermute | solution.py:29
  22.6 3.3 %collective-permute-start.3 = (f32[16,1152]{1,0:T(8,128)S(1)}, f32[16,1152]{1,0:T(8,128)S(1)}, u32[]{:S(2)}, u32[]{:S(2)}) collective-permute-start(f32[16,1152]{1,0:T(8,128)S(1)} %add.120), channel_id=1, source_target_pairs={{0,64},{8,72},{16,80},{24,88},{32,96},{40,104},{48,112},{56,120},{... | collective-permute-start | bytes 221192 | tf_op jit(solution)/shard_map/ppermute | solution.py:29
  25.9 5.1 %collective-permute-start.4 = (f32[16,1152]{1,0:T(8,128)S(1)}, f32[16,1152]{1,0:T(8,128)S(1)}, u32[]{:S(2)}, u32[]{:S(2)}) collective-permute-start(f32[16,1152]{1,0:T(8,128)S(1)} %add.121), channel_id=1, source_target_pairs={{0,192},{8,200},{16,208},{24,216},{32,224},{40,232},{48,240},{56,2... | collective-permute-start | bytes 221192 | tf_op jit(solution)/shard_map/ppermute | solution.py:29
  28.5 10.9 %collective-permute-start.11 = (f32[16,1792]{1,0:T(8,128)S(1)}, f32[16,1792]{1,0:T(8,128)S(1)}, u32[]{:S(2)}, u32[]{:S(2)}) collective-permute-start(f32[16,1792]{1,0:T(8,128)S(1)} %fusion.81), channel_id=1, source_target_pairs={{0,16},{8,24},{16,0},{24,8},{32,48},{40,56},{48,32},{56,40},{64,80... | collective-permute-start | bytes 344072 | tf_op jit(solution)/shard_map/ppermute | solution.py:29
  38.1 26.6 %copy-start.1 = (bf16[896,112]{0,1:T(8,128)(2,1)S(1)}, bf16[896,112]{0,1:T(8,128)(2,1)}, u32[]{:S(2)}) copy-start(bf16[896,112]{0,1:T(8,128)(2,1)} %param.16) | copy-start | bytes 602116
  38.2 4.3 %collective-permute-start.5 = (f32[16,1024]{1,0:T(8,128)S(1)}, f32[16,1024]{1,0:T(8,128)S(1)}, u32[]{:S(2)}, u32[]{:S(2)}) collective-permute-start(f32[16,1024]{1,0:T(8,128)S(1)} %maximum_maximum_fusion), channel_id=1, source_target_pairs={{0,8},{8,0},{16,24},{24,16},{32,40},{40,32},{48,56},{56,48},{64,72... | collective-permute-start | bytes 196616 | tf_op jit(solution)/shard_map/ppermute | solution.py:46
  39.4 6.0 %collective-permute-start.12 = (f32[16,1792]{1,0:T(8,128)S(1)}, f32[16,1792]{1,0:T(8,128)S(1)}, u32[]{:S(2)}, u32[]{:S(2)}) collective-permute-start(f32[16,1792]{1,0:T(8,128)S(1)} %add.135), channel_id=1, source_target_pairs={{0,48},{8,56},{16,32},{24,40},{32,16},{40,24},{48,0},{56,8},{64,11... | collective-permute-start | bytes 344072 | tf_op jit(solution)/shard_map/ppermute | solution.py:29
  43.1 4.6 %collective-permute-start.6 = (f32[16,1024]{1,0:T(8,128)S(1)}, f32[16,1024]{1,0:T(8,128)S(1)}, u32[]{:S(2)}, u32[]{:S(2)}) collective-permute-start(f32[16,1024]{1,0:T(8,128)S(1)} %maximum_maximum_fusion.1), channel_id=1, source_target_pairs={{0,16},{8,24},{16,0},{24,8},{32,48},{40,56},{48,32},{56,40},{64,80... | collective-permute-start | bytes 196616 | tf_op jit(solution)/shard_map/ppermute | solution.py:46
  45.4 5.2 %collective-permute-start.13 = (f32[16,1792]{1,0:T(8,128)S(1)}, f32[16,1792]{1,0:T(8,128)S(1)}, u32[]{:S(2)}, u32[]{:S(2)}) collective-permute-start(f32[16,1792]{1,0:T(8,128)S(1)} %add.136), channel_id=1, source_target_pairs={{0,64},{8,72},{16,80},{24,88},{32,96},{40,104},{48,112},{56,120},{... | collective-permute-start | bytes 344072 | tf_op jit(solution)/shard_map/ppermute | solution.py:29
  48.3 5.3 %collective-permute-start.7 = (f32[16,1024]{1,0:T(8,128)S(1)}, f32[16,1024]{1,0:T(8,128)S(1)}, u32[]{:S(2)}, u32[]{:S(2)}) collective-permute-start(f32[16,1024]{1,0:T(8,128)S(1)} %maximum_maximum_fusion.2), channel_id=1, source_target_pairs={{0,48},{8,56},{16,32},{24,40},{32,16},{40,24},{48,0},{56,8},{64,11... | collective-permute-start | bytes 196616 | tf_op jit(solution)/shard_map/ppermute | solution.py:46
  50.6 4.9 %collective-permute-start.14 = (f32[16,1792]{1,0:T(8,128)S(1)}, f32[16,1792]{1,0:T(8,128)S(1)}, u32[]{:S(2)}, u32[]{:S(2)}) collective-permute-start(f32[16,1792]{1,0:T(8,128)S(1)} %add.137), channel_id=1, source_target_pairs={{0,192},{8,200},{16,208},{24,216},{32,224},{40,232},{48,240},{56,2... | collective-permute-start | bytes 344072 | tf_op jit(solution)/shard_map/ppermute | solution.py:29
  54.1 4.1 %collective-permute-start.8 = (f32[16,1024]{1,0:T(8,128)S(1)}, f32[16,1024]{1,0:T(8,128)S(1)}, u32[]{:S(2)}, u32[]{:S(2)}) collective-permute-start(f32[16,1024]{1,0:T(8,128)S(1)} %maximum_maximum_fusion.3), channel_id=1, source_target_pairs={{0,64},{8,72},{16,80},{24,88},{32,96},{40,104},{48,112},{56,120},{... | collective-permute-start | bytes 196616 | tf_op jit(solution)/shard_map/ppermute | solution.py:46
  58.8 4.4 %collective-permute-start.9 = (f32[16,1024]{1,0:T(8,128)S(1)}, f32[16,1024]{1,0:T(8,128)S(1)}, u32[]{:S(2)}, u32[]{:S(2)}) collective-permute-start(f32[16,1024]{1,0:T(8,128)S(1)} %maximum_maximum_fusion.4), channel_id=1, source_target_pairs={{0,192},{8,200},{16,208},{24,216},{32,224},{40,232},{48,240},{56,2... | collective-permute-start | bytes 196616 | tf_op jit(solution)/shard_map/ppermute | solution.py:46
  64.9 10.5 %collective-permute-start.15 = (f32[16,112]{1,0:T(8,128)S(1)}, f32[16,112]{1,0:T(8,128)S(1)}, u32[]{:S(2)}, u32[]{:S(2)}) collective-permute-start(f32[16,112]{1,0:T(8,128)S(1)} %fusion.42), channel_id=1, source_target_pairs={{0,1},{1,0},{2,3},{3,2},{4,5},{5,4},{6,7},{7,6},{8,9},{9,8},{10,11... | collective-permute-start | bytes 21512 | tf_op jit(solution)/shard_map/ppermute | solution.py:29
  75.4 2.5 %collective-permute-start.16 = (f32[16,112]{1,0:T(8,128)S(1)}, f32[16,112]{1,0:T(8,128)S(1)}, u32[]{:S(2)}, u32[]{:S(2)}) collective-permute-start(f32[16,112]{1,0:T(8,128)S(1)} %add.142), channel_id=1, source_target_pairs={{0,2},{1,3},{2,0},{3,1},{4,6},{5,7},{6,4},{7,5},{8,10},{9,11},{10,... | collective-permute-start | bytes 21512 | tf_op jit(solution)/shard_map/ppermute | solution.py:29
  77.9 3.8 %collective-permute-start.17 = (f32[16,112]{1,0:T(8,128)S(1)}, f32[16,112]{1,0:T(8,128)S(1)}, u32[]{:S(2)}, u32[]{:S(2)}) collective-permute-start(f32[16,112]{1,0:T(8,128)S(1)} %add.143), channel_id=1, source_target_pairs={{0,6},{1,7},{2,4},{3,5},{4,2},{5,3},{6,0},{7,1},{8,14},{9,15},{10,... | collective-permute-start | bytes 21512 | tf_op jit(solution)/shard_map/ppermute | solution.py:29

commit v4 on v3

--- a/solution.py
+++ b/solution.py
@@ -12,21 +12,31 @@
 CUT = -1e29
 
 
-def butterfly_masks(axes):
-    masks, shift = [], 0
+def butterfly_rounds(axes):
+    rounds, shift = [], 0
     for size in reversed(axes):
-        bit = 1
+        masks, bit = [], 1
         while bit < size:
             masks.append((bit if 2 * bit < size or size <= 2 else size - 2 if size > 4 else size - 1) << shift)
             bit *= 2
+        rounds += [tuple(masks[i : i + 2]) for i in range(0, len(masks), 2)]
         shift += size.bit_length() - 1
-    return masks
-
-
-def butterfly_sum(x, axis, masks):
-    size = 1 << len(masks)
-    for mask in masks:
-        x = x + lax.ppermute(x, axis, [(i, i ^ mask) for i in range(size)])
+    return rounds
+
+
+def exchange(x, axis, mask, size):
+    return lax.ppermute(x, axis, [(i, i ^ mask) for i in range(size)])
+
+
+def butterfly_sum(x, axis, rounds):
+    size = 1 << sum(len(r) for r in rounds)
+    for r in rounds:
+        if len(r) == 1:
+            x = x + exchange(x, axis, r[0], size)
+        else:
+            a, b = r
+            pa, pb, pc = (exchange(x, axis, m, size) for m in (a, b, a ^ b))
+            x = (x + pa) + (pb + pc)
     return x
 
 
@@ -40,11 +50,15 @@
     return jnp.concatenate([values, totals, top, jnp.zeros((a.shape[0], pad), jnp.float32)], axis=1)
 
 
-def butterfly_softmax(x, axis, masks, width, heads):
-    size = 1 << len(masks)
-    for mask in masks:
-        other = lax.ppermute(x, axis, [(i, i ^ mask) for i in range(size)])
-        x = merge_softmax(x, other, width, heads)
+def butterfly_softmax(x, axis, rounds, width, heads):
+    size = 1 << sum(len(r) for r in rounds)
+    for r in rounds:
+        if len(r) == 1:
+            x = merge_softmax(x, exchange(x, axis, r[0], size), width, heads)
+        else:
+            a, b = r
+            pa, pb, pc = (exchange(x, axis, m, size) for m in (a, b, a ^ b))
+            x = merge_softmax(merge_softmax(x, pa, width, heads), merge_softmax(pb, pc, width, heads), width, heads)
     return x
 
 
@@ -53,7 +67,7 @@
 
 def axis_masks(axis, size):
     rings = RINGS[axis].get(size, (size,))
-    return butterfly_masks(rings)
+    return butterfly_rounds(rings)
 
 
 def shards(

time: 83.7 us -> 83.1 us (level); the launches traced: 82.3 us -> 82.8 us
  starting transfers between devices: 43.6 us -> 37.6 us
  waiting for transfers between devices: 16.6 us -> 22.6 us
    ppermute x18 -> x25, waiting for transfers between devices: 16.6 us -> 22.6 us  [exchange(): return lax.ppermute(x, axis, [(i, i ^ mask) for i in range(size)])]
    ppermute x18 -> x25, starting transfers between devices: 43.6 us -> 37.6 us  [exchange(): return lax.ppermute(x, axis, [(i, i ^ mask) for i in range(size)])]
  transfers between devices with their start and end apart: 18 -> 25, of which waited for: 12 -> 12; matrix products, arithmetic and copies ran while one was open for 18% -> 18% of each run, Pallas kernels for 0% -> 0%
where the time goes in v4:
time: 83.1 us; the launch traced here: 82.8 us
  starting transfers between devices  37.6 us (45%)
  waiting for transfers between devices  22.6 us (27%)
  matrix products  11.2 us (13%)
  other arithmetic  5.72 us (7%)
  local copies, waits for them, and re-layouts  4.56 us (5%)
  between operations  1.04 us (1%)
    ppermute x25, starting transfers between devices, exchange(): return lax.ppermute(x, axis, [(i, i ^ mask) for i in range(size)])  37.6 us
    ppermute x25, waiting for transfers between devices, exchange(): return lax.ppermute(x, axis, [(i, i ^ mask) for i in range(size)])  22.6 us
    dot_general x3, matrix products, project(): jnp.dot(scaled, query_key_value_weight[:, j, :], preferred_element_type=f32)  3.6 us
    dot_general x1, matrix products, shards(): jnp.einsum('rnc,rpc->rnp', q_block, cached_key_rows, preferred_element_ty...  3.17 us
    dot_general x1, matrix products, shards(): jnp.einsum('rnp,rpc->rnc', expo.astype(bf16), cached_value_rows, preferre...  2.68 us
  transfers between devices with their start and end apart: 25, of which 12 were waited for; matrix products, arithmetic and copies ran while one was open for 18% of the time, Pallas kernels for 0%

profile of v4, /device:TPU:1, one launch (start us, length us, event | category | flops | bytes accessed | tf_op | source)
XLA Modules:
  0.0 82.8 jit_solution(4704162440668079468)
XLA Ops:
  0.6 0.9 %fusion.51 = f32[16]{0:T(128)S(1)} fusion(bf16[16,224]{1,0:T(8,128)(2,1)} %param.11), kind=kLoop, calls=%fused_computation.81 | loop fusion | flops 10736 | bytes 7232 | tf_op jit(solution)/shard_map/reduce_sum | solution.py:102
  1.6 1.0 %fusion.84 = f32[16,128]{1,0:T(8,128)S(1)} fusion(bf16[224,128]{1,0:T(8,128)(2,1)} %param.14, bf16[16,224]{1,0:T(8,128)(2,1)} %param.11, f32[224]{0:T(256)} %param.12), kind=kOutput, calls=%fused_computation.146 | convolution fusion | flops 928256 | bytes 73600 | tf_op jit(solution)/shard_map/dot_general | solution.py:101
  2.6 1.2 %fusion.6 = f32[16,896]{1,0:T(8,128)S(1)} fusion(bf16[224,3,896]{2,0,1:T(8,128)(2,1)} %param.13, bf16[16,224]{1,0:T(8,128)(2,1)} %param.11, f32[224]{0:T(256)} %param.12), kind=kOutput, calls=%fused_computation.9 | convolution fusion | flops 6433280 | bytes 467968 | tf_op jit(solution)/shard_map/dot_general | solution.py:99
  3.9 5.2 %collective-permute-start.2 = (f32[16,1152]{1,0:T(8,128)S(1)}, f32[16,1152]{1,0:T(8,128)S(1)}, u32[]{:S(2)}, u32[]{:S(2)}) collective-permute-start(f32[16,1152]{1,0:T(8,128)S(1)} %concatenate.15), channel_id=1, source_target_pairs={{0,24},{8,16},{16,8},{24,0},{32,56},{40,48},{48,40},{56,32},{64,88... | collective-permute-start | bytes 221192 | tf_op jit(solution)/shard_map/ppermute | solution.py:28
  9.1 0.4 collective-permute-start
  9.5 1.2 %fusion.2 = f32[16,896]{1,0:T(8,128)S(1)} fusion(bf16[224,3,896]{2,0,1:T(8,128)(2,1)} %param.13, bf16[16,224]{1,0:T(8,128)(2,1)} %param.11, f32[224]{0:T(256)} %param.12), kind=kOutput, calls=%fused_computation.5 | convolution fusion | flops 6433280 | bytes 467968 | tf_op jit(solution)/shard_map/dot_general | solution.py:99
  10.6 1.2 %fusion.4 = f32[16,896]{1,0:T(8,128)S(1)} fusion(bf16[224,3,896]{2,0,1:T(8,128)(2,1)} %param.13, bf16[16,224]{1,0:T(8,128)(2,1)} %param.11, f32[224]{0:T(256)} %param.12), kind=kOutput, calls=%fused_computation.7 | convolution fusion | flops 6433280 | bytes 467968 | tf_op jit(solution)/shard_map/dot_general | solution.py:99
  11.9 2.1 %collective-permute-start.15 = (f32[16,1792]{1,0:T(8,128)S(1)}, f32[16,1792]{1,0:T(8,128)S(1)}, u32[]{:S(2)}, u32[]{:S(2)}) collective-permute-start(f32[16,1792]{1,0:T(8,128)S(1)} %pad_maximum_fusion), channel_id=1, source_target_pairs={{0,16},{8,24},{16,0},{24,8},{32,48},{40,56},{48,32},{56,40},{64,80... | collective-permute-start | bytes 344072 | tf_op jit(solution)/shard_map/ppermute | solution.py:28
  14.0 1.3 %collective-permute-start.16 = (f32[16,1792]{1,0:T(8,128)S(1)}, f32[16,1792]{1,0:T(8,128)S(1)}, u32[]{:S(2)}, u32[]{:S(2)}) collective-permute-start(f32[16,1792]{1,0:T(8,128)S(1)} %pad_maximum_fusion), channel_id=1, source_target_pairs={{0,24},{8,16},{16,8},{24,0},{32,56},{40,48},{48,40},{56,32},{64,88... | collective-permute-start | bytes 344072 | tf_op jit(solution)/shard_map/ppermute | solution.py:28
  15.2 0.7 iota_add_fusion
  16.0 0.7 broadcast_compare_fusion.1
  16.7 0.7 fusion.47
  17.5 0.3 collective-permute-start.14
  17.8 4.3 %collective-permute-start.3 = (f32[16,1152]{1,0:T(8,128)S(1)}, f32[16,1152]{1,0:T(8,128)S(1)}, u32[]{:S(2)}, u32[]{:S(2)}) collective-permute-start(f32[16,1152]{1,0:T(8,128)S(1)} %add_add_fusion.3), channel_id=1, source_target_pairs={{0,48},{8,56},{16,32},{24,40},{32,16},{40,24},{48,0},{56,8},{64,11... | collective-permute-start | bytes 221192 | tf_op jit(solution)/shard_map/ppermute | solution.py:28
  22.3 8.4 %collective-permute-done.3 = f32[16,1152]{1,0:T(8,128)S(1)} collective-permute-done((f32[16,1152]{1,0:T(8,128)S(1)}, f32[16,1152]{1,0:T(8,128)S(1)}, u32[]{:S(2)}, u32[]{:S(2)}) %collective-permute-start.3) | collective-permute-done | bytes 73760 | tf_op jit(solution)/shard_map/ppermute | solution.py:28
  30.7 2.8 %collective-permute-start.6 = (f32[16,1152]{1,0:T(8,128)S(1)}, f32[16,1152]{1,0:T(8,128)S(1)}, u32[]{:S(2)}, u32[]{:S(2)}) collective-permute-start(f32[16,1152]{1,0:T(8,128)S(1)} %add.148), channel_id=1, source_target_pairs={{0,128},{8,136},{16,144},{24,152},{32,160},{40,168},{48,176},{56,1... | collective-permute-start | bytes 221192 | tf_op jit(solution)/shard_map/ppermute | solution.py:28
  33.5 0.9 %collective-permute-start.5 = (f32[16,1152]{1,0:T(8,128)S(1)}, f32[16,1152]{1,0:T(8,128)S(1)}, u32[]{:S(2)}, u32[]{:S(2)}) collective-permute-start(f32[16,1152]{1,0:T(8,128)S(1)} %add.148), channel_id=1, source_target_pairs={{0,192},{8,200},{16,208},{24,216},{32,224},{40,232},{48,240},{56,2... | collective-permute-start | bytes 221192 | tf_op jit(solution)/shard_map/ppermute | solution.py:28
  34.6 0.9 %collective-permute-done.6 = f32[16,1152]{1,0:T(8,128)S(1)} collective-permute-done((f32[16,1152]{1,0:T(8,128)S(1)}, f32[16,1152]{1,0:T(8,128)S(1)}, u32[]{:S(2)}, u32[]{:S(2)}) %collective-permute-start.6) | collective-permute-done | bytes 73760 | tf_op jit(solution)/shard_map/ppermute | solution.py:28
  35.5 2.5 %collective-permute-done.5 = f32[16,1152]{1,0:T(8,128)S(1)} collective-permute-done((f32[16,1152]{1,0:T(8,128)S(1)}, f32[16,1152]{1,0:T(8,128)S(1)}, u32[]{:S(2)}, u32[]{:S(2)}) %collective-permute-start.5) | collective-permute-done | bytes 73760 | tf_op jit(solution)/shard_map/ppermute | solution.py:28
  38.0 0.1 fusion.71
  38.1 0.2 fusion.35
  38.4 3.2 %fusion.98 = (f32[4,16]{1,0:T(4,128)S(1)}, f32[4,16,512]{2,1,0:T(8,128)S(1)}) fusion(pred[4,16,512]{2,1,0:T(8,128)(4,1)S(1)} %reshape.227, bf16[4,512,896]{2,1,0:T(8,128)(2,1)} %param.17, bf16[4,16,896]{2,1,0:T(8,128)(2,1)S(1)} %broadcast_in_dim.148, pred[16,896]{1,0:T(8,128)(4,1)S(1)} %broadcast_in_dim.142), kind=kOutput, calls=%fused_computation.159 | convolution fusion | flops 58875840 | bytes 3963136 | tf_op jit(solution)/shard_map/rnc,rpc->rnp/dot_general | solution.py:124
  41.7 0.2 fusion.13
  42.0 0.1 copy.64
  42.1 0.1 copy.62
  42.2 2.7 %fusion.15 = f32[4,16,896]{2,1,0:T(8,128)S(1)} fusion(bf16[4,512,896]{2,1,0:T(8,128)(2,1)} %param.18, f32[4,16,512]{2,1,0:T(8,128)S(1)} %get-tuple-element.34, f32[4,16]{1,0:T(4,128)S(1)} %get-tuple-element.33, u8[16,512]{1,0:T(8,128)(4,1)S(1)} %fusion.42), kind=kOutput, calls=%fused_computation.28 | convolution fusion | flops 58949632 | bytes 4038912 | tf_op jit(solution)/shard_map/rnp,rpc->rnc/dot_general | solution.py:140
  45.1 1.6 %collective-permute-start.9 = (f32[16,1024]{1,0:T(8,128)S(1)}, f32[16,1024]{1,0:T(8,128)S(1)}, u32[]{:S(2)}, u32[]{:S(2)}) collective-permute-start(f32[16,1024]{1,0:T(8,128)S(1)} %maximum_maximum_fusion), channel_id=1, source_target_pairs={{0,24},{8,16},{16,8},{24,0},{32,56},{40,48},{48,40},{56,32},{64,88... | collective-permute-start | bytes 196616 | tf_op jit(solution)/shard_map/ppermute | solution.py:28
  46.8 1.9 %collective-permute-start.7 = (f32[16,1024]{1,0:T(8,128)S(1)}, f32[16,1024]{1,0:T(8,128)S(1)}, u32[]{:S(2)}, u32[]{:S(2)}) collective-permute-start(f32[16,1024]{1,0:T(8,128)S(1)} %maximum_maximum_fusion), channel_id=1, source_target_pairs={{0,8},{8,0},{16,24},{24,16},{32,40},{40,32},{48,56},{56,48},{64,72... | collective-permute-start | bytes 196616 | tf_op jit(solution)/shard_map/ppermute | solution.py:28
  48.9 1.7 %collective-permute-start.20 = (f32[16,1792]{1,0:T(8,128)S(1)}, f32[16,1792]{1,0:T(8,128)S(1)}, u32[]{:S(2)}, u32[]{:S(2)}) collective-permute-start(f32[16,1792]{1,0:T(8,128)S(1)} %add.168), channel_id=1, source_target_pairs={{0,128},{8,136},{16,144},{24,152},{32,160},{40,168},{48,176},{56,1... | collective-permute-start | bytes 344072 | tf_op jit(solution)/shard_map/ppermute | solution.py:28
  50.6 1.7 %collective-permute-start.19 = (f32[16,1792]{1,0:T(8,128)S(1)}, f32[16,1792]{1,0:T(8,128)S(1)}, u32[]{:S(2)}, u32[]{:S(2)}) collective-permute-start(f32[16,1792]{1,0:T(8,128)S(1)} %add.168), channel_id=1, source_target_pairs={{0,192},{8,200},{16,208},{24,216},{32,224},{40,232},{48,240},{56,2... | collective-permute-start | bytes 344072 | tf_op jit(solution)/shard_map/ppermute | solution.py:28
  52.5 0.1 reshape.234
  52.7 0.1 reshape.235
  52.8 0.1 reshape.236
  53.0 0.1 reshape.237
  53.2 0.1 reshape.238
  53.4 0.1 reshape.239
  53.6 0.2 collective-permute-start.10
  53.9 0.2 collective-permute-done.20
  54.1 1.3 %collective-permute-done.19 = f32[16,1792]{1,0:T(8,128)S(1)} collective-permute-done((f32[16,1792]{1,0:T(8,128)S(1)}, f32[16,1792]{1,0:T(8,128)S(1)}, u32[]{:S(2)}, u32[]{:S(2)}) %collective-permute-start.19) | collective-permute-done | bytes 114720 | tf_op jit(solution)/shard_map/ppermute | solution.py:28
  55.4 0.7 collective-permute-done.18
  56.4 0.2 fusion.97
  56.6 0.1 copy.58
  56.8 2.3 %collective-permute-done.10 = f32[16,1024]{1,0:T(8,128)S(1)} collective-permute-done((f32[16,1024]{1,0:T(8,128)S(1)}, f32[16,1024]{1,0:T(8,128)S(1)}, u32[]{:S(2)}, u32[]{:S(2)}) %collective-permute-start.10) | collective-permute-done | bytes 65568 | tf_op jit(solution)/shard_map/ppermute | solution.py:28
  59.3 0.1 reshape.240
  59.4 0.1 reshape.241
  59.6 2.9 %collective-permute-start.13 = (f32[16,1024]{1,0:T(8,128)S(1)}, f32[16,1024]{1,0:T(8,128)S(1)}, u32[]{:S(2)}, u32[]{:S(2)}) collective-permute-start(f32[16,1024]{1,0:T(8,128)S(1)} %maximum_maximum_fusion.2), channel_id=1, source_target_pairs={{0,128},{8,136},{16,144},{24,152},{32,160},{40,168},{48,176},{56,1... | collective-permute-start | bytes 196616 | tf_op jit(solution)/shard_map/ppermute | solution.py:28
  62.6 1.6 %collective-permute-start.12 = (f32[16,1024]{1,0:T(8,128)S(1)}, f32[16,1024]{1,0:T(8,128)S(1)}, u32[]{:S(2)}, u32[]{:S(2)}) collective-permute-start(f32[16,1024]{1,0:T(8,128)S(1)} %maximum_maximum_fusion.2), channel_id=1, source_target_pairs={{0,192},{8,200},{16,208},{24,216},{32,224},{40,232},{48,240},{56,2... | collective-permute-start | bytes 196616 | tf_op jit(solution)/shard_map/ppermute | solution.py:28
  64.2 0.1 collective-permute-done.13
  64.3 2.6 %collective-permute-done.12 = f32[16,1024]{1,0:T(8,128)S(1)} collective-permute-done((f32[16,1024]{1,0:T(8,128)S(1)}, f32[16,1024]{1,0:T(8,128)S(1)}, u32[]{:S(2)}, u32[]{:S(2)}) %collective-permute-start.12) | collective-permute-done | bytes 65568 | tf_op jit(solution)/shard_map/ppermute | solution.py:28
  66.9 0.4 collective-permute-done.11
  67.3 0.1 copy.51
  67.5 0.2 convolution_bitcast_fusion
  67.8 0.1 reshape.254
  67.9 0.1 copy.61
  68.1 0.1 reshape.256
  68.3 0.1 reshape.242
  69.6 0.2 fusion.48
  69.8 4.9 %collective-permute-start.21 = (f32[16,112]{1,0:T(8,128)S(1)}, f32[16,112]{1,0:T(8,128)S(1)}, u32[]{:S(2)}, u32[]{:S(2)}) collective-permute-start(f32[16,112]{1,0:T(8,128)S(1)} %fusion.48), channel_id=1, source_target_pairs={{0,1},{1,0},{2,3},{3,2},{4,5},{5,4},{6,7},{7,6},{8,9},{9,8},{10,11... | collective-permute-start | bytes 21512 | tf_op jit(solution)/shard_map/ppermute | solution.py:28
  74.7 0.8 %collective-permute-done.21 = f32[16,112]{1,0:T(8,128)S(1)} collective-permute-done((f32[16,112]{1,0:T(8,128)S(1)}, f32[16,112]{1,0:T(8,128)S(1)}, u32[]{:S(2)}, u32[]{:S(2)}) %collective-permute-start.21) | collective-permute-done | bytes 7200 | tf_op jit(solution)/shard_map/ppermute | solution.py:28
  75.5 2.9 %collective-permute-start.24 = (f32[16,112]{1,0:T(8,128)S(1)}, f32[16,112]{1,0:T(8,128)S(1)}, u32[]{:S(2)}, u32[]{:S(2)}) collective-permute-start(f32[16,112]{1,0:T(8,128)S(1)} %add.177), channel_id=1, source_target_pairs={{0,4},{1,5},{2,6},{3,7},{4,0},{5,1},{6,2},{7,3},{8,12},{9,13},{10,... | collective-permute-start | bytes 21512 | tf_op jit(solution)/shard_map/ppermute | solution.py:28
  78.4 0.8 collective-permute-start.23
  79.2 0.7 pad_maximum_fusion.1
  79.9 2.3 %collective-permute-done.23 = f32[16,112]{1,0:T(8,128)S(1)} collective-permute-done((f32[16,112]{1,0:T(8,128)S(1)}, f32[16,112]{1,0:T(8,128)S(1)}, u32[]{:S(2)}, u32[]{:S(2)}) %collective-permute-start.23) | collective-permute-done | bytes 7200 | tf_op jit(solution)/shard_map/ppermute | solution.py:28
  82.2 0.6 add_add_fusion.4
  (92 shorter events, 4.1 us)
Async XLA Ops:
  0.6 37.5 %copy-start = (bf16[128,896]{1,0:T(8,128)(2,1)S(1)}, bf16[128,896]{1,0:T(8,128)(2,1)}, u32[]{:S(2)}) copy-start(bf16[128,896]{1,0:T(8,128)(2,1)} %param.15) | copy-start | bytes 688132
  3.9 13.6 %collective-permute-start.2 = (f32[16,1152]{1,0:T(8,128)S(1)}, f32[16,1152]{1,0:T(8,128)S(1)}, u32[]{:S(2)}, u32[]{:S(2)}) collective-permute-start(f32[16,1152]{1,0:T(8,128)S(1)} %concatenate.15), channel_id=1, source_target_pairs={{0,24},{8,16},{16,8},{24,0},{32,56},{40,48},{48,40},{56,32},{64,88... | collective-permute-start | bytes 221192 | tf_op jit(solution)/shard_map/ppermute | solution.py:28
  9.1 8.7 %collective-permute-start.1 = (f32[16,1152]{1,0:T(8,128)S(1)}, f32[16,1152]{1,0:T(8,128)S(1)}, u32[]{:S(2)}, u32[]{:S(2)}) collective-permute-start(f32[16,1152]{1,0:T(8,128)S(1)} %concatenate.15), channel_id=1, source_target_pairs={{0,16},{8,24},{16,0},{24,8},{32,48},{40,56},{48,32},{56,40},{64,80... | collective-permute-start | bytes 221192 | tf_op jit(solution)/shard_map/ppermute | solution.py:28
  9.1 8.7 %collective-permute-start = (f32[16,1152]{1,0:T(8,128)S(1)}, f32[16,1152]{1,0:T(8,128)S(1)}, u32[]{:S(2)}, u32[]{:S(2)}) collective-permute-start(f32[16,1152]{1,0:T(8,128)S(1)} %concatenate.15), channel_id=1, source_target_pairs={{0,8},{8,0},{16,24},{24,16},{32,40},{40,32},{48,56},{56,48},{64,72... | collective-permute-start | bytes 221192 | tf_op jit(solution)/shard_map/ppermute | solution.py:28
  11.9 22.5 %collective-permute-start.15 = (f32[16,1792]{1,0:T(8,128)S(1)}, f32[16,1792]{1,0:T(8,128)S(1)}, u32[]{:S(2)}, u32[]{:S(2)}) collective-permute-start(f32[16,1792]{1,0:T(8,128)S(1)} %pad_maximum_fusion), channel_id=1, source_target_pairs={{0,16},{8,24},{16,0},{24,8},{32,48},{40,56},{48,32},{56,40},{64,80... | collective-permute-start | bytes 344072 | tf_op jit(solution)/shard_map/ppermute | solution.py:28
  14.0 20.5 %collective-permute-start.16 = (f32[16,1792]{1,0:T(8,128)S(1)}, f32[16,1792]{1,0:T(8,128)S(1)}, u32[]{:S(2)}, u32[]{:S(2)}) collective-permute-start(f32[16,1792]{1,0:T(8,128)S(1)} %pad_maximum_fusion), channel_id=1, source_target_pairs={{0,24},{8,16},{16,8},{24,0},{32,56},{40,48},{48,40},{56,32},{64,88... | collective-permute-start | bytes 344072 | tf_op jit(solution)/shard_map/ppermute | solution.py:28
  17.5 16.9 %collective-permute-start.14 = (f32[16,1792]{1,0:T(8,128)S(1)}, f32[16,1792]{1,0:T(8,128)S(1)}, u32[]{:S(2)}, u32[]{:S(2)}) collective-permute-start(f32[16,1792]{1,0:T(8,128)S(1)} %pad_maximum_fusion), channel_id=1, source_target_pairs={{0,8},{8,0},{16,24},{24,16},{32,40},{40,32},{48,56},{56,48},{64,72... | collective-permute-start | bytes 344072 | tf_op jit(solution)/shard_map/ppermute | solution.py:28
  17.8 12.9 %collective-permute-start.3 = (f32[16,1152]{1,0:T(8,128)S(1)}, f32[16,1152]{1,0:T(8,128)S(1)}, u32[]{:S(2)}, u32[]{:S(2)}) collective-permute-start(f32[16,1152]{1,0:T(8,128)S(1)} %add_add_fusion.3), channel_id=1, source_target_pairs={{0,48},{8,56},{16,32},{24,40},{32,16},{40,24},{48,0},{56,8},{64,11... | collective-permute-start | bytes 221192 | tf_op jit(solution)/shard_map/ppermute | solution.py:28
  30.7 4.8 %collective-permute-start.6 = (f32[16,1152]{1,0:T(8,128)S(1)}, f32[16,1152]{1,0:T(8,128)S(1)}, u32[]{:S(2)}, u32[]{:S(2)}) collective-permute-start(f32[16,1152]{1,0:T(8,128)S(1)} %add.148), channel_id=1, source_target_pairs={{0,128},{8,136},{16,144},{24,152},{32,160},{40,168},{48,176},{56,1... | collective-permute-start | bytes 221192 | tf_op jit(solution)/shard_map/ppermute | solution.py:28
  33.5 4.4 %collective-permute-start.5 = (f32[16,1152]{1,0:T(8,128)S(1)}, f32[16,1152]{1,0:T(8,128)S(1)}, u32[]{:S(2)}, u32[]{:S(2)}) collective-permute-start(f32[16,1152]{1,0:T(8,128)S(1)} %add.148), channel_id=1, source_target_pairs={{0,192},{8,200},{16,208},{24,216},{32,224},{40,232},{48,240},{56,2... | collective-permute-start | bytes 221192 | tf_op jit(solution)/shard_map/ppermute | solution.py:28
  34.4 3.6 %collective-permute-start.4 = (f32[16,1152]{1,0:T(8,128)S(1)}, f32[16,1152]{1,0:T(8,128)S(1)}, u32[]{:S(2)}, u32[]{:S(2)}) collective-permute-start(f32[16,1152]{1,0:T(8,128)S(1)} %add.148), channel_id=1, source_target_pairs={{0,64},{8,72},{16,80},{24,88},{32,96},{40,104},{48,112},{56,120},{... | collective-permute-start | bytes 221192 | tf_op jit(solution)/shard_map/ppermute | solution.py:28
  34.5 14.4 %collective-permute-start.17 = (f32[16,1792]{1,0:T(8,128)S(1)}, f32[16,1792]{1,0:T(8,128)S(1)}, u32[]{:S(2)}, u32[]{:S(2)}) collective-permute-start(f32[16,1792]{1,0:T(8,128)S(1)} %add_add_fusion.1), channel_id=1, source_target_pairs={{0,48},{8,56},{16,32},{24,40},{32,16},{40,24},{48,0},{56,8},{64,11... | collective-permute-start | bytes 344072 | tf_op jit(solution)/shard_map/ppermute | solution.py:28
  45.0 24.5 %copy-start.1 = (bf16[896,112]{0,1:T(8,128)(2,1)S(1)}, bf16[896,112]{0,1:T(8,128)(2,1)}, u32[]{:S(2)}) copy-start(bf16[896,112]{0,1:T(8,128)(2,1)} %param.16) | copy-start | bytes 602116
  45.1 7.1 %collective-permute-start.9 = (f32[16,1024]{1,0:T(8,128)S(1)}, f32[16,1024]{1,0:T(8,128)S(1)}, u32[]{:S(2)}, u32[]{:S(2)}) collective-permute-start(f32[16,1024]{1,0:T(8,128)S(1)} %maximum_maximum_fusion), channel_id=1, source_target_pairs={{0,24},{8,16},{16,8},{24,0},{32,56},{40,48},{48,40},{56,32},{64,88... | collective-permute-start | bytes 196616 | tf_op jit(solution)/shard_map/ppermute | solution.py:28
  46.8 5.5 %collective-permute-start.8 = (f32[16,1024]{1,0:T(8,128)S(1)}, f32[16,1024]{1,0:T(8,128)S(1)}, u32[]{:S(2)}, u32[]{:S(2)}) collective-permute-start(f32[16,1024]{1,0:T(8,128)S(1)} %maximum_maximum_fusion), channel_id=1, source_target_pairs={{0,16},{8,24},{16,0},{24,8},{32,48},{40,56},{48,32},{56,40},{64,80... | collective-permute-start | bytes 196616 | tf_op jit(solution)/shard_map/ppermute | solution.py:28
  46.8 5.5 %collective-permute-start.7 = (f32[16,1024]{1,0:T(8,128)S(1)}, f32[16,1024]{1,0:T(8,128)S(1)}, u32[]{:S(2)}, u32[]{:S(2)}) collective-permute-start(f32[16,1024]{1,0:T(8,128)S(1)} %maximum_maximum_fusion), channel_id=1, source_target_pairs={{0,8},{8,0},{16,24},{24,16},{32,40},{40,32},{48,56},{56,48},{64,72... | collective-permute-start | bytes 196616 | tf_op jit(solution)/shard_map/ppermute | solution.py:28
  48.9 5.2 %collective-permute-start.20 = (f32[16,1792]{1,0:T(8,128)S(1)}, f32[16,1792]{1,0:T(8,128)S(1)}, u32[]{:S(2)}, u32[]{:S(2)}) collective-permute-start(f32[16,1792]{1,0:T(8,128)S(1)} %add.168), channel_id=1, source_target_pairs={{0,128},{8,136},{16,144},{24,152},{32,160},{40,168},{48,176},{56,1... | collective-permute-start | bytes 344072 | tf_op jit(solution)/shard_map/ppermute | solution.py:28
  50.6 4.9 %collective-permute-start.19 = (f32[16,1792]{1,0:T(8,128)S(1)}, f32[16,1792]{1,0:T(8,128)S(1)}, u32[]{:S(2)}, u32[]{:S(2)}) collective-permute-start(f32[16,1792]{1,0:T(8,128)S(1)} %add.168), channel_id=1, source_target_pairs={{0,192},{8,200},{16,208},{24,216},{32,224},{40,232},{48,240},{56,2... | collective-permute-start | bytes 344072 | tf_op jit(solution)/shard_map/ppermute | solution.py:28
  52.3 3.9 %collective-permute-start.18 = (f32[16,1792]{1,0:T(8,128)S(1)}, f32[16,1792]{1,0:T(8,128)S(1)}, u32[]{:S(2)}, u32[]{:S(2)}) collective-permute-start(f32[16,1792]{1,0:T(8,128)S(1)} %add.168), channel_id=1, source_target_pairs={{0,64},{8,72},{16,80},{24,88},{32,96},{40,104},{48,112},{56,120},{... | collective-permute-start | bytes 344072 | tf_op jit(solution)/shard_map/ppermute | solution.py:28
  53.6 5.4 %collective-permute-start.10 = (f32[16,1024]{1,0:T(8,128)S(1)}, f32[16,1024]{1,0:T(8,128)S(1)}, u32[]{:S(2)}, u32[]{:S(2)}) collective-permute-start(f32[16,1024]{1,0:T(8,128)S(1)} %maximum_maximum_fusion.1), channel_id=1, source_target_pairs={{0,48},{8,56},{16,32},{24,40},{32,16},{40,24},{48,0},{56,8},{64,11... | collective-permute-start | bytes 196616 | tf_op jit(solution)/shard_map/ppermute | solution.py:28
  59.6 4.6 %collective-permute-start.13 = (f32[16,1024]{1,0:T(8,128)S(1)}, f32[16,1024]{1,0:T(8,128)S(1)}, u32[]{:S(2)}, u32[]{:S(2)}) collective-permute-start(f32[16,1024]{1,0:T(8,128)S(1)} %maximum_maximum_fusion.2), channel_id=1, source_target_pairs={{0,128},{8,136},{16,144},{24,152},{32,160},{40,168},{48,176},{56,1... | collective-permute-start | bytes 196616 | tf_op jit(solution)/shard_map/ppermute | solution.py:28
  62.6 4.3 %collective-permute-start.12 = (f32[16,1024]{1,0:T(8,128)S(1)}, f32[16,1024]{1,0:T(8,128)S(1)}, u32[]{:S(2)}, u32[]{:S(2)}) collective-permute-start(f32[16,1024]{1,0:T(8,128)S(1)} %maximum_maximum_fusion.2), channel_id=1, source_target_pairs={{0,192},{8,200},{16,208},{24,216},{32,224},{40,232},{48,240},{56,2... | collective-permute-start | bytes 196616 | tf_op jit(solution)/shard_map/ppermute | solution.py:28
  64.1 3.1 %collective-permute-start.11 = (f32[16,1024]{1,0:T(8,128)S(1)}, f32[16,1024]{1,0:T(8,128)S(1)}, u32[]{:S(2)}, u32[]{:S(2)}) collective-permute-start(f32[16,1024]{1,0:T(8,128)S(1)} %maximum_maximum_fusion.2), channel_id=1, source_target_pairs={{0,64},{8,72},{16,80},{24,88},{32,96},{40,104},{48,112},{56,120},{... | collective-permute-start | bytes 196616 | tf_op jit(solution)/shard_map/ppermute | solution.py:28
  69.8 5.8 %collective-permute-start.21 = (f32[16,112]{1,0:T(8,128)S(1)}, f32[16,112]{1,0:T(8,128)S(1)}, u32[]{:S(2)}, u32[]{:S(2)}) collective-permute-start(f32[16,112]{1,0:T(8,128)S(1)} %fusion.48), channel_id=1, source_target_pairs={{0,1},{1,0},{2,3},{3,2},{4,5},{5,4},{6,7},{7,6},{8,9},{9,8},{10,11... | collective-permute-start | bytes 21512 | tf_op jit(solution)/shard_map/ppermute | solution.py:28
  75.5 4.4 %collective-permute-start.24 = (f32[16,112]{1,0:T(8,128)S(1)}, f32[16,112]{1,0:T(8,128)S(1)}, u32[]{:S(2)}, u32[]{:S(2)}) collective-permute-start(f32[16,112]{1,0:T(8,128)S(1)} %add.177), channel_id=1, source_target_pairs={{0,4},{1,5},{2,6},{3,7},{4,0},{5,1},{6,2},{7,3},{8,12},{9,13},{10,... | collective-permute-start | bytes 21512 | tf_op jit(solution)/shard_map/ppermute | solution.py:28
  78.4 3.7 %collective-permute-start.23 = (f32[16,112]{1,0:T(8,128)S(1)}, f32[16,112]{1,0:T(8,128)S(1)}, u32[]{:S(2)}, u32[]{:S(2)}) collective-permute-start(f32[16,112]{1,0:T(8,128)S(1)} %add.177), channel_id=1, source_target_pairs={{0,6},{1,7},{2,4},{3,5},{4,2},{5,3},{6,0},{7,1},{8,14},{9,15},{10,... | collective-permute-start | bytes 21512 | tf_op jit(solution)/shard_map/ppermute | solution.py:28
  79.2 2.9 %collective-permute-start.22 = (f32[16,112]{1,0:T(8,128)S(1)}, f32[16,112]{1,0:T(8,128)S(1)}, u32[]{:S(2)}, u32[]{:S(2)}) collective-permute-start(f32[16,112]{1,0:T(8,128)S(1)} %add.177), channel_id=1, source_target_pairs={{0,2},{1,3},{2,0},{3,1},{4,6},{5,7},{6,4},{7,5},{8,10},{9,11},{10,... | collective-permute-start | bytes 21512 | tf_op jit(solution)/shard_map/ppermute | solution.py:28

commit v5 on v4

--- a/solution.py
+++ b/solution.py
@@ -104,7 +104,10 @@
         [project(0), partial_low, partial_sq, jnp.zeros((rows, 127), f32)], axis=1
     )
     summed = butterfly_sum(packed, "seq", seq_masks)
-    kv_summed = butterfly_sum(jnp.concatenate([project(1), project(2)], axis=1), "seq", seq_masks)
+    kv_partial, summed = lax.optimization_barrier(
+        (jnp.concatenate([project(1), project(2)], axis=1), summed)
+    )
+    kv_summed = butterfly_sum(kv_partial, "seq", seq_masks)
     low = summed[:, local : local + rank]
     total_sq = summed[:, local + rank]
     scale_rows = lax.rsqrt(total_sq / INPUT_WIDTH + 1e-05)[:, None]

time: 83.1 us -> 87.8 us (1.057)
  starting transfers between devices: 37.6 us -> 40.3 us
  waiting for transfers between devices: 22.6 us -> 23.8 us
    ppermute x25, starting transfers between devices: 37.6 us -> 40.3 us  [exchange(): return lax.ppermute(x, axis, [(i, i ^ mask) for i in range(size)])]
    ppermute x25, waiting for transfers between devices: 22.6 us -> 23.8 us  [exchange(): return lax.ppermute(x, axis, [(i, i ^ mask) for i in range(size)])]
  transfers between devices with their start and end apart: 25 -> 25, of which waited for: 12 -> 10; matrix products, arithmetic and copies ran while one was open for 18% -> 9% of each run, Pallas kernels for 0% -> 0%
where the time goes in v5:
time: 87.8 us; the launch traced here: 86.6 us
  starting transfers between devices  40.3 us (46%)
  waiting for transfers between devices  23.8 us (27%)
  matrix products  11.2 us (13%)
  other arithmetic  5.73 us (7%)
  local copies, waits for them, and re-layouts  4.56 us (5%)
  between operations  1 us (1%)
    ppermute x25, starting transfers between devices, exchange(): return lax.ppermute(x, axis, [(i, i ^ mask) for i in range(size)])  40.3 us
    ppermute x25, waiting for transfers between devices, exchange(): return lax.ppermute(x, axis, [(i, i ^ mask) for i in range(size)])  23.8 us
    dot_general x3, matrix products, project(): jnp.dot(scaled, query_key_value_weight[:, j, :], preferred_element_type=f32)  3.6 us
    dot_general x1, matrix products, shards(): jnp.einsum('rnc,rpc->rnp', q_block, cached_key_rows, preferred_element_ty...  3.17 us
    dot_general x1, matrix products, shards(): jnp.einsum('rnp,rpc->rnc', expo.astype(bf16), cached_value_rows, preferre...  2.68 us
  transfers between devices with their start and end apart: 25, of which 10 were waited for; matrix products, arithmetic and copies ran while one was open for 9% of the time, Pallas kernels for 0%

profile of v5, /device:TPU:1, one launch (start us, length us, event | category | flops | bytes accessed | tf_op | source)
XLA Modules:
  0.0 86.6 jit_solution(11418161627925599120)
XLA Ops:
  0.6 0.9 fusion.50
  1.6 1.0 %fusion.73 = f32[16,128]{1,0:T(8,128)S(1)} fusion(bf16[224,128]{1,0:T(8,128)(2,1)} %param.14, bf16[16,224]{1,0:T(8,128)(2,1)} %param.11, f32[224]{0:T(256)} %param.12), kind=kOutput, calls=%fused_computation.140 | convolution fusion | flops 928256 | bytes 73600 | tf_op jit(solution)/shard_map/dot_general | solution.py:101
  2.6 1.2 %fusion.3 = f32[16,896]{1,0:T(8,128)S(1)} fusion(bf16[224,3,896]{2,0,1:T(8,128)(2,1)} %param.13, bf16[16,224]{1,0:T(8,128)(2,1)} %param.11, f32[224]{0:T(256)} %param.12), kind=kOutput, calls=%fused_computation.7 | convolution fusion | flops 6433280 | bytes 467968 | tf_op jit(solution)/shard_map/dot_general | solution.py:99
  3.9 5.2 %collective-permute-start.2 = (f32[16,1152]{1,0:T(8,128)S(1)}, f32[16,1152]{1,0:T(8,128)S(1)}, u32[]{:S(2)}, u32[]{:S(2)}) collective-permute-start(f32[16,1152]{1,0:T(8,128)S(1)} %concatenate.16), channel_id=1, source_target_pairs={{0,24},{8,16},{16,8},{24,0},{32,56},{40,48},{48,40},{56,32},{64,88... | collective-permute-start | bytes 221192 | tf_op jit(solution)/shard_map/ppermute | solution.py:28
  9.1 0.4 collective-permute-start
  9.5 1.2 %fusion.7 = f32[16,896]{1,0:T(8,128)S(1)} fusion(bf16[224,3,896]{2,0,1:T(8,128)(2,1)} %param.13, bf16[16,224]{1,0:T(8,128)(2,1)} %param.11, f32[224]{0:T(256)} %param.12), kind=kOutput, calls=%fused_computation.11 | convolution fusion | flops 6433280 | bytes 467968 | tf_op jit(solution)/shard_map/dot_general | solution.py:99
  10.6 1.2 %fusion.5 = f32[16,896]{1,0:T(8,128)S(1)} fusion(bf16[224,3,896]{2,0,1:T(8,128)(2,1)} %param.13, bf16[16,224]{1,0:T(8,128)(2,1)} %param.11, f32[224]{0:T(256)} %param.12), kind=kOutput, calls=%fused_computation.9 | convolution fusion | flops 6433280 | bytes 467968 | tf_op jit(solution)/shard_map/dot_general | solution.py:99
  11.9 0.7 iota_add_fusion
  12.6 0.7 broadcast_compare_fusion.1
  13.4 0.7 fusion.46
  14.1 1.2 %collective-permute-done.1 = f32[16,1152]{1,0:T(8,128)S(1)} collective-permute-done((f32[16,1152]{1,0:T(8,128)S(1)}, f32[16,1152]{1,0:T(8,128)S(1)}, u32[]{:S(2)}, u32[]{:S(2)}) %collective-permute-start.1) | collective-permute-done | bytes 73760 | tf_op jit(solution)/shard_map/ppermute | solution.py:28
  15.3 3.1 %collective-permute-start.3 = (f32[16,1152]{1,0:T(8,128)S(1)}, f32[16,1152]{1,0:T(8,128)S(1)}, u32[]{:S(2)}, u32[]{:S(2)}) collective-permute-start(f32[16,1152]{1,0:T(8,128)S(1)} %add_add_fusion.3), channel_id=1, source_target_pairs={{0,48},{8,56},{16,32},{24,40},{32,16},{40,24},{48,0},{56,8},{64,11... | collective-permute-start | bytes 221192 | tf_op jit(solution)/shard_map/ppermute | solution.py:28
  18.4 2.3 %collective-permute-done.3 = f32[16,1152]{1,0:T(8,128)S(1)} collective-permute-done((f32[16,1152]{1,0:T(8,128)S(1)}, f32[16,1152]{1,0:T(8,128)S(1)}, u32[]{:S(2)}, u32[]{:S(2)}) %collective-permute-start.3) | collective-permute-done | bytes 73760 | tf_op jit(solution)/shard_map/ppermute | solution.py:28
  20.7 2.8 %collective-permute-start.6 = (f32[16,1152]{1,0:T(8,128)S(1)}, f32[16,1152]{1,0:T(8,128)S(1)}, u32[]{:S(2)}, u32[]{:S(2)}) collective-permute-start(f32[16,1152]{1,0:T(8,128)S(1)} %add.148), channel_id=1, source_target_pairs={{0,128},{8,136},{16,144},{24,152},{32,160},{40,168},{48,176},{56,1... | collective-permute-start | bytes 221192 | tf_op jit(solution)/shard_map/ppermute | solution.py:28
  23.6 0.9 collective-permute-start.5
  24.6 0.9 %collective-permute-done.6 = f32[16,1152]{1,0:T(8,128)S(1)} collective-permute-done((f32[16,1152]{1,0:T(8,128)S(1)}, f32[16,1152]{1,0:T(8,128)S(1)}, u32[]{:S(2)}, u32[]{:S(2)}) %collective-permute-start.6) | collective-permute-done | bytes 73760 | tf_op jit(solution)/shard_map/ppermute | solution.py:28
  25.5 3.2 %collective-permute-done.5 = f32[16,1152]{1,0:T(8,128)S(1)} collective-permute-done((f32[16,1152]{1,0:T(8,128)S(1)}, f32[16,1152]{1,0:T(8,128)S(1)}, u32[]{:S(2)}, u32[]{:S(2)}) %collective-permute-start.5) | collective-permute-done | bytes 73760 | tf_op jit(solution)/shard_map/ppermute | solution.py:28
  28.8 0.1 rsqrt_reduce_fusion
  28.9 0.2 fusion.1
  29.2 3.2 %fusion.89 = (f32[4,16]{1,0:T(4,128)S(1)}, f32[4,16,512]{2,1,0:T(8,128)S(1)}) fusion(pred[4,16,512]{2,1,0:T(8,128)(4,1)S(1)} %reshape.227, bf16[4,512,896]{2,1,0:T(8,128)(2,1)} %param.17, bf16[4,16,896]{2,1,0:T(8,128)(2,1)S(1)} %broadcast_in_dim.148, pred[16,896]{1,0:T(8,128)(4,1)S(1)} %broadcast_in_dim.142), kind=kOutput, calls=%fused_computation.153 | convolution fusion | flops 58875840 | bytes 3963136 | tf_op jit(solution)/shard_map/rnc,rpc->rnp/dot_general | solution.py:127
  32.5 0.2 fusion.14
  32.8 0.1 copy.64
  32.9 0.1 copy.62
  33.0 2.7 %fusion.16 = f32[4,16,896]{2,1,0:T(8,128)S(1)} fusion(bf16[4,512,896]{2,1,0:T(8,128)(2,1)} %param.18, f32[4,16,512]{2,1,0:T(8,128)S(1)} %get-tuple-element.38, f32[4,16]{1,0:T(4,128)S(1)} %get-tuple-element.37, u8[16,512]{1,0:T(8,128)(4,1)S(1)} %fusion.41), kind=kOutput, calls=%fused_computation.30 | convolution fusion | flops 58949632 | bytes 4038912 | tf_op jit(solution)/shard_map/rnp,rpc->rnc/dot_general | solution.py:143
  35.9 1.6 %collective-permute-start.9 = (f32[16,1024]{1,0:T(8,128)S(1)}, f32[16,1024]{1,0:T(8,128)S(1)}, u32[]{:S(2)}, u32[]{:S(2)}) collective-permute-start(f32[16,1024]{1,0:T(8,128)S(1)} %maximum_maximum_fusion), channel_id=1, source_target_pairs={{0,24},{8,16},{16,8},{24,0},{32,56},{40,48},{48,40},{56,32},{64,88... | collective-permute-start | bytes 196616 | tf_op jit(solution)/shard_map/ppermute | solution.py:28
  37.5 2.2 %collective-permute-start.8 = (f32[16,1024]{1,0:T(8,128)S(1)}, f32[16,1024]{1,0:T(8,128)S(1)}, u32[]{:S(2)}, u32[]{:S(2)}) collective-permute-start(f32[16,1024]{1,0:T(8,128)S(1)} %maximum_maximum_fusion), channel_id=1, source_target_pairs={{0,16},{8,24},{16,0},{24,8},{32,48},{40,56},{48,32},{56,40},{64,80... | collective-permute-start | bytes 196616 | tf_op jit(solution)/shard_map/ppermute | solution.py:28
  39.9 1.7 %collective-permute-start.16 = (f32[16,1792]{1,0:T(8,128)S(1)}, f32[16,1792]{1,0:T(8,128)S(1)}, u32[]{:S(2)}, u32[]{:S(2)}) collective-permute-start(f32[16,1792]{1,0:T(8,128)S(1)} %pad_maximum_fusion), channel_id=1, source_target_pairs={{0,24},{8,16},{16,8},{24,0},{32,56},{40,48},{48,40},{56,32},{64,88... | collective-permute-start | bytes 344072 | tf_op jit(solution)/shard_map/ppermute | solution.py:28
  41.6 1.0 %collective-permute-start.15 = (f32[16,1792]{1,0:T(8,128)S(1)}, f32[16,1792]{1,0:T(8,128)S(1)}, u32[]{:S(2)}, u32[]{:S(2)}) collective-permute-start(f32[16,1792]{1,0:T(8,128)S(1)} %pad_maximum_fusion), channel_id=1, source_target_pairs={{0,16},{8,24},{16,0},{24,8},{32,48},{40,56},{48,32},{56,40},{64,80... | collective-permute-start | bytes 344072 | tf_op jit(solution)/shard_map/ppermute | solution.py:28
  42.6 0.9 %collective-permute-start.14 = (f32[16,1792]{1,0:T(8,128)S(1)}, f32[16,1792]{1,0:T(8,128)S(1)}, u32[]{:S(2)}, u32[]{:S(2)}) collective-permute-start(f32[16,1792]{1,0:T(8,128)S(1)} %pad_maximum_fusion), channel_id=1, source_target_pairs={{0,8},{8,0},{16,24},{24,16},{32,40},{40,32},{48,56},{56,48},{64,72... | collective-permute-start | bytes 344072 | tf_op jit(solution)/shard_map/ppermute | solution.py:28
  43.7 0.1 reshape.234
  43.9 0.1 reshape.235
  44.1 0.1 reshape.236
  44.9 3.9 %collective-permute-start.10 = (f32[16,1024]{1,0:T(8,128)S(1)}, f32[16,1024]{1,0:T(8,128)S(1)}, u32[]{:S(2)}, u32[]{:S(2)}) collective-permute-start(f32[16,1024]{1,0:T(8,128)S(1)} %maximum_maximum_fusion.1), channel_id=1, source_target_pairs={{0,48},{8,56},{16,32},{24,40},{32,16},{40,24},{48,0},{56,8},{64,11... | collective-permute-start | bytes 196616 | tf_op jit(solution)/shard_map/ppermute | solution.py:28
  48.8 5.8 %collective-permute-done.15 = f32[16,1792]{1,0:T(8,128)S(1)} collective-permute-done((f32[16,1792]{1,0:T(8,128)S(1)}, f32[16,1792]{1,0:T(8,128)S(1)}, u32[]{:S(2)}, u32[]{:S(2)}) %collective-permute-start.15) | collective-permute-done | bytes 114720 | tf_op jit(solution)/shard_map/ppermute | solution.py:28
  54.7 2.5 %collective-permute-start.17 = (f32[16,1792]{1,0:T(8,128)S(1)}, f32[16,1792]{1,0:T(8,128)S(1)}, u32[]{:S(2)}, u32[]{:S(2)}) collective-permute-start(f32[16,1792]{1,0:T(8,128)S(1)} %add_add_fusion.1), channel_id=1, source_target_pairs={{0,48},{8,56},{16,32},{24,40},{32,16},{40,24},{48,0},{56,8},{64,11... | collective-permute-start | bytes 344072 | tf_op jit(solution)/shard_map/ppermute | solution.py:28
  57.5 0.1 reshape.241
  57.6 3.5 %collective-permute-done.17 = f32[16,1792]{1,0:T(8,128)S(1)} collective-permute-done((f32[16,1792]{1,0:T(8,128)S(1)}, f32[16,1792]{1,0:T(8,128)S(1)}, u32[]{:S(2)}, u32[]{:S(2)}) %collective-permute-start.17) | collective-permute-done | bytes 114720 | tf_op jit(solution)/shard_map/ppermute | solution.py:28
  61.1 1.3 %collective-permute-start.20 = (f32[16,1792]{1,0:T(8,128)S(1)}, f32[16,1792]{1,0:T(8,128)S(1)}, u32[]{:S(2)}, u32[]{:S(2)}) collective-permute-start(f32[16,1792]{1,0:T(8,128)S(1)} %add.168), channel_id=1, source_target_pairs={{0,128},{8,136},{16,144},{24,152},{32,160},{40,168},{48,176},{56,1... | collective-permute-start | bytes 344072 | tf_op jit(solution)/shard_map/ppermute | solution.py:28
  62.4 1.3 %collective-permute-start.19 = (f32[16,1792]{1,0:T(8,128)S(1)}, f32[16,1792]{1,0:T(8,128)S(1)}, u32[]{:S(2)}, u32[]{:S(2)}) collective-permute-start(f32[16,1792]{1,0:T(8,128)S(1)} %add.168), channel_id=1, source_target_pairs={{0,192},{8,200},{16,208},{24,216},{32,224},{40,232},{48,240},{56,2... | collective-permute-start | bytes 344072 | tf_op jit(solution)/shard_map/ppermute | solution.py:28
  63.7 0.1 collective-permute-start.18
  63.9 2.4 %collective-permute-start.13 = (f32[16,1024]{1,0:T(8,128)S(1)}, f32[16,1024]{1,0:T(8,128)S(1)}, u32[]{:S(2)}, u32[]{:S(2)}) collective-permute-start(f32[16,1024]{1,0:T(8,128)S(1)} %maximum_maximum_fusion.2), channel_id=1, source_target_pairs={{0,128},{8,136},{16,144},{24,152},{32,160},{40,168},{48,176},{56,1... | collective-permute-start | bytes 196616 | tf_op jit(solution)/shard_map/ppermute | solution.py:28
  66.3 1.3 %collective-permute-start.12 = (f32[16,1024]{1,0:T(8,128)S(1)}, f32[16,1024]{1,0:T(8,128)S(1)}, u32[]{:S(2)}, u32[]{:S(2)}) collective-permute-start(f32[16,1024]{1,0:T(8,128)S(1)} %maximum_maximum_fusion.2), channel_id=1, source_target_pairs={{0,192},{8,200},{16,208},{24,216},{32,224},{40,232},{48,240},{56,2... | collective-permute-start | bytes 196616 | tf_op jit(solution)/shard_map/ppermute | solution.py:28
  68.0 0.2 fusion.88
  68.2 0.1 copy.58
  68.3 1.8 %collective-permute-done.13 = f32[16,1024]{1,0:T(8,128)S(1)} collective-permute-done((f32[16,1024]{1,0:T(8,128)S(1)}, f32[16,1024]{1,0:T(8,128)S(1)}, u32[]{:S(2)}, u32[]{:S(2)}) %collective-permute-start.13) | collective-permute-done | bytes 65568 | tf_op jit(solution)/shard_map/ppermute | solution.py:28
  70.1 2.0 %collective-permute-done.12 = f32[16,1024]{1,0:T(8,128)S(1)} collective-permute-done((f32[16,1024]{1,0:T(8,128)S(1)}, f32[16,1024]{1,0:T(8,128)S(1)}, u32[]{:S(2)}, u32[]{:S(2)}) %collective-permute-start.12) | collective-permute-done | bytes 65568 | tf_op jit(solution)/shard_map/ppermute | solution.py:28
  72.2 0.1 copy.51
  72.3 0.2 convolution_bitcast_fusion
  72.6 0.1 reshape.254
  72.7 0.1 copy.61
  73.2 0.1 reshape.242
  73.4 0.1 reshape.243
  73.5 0.1 reshape.244
  73.7 0.1 reshape.245
  73.9 0.1 reshape.246
  74.1 0.1 reshape.247
  74.4 0.2 fusion.47
  74.6 4.0 %collective-permute-start.21 = (f32[16,112]{1,0:T(8,128)S(1)}, f32[16,112]{1,0:T(8,128)S(1)}, u32[]{:S(2)}, u32[]{:S(2)}) collective-permute-start(f32[16,112]{1,0:T(8,128)S(1)} %fusion.47), channel_id=1, source_target_pairs={{0,1},{1,0},{2,3},{3,2},{4,5},{5,4},{6,7},{7,6},{8,9},{9,8},{10,11... | collective-permute-start | bytes 21512 | tf_op jit(solution)/shard_map/ppermute | solution.py:28
  78.6 0.8 collective-permute-done.21
  79.4 2.9 %collective-permute-start.24 = (f32[16,112]{1,0:T(8,128)S(1)}, f32[16,112]{1,0:T(8,128)S(1)}, u32[]{:S(2)}, u32[]{:S(2)}) collective-permute-start(f32[16,112]{1,0:T(8,128)S(1)} %add.177), channel_id=1, source_target_pairs={{0,4},{1,5},{2,6},{3,7},{4,0},{5,1},{6,2},{7,3},{8,12},{9,13},{10,... | collective-permute-start | bytes 21512 | tf_op jit(solution)/shard_map/ppermute | solution.py:28
  82.3 0.8 collective-permute-start.23
  83.1 0.7 pad_maximum_fusion.1
  83.8 2.3 %collective-permute-done.23 = f32[16,112]{1,0:T(8,128)S(1)} collective-permute-done((f32[16,112]{1,0:T(8,128)S(1)}, f32[16,112]{1,0:T(8,128)S(1)}, u32[]{:S(2)}, u32[]{:S(2)}) %collective-permute-start.23) | collective-permute-done | bytes 7200 | tf_op jit(solution)/shard_map/ppermute | solution.py:28
  86.0 0.6 add_add_fusion.4
  (92 shorter events, 4.0 us)
Async XLA Ops:
  0.6 28.3 %copy-start = (bf16[128,896]{1,0:T(8,128)(2,1)S(1)}, bf16[128,896]{1,0:T(8,128)(2,1)}, u32[]{:S(2)}) copy-start(bf16[128,896]{1,0:T(8,128)(2,1)} %param.15) | copy-start | bytes 688132
  3.9 10.2 %collective-permute-start.2 = (f32[16,1152]{1,0:T(8,128)S(1)}, f32[16,1152]{1,0:T(8,128)S(1)}, u32[]{:S(2)}, u32[]{:S(2)}) collective-permute-start(f32[16,1152]{1,0:T(8,128)S(1)} %concatenate.16), channel_id=1, source_target_pairs={{0,24},{8,16},{16,8},{24,0},{32,56},{40,48},{48,40},{56,32},{64,88... | collective-permute-start | bytes 221192 | tf_op jit(solution)/shard_map/ppermute | solution.py:28
  9.1 6.2 %collective-permute-start.1 = (f32[16,1152]{1,0:T(8,128)S(1)}, f32[16,1152]{1,0:T(8,128)S(1)}, u32[]{:S(2)}, u32[]{:S(2)}) collective-permute-start(f32[16,1152]{1,0:T(8,128)S(1)} %concatenate.16), channel_id=1, source_target_pairs={{0,16},{8,24},{16,0},{24,8},{32,48},{40,56},{48,32},{56,40},{64,80... | collective-permute-start | bytes 221192 | tf_op jit(solution)/shard_map/ppermute | solution.py:28
  9.1 6.2 %collective-permute-start = (f32[16,1152]{1,0:T(8,128)S(1)}, f32[16,1152]{1,0:T(8,128)S(1)}, u32[]{:S(2)}, u32[]{:S(2)}) collective-permute-start(f32[16,1152]{1,0:T(8,128)S(1)} %concatenate.16), channel_id=1, source_target_pairs={{0,8},{8,0},{16,24},{24,16},{32,40},{40,32},{48,56},{56,48},{64,72... | collective-permute-start | bytes 221192 | tf_op jit(solution)/shard_map/ppermute | solution.py:28
  15.3 5.4 %collective-permute-start.3 = (f32[16,1152]{1,0:T(8,128)S(1)}, f32[16,1152]{1,0:T(8,128)S(1)}, u32[]{:S(2)}, u32[]{:S(2)}) collective-permute-start(f32[16,1152]{1,0:T(8,128)S(1)} %add_add_fusion.3), channel_id=1, source_target_pairs={{0,48},{8,56},{16,32},{24,40},{32,16},{40,24},{48,0},{56,8},{64,11... | collective-permute-start | bytes 221192 | tf_op jit(solution)/shard_map/ppermute | solution.py:28
  20.7 4.8 %collective-permute-start.6 = (f32[16,1152]{1,0:T(8,128)S(1)}, f32[16,1152]{1,0:T(8,128)S(1)}, u32[]{:S(2)}, u32[]{:S(2)}) collective-permute-start(f32[16,1152]{1,0:T(8,128)S(1)} %add.148), channel_id=1, source_target_pairs={{0,128},{8,136},{16,144},{24,152},{32,160},{40,168},{48,176},{56,1... | collective-permute-start | bytes 221192 | tf_op jit(solution)/shard_map/ppermute | solution.py:28
  23.6 5.2 %collective-permute-start.5 = (f32[16,1152]{1,0:T(8,128)S(1)}, f32[16,1152]{1,0:T(8,128)S(1)}, u32[]{:S(2)}, u32[]{:S(2)}) collective-permute-start(f32[16,1152]{1,0:T(8,128)S(1)} %add.148), channel_id=1, source_target_pairs={{0,192},{8,200},{16,208},{24,216},{32,224},{40,232},{48,240},{56,2... | collective-permute-start | bytes 221192 | tf_op jit(solution)/shard_map/ppermute | solution.py:28
  24.4 4.3 %collective-permute-start.4 = (f32[16,1152]{1,0:T(8,128)S(1)}, f32[16,1152]{1,0:T(8,128)S(1)}, u32[]{:S(2)}, u32[]{:S(2)}) collective-permute-start(f32[16,1152]{1,0:T(8,128)S(1)} %add.148), channel_id=1, source_target_pairs={{0,64},{8,72},{16,80},{24,88},{32,96},{40,104},{48,112},{56,120},{... | collective-permute-start | bytes 221192 | tf_op jit(solution)/shard_map/ppermute | solution.py:28
  35.9 6.7 %collective-permute-start.9 = (f32[16,1024]{1,0:T(8,128)S(1)}, f32[16,1024]{1,0:T(8,128)S(1)}, u32[]{:S(2)}, u32[]{:S(2)}) collective-permute-start(f32[16,1024]{1,0:T(8,128)S(1)} %maximum_maximum_fusion), channel_id=1, source_target_pairs={{0,24},{8,16},{16,8},{24,0},{32,56},{40,48},{48,40},{56,32},{64,88... | collective-permute-start | bytes 196616 | tf_op jit(solution)/shard_map/ppermute | solution.py:28
  37.5 6.0 %collective-permute-start.8 = (f32[16,1024]{1,0:T(8,128)S(1)}, f32[16,1024]{1,0:T(8,128)S(1)}, u32[]{:S(2)}, u32[]{:S(2)}) collective-permute-start(f32[16,1024]{1,0:T(8,128)S(1)} %maximum_maximum_fusion), channel_id=1, source_target_pairs={{0,16},{8,24},{16,0},{24,8},{32,48},{40,56},{48,32},{56,40},{64,80... | collective-permute-start | bytes 196616 | tf_op jit(solution)/shard_map/ppermute | solution.py:28
  39.8 3.8 %collective-permute-start.7 = (f32[16,1024]{1,0:T(8,128)S(1)}, f32[16,1024]{1,0:T(8,128)S(1)}, u32[]{:S(2)}, u32[]{:S(2)}) collective-permute-start(f32[16,1024]{1,0:T(8,128)S(1)} %maximum_maximum_fusion), channel_id=1, source_target_pairs={{0,8},{8,0},{16,24},{24,16},{32,40},{40,32},{48,56},{56,48},{64,72... | collective-permute-start | bytes 196616 | tf_op jit(solution)/shard_map/ppermute | solution.py:28
  39.9 8.9 %collective-permute-start.16 = (f32[16,1792]{1,0:T(8,128)S(1)}, f32[16,1792]{1,0:T(8,128)S(1)}, u32[]{:S(2)}, u32[]{:S(2)}) collective-permute-start(f32[16,1792]{1,0:T(8,128)S(1)} %pad_maximum_fusion), channel_id=1, source_target_pairs={{0,24},{8,16},{16,8},{24,0},{32,56},{40,48},{48,40},{56,32},{64,88... | collective-permute-start | bytes 344072 | tf_op jit(solution)/shard_map/ppermute | solution.py:28
  41.6 13.0 %collective-permute-start.15 = (f32[16,1792]{1,0:T(8,128)S(1)}, f32[16,1792]{1,0:T(8,128)S(1)}, u32[]{:S(2)}, u32[]{:S(2)}) collective-permute-start(f32[16,1792]{1,0:T(8,128)S(1)} %pad_maximum_fusion), channel_id=1, source_target_pairs={{0,16},{8,24},{16,0},{24,8},{32,48},{40,56},{48,32},{56,40},{64,80... | collective-permute-start | bytes 344072 | tf_op jit(solution)/shard_map/ppermute | solution.py:28
  42.6 12.0 %collective-permute-start.14 = (f32[16,1792]{1,0:T(8,128)S(1)}, f32[16,1792]{1,0:T(8,128)S(1)}, u32[]{:S(2)}, u32[]{:S(2)}) collective-permute-start(f32[16,1792]{1,0:T(8,128)S(1)} %pad_maximum_fusion), channel_id=1, source_target_pairs={{0,8},{8,0},{16,24},{24,16},{32,40},{40,32},{48,56},{56,48},{64,72... | collective-permute-start | bytes 344072 | tf_op jit(solution)/shard_map/ppermute | solution.py:28
  43.8 30.6 %copy-start.1 = (bf16[896,112]{0,1:T(8,128)(2,1)S(1)}, bf16[896,112]{0,1:T(8,128)(2,1)}, u32[]{:S(2)}) copy-start(bf16[896,112]{0,1:T(8,128)(2,1)} %param.16) | copy-start | bytes 602116
  44.9 12.2 %collective-permute-start.10 = (f32[16,1024]{1,0:T(8,128)S(1)}, f32[16,1024]{1,0:T(8,128)S(1)}, u32[]{:S(2)}, u32[]{:S(2)}) collective-permute-start(f32[16,1024]{1,0:T(8,128)S(1)} %maximum_maximum_fusion.1), channel_id=1, source_target_pairs={{0,48},{8,56},{16,32},{24,40},{32,16},{40,24},{48,0},{56,8},{64,11... | collective-permute-start | bytes 196616 | tf_op jit(solution)/shard_map/ppermute | solution.py:28
  54.7 6.4 %collective-permute-start.17 = (f32[16,1792]{1,0:T(8,128)S(1)}, f32[16,1792]{1,0:T(8,128)S(1)}, u32[]{:S(2)}, u32[]{:S(2)}) collective-permute-start(f32[16,1792]{1,0:T(8,128)S(1)} %add_add_fusion.1), channel_id=1, source_target_pairs={{0,48},{8,56},{16,32},{24,40},{32,16},{40,24},{48,0},{56,8},{64,11... | collective-permute-start | bytes 344072 | tf_op jit(solution)/shard_map/ppermute | solution.py:28
  61.1 6.6 %collective-permute-start.20 = (f32[16,1792]{1,0:T(8,128)S(1)}, f32[16,1792]{1,0:T(8,128)S(1)}, u32[]{:S(2)}, u32[]{:S(2)}) collective-permute-start(f32[16,1792]{1,0:T(8,128)S(1)} %add.168), channel_id=1, source_target_pairs={{0,128},{8,136},{16,144},{24,152},{32,160},{40,168},{48,176},{56,1... | collective-permute-start | bytes 344072 | tf_op jit(solution)/shard_map/ppermute | solution.py:28
  62.4 5.3 %collective-permute-start.19 = (f32[16,1792]{1,0:T(8,128)S(1)}, f32[16,1792]{1,0:T(8,128)S(1)}, u32[]{:S(2)}, u32[]{:S(2)}) collective-permute-start(f32[16,1792]{1,0:T(8,128)S(1)} %add.168), channel_id=1, source_target_pairs={{0,192},{8,200},{16,208},{24,216},{32,224},{40,232},{48,240},{56,2... | collective-permute-start | bytes 344072 | tf_op jit(solution)/shard_map/ppermute | solution.py:28
  63.7 4.0 %collective-permute-start.18 = (f32[16,1792]{1,0:T(8,128)S(1)}, f32[16,1792]{1,0:T(8,128)S(1)}, u32[]{:S(2)}, u32[]{:S(2)}) collective-permute-start(f32[16,1792]{1,0:T(8,128)S(1)} %add.168), channel_id=1, source_target_pairs={{0,64},{8,72},{16,80},{24,88},{32,96},{40,104},{48,112},{56,120},{... | collective-permute-start | bytes 344072 | tf_op jit(solution)/shard_map/ppermute | solution.py:28
  63.9 6.2 %collective-permute-start.13 = (f32[16,1024]{1,0:T(8,128)S(1)}, f32[16,1024]{1,0:T(8,128)S(1)}, u32[]{:S(2)}, u32[]{:S(2)}) collective-permute-start(f32[16,1024]{1,0:T(8,128)S(1)} %maximum_maximum_fusion.2), channel_id=1, source_target_pairs={{0,128},{8,136},{16,144},{24,152},{32,160},{40,168},{48,176},{56,1... | collective-permute-start | bytes 196616 | tf_op jit(solution)/shard_map/ppermute | solution.py:28
  66.3 5.8 %collective-permute-start.12 = (f32[16,1024]{1,0:T(8,128)S(1)}, f32[16,1024]{1,0:T(8,128)S(1)}, u32[]{:S(2)}, u32[]{:S(2)}) collective-permute-start(f32[16,1024]{1,0:T(8,128)S(1)} %maximum_maximum_fusion.2), channel_id=1, source_target_pairs={{0,192},{8,200},{16,208},{24,216},{32,224},{40,232},{48,240},{56,2... | collective-permute-start | bytes 196616 | tf_op jit(solution)/shard_map/ppermute | solution.py:28
  67.7 4.4 %collective-permute-start.11 = (f32[16,1024]{1,0:T(8,128)S(1)}, f32[16,1024]{1,0:T(8,128)S(1)}, u32[]{:S(2)}, u32[]{:S(2)}) collective-permute-start(f32[16,1024]{1,0:T(8,128)S(1)} %maximum_maximum_fusion.2), channel_id=1, source_target_pairs={{0,64},{8,72},{16,80},{24,88},{32,96},{40,104},{48,112},{56,120},{... | collective-permute-start | bytes 196616 | tf_op jit(solution)/shard_map/ppermute | solution.py:28
  74.6 4.8 %collective-permute-start.21 = (f32[16,112]{1,0:T(8,128)S(1)}, f32[16,112]{1,0:T(8,128)S(1)}, u32[]{:S(2)}, u32[]{:S(2)}) collective-permute-start(f32[16,112]{1,0:T(8,128)S(1)} %fusion.47), channel_id=1, source_target_pairs={{0,1},{1,0},{2,3},{3,2},{4,5},{5,4},{6,7},{7,6},{8,9},{9,8},{10,11... | collective-permute-start | bytes 21512 | tf_op jit(solution)/shard_map/ppermute | solution.py:28
  79.4 4.4 %collective-permute-start.24 = (f32[16,112]{1,0:T(8,128)S(1)}, f32[16,112]{1,0:T(8,128)S(1)}, u32[]{:S(2)}, u32[]{:S(2)}) collective-permute-start(f32[16,112]{1,0:T(8,128)S(1)} %add.177), channel_id=1, source_target_pairs={{0,4},{1,5},{2,6},{3,7},{4,0},{5,1},{6,2},{7,3},{8,12},{9,13},{10,... | collective-permute-start | bytes 21512 | tf_op jit(solution)/shard_map/ppermute | solution.py:28
  82.3 3.7 %collective-permute-start.23 = (f32[16,112]{1,0:T(8,128)S(1)}, f32[16,112]{1,0:T(8,128)S(1)}, u32[]{:S(2)}, u32[]{:S(2)}) collective-permute-start(f32[16,112]{1,0:T(8,128)S(1)} %add.177), channel_id=1, source_target_pairs={{0,6},{1,7},{2,4},{3,5},{4,2},{5,3},{6,0},{7,1},{8,14},{9,15},{10,... | collective-permute-start | bytes 21512 | tf_op jit(solution)/shard_map/ppermute | solution.py:28
  83.1 2.9 %collective-permute-start.22 = (f32[16,112]{1,0:T(8,128)S(1)}, f32[16,112]{1,0:T(8,128)S(1)}, u32[]{:S(2)}, u32[]{:S(2)}) collective-permute-start(f32[16,112]{1,0:T(8,128)S(1)} %add.177), channel_id=1, source_target_pairs={{0,2},{1,3},{2,0},{3,1},{4,6},{5,7},{6,4},{7,5},{8,10},{9,11},{10,... | collective-permute-start | bytes 21512 | tf_op jit(solution)/shard_map/ppermute | solution.py:28

commit v6 on v4

--- a/solution.py
+++ b/solution.py
@@ -13,31 +13,70 @@
 
 
 def butterfly_rounds(axes):
-    rounds, shift = [], 0
+    masks, rings, shift = [], [], 0
     for size in reversed(axes):
-        masks, bit = [], 1
+        bit, ring = 1, []
         while bit < size:
-            masks.append((bit if 2 * bit < size or size <= 2 else size - 2 if size > 4 else size - 1) << shift)
+            ring.append((bit if 2 * bit < size or size <= 2 else size - 2 if size > 4 else size - 1) << shift)
             bit *= 2
-        rounds += [tuple(masks[i : i + 2]) for i in range(0, len(masks), 2)]
+        rings.append(ring)
+        masks += ring
         shift += size.bit_length() - 1
-    return rounds
+    duals = [
+        next(c for c in range(1 << len(masks)) if all(bin(c & m).count("1") % 2 == (j == k) for k, m in enumerate(masks)))
+        for j in range(len(masks))
+    ]
+    pairs = dict(zip(masks, duals))
+    return [tuple((m, pairs[m]) for m in ring[i : i + 2]) for ring in rings for i in range(0, len(ring), 2)]
 
 
 def exchange(x, axis, mask, size):
     return lax.ppermute(x, axis, [(i, i ^ mask) for i in range(size)])
 
 
-def butterfly_sum(x, axis, rounds):
+def partners(r):
+    if len(r) == 1:
+        return [(r[0][0], 1)]
+    a, b = r[0][0], r[1][0]
+    return [(a, 1), (b, 2), (a ^ b, 3)]
+
+
+def digit_of(index, r):
+    return sum((lax.population_count(index & c) & 1) << k for k, (_, c) in enumerate(r))
+
+
+def pieces(x, n):
+    w = x.shape[1] // n
+    return [x[:, j * w : (j + 1) * w] for j in range(n)]
+
+
+def butterfly_sum(x, axis, rounds, spread=None):
     size = 1 << sum(len(r) for r in rounds)
+    index = lax.axis_index(axis)
+    width = x.shape[1]
     for r in rounds:
+        ways = partners(r)
+        digit = digit_of(index, r)
+        if spread is not None:
+            parts = pieces(spread, 2 ** len(r))
+            mine = lax.select_n(digit, *parts)
+            got = [
+                exchange(jnp.concatenate([x, lax.select_n(digit ^ d, *parts)], axis=1), axis, m, size)
+                for m, d in ways
+            ]
+            recv = [g[:, :width] for g in got]
+            bits = [g[:, width:] for g in got]
+        else:
+            recv = [exchange(x, axis, m, size) for m, _ in ways]
         if len(r) == 1:
-            x = x + exchange(x, axis, r[0], size)
+            x = x + recv[0]
+            if spread is not None:
+                spread = mine + bits[0]
         else:
-            a, b = r
-            pa, pb, pc = (exchange(x, axis, m, size) for m in (a, b, a ^ b))
-            x = (x + pa) + (pb + pc)
-    return x
+            x = (x + recv[0]) + (recv[1] + recv[2])
+            if spread is not None:
+                spread = (mine + bits[0]) + (bits[1] + bits[2])
+    return x, spread
 
 
 def merge_softmax(a, b, width, heads):
@@ -50,16 +89,26 @@
     return jnp.concatenate([values, totals, top, jnp.zeros((a.shape[0], pad), jnp.float32)], axis=1)
 
 
-def butterfly_softmax(x, axis, rounds, width, heads):
+def butterfly_softmax(x, axis, rounds, width, heads, gather):
     size = 1 << sum(len(r) for r in rounds)
-    for r in rounds:
+    index = lax.axis_index(axis)
+    full = x.shape[1]
+    for r in reversed(rounds):
+        ways = partners(r)
+        digit = digit_of(index, r)
+        got = [exchange(jnp.concatenate([x, gather], axis=1), axis, m, size) for m, _ in ways]
+        recv = [g[:, :full] for g in got]
+        by_diff = [gather] + [g[:, full:] for g in got]
+        order = [0] + [d for _, d in ways]
+        slots = [by_diff[order.index(d)] for d in range(2 ** len(r))]
+        gather = jnp.concatenate([lax.select_n(digit ^ j, *slots) for j in range(2 ** len(r))], axis=1)
         if len(r) == 1:
-            x = merge_softmax(x, exchange(x, axis, r[0], size), width, heads)
+            x = merge_softmax(x, recv[0], width, heads)
         else:
-            a, b = r
-            pa, pb, pc = (exchange(x, axis, m, size) for m in (a, b, a ^ b))
-            x = merge_softmax(merge_softmax(x, pa, width, heads), merge_softmax(pb, pc, width, heads), width, heads)
-    return x
+            x = merge_softmax(
+                merge_softmax(x, recv[0], width, heads), merge_softmax(recv[1], recv[2], width, heads), width, heads
+            )
+    return x, gather
 
 
 RINGS = {"seq": {32: (4, 8)}, "tensor": {8: (4, 2)}}
@@ -103,18 +152,15 @@
     packed = jnp.concatenate(
         [project(0), partial_low, partial_sq, jnp.zeros((rows, 127), f32)], axis=1
     )
-    summed = butterfly_sum(packed, "seq", seq_masks)
-    kv_summed = butterfly_sum(jnp.concatenate([project(1), project(2)], axis=1), "seq", seq_masks)
+    summed, kv_piece = butterfly_sum(
+        packed, "seq", seq_masks, jnp.concatenate([project(1), project(2)], axis=1)
+    )
     low = summed[:, local : local + rank]
     total_sq = summed[:, local + rank]
     scale_rows = lax.rsqrt(total_sq / INPUT_WIDTH + 1e-05)[:, None]
     lowrank = (low * scale_rows).astype(bf16)
     query_adapter = jnp.dot(lowrank, adapter_up_weight, preferred_element_type=f32)
     queries = (summed[:, :local] * scale_rows + query_adapter).astype(bf16)
-    keys_full = kv_summed[:, :local] * scale_rows
-    values_full = kv_summed[:, local:] * scale_rows
-    new_keys = keys_full.astype(bf16)
-    new_values = values_full.astype(bf16)
 
     col_head = jnp.arange(local, dtype=jnp.int32) // HD
     head_mask = col_head[None, :] == jnp.arange(heads, dtype=jnp.int32)[:, None]
@@ -157,7 +203,11 @@
         ],
         axis=1,
     )
-    merged = butterfly_softmax(packed, "seq", seq_masks, local, heads)
+    merged, kv_summed = butterfly_softmax(packed, "seq", seq_masks, local, heads, kv_piece)
+    keys_full = kv_summed[:, :local] * scale_rows
+    values_full = kv_summed[:, local:] * scale_rows
+    new_keys = keys_full.astype(bf16)
+    new_values = values_full.astype(bf16)
     cache_out = merged[:, :local]
     cache_total = merged[:, local : local + heads]
     cache_top = merged[:, local + heads : local + 2 * heads]
@@ -183,7 +233,7 @@
     total = cache_total * cache_scale + own_total
     attn = (output / jnp.repeat(total, HD, axis=1)).astype(bf16)
     partial_out = jnp.dot(attn, output_weight, preferred_element_type=f32)
-    mixed = butterfly_sum(partial_out, "tensor", tensor_masks)
+    mixed, _ = butterfly_sum(partial_out, "tensor", tensor_masks)
     return (mixed, jnp.stack([keys_full, values_full]))
 
 

time: 83.1 us -> 86.2 us (1.037)
  waiting for transfers between devices: 22.6 us -> 29.2 us
  starting transfers between devices: 37.6 us -> 32.3 us
    ppermute x25 -> x18, waiting for transfers between devices: 22.6 us -> 29.2 us  [exchange(): return lax.ppermute(x, axis, [(i, i ^ mask) for i in range(size)])]
    ppermute x25 -> x18, starting transfers between devices: 37.6 us -> 32.3 us  [exchange(): return lax.ppermute(x, axis, [(i, i ^ mask) for i in range(size)])]
  transfers between devices with their start and end apart: 25 -> 18, of which waited for: 12 -> 14; matrix products, arithmetic and copies ran while one was open for 18% -> 4% of each run, Pallas kernels for 0% -> 0%
where the time goes in v6:
time: 86.2 us; the launch traced here: 85.5 us
  starting transfers between devices  32.3 us (37%)
  waiting for transfers between devices  29.2 us (34%)
  matrix products  11.4 us (13%)
  other arithmetic  6.37 us (7%)
  local copies, waits for them, and re-layouts  5.06 us (6%)
  between operations  1.11 us (1%)
    ppermute x18, starting transfers between devices, exchange(): return lax.ppermute(x, axis, [(i, i ^ mask) for i in range(size)])  32.3 us
    ppermute x18, waiting for transfers between devices, exchange(): return lax.ppermute(x, axis, [(i, i ^ mask) for i in range(size)])  29.2 us
    dot_general x3, matrix products, project(): jnp.dot(scaled, query_key_value_weight[:, j, :], preferred_element_type=f32)  3.66 us
    dot_general x1, matrix products, shards(): jnp.einsum('rnc,rpc->rnp', q_block, cached_key_rows, preferred_element_ty...  3.17 us
    dot_general x1, matrix products, shards(): jnp.einsum('rnp,rpc->rnc', expo.astype(bf16), cached_value_rows, preferre...  2.68 us
  transfers between devices with their start and end apart: 18, of which 14 were waited for; matrix products, arithmetic and copies ran while one was open for 4% of the time, Pallas kernels for 0%

profile of v6, /device:TPU:1, one launch (start us, length us, event | category | flops | bytes accessed | tf_op | source)
XLA Modules:
  0.0 85.5 jit_solution(5326157337369499056)
XLA Ops:
  0.7 1.3 %fusion.2 = f32[16,896]{1,0:T(8,128)S(1)} fusion(bf16[224,3,896]{2,0,1:T(8,128)(2,1)} %param.13, bf16[16,224]{1,0:T(8,128)(2,1)} %param.11, f32[224]{0:T(256)} %param.12), kind=kOutput, calls=%fused_computation.5 | convolution fusion | flops 6433280 | bytes 467968 | tf_op jit(solution)/shard_map/dot_general | solution.py:148
  1.9 1.2 %fusion.4 = f32[16,896]{1,0:T(8,128)S(1)} fusion(bf16[224,3,896]{2,0,1:T(8,128)(2,1)} %param.13, bf16[16,224]{1,0:T(8,128)(2,1)} %param.11, f32[224]{0:T(256)} %param.12), kind=kOutput, calls=%fused_computation.7 | convolution fusion | flops 6433280 | bytes 467968 | tf_op jit(solution)/shard_map/dot_general | solution.py:148
  3.1 1.2 %fusion.6 = f32[16,896]{1,0:T(8,128)S(1)} fusion(bf16[224,3,896]{2,0,1:T(8,128)(2,1)} %param.13, bf16[16,224]{1,0:T(8,128)(2,1)} %param.11, f32[224]{0:T(256)} %param.12), kind=kOutput, calls=%fused_computation.9 | convolution fusion | flops 6433280 | bytes 467968 | tf_op jit(solution)/shard_map/dot_general | solution.py:148
  4.3 0.8 fusion.54
  5.3 1.0 %fusion.88 = f32[16,128]{1,0:T(8,128)S(1)} fusion(bf16[224,128]{1,0:T(8,128)(2,1)} %param.14, bf16[16,224]{1,0:T(8,128)(2,1)} %param.11, f32[224]{0:T(256)} %param.12), kind=kOutput, calls=%fused_computation.177 | convolution fusion | flops 928256 | bytes 73600 | tf_op jit(solution)/shard_map/dot_general | solution.py:150
  6.4 2.5 %collective-permute-start = (f32[16,1600]{1,0:T(8,128)S(1)}, f32[16,1600]{1,0:T(8,128)S(1)}, u32[]{:S(2)}, u32[]{:S(2)}) collective-permute-start(f32[16,1600]{1,0:T(8,128)S(1)} %concatenate.89), channel_id=1, source_target_pairs={{0,8},{8,0},{16,24},{24,16},{32,40},{40,32},{48,56},{56,48},{64,72... | collective-permute-start | bytes 307208 | tf_op jit(solution)/shard_map/ppermute | solution.py:34
  9.0 2.8 %collective-permute-start.2 = (f32[16,1600]{1,0:T(8,128)S(1)}, f32[16,1600]{1,0:T(8,128)S(1)}, u32[]{:S(2)}, u32[]{:S(2)}) collective-permute-start(f32[16,1600]{1,0:T(8,128)S(1)} %concatenate.91), channel_id=1, source_target_pairs={{0,24},{8,16},{16,8},{24,0},{32,56},{40,48},{48,40},{56,32},{64,88... | collective-permute-start | bytes 307208 | tf_op jit(solution)/shard_map/ppermute | solution.py:34
  11.9 0.3 collective-permute-start.1
  12.3 0.7 iota_add_fusion
  13.0 0.7 broadcast_compare_fusion.1
  13.7 0.7 fusion.50
  14.6 1.9 %collective-permute-done.2 = f32[16,1600]{1,0:T(8,128)S(1)} collective-permute-done((f32[16,1600]{1,0:T(8,128)S(1)}, f32[16,1600]{1,0:T(8,128)S(1)}, u32[]{:S(2)}, u32[]{:S(2)}) %collective-permute-start.2) | collective-permute-done | bytes 102432 | tf_op jit(solution)/shard_map/ppermute | solution.py:34
  16.5 5.3 %collective-permute-done.1 = f32[16,1600]{1,0:T(8,128)S(1)} collective-permute-done((f32[16,1600]{1,0:T(8,128)S(1)}, f32[16,1600]{1,0:T(8,128)S(1)}, u32[]{:S(2)}, u32[]{:S(2)}) %collective-permute-start.1) | collective-permute-done | bytes 102432 | tf_op jit(solution)/shard_map/ppermute | solution.py:34
  22.0 2.3 %collective-permute-start.3 = (f32[16,1376]{1,0:T(8,128)S(1)}, f32[16,1376]{1,0:T(8,128)S(1)}, u32[]{:S(2)}, u32[]{:S(2)}) collective-permute-start(f32[16,1376]{1,0:T(8,128)S(1)} %pad_maximum_fusion.1), channel_id=1, source_target_pairs={{0,48},{8,56},{16,32},{24,40},{32,16},{40,24},{48,0},{56,8},{64,11... | collective-permute-start | bytes 264200 | tf_op jit(solution)/shard_map/ppermute | solution.py:34
  24.3 3.3 %collective-permute-done.3 = f32[16,1376]{1,0:T(8,128)S(1)} collective-permute-done((f32[16,1376]{1,0:T(8,128)S(1)}, f32[16,1376]{1,0:T(8,128)S(1)}, u32[]{:S(2)}, u32[]{:S(2)}) %collective-permute-start.3) | collective-permute-done | bytes 88096 | tf_op jit(solution)/shard_map/ppermute | solution.py:34
  27.9 1.3 %collective-permute-start.4 = (f32[16,1208]{1,0:T(8,128)S(1)}, f32[16,1208]{1,0:T(8,128)S(1)}, u32[]{:S(2)}, u32[]{:S(2)}) collective-permute-start(f32[16,1208]{1,0:T(8,128)S(1)} %get-tuple-element.36), channel_id=1, source_target_pairs={{0,64},{8,72},{16,80},{24,88},{32,96},{40,104},{48,112},{56,120},{... | collective-permute-start | bytes 231944 | tf_op jit(solution)/shard_map/ppermute | solution.py:34
  29.2 1.8 %collective-permute-start.5 = (f32[16,1208]{1,0:T(8,128)S(1)}, f32[16,1208]{1,0:T(8,128)S(1)}, u32[]{:S(2)}, u32[]{:S(2)}) collective-permute-start(f32[16,1208]{1,0:T(8,128)S(1)} %get-tuple-element.37), channel_id=1, source_target_pairs={{0,192},{8,200},{16,208},{24,216},{32,224},{40,232},{48,240},{56,2... | collective-permute-start | bytes 231944 | tf_op jit(solution)/shard_map/ppermute | solution.py:34
  31.0 0.6 collective-permute-start.6
  31.8 1.9 %collective-permute-done.5 = f32[16,1208]{1,0:T(8,128)S(1)} collective-permute-done((f32[16,1208]{1,0:T(8,128)S(1)}, f32[16,1208]{1,0:T(8,128)S(1)}, u32[]{:S(2)}, u32[]{:S(2)}) %collective-permute-start.5) | collective-permute-done | bytes 77344 | tf_op jit(solution)/shard_map/ppermute | solution.py:34
  33.7 2.8 %collective-permute-done.6 = f32[16,1208]{1,0:T(8,128)S(1)} collective-permute-done((f32[16,1208]{1,0:T(8,128)S(1)}, f32[16,1208]{1,0:T(8,128)S(1)}, u32[]{:S(2)}, u32[]{:S(2)}) %collective-permute-start.6) | collective-permute-done | bytes 77344 | tf_op jit(solution)/shard_map/ppermute | solution.py:34
  36.5 0.1 fusion.75
  36.6 0.2 fusion.39
  36.9 3.2 %fusion.101 = (f32[4,16]{1,0:T(4,128)S(1)}, f32[4,16,512]{2,1,0:T(8,128)S(1)}) fusion(pred[4,16,512]{2,1,0:T(8,128)(4,1)S(1)} %reshape.317, bf16[4,512,896]{2,1,0:T(8,128)(2,1)} %param.17, bf16[4,16,896]{2,1,0:T(8,128)(2,1)S(1)} %broadcast_in_dim.148, pred[16,896]{1,0:T(8,128)(4,1)S(1)} %broadcast_in_dim.142), kind=kOutput, calls=%fused_computation.189 | convolution fusion | flops 58875840 | bytes 3963136 | tf_op jit(solution)/shard_map/rnc,rpc->rnp/dot_general | solution.py:170
  40.2 0.2 fusion.13
  40.5 0.1 copy.82
  40.6 2.7 %fusion.17 = f32[4,16,896]{2,1,0:T(8,128)S(1)} fusion(bf16[4,512,896]{2,1,0:T(8,128)(2,1)} %param.18, f32[4,16,512]{2,1,0:T(8,128)S(1)} %get-tuple-element.46, f32[4,16]{1,0:T(4,128)S(1)} %get-tuple-element.45, u8[16,512]{1,0:T(8,128)(4,1)S(1)} %fusion.44), kind=kOutput, calls=%fused_computation.34 | convolution fusion | flops 58949632 | bytes 4038912 | tf_op jit(solution)/shard_map/rnp,rpc->rnc/dot_general | solution.py:186
  43.5 0.1 copy.80
  43.8 0.4 collective-permute-start.7
  44.2 0.6 collective-permute-start.8
  44.8 2.2 %collective-permute-start.9 = (f32[16,1080]{1,0:T(8,128)S(1)}, f32[16,1080]{1,0:T(8,128)S(1)}, u32[]{:S(2)}, u32[]{:S(2)}) collective-permute-start(f32[16,1080]{1,0:T(8,128)S(1)} %concatenate.96), channel_id=1, source_target_pairs={{0,128},{8,136},{16,144},{24,152},{32,160},{40,168},{48,176},{56,1... | collective-permute-start | bytes 207368 | tf_op jit(solution)/shard_map/ppermute | solution.py:34
  47.0 1.5 %collective-permute-done.8 = f32[16,1080]{1,0:T(8,128)S(1)} collective-permute-done((f32[16,1080]{1,0:T(8,128)S(1)}, f32[16,1080]{1,0:T(8,128)S(1)}, u32[]{:S(2)}, u32[]{:S(2)}) %collective-permute-start.8) | collective-permute-done | bytes 69152 | tf_op jit(solution)/shard_map/ppermute | solution.py:34
  48.6 0.9 %collective-permute-done.9 = f32[16,1080]{1,0:T(8,128)S(1)} collective-permute-done((f32[16,1080]{1,0:T(8,128)S(1)}, f32[16,1080]{1,0:T(8,128)S(1)}, u32[]{:S(2)}, u32[]{:S(2)}) %collective-permute-start.9) | collective-permute-done | bytes 69152 | tf_op jit(solution)/shard_map/ppermute | solution.py:34
  49.7 0.1 reshape.324
  50.9 1.7 %collective-permute-start.10 = (f32[16,1248]{1,0:T(8,128)S(1)}, f32[16,1248]{1,0:T(8,128)S(1)}, u32[]{:S(2)}, u32[]{:S(2)}) collective-permute-start(f32[16,1248]{1,0:T(8,128)S(1)} %concatenate.97), channel_id=1, source_target_pairs={{0,48},{8,56},{16,32},{24,40},{32,16},{40,24},{48,0},{56,8},{64,11... | collective-permute-start | bytes 239624 | tf_op jit(solution)/shard_map/ppermute | solution.py:34
  52.6 3.8 %collective-permute-done.10 = f32[16,1248]{1,0:T(8,128)S(1)} collective-permute-done((f32[16,1248]{1,0:T(8,128)S(1)}, f32[16,1248]{1,0:T(8,128)S(1)}, u32[]{:S(2)}, u32[]{:S(2)}) %collective-permute-start.10) | collective-permute-done | bytes 79904 | tf_op jit(solution)/shard_map/ppermute | solution.py:34
  56.6 0.1 reshape.330
  57.1 3.2 %collective-permute-start.11 = (f32[16,1472]{1,0:T(8,128)S(1)}, f32[16,1472]{1,0:T(8,128)S(1)}, u32[]{:S(2)}, u32[]{:S(2)}) collective-permute-start(f32[16,1472]{1,0:T(8,128)S(1)} %concatenate.99), channel_id=1, source_target_pairs={{0,8},{8,0},{16,24},{24,16},{32,40},{40,32},{48,56},{56,48},{64,72... | collective-permute-start | bytes 282632 | tf_op jit(solution)/shard_map/ppermute | solution.py:34
  60.2 0.6 collective-permute-start.12
  60.8 1.6 %collective-permute-start.13 = (f32[16,1472]{1,0:T(8,128)S(1)}, f32[16,1472]{1,0:T(8,128)S(1)}, u32[]{:S(2)}, u32[]{:S(2)}) collective-permute-start(f32[16,1472]{1,0:T(8,128)S(1)} %concatenate.99), channel_id=1, source_target_pairs={{0,24},{8,16},{16,8},{24,0},{32,56},{40,48},{48,40},{56,32},{64,88... | collective-permute-start | bytes 282632 | tf_op jit(solution)/shard_map/ppermute | solution.py:34
  62.7 1.9 %collective-permute-done.12 = f32[16,1472]{1,0:T(8,128)S(1)} collective-permute-done((f32[16,1472]{1,0:T(8,128)S(1)}, f32[16,1472]{1,0:T(8,128)S(1)}, u32[]{:S(2)}, u32[]{:S(2)}) %collective-permute-start.12) | collective-permute-done | bytes 94240 | tf_op jit(solution)/shard_map/ppermute | solution.py:34
  64.6 2.5 %collective-permute-done.13 = f32[16,1472]{1,0:T(8,128)S(1)} collective-permute-done((f32[16,1472]{1,0:T(8,128)S(1)}, f32[16,1472]{1,0:T(8,128)S(1)}, u32[]{:S(2)}, u32[]{:S(2)}) %collective-permute-start.13) | collective-permute-done | bytes 94240 | tf_op jit(solution)/shard_map/ppermute | solution.py:34
  67.3 0.1 concatenate.102
  67.4 0.2 fusion.102
  67.6 0.1 copy.76
  67.8 0.1 copy.70
  68.0 0.1 concatenate.104
  68.1 0.2 convolution_bitcast_fusion
  68.5 0.1 copy.79
  69.2 0.1 reshape.334
  69.4 0.1 reshape.335
  69.6 0.1 reshape.336
  69.7 0.1 reshape.337
  69.9 0.1 reshape.340
  70.1 0.1 reshape.344
  70.2 0.2 fusion.51
  70.4 6.4 %collective-permute-start.14 = (f32[16,112]{1,0:T(8,128)S(1)}, f32[16,112]{1,0:T(8,128)S(1)}, u32[]{:S(2)}, u32[]{:S(2)}) collective-permute-start(f32[16,112]{1,0:T(8,128)S(1)} %fusion.51), channel_id=1, source_target_pairs={{0,1},{1,0},{2,3},{3,2},{4,5},{5,4},{6,7},{7,6},{8,9},{9,8},{10,11... | collective-permute-start | bytes 21512 | tf_op jit(solution)/shard_map/ppermute | solution.py:34
  76.9 0.7 collective-permute-done.14
  77.7 1.3 %collective-permute-start.15 = (f32[16,112]{1,0:T(8,128)S(1)}, f32[16,112]{1,0:T(8,128)S(1)}, u32[]{:S(2)}, u32[]{:S(2)}) collective-permute-start(f32[16,112]{1,0:T(8,128)S(1)} %add.187), channel_id=1, source_target_pairs={{0,2},{1,3},{2,0},{3,1},{4,6},{5,7},{6,4},{7,5},{8,10},{9,11},{10,... | collective-permute-start | bytes 21512 | tf_op jit(solution)/shard_map/ppermute | solution.py:34
  79.0 1.9 %collective-permute-start.16 = (f32[16,112]{1,0:T(8,128)S(1)}, f32[16,112]{1,0:T(8,128)S(1)}, u32[]{:S(2)}, u32[]{:S(2)}) collective-permute-start(f32[16,112]{1,0:T(8,128)S(1)} %add.187), channel_id=1, source_target_pairs={{0,6},{1,7},{2,4},{3,5},{4,2},{5,3},{6,0},{7,1},{8,14},{9,15},{10,... | collective-permute-start | bytes 21512 | tf_op jit(solution)/shard_map/ppermute | solution.py:34
  80.9 0.7 collective-permute-start.17
  81.6 0.7 pad_maximum_fusion
  82.3 0.4 collective-permute-done.16
  82.7 2.2 %collective-permute-done.17 = f32[16,112]{1,0:T(8,128)S(1)} collective-permute-done((f32[16,112]{1,0:T(8,128)S(1)}, f32[16,112]{1,0:T(8,128)S(1)}, u32[]{:S(2)}, u32[]{:S(2)}) %collective-permute-start.17) | collective-permute-done | bytes 7200 | tf_op jit(solution)/shard_map/ppermute | solution.py:34
  84.9 0.6 add_add_fusion
  (93 shorter events, 5.3 us)
Async XLA Ops:
  0.6 36.0 %copy-start = (bf16[128,896]{1,0:T(8,128)(2,1)S(1)}, bf16[128,896]{1,0:T(8,128)(2,1)}, u32[]{:S(2)}) copy-start(bf16[128,896]{1,0:T(8,128)(2,1)} %param.15) | copy-start | bytes 688132
  6.4 8.1 %collective-permute-start = (f32[16,1600]{1,0:T(8,128)S(1)}, f32[16,1600]{1,0:T(8,128)S(1)}, u32[]{:S(2)}, u32[]{:S(2)}) collective-permute-start(f32[16,1600]{1,0:T(8,128)S(1)} %concatenate.89), channel_id=1, source_target_pairs={{0,8},{8,0},{16,24},{24,16},{32,40},{40,32},{48,56},{56,48},{64,72... | collective-permute-start | bytes 307208 | tf_op jit(solution)/shard_map/ppermute | solution.py:34
  9.0 7.5 %collective-permute-start.2 = (f32[16,1600]{1,0:T(8,128)S(1)}, f32[16,1600]{1,0:T(8,128)S(1)}, u32[]{:S(2)}, u32[]{:S(2)}) collective-permute-start(f32[16,1600]{1,0:T(8,128)S(1)} %concatenate.91), channel_id=1, source_target_pairs={{0,24},{8,16},{16,8},{24,0},{32,56},{40,48},{48,40},{56,32},{64,88... | collective-permute-start | bytes 307208 | tf_op jit(solution)/shard_map/ppermute | solution.py:34
  11.9 9.8 %collective-permute-start.1 = (f32[16,1600]{1,0:T(8,128)S(1)}, f32[16,1600]{1,0:T(8,128)S(1)}, u32[]{:S(2)}, u32[]{:S(2)}) collective-permute-start(f32[16,1600]{1,0:T(8,128)S(1)} %concatenate.90), channel_id=1, source_target_pairs={{0,16},{8,24},{16,0},{24,8},{32,48},{40,56},{48,32},{56,40},{64,80... | collective-permute-start | bytes 307208 | tf_op jit(solution)/shard_map/ppermute | solution.py:34
  22.0 5.7 %collective-permute-start.3 = (f32[16,1376]{1,0:T(8,128)S(1)}, f32[16,1376]{1,0:T(8,128)S(1)}, u32[]{:S(2)}, u32[]{:S(2)}) collective-permute-start(f32[16,1376]{1,0:T(8,128)S(1)} %pad_maximum_fusion.1), channel_id=1, source_target_pairs={{0,48},{8,56},{16,32},{24,40},{32,16},{40,24},{48,0},{56,8},{64,11... | collective-permute-start | bytes 264200 | tf_op jit(solution)/shard_map/ppermute | solution.py:34
  27.9 3.9 %collective-permute-start.4 = (f32[16,1208]{1,0:T(8,128)S(1)}, f32[16,1208]{1,0:T(8,128)S(1)}, u32[]{:S(2)}, u32[]{:S(2)}) collective-permute-start(f32[16,1208]{1,0:T(8,128)S(1)} %get-tuple-element.36), channel_id=1, source_target_pairs={{0,64},{8,72},{16,80},{24,88},{32,96},{40,104},{48,112},{56,120},{... | collective-permute-start | bytes 231944 | tf_op jit(solution)/shard_map/ppermute | solution.py:34
  29.2 4.5 %collective-permute-start.5 = (f32[16,1208]{1,0:T(8,128)S(1)}, f32[16,1208]{1,0:T(8,128)S(1)}, u32[]{:S(2)}, u32[]{:S(2)}) collective-permute-start(f32[16,1208]{1,0:T(8,128)S(1)} %get-tuple-element.37), channel_id=1, source_target_pairs={{0,192},{8,200},{16,208},{24,216},{32,224},{40,232},{48,240},{56,2... | collective-permute-start | bytes 231944 | tf_op jit(solution)/shard_map/ppermute | solution.py:34
  31.0 5.4 %collective-permute-start.6 = (f32[16,1208]{1,0:T(8,128)S(1)}, f32[16,1208]{1,0:T(8,128)S(1)}, u32[]{:S(2)}, u32[]{:S(2)}) collective-permute-start(f32[16,1208]{1,0:T(8,128)S(1)} %get-tuple-element.38), channel_id=1, source_target_pairs={{0,128},{8,136},{16,144},{24,152},{32,160},{40,168},{48,176},{56,1... | collective-permute-start | bytes 231944 | tf_op jit(solution)/shard_map/ppermute | solution.py:34
  43.5 26.7 %copy-start.1 = (bf16[896,112]{0,1:T(8,128)(2,1)S(1)}, bf16[896,112]{0,1:T(8,128)(2,1)}, u32[]{:S(2)}) copy-start(bf16[896,112]{0,1:T(8,128)(2,1)} %param.16) | copy-start | bytes 602116
  43.8 3.3 %collective-permute-start.7 = (f32[16,1080]{1,0:T(8,128)S(1)}, f32[16,1080]{1,0:T(8,128)S(1)}, u32[]{:S(2)}, u32[]{:S(2)}) collective-permute-start(f32[16,1080]{1,0:T(8,128)S(1)} %concatenate.96), channel_id=1, source_target_pairs={{0,64},{8,72},{16,80},{24,88},{32,96},{40,104},{48,112},{56,120},{... | collective-permute-start | bytes 207368 | tf_op jit(solution)/shard_map/ppermute | solution.py:34
  44.2 4.4 %collective-permute-start.8 = (f32[16,1080]{1,0:T(8,128)S(1)}, f32[16,1080]{1,0:T(8,128)S(1)}, u32[]{:S(2)}, u32[]{:S(2)}) collective-permute-start(f32[16,1080]{1,0:T(8,128)S(1)} %concatenate.96), channel_id=1, source_target_pairs={{0,192},{8,200},{16,208},{24,216},{32,224},{40,232},{48,240},{56,2... | collective-permute-start | bytes 207368 | tf_op jit(solution)/shard_map/ppermute | solution.py:34
  44.8 4.7 %collective-permute-start.9 = (f32[16,1080]{1,0:T(8,128)S(1)}, f32[16,1080]{1,0:T(8,128)S(1)}, u32[]{:S(2)}, u32[]{:S(2)}) collective-permute-start(f32[16,1080]{1,0:T(8,128)S(1)} %concatenate.96), channel_id=1, source_target_pairs={{0,128},{8,136},{16,144},{24,152},{32,160},{40,168},{48,176},{56,1... | collective-permute-start | bytes 207368 | tf_op jit(solution)/shard_map/ppermute | solution.py:34
  50.9 5.5 %collective-permute-start.10 = (f32[16,1248]{1,0:T(8,128)S(1)}, f32[16,1248]{1,0:T(8,128)S(1)}, u32[]{:S(2)}, u32[]{:S(2)}) collective-permute-start(f32[16,1248]{1,0:T(8,128)S(1)} %concatenate.97), channel_id=1, source_target_pairs={{0,48},{8,56},{16,32},{24,40},{32,16},{40,24},{48,0},{56,8},{64,11... | collective-permute-start | bytes 239624 | tf_op jit(solution)/shard_map/ppermute | solution.py:34
  57.1 5.6 %collective-permute-start.11 = (f32[16,1472]{1,0:T(8,128)S(1)}, f32[16,1472]{1,0:T(8,128)S(1)}, u32[]{:S(2)}, u32[]{:S(2)}) collective-permute-start(f32[16,1472]{1,0:T(8,128)S(1)} %concatenate.99), channel_id=1, source_target_pairs={{0,8},{8,0},{16,24},{24,16},{32,40},{40,32},{48,56},{56,48},{64,72... | collective-permute-start | bytes 282632 | tf_op jit(solution)/shard_map/ppermute | solution.py:34
  60.2 4.4 %collective-permute-start.12 = (f32[16,1472]{1,0:T(8,128)S(1)}, f32[16,1472]{1,0:T(8,128)S(1)}, u32[]{:S(2)}, u32[]{:S(2)}) collective-permute-start(f32[16,1472]{1,0:T(8,128)S(1)} %concatenate.99), channel_id=1, source_target_pairs={{0,16},{8,24},{16,0},{24,8},{32,48},{40,56},{48,32},{56,40},{64,80... | collective-permute-start | bytes 282632 | tf_op jit(solution)/shard_map/ppermute | solution.py:34
  60.8 6.2 %collective-permute-start.13 = (f32[16,1472]{1,0:T(8,128)S(1)}, f32[16,1472]{1,0:T(8,128)S(1)}, u32[]{:S(2)}, u32[]{:S(2)}) collective-permute-start(f32[16,1472]{1,0:T(8,128)S(1)} %concatenate.99), channel_id=1, source_target_pairs={{0,24},{8,16},{16,8},{24,0},{32,56},{40,48},{48,40},{56,32},{64,88... | collective-permute-start | bytes 282632 | tf_op jit(solution)/shard_map/ppermute | solution.py:34
  70.4 7.3 %collective-permute-start.14 = (f32[16,112]{1,0:T(8,128)S(1)}, f32[16,112]{1,0:T(8,128)S(1)}, u32[]{:S(2)}, u32[]{:S(2)}) collective-permute-start(f32[16,112]{1,0:T(8,128)S(1)} %fusion.51), channel_id=1, source_target_pairs={{0,1},{1,0},{2,3},{3,2},{4,5},{5,4},{6,7},{7,6},{8,9},{9,8},{10,11... | collective-permute-start | bytes 21512 | tf_op jit(solution)/shard_map/ppermute | solution.py:34
  77.7 4.6 %collective-permute-start.15 = (f32[16,112]{1,0:T(8,128)S(1)}, f32[16,112]{1,0:T(8,128)S(1)}, u32[]{:S(2)}, u32[]{:S(2)}) collective-permute-start(f32[16,112]{1,0:T(8,128)S(1)} %add.187), channel_id=1, source_target_pairs={{0,2},{1,3},{2,0},{3,1},{4,6},{5,7},{6,4},{7,5},{8,10},{9,11},{10,... | collective-permute-start | bytes 21512 | tf_op jit(solution)/shard_map/ppermute | solution.py:34
  79.0 3.7 %collective-permute-start.16 = (f32[16,112]{1,0:T(8,128)S(1)}, f32[16,112]{1,0:T(8,128)S(1)}, u32[]{:S(2)}, u32[]{:S(2)}) collective-permute-start(f32[16,112]{1,0:T(8,128)S(1)} %add.187), channel_id=1, source_target_pairs={{0,6},{1,7},{2,4},{3,5},{4,2},{5,3},{6,0},{7,1},{8,14},{9,15},{10,... | collective-permute-start | bytes 21512 | tf_op jit(solution)/shard_map/ppermute | solution.py:34
  80.9 4.0 %collective-permute-start.17 = (f32[16,112]{1,0:T(8,128)S(1)}, f32[16,112]{1,0:T(8,128)S(1)}, u32[]{:S(2)}, u32[]{:S(2)}) collective-permute-start(f32[16,112]{1,0:T(8,128)S(1)} %add.187), channel_id=1, source_target_pairs={{0,4},{1,5},{2,6},{3,7},{4,0},{5,1},{6,2},{7,3},{8,12},{9,13},{10,... | collective-permute-start | bytes 21512 | tf_op jit(solution)/shard_map/ppermute | solution.py:34

commit v7 on v5

--- a/solution.py
+++ b/solution.py
@@ -107,7 +107,7 @@
     kv_partial, summed = lax.optimization_barrier(
         (jnp.concatenate([project(1), project(2)], axis=1), summed)
     )
-    kv_summed = butterfly_sum(kv_partial, "seq", seq_masks)
+    kv_summed = butterfly_sum(kv_partial, "seq", [(m,) for r in seq_masks for m in r])
     low = summed[:, local : local + rank]
     total_sq = summed[:, local + rank]
     scale_rows = lax.rsqrt(total_sq / INPUT_WIDTH + 1e-05)[:, None]

time: 87.8 us -> 89.7 us (1.022)
  starting transfers between devices: 40.3 us -> 43.1 us
    ppermute x25 -> x23, starting transfers between devices: 40.3 us -> 43.1 us  [exchange(): return lax.ppermute(x, axis, [(i, i ^ mask) for i in range(size)])]
    ppermute x25 -> x23, waiting for transfers between devices: 23.8 us -> 23.6 us  [exchange(): return lax.ppermute(x, axis, [(i, i ^ mask) for i in range(size)])]
  transfers between devices with their start and end apart: 25 -> 23, of which waited for: 10 -> 14; matrix products, arithmetic and copies ran while one was open for 9% -> 9% of each run, Pallas kernels for 0% -> 0%
where the time goes in v7:
time: 89.7 us; the launch traced here: 89.2 us
  starting transfers between devices  43.1 us (48%)
  waiting for transfers between devices  23.6 us (26%)
  matrix products  11.2 us (12%)
  other arithmetic  5.73 us (6%)
  local copies, waits for them, and re-layouts  4.55 us (5%)
  between operations  1 us (1%)
    ppermute x23, starting transfers between devices, exchange(): return lax.ppermute(x, axis, [(i, i ^ mask) for i in range(size)])  43.1 us
    ppermute x23, waiting for transfers between devices, exchange(): return lax.ppermute(x, axis, [(i, i ^ mask) for i in range(size)])  23.6 us
    dot_general x3, matrix products, project(): jnp.dot(scaled, query_key_value_weight[:, j, :], preferred_element_type=f32)  3.6 us
    dot_general x1, matrix products, shards(): jnp.einsum('rnc,rpc->rnp', q_block, cached_key_rows, preferred_element_ty...  3.17 us
    dot_general x1, matrix products, shards(): jnp.einsum('rnp,rpc->rnc', expo.astype(bf16), cached_value_rows, preferre...  2.68 us
  transfers between devices with their start and end apart: 23, of which 14 were waited for; matrix products, arithmetic and copies ran while one was open for 9% of the time, Pallas kernels for 0%

profile of v7, /device:TPU:1, one launch (start us, length us, event | category | flops | bytes accessed | tf_op | source)
XLA Modules:
  0.0 89.2 jit_solution(11645932103113979909)
XLA Ops:
  0.6 0.9 fusion.50
  1.6 1.0 %fusion.73 = f32[16,128]{1,0:T(8,128)S(1)} fusion(bf16[224,128]{1,0:T(8,128)(2,1)} %param.14, bf16[16,224]{1,0:T(8,128)(2,1)} %param.11, f32[224]{0:T(256)} %param.12), kind=kOutput, calls=%fused_computation.138 | convolution fusion | flops 928256 | bytes 73600 | tf_op jit(solution)/shard_map/dot_general | solution.py:101
  2.6 1.2 %fusion.3 = f32[16,896]{1,0:T(8,128)S(1)} fusion(bf16[224,3,896]{2,0,1:T(8,128)(2,1)} %param.13, bf16[16,224]{1,0:T(8,128)(2,1)} %param.11, f32[224]{0:T(256)} %param.12), kind=kOutput, calls=%fused_computation.7 | convolution fusion | flops 6433280 | bytes 467968 | tf_op jit(solution)/shard_map/dot_general | solution.py:99
  3.9 5.2 %collective-permute-start.2 = (f32[16,1152]{1,0:T(8,128)S(1)}, f32[16,1152]{1,0:T(8,128)S(1)}, u32[]{:S(2)}, u32[]{:S(2)}) collective-permute-start(f32[16,1152]{1,0:T(8,128)S(1)} %concatenate.16), channel_id=1, source_target_pairs={{0,24},{8,16},{16,8},{24,0},{32,56},{40,48},{48,40},{56,32},{64,88... | collective-permute-start | bytes 221192 | tf_op jit(solution)/shard_map/ppermute | solution.py:28
  9.1 0.4 collective-permute-start
  9.5 1.2 %fusion.7 = f32[16,896]{1,0:T(8,128)S(1)} fusion(bf16[224,3,896]{2,0,1:T(8,128)(2,1)} %param.13, bf16[16,224]{1,0:T(8,128)(2,1)} %param.11, f32[224]{0:T(256)} %param.12), kind=kOutput, calls=%fused_computation.11 | convolution fusion | flops 6433280 | bytes 467968 | tf_op jit(solution)/shard_map/dot_general | solution.py:99
  10.6 1.2 %fusion.5 = f32[16,896]{1,0:T(8,128)S(1)} fusion(bf16[224,3,896]{2,0,1:T(8,128)(2,1)} %param.13, bf16[16,224]{1,0:T(8,128)(2,1)} %param.11, f32[224]{0:T(256)} %param.12), kind=kOutput, calls=%fused_computation.9 | convolution fusion | flops 6433280 | bytes 467968 | tf_op jit(solution)/shard_map/dot_general | solution.py:99
  11.9 0.7 iota_add_fusion
  12.6 0.7 broadcast_compare_fusion.1
  13.4 0.7 fusion.46
  14.1 1.2 %collective-permute-done.1 = f32[16,1152]{1,0:T(8,128)S(1)} collective-permute-done((f32[16,1152]{1,0:T(8,128)S(1)}, f32[16,1152]{1,0:T(8,128)S(1)}, u32[]{:S(2)}, u32[]{:S(2)}) %collective-permute-start.1) | collective-permute-done | bytes 73760 | tf_op jit(solution)/shard_map/ppermute | solution.py:28
  15.3 3.1 %collective-permute-start.3 = (f32[16,1152]{1,0:T(8,128)S(1)}, f32[16,1152]{1,0:T(8,128)S(1)}, u32[]{:S(2)}, u32[]{:S(2)}) collective-permute-start(f32[16,1152]{1,0:T(8,128)S(1)} %add_add_fusion.1), channel_id=1, source_target_pairs={{0,48},{8,56},{16,32},{24,40},{32,16},{40,24},{48,0},{56,8},{64,11... | collective-permute-start | bytes 221192 | tf_op jit(solution)/shard_map/ppermute | solution.py:28
  18.4 2.3 %collective-permute-done.3 = f32[16,1152]{1,0:T(8,128)S(1)} collective-permute-done((f32[16,1152]{1,0:T(8,128)S(1)}, f32[16,1152]{1,0:T(8,128)S(1)}, u32[]{:S(2)}, u32[]{:S(2)}) %collective-permute-start.3) | collective-permute-done | bytes 73760 | tf_op jit(solution)/shard_map/ppermute | solution.py:28
  20.7 2.8 %collective-permute-start.6 = (f32[16,1152]{1,0:T(8,128)S(1)}, f32[16,1152]{1,0:T(8,128)S(1)}, u32[]{:S(2)}, u32[]{:S(2)}) collective-permute-start(f32[16,1152]{1,0:T(8,128)S(1)} %add.142), channel_id=1, source_target_pairs={{0,128},{8,136},{16,144},{24,152},{32,160},{40,168},{48,176},{56,1... | collective-permute-start | bytes 221192 | tf_op jit(solution)/shard_map/ppermute | solution.py:28
  23.6 0.9 collective-permute-start.5
  24.6 0.9 %collective-permute-done.6 = f32[16,1152]{1,0:T(8,128)S(1)} collective-permute-done((f32[16,1152]{1,0:T(8,128)S(1)}, f32[16,1152]{1,0:T(8,128)S(1)}, u32[]{:S(2)}, u32[]{:S(2)}) %collective-permute-start.6) | collective-permute-done | bytes 73760 | tf_op jit(solution)/shard_map/ppermute | solution.py:28
  25.5 3.2 %collective-permute-done.5 = f32[16,1152]{1,0:T(8,128)S(1)} collective-permute-done((f32[16,1152]{1,0:T(8,128)S(1)}, f32[16,1152]{1,0:T(8,128)S(1)}, u32[]{:S(2)}, u32[]{:S(2)}) %collective-permute-start.5) | collective-permute-done | bytes 73760 | tf_op jit(solution)/shard_map/ppermute | solution.py:28
  28.8 0.1 rsqrt_reduce_fusion
  28.9 0.2 fusion.1
  29.2 3.2 %fusion.89 = (f32[4,16]{1,0:T(4,128)S(1)}, f32[4,16,512]{2,1,0:T(8,128)S(1)}) fusion(pred[4,16,512]{2,1,0:T(8,128)(4,1)S(1)} %reshape.227, bf16[4,512,896]{2,1,0:T(8,128)(2,1)} %param.17, bf16[4,16,896]{2,1,0:T(8,128)(2,1)S(1)} %broadcast_in_dim.148, pred[16,896]{1,0:T(8,128)(4,1)S(1)} %broadcast_in_dim.142), kind=kOutput, calls=%fused_computation.151 | convolution fusion | flops 58875840 | bytes 3963136 | tf_op jit(solution)/shard_map/rnc,rpc->rnp/dot_general | solution.py:127
  32.5 0.2 fusion.14
  32.8 0.1 copy.64
  32.9 0.1 copy.62
  33.0 2.7 %fusion.16 = f32[4,16,896]{2,1,0:T(8,128)S(1)} fusion(bf16[4,512,896]{2,1,0:T(8,128)(2,1)} %param.18, f32[4,16,512]{2,1,0:T(8,128)S(1)} %get-tuple-element.38, f32[4,16]{1,0:T(4,128)S(1)} %get-tuple-element.37, u8[16,512]{1,0:T(8,128)(4,1)S(1)} %fusion.41), kind=kOutput, calls=%fused_computation.28 | convolution fusion | flops 58949632 | bytes 4038912 | tf_op jit(solution)/shard_map/rnp,rpc->rnc/dot_general | solution.py:143
  35.9 1.6 %collective-permute-start.9 = (f32[16,1024]{1,0:T(8,128)S(1)}, f32[16,1024]{1,0:T(8,128)S(1)}, u32[]{:S(2)}, u32[]{:S(2)}) collective-permute-start(f32[16,1024]{1,0:T(8,128)S(1)} %maximum_maximum_fusion), channel_id=1, source_target_pairs={{0,24},{8,16},{16,8},{24,0},{32,56},{40,48},{48,40},{56,32},{64,88... | collective-permute-start | bytes 196616 | tf_op jit(solution)/shard_map/ppermute | solution.py:28
  37.5 2.2 %collective-permute-start.8 = (f32[16,1024]{1,0:T(8,128)S(1)}, f32[16,1024]{1,0:T(8,128)S(1)}, u32[]{:S(2)}, u32[]{:S(2)}) collective-permute-start(f32[16,1024]{1,0:T(8,128)S(1)} %maximum_maximum_fusion), channel_id=1, source_target_pairs={{0,16},{8,24},{16,0},{24,8},{32,48},{40,56},{48,32},{56,40},{64,80... | collective-permute-start | bytes 196616 | tf_op jit(solution)/shard_map/ppermute | solution.py:28
  39.8 1.5 %collective-permute-start.14 = (f32[16,1792]{1,0:T(8,128)S(1)}, f32[16,1792]{1,0:T(8,128)S(1)}, u32[]{:S(2)}, u32[]{:S(2)}) collective-permute-start(f32[16,1792]{1,0:T(8,128)S(1)} %pad_maximum_fusion), channel_id=1, source_target_pairs={{0,8},{8,0},{16,24},{24,16},{32,40},{40,32},{48,56},{56,48},{64,72... | collective-permute-start | bytes 344072 | tf_op jit(solution)/shard_map/ppermute | solution.py:28
  41.2 1.1 %collective-permute-done.8 = f32[16,1024]{1,0:T(8,128)S(1)} collective-permute-done((f32[16,1024]{1,0:T(8,128)S(1)}, f32[16,1024]{1,0:T(8,128)S(1)}, u32[]{:S(2)}, u32[]{:S(2)}) %collective-permute-start.8) | collective-permute-done | bytes 65568 | tf_op jit(solution)/shard_map/ppermute | solution.py:28
  42.3 0.7 collective-permute-done.7
  43.2 0.1 reshape.234
  43.4 0.1 reshape.235
  43.6 0.1 reshape.236
  43.7 0.1 reshape.237
  43.9 0.1 reshape.238
  44.1 0.1 reshape.239
  44.3 0.7 collective-permute-done.14
  45.0 1.3 %collective-permute-start.15 = (f32[16,1792]{1,0:T(8,128)S(1)}, f32[16,1792]{1,0:T(8,128)S(1)}, u32[]{:S(2)}, u32[]{:S(2)}) collective-permute-start(f32[16,1792]{1,0:T(8,128)S(1)} %add.159), channel_id=1, source_target_pairs={{0,16},{8,24},{16,0},{24,8},{32,48},{40,56},{48,32},{56,40},{64,80... | collective-permute-start | bytes 344072 | tf_op jit(solution)/shard_map/ppermute | solution.py:28
  46.4 4.3 %collective-permute-start.10 = (f32[16,1024]{1,0:T(8,128)S(1)}, f32[16,1024]{1,0:T(8,128)S(1)}, u32[]{:S(2)}, u32[]{:S(2)}) collective-permute-start(f32[16,1024]{1,0:T(8,128)S(1)} %maximum_maximum_fusion.1), channel_id=1, source_target_pairs={{0,48},{8,56},{16,32},{24,40},{32,16},{40,24},{48,0},{56,8},{64,11... | collective-permute-start | bytes 196616 | tf_op jit(solution)/shard_map/ppermute | solution.py:28
  50.8 2.7 %collective-permute-start.16 = (f32[16,1792]{1,0:T(8,128)S(1)}, f32[16,1792]{1,0:T(8,128)S(1)}, u32[]{:S(2)}, u32[]{:S(2)}) collective-permute-start(f32[16,1792]{1,0:T(8,128)S(1)} %add.160), channel_id=1, source_target_pairs={{0,48},{8,56},{16,32},{24,40},{32,16},{40,24},{48,0},{56,8},{64,11... | collective-permute-start | bytes 344072 | tf_op jit(solution)/shard_map/ppermute | solution.py:28
  54.0 4.6 %collective-permute-done.16 = f32[16,1792]{1,0:T(8,128)S(1)} collective-permute-done((f32[16,1792]{1,0:T(8,128)S(1)}, f32[16,1792]{1,0:T(8,128)S(1)}, u32[]{:S(2)}, u32[]{:S(2)}) %collective-permute-start.16) | collective-permute-done | bytes 114720 | tf_op jit(solution)/shard_map/ppermute | solution.py:28
  58.6 0.9 %collective-permute-start.17 = (f32[16,1792]{1,0:T(8,128)S(1)}, f32[16,1792]{1,0:T(8,128)S(1)}, u32[]{:S(2)}, u32[]{:S(2)}) collective-permute-start(f32[16,1792]{1,0:T(8,128)S(1)} %add.161), channel_id=1, source_target_pairs={{0,64},{8,72},{16,80},{24,88},{32,96},{40,104},{48,112},{56,120},{... | collective-permute-start | bytes 344072 | tf_op jit(solution)/shard_map/ppermute | solution.py:28
  59.5 3.1 %collective-permute-done.17 = f32[16,1792]{1,0:T(8,128)S(1)} collective-permute-done((f32[16,1792]{1,0:T(8,128)S(1)}, f32[16,1792]{1,0:T(8,128)S(1)}, u32[]{:S(2)}, u32[]{:S(2)}) %collective-permute-start.17) | collective-permute-done | bytes 114720 | tf_op jit(solution)/shard_map/ppermute | solution.py:28
  62.8 2.5 %collective-permute-start.13 = (f32[16,1024]{1,0:T(8,128)S(1)}, f32[16,1024]{1,0:T(8,128)S(1)}, u32[]{:S(2)}, u32[]{:S(2)}) collective-permute-start(f32[16,1024]{1,0:T(8,128)S(1)} %maximum_maximum_fusion.2), channel_id=1, source_target_pairs={{0,128},{8,136},{16,144},{24,152},{32,160},{40,168},{48,176},{56,1... | collective-permute-start | bytes 196616 | tf_op jit(solution)/shard_map/ppermute | solution.py:28
  65.3 1.0 %collective-permute-start.12 = (f32[16,1024]{1,0:T(8,128)S(1)}, f32[16,1024]{1,0:T(8,128)S(1)}, u32[]{:S(2)}, u32[]{:S(2)}) collective-permute-start(f32[16,1024]{1,0:T(8,128)S(1)} %maximum_maximum_fusion.2), channel_id=1, source_target_pairs={{0,192},{8,200},{16,208},{24,216},{32,224},{40,232},{48,240},{56,2... | collective-permute-start | bytes 196616 | tf_op jit(solution)/shard_map/ppermute | solution.py:28
  66.3 2.0 %collective-permute-done.18 = f32[16,1792]{1,0:T(8,128)S(1)} collective-permute-done((f32[16,1792]{1,0:T(8,128)S(1)}, f32[16,1792]{1,0:T(8,128)S(1)}, u32[]{:S(2)}, u32[]{:S(2)}) %collective-permute-start.18) | collective-permute-done | bytes 114720 | tf_op jit(solution)/shard_map/ppermute | solution.py:28
  68.6 0.2 fusion.88
  68.8 0.1 copy.58
  68.9 0.7 collective-permute-done.12
  69.7 0.1 copy.51
  69.9 0.2 convolution_bitcast_fusion
  70.2 0.1 reshape.254
  70.3 0.1 copy.61
  70.5 0.1 reshape.256
  70.7 0.1 reshape.242
  70.9 0.1 reshape.243
  71.1 0.1 reshape.244
  72.0 0.2 fusion.47
  72.2 9.0 %collective-permute-start.19 = (f32[16,112]{1,0:T(8,128)S(1)}, f32[16,112]{1,0:T(8,128)S(1)}, u32[]{:S(2)}, u32[]{:S(2)}) collective-permute-start(f32[16,112]{1,0:T(8,128)S(1)} %fusion.47), channel_id=1, source_target_pairs={{0,1},{1,0},{2,3},{3,2},{4,5},{5,4},{6,7},{7,6},{8,9},{9,8},{10,11... | collective-permute-start | bytes 21512 | tf_op jit(solution)/shard_map/ppermute | solution.py:28
  81.2 0.8 collective-permute-done.19
  82.0 2.9 %collective-permute-start.22 = (f32[16,112]{1,0:T(8,128)S(1)}, f32[16,112]{1,0:T(8,128)S(1)}, u32[]{:S(2)}, u32[]{:S(2)}) collective-permute-start(f32[16,112]{1,0:T(8,128)S(1)} %add.169), channel_id=1, source_target_pairs={{0,4},{1,5},{2,6},{3,7},{4,0},{5,1},{6,2},{7,3},{8,12},{9,13},{10,... | collective-permute-start | bytes 21512 | tf_op jit(solution)/shard_map/ppermute | solution.py:28
  84.9 0.8 collective-permute-start.21
  85.7 0.7 pad_maximum_fusion.1
  86.3 2.3 %collective-permute-done.21 = f32[16,112]{1,0:T(8,128)S(1)} collective-permute-done((f32[16,112]{1,0:T(8,128)S(1)}, f32[16,112]{1,0:T(8,128)S(1)}, u32[]{:S(2)}, u32[]{:S(2)}) %collective-permute-start.21) | collective-permute-done | bytes 7200 | tf_op jit(solution)/shard_map/ppermute | solution.py:28
  88.6 0.6 add_add_fusion.2
  (90 shorter events, 4.2 us)
Async XLA Ops:
  0.6 28.3 %copy-start = (bf16[128,896]{1,0:T(8,128)(2,1)S(1)}, bf16[128,896]{1,0:T(8,128)(2,1)}, u32[]{:S(2)}) copy-start(bf16[128,896]{1,0:T(8,128)(2,1)} %param.15) | copy-start | bytes 688132
  3.9 10.2 %collective-permute-start.2 = (f32[16,1152]{1,0:T(8,128)S(1)}, f32[16,1152]{1,0:T(8,128)S(1)}, u32[]{:S(2)}, u32[]{:S(2)}) collective-permute-start(f32[16,1152]{1,0:T(8,128)S(1)} %concatenate.16), channel_id=1, source_target_pairs={{0,24},{8,16},{16,8},{24,0},{32,56},{40,48},{48,40},{56,32},{64,88... | collective-permute-start | bytes 221192 | tf_op jit(solution)/shard_map/ppermute | solution.py:28
  9.1 6.2 %collective-permute-start.1 = (f32[16,1152]{1,0:T(8,128)S(1)}, f32[16,1152]{1,0:T(8,128)S(1)}, u32[]{:S(2)}, u32[]{:S(2)}) collective-permute-start(f32[16,1152]{1,0:T(8,128)S(1)} %concatenate.16), channel_id=1, source_target_pairs={{0,16},{8,24},{16,0},{24,8},{32,48},{40,56},{48,32},{56,40},{64,80... | collective-permute-start | bytes 221192 | tf_op jit(solution)/shard_map/ppermute | solution.py:28
  9.1 6.2 %collective-permute-start = (f32[16,1152]{1,0:T(8,128)S(1)}, f32[16,1152]{1,0:T(8,128)S(1)}, u32[]{:S(2)}, u32[]{:S(2)}) collective-permute-start(f32[16,1152]{1,0:T(8,128)S(1)} %concatenate.16), channel_id=1, source_target_pairs={{0,8},{8,0},{16,24},{24,16},{32,40},{40,32},{48,56},{56,48},{64,72... | collective-permute-start | bytes 221192 | tf_op jit(solution)/shard_map/ppermute | solution.py:28
  15.3 5.4 %collective-permute-start.3 = (f32[16,1152]{1,0:T(8,128)S(1)}, f32[16,1152]{1,0:T(8,128)S(1)}, u32[]{:S(2)}, u32[]{:S(2)}) collective-permute-start(f32[16,1152]{1,0:T(8,128)S(1)} %add_add_fusion.1), channel_id=1, source_target_pairs={{0,48},{8,56},{16,32},{24,40},{32,16},{40,24},{48,0},{56,8},{64,11... | collective-permute-start | bytes 221192 | tf_op jit(solution)/shard_map/ppermute | solution.py:28
  20.7 4.8 %collective-permute-start.6 = (f32[16,1152]{1,0:T(8,128)S(1)}, f32[16,1152]{1,0:T(8,128)S(1)}, u32[]{:S(2)}, u32[]{:S(2)}) collective-permute-start(f32[16,1152]{1,0:T(8,128)S(1)} %add.142), channel_id=1, source_target_pairs={{0,128},{8,136},{16,144},{24,152},{32,160},{40,168},{48,176},{56,1... | collective-permute-start | bytes 221192 | tf_op jit(solution)/shard_map/ppermute | solution.py:28
  23.6 5.2 %collective-permute-start.5 = (f32[16,1152]{1,0:T(8,128)S(1)}, f32[16,1152]{1,0:T(8,128)S(1)}, u32[]{:S(2)}, u32[]{:S(2)}) collective-permute-start(f32[16,1152]{1,0:T(8,128)S(1)} %add.142), channel_id=1, source_target_pairs={{0,192},{8,200},{16,208},{24,216},{32,224},{40,232},{48,240},{56,2... | collective-permute-start | bytes 221192 | tf_op jit(solution)/shard_map/ppermute | solution.py:28
  24.4 4.3 %collective-permute-start.4 = (f32[16,1152]{1,0:T(8,128)S(1)}, f32[16,1152]{1,0:T(8,128)S(1)}, u32[]{:S(2)}, u32[]{:S(2)}) collective-permute-start(f32[16,1152]{1,0:T(8,128)S(1)} %add.142), channel_id=1, source_target_pairs={{0,64},{8,72},{16,80},{24,88},{32,96},{40,104},{48,112},{56,120},{... | collective-permute-start | bytes 221192 | tf_op jit(solution)/shard_map/ppermute | solution.py:28
  35.9 5.3 %collective-permute-start.9 = (f32[16,1024]{1,0:T(8,128)S(1)}, f32[16,1024]{1,0:T(8,128)S(1)}, u32[]{:S(2)}, u32[]{:S(2)}) collective-permute-start(f32[16,1024]{1,0:T(8,128)S(1)} %maximum_maximum_fusion), channel_id=1, source_target_pairs={{0,24},{8,16},{16,8},{24,0},{32,56},{40,48},{48,40},{56,32},{64,88... | collective-permute-start | bytes 196616 | tf_op jit(solution)/shard_map/ppermute | solution.py:28
  37.5 4.7 %collective-permute-start.8 = (f32[16,1024]{1,0:T(8,128)S(1)}, f32[16,1024]{1,0:T(8,128)S(1)}, u32[]{:S(2)}, u32[]{:S(2)}) collective-permute-start(f32[16,1024]{1,0:T(8,128)S(1)} %maximum_maximum_fusion), channel_id=1, source_target_pairs={{0,16},{8,24},{16,0},{24,8},{32,48},{40,56},{48,32},{56,40},{64,80... | collective-permute-start | bytes 196616 | tf_op jit(solution)/shard_map/ppermute | solution.py:28
  39.8 3.2 %collective-permute-start.7 = (f32[16,1024]{1,0:T(8,128)S(1)}, f32[16,1024]{1,0:T(8,128)S(1)}, u32[]{:S(2)}, u32[]{:S(2)}) collective-permute-start(f32[16,1024]{1,0:T(8,128)S(1)} %maximum_maximum_fusion), channel_id=1, source_target_pairs={{0,8},{8,0},{16,24},{24,16},{32,40},{40,32},{48,56},{56,48},{64,72... | collective-permute-start | bytes 196616 | tf_op jit(solution)/shard_map/ppermute | solution.py:28
  39.8 5.2 %collective-permute-start.14 = (f32[16,1792]{1,0:T(8,128)S(1)}, f32[16,1792]{1,0:T(8,128)S(1)}, u32[]{:S(2)}, u32[]{:S(2)}) collective-permute-start(f32[16,1792]{1,0:T(8,128)S(1)} %pad_maximum_fusion), channel_id=1, source_target_pairs={{0,8},{8,0},{16,24},{24,16},{32,40},{40,32},{48,56},{56,48},{64,72... | collective-permute-start | bytes 344072 | tf_op jit(solution)/shard_map/ppermute | solution.py:28
  43.5 28.4 %copy-start.1 = (bf16[896,112]{0,1:T(8,128)(2,1)S(1)}, bf16[896,112]{0,1:T(8,128)(2,1)}, u32[]{:S(2)}) copy-start(bf16[896,112]{0,1:T(8,128)(2,1)} %param.16) | copy-start | bytes 602116
  45.0 5.9 %collective-permute-start.15 = (f32[16,1792]{1,0:T(8,128)S(1)}, f32[16,1792]{1,0:T(8,128)S(1)}, u32[]{:S(2)}, u32[]{:S(2)}) collective-permute-start(f32[16,1792]{1,0:T(8,128)S(1)} %add.159), channel_id=1, source_target_pairs={{0,16},{8,24},{16,0},{24,8},{32,48},{40,56},{48,32},{56,40},{64,80... | collective-permute-start | bytes 344072 | tf_op jit(solution)/shard_map/ppermute | solution.py:28
  46.4 7.2 %collective-permute-start.10 = (f32[16,1024]{1,0:T(8,128)S(1)}, f32[16,1024]{1,0:T(8,128)S(1)}, u32[]{:S(2)}, u32[]{:S(2)}) collective-permute-start(f32[16,1024]{1,0:T(8,128)S(1)} %maximum_maximum_fusion.1), channel_id=1, source_target_pairs={{0,48},{8,56},{16,32},{24,40},{32,16},{40,24},{48,0},{56,8},{64,11... | collective-permute-start | bytes 196616 | tf_op jit(solution)/shard_map/ppermute | solution.py:28
  50.8 7.8 %collective-permute-start.16 = (f32[16,1792]{1,0:T(8,128)S(1)}, f32[16,1792]{1,0:T(8,128)S(1)}, u32[]{:S(2)}, u32[]{:S(2)}) collective-permute-start(f32[16,1792]{1,0:T(8,128)S(1)} %add.160), channel_id=1, source_target_pairs={{0,48},{8,56},{16,32},{24,40},{32,16},{40,24},{48,0},{56,8},{64,11... | collective-permute-start | bytes 344072 | tf_op jit(solution)/shard_map/ppermute | solution.py:28
  58.6 4.0 %collective-permute-start.17 = (f32[16,1792]{1,0:T(8,128)S(1)}, f32[16,1792]{1,0:T(8,128)S(1)}, u32[]{:S(2)}, u32[]{:S(2)}) collective-permute-start(f32[16,1792]{1,0:T(8,128)S(1)} %add.161), channel_id=1, source_target_pairs={{0,64},{8,72},{16,80},{24,88},{32,96},{40,104},{48,112},{56,120},{... | collective-permute-start | bytes 344072 | tf_op jit(solution)/shard_map/ppermute | solution.py:28
  62.7 5.6 %collective-permute-start.18 = (f32[16,1792]{1,0:T(8,128)S(1)}, f32[16,1792]{1,0:T(8,128)S(1)}, u32[]{:S(2)}, u32[]{:S(2)}) collective-permute-start(f32[16,1792]{1,0:T(8,128)S(1)} %add.162), channel_id=1, source_target_pairs={{0,192},{8,200},{16,208},{24,216},{32,224},{40,232},{48,240},{56,2... | collective-permute-start | bytes 344072 | tf_op jit(solution)/shard_map/ppermute | solution.py:28
  62.8 6.1 %collective-permute-start.13 = (f32[16,1024]{1,0:T(8,128)S(1)}, f32[16,1024]{1,0:T(8,128)S(1)}, u32[]{:S(2)}, u32[]{:S(2)}) collective-permute-start(f32[16,1024]{1,0:T(8,128)S(1)} %maximum_maximum_fusion.2), channel_id=1, source_target_pairs={{0,128},{8,136},{16,144},{24,152},{32,160},{40,168},{48,176},{56,1... | collective-permute-start | bytes 196616 | tf_op jit(solution)/shard_map/ppermute | solution.py:28
  65.3 4.3 %collective-permute-start.12 = (f32[16,1024]{1,0:T(8,128)S(1)}, f32[16,1024]{1,0:T(8,128)S(1)}, u32[]{:S(2)}, u32[]{:S(2)}) collective-permute-start(f32[16,1024]{1,0:T(8,128)S(1)} %maximum_maximum_fusion.2), channel_id=1, source_target_pairs={{0,192},{8,200},{16,208},{24,216},{32,224},{40,232},{48,240},{56,2... | collective-permute-start | bytes 196616 | tf_op jit(solution)/shard_map/ppermute | solution.py:28
  66.3 3.3 %collective-permute-start.11 = (f32[16,1024]{1,0:T(8,128)S(1)}, f32[16,1024]{1,0:T(8,128)S(1)}, u32[]{:S(2)}, u32[]{:S(2)}) collective-permute-start(f32[16,1024]{1,0:T(8,128)S(1)} %maximum_maximum_fusion.2), channel_id=1, source_target_pairs={{0,64},{8,72},{16,80},{24,88},{32,96},{40,104},{48,112},{56,120},{... | collective-permute-start | bytes 196616 | tf_op jit(solution)/shard_map/ppermute | solution.py:28
  72.2 9.8 %collective-permute-start.19 = (f32[16,112]{1,0:T(8,128)S(1)}, f32[16,112]{1,0:T(8,128)S(1)}, u32[]{:S(2)}, u32[]{:S(2)}) collective-permute-start(f32[16,112]{1,0:T(8,128)S(1)} %fusion.47), channel_id=1, source_target_pairs={{0,1},{1,0},{2,3},{3,2},{4,5},{5,4},{6,7},{7,6},{8,9},{9,8},{10,11... | collective-permute-start | bytes 21512 | tf_op jit(solution)/shard_map/ppermute | solution.py:28
  82.0 4.4 %collective-permute-start.22 = (f32[16,112]{1,0:T(8,128)S(1)}, f32[16,112]{1,0:T(8,128)S(1)}, u32[]{:S(2)}, u32[]{:S(2)}) collective-permute-start(f32[16,112]{1,0:T(8,128)S(1)} %add.169), channel_id=1, source_target_pairs={{0,4},{1,5},{2,6},{3,7},{4,0},{5,1},{6,2},{7,3},{8,12},{9,13},{10,... | collective-permute-start | bytes 21512 | tf_op jit(solution)/shard_map/ppermute | solution.py:28
  84.9 3.7 %collective-permute-start.21 = (f32[16,112]{1,0:T(8,128)S(1)}, f32[16,112]{1,0:T(8,128)S(1)}, u32[]{:S(2)}, u32[]{:S(2)}) collective-permute-start(f32[16,112]{1,0:T(8,128)S(1)} %add.169), channel_id=1, source_target_pairs={{0,6},{1,7},{2,4},{3,5},{4,2},{5,3},{6,0},{7,1},{8,14},{9,15},{10,... | collective-permute-start | bytes 21512 | tf_op jit(solution)/shard_map/ppermute | solution.py:28
  85.7 2.9 %collective-permute-start.20 = (f32[16,112]{1,0:T(8,128)S(1)}, f32[16,112]{1,0:T(8,128)S(1)}, u32[]{:S(2)}, u32[]{:S(2)}) collective-permute-start(f32[16,112]{1,0:T(8,128)S(1)} %add.169), channel_id=1, source_target_pairs={{0,2},{1,3},{2,0},{3,1},{4,6},{5,7},{6,4},{7,5},{8,10},{9,11},{10,... | collective-permute-start | bytes 21512 | tf_op jit(solution)/shard_map/ppermute | solution.py:28

commit v8 on v4

--- a/solution.py
+++ b/solution.py
@@ -40,25 +40,31 @@
     return x
 
 
-def merge_softmax(a, b, width, heads):
+def merge_softmax(a, b, width, heads, extra):
+    n = a.shape[1] - extra
     top = jnp.maximum(a[:, width + heads : width + 2 * heads], b[:, width + heads : width + 2 * heads])
     sa = jnp.exp(a[:, width + heads : width + 2 * heads] - top)
     sb = jnp.exp(b[:, width + heads : width + 2 * heads] - top)
     values = a[:, :width] * jnp.repeat(sa, HD, axis=1) + b[:, :width] * jnp.repeat(sb, HD, axis=1)
     totals = a[:, width : width + heads] * sa + b[:, width : width + heads] * sb
-    pad = a.shape[1] - width - 2 * heads
-    return jnp.concatenate([values, totals, top, jnp.zeros((a.shape[0], pad), jnp.float32)], axis=1)
-
-
-def butterfly_softmax(x, axis, rounds, width, heads):
+    pad = n - width - 2 * heads
+    return jnp.concatenate(
+        [values, totals, top, jnp.zeros((a.shape[0], pad), jnp.float32), a[:, n:] + b[:, n:]], axis=1
+    )
+
+
+def butterfly_softmax(x, axis, rounds, width, heads, extra):
     size = 1 << sum(len(r) for r in rounds)
     for r in rounds:
         if len(r) == 1:
-            x = merge_softmax(x, exchange(x, axis, r[0], size), width, heads)
+            x = merge_softmax(x, exchange(x, axis, r[0], size), width, heads, extra)
         else:
             a, b = r
             pa, pb, pc = (exchange(x, axis, m, size) for m in (a, b, a ^ b))
-            x = merge_softmax(merge_softmax(x, pa, width, heads), merge_softmax(pb, pc, width, heads), width, heads)
+            x = merge_softmax(
+                merge_softmax(x, pa, width, heads, extra), merge_softmax(pb, pc, width, heads, extra),
+                width, heads, extra,
+            )
     return x
 
 
@@ -104,17 +110,13 @@
         [project(0), partial_low, partial_sq, jnp.zeros((rows, 127), f32)], axis=1
     )
     summed = butterfly_sum(packed, "seq", seq_masks)
-    kv_summed = butterfly_sum(jnp.concatenate([project(1), project(2)], axis=1), "seq", seq_masks)
+    kv_partial = jnp.concatenate([project(1), project(2)], axis=1)
     low = summed[:, local : local + rank]
     total_sq = summed[:, local + rank]
     scale_rows = lax.rsqrt(total_sq / INPUT_WIDTH + 1e-05)[:, None]
     lowrank = (low * scale_rows).astype(bf16)
     query_adapter = jnp.dot(lowrank, adapter_up_weight, preferred_element_type=f32)
     queries = (summed[:, :local] * scale_rows + query_adapter).astype(bf16)
-    keys_full = kv_summed[:, :local] * scale_rows
-    values_full = kv_summed[:, local:] * scale_rows
-    new_keys = keys_full.astype(bf16)
-    new_values = values_full.astype(bf16)
 
     col_head = jnp.arange(local, dtype=jnp.int32) // HD
     head_mask = col_head[None, :] == jnp.arange(heads, dtype=jnp.int32)[:, None]
@@ -154,10 +156,16 @@
             by_row(local_total),
             by_row(local_top),
             jnp.zeros((rows, 128 - 2 * heads), f32),
+            kv_partial,
         ],
         axis=1,
     )
-    merged = butterfly_softmax(packed, "seq", seq_masks, local, heads)
+    merged = butterfly_softmax(packed, "seq", seq_masks, local, heads, kv_partial.shape[1])
+    kv_summed = merged[:, local + 128 :]
+    keys_full = kv_summed[:, :local] * scale_rows
+    values_full = kv_summed[:, local:] * scale_rows
+    new_keys = keys_full.astype(bf16)
+    new_values = values_full.astype(bf16)
     cache_out = merged[:, :local]
     cache_total = merged[:, local : local + heads]
     cache_top = merged[:, local + heads : local + 2 * heads]

time: 83.1 us -> 89.1 us (1.072)
  waiting for transfers between devices: 22.6 us -> 42.9 us
  starting transfers between devices: 37.6 us -> 23.5 us
    ppermute x25 -> x18, waiting for transfers between devices: 22.6 us -> 42.9 us  [exchange(): return lax.ppermute(x, axis, [(i, i ^ mask) for i in range(size)])]
    ppermute x25 -> x18, starting transfers between devices: 37.6 us -> 23.5 us  [exchange(): return lax.ppermute(x, axis, [(i, i ^ mask) for i in range(size)])]
  transfers between devices with their start and end apart: 25 -> 18, of which waited for: 12 -> 11; matrix products, arithmetic and copies ran while one was open for 18% -> 6% of each run, Pallas kernels for 0% -> 0%
where the time goes in v8:
time: 89.1 us; the launch traced here: 88.8 us
  waiting for transfers between devices  42.9 us (48%)
  starting transfers between devices  23.5 us (26%)
  matrix products  11.2 us (13%)
  other arithmetic  5.47 us (6%)
  local copies, waits for them, and re-layouts  4.72 us (5%)
  between operations  0.98 us (1%)
    ppermute x18, waiting for transfers between devices, exchange(): return lax.ppermute(x, axis, [(i, i ^ mask) for i in range(size)])  42.9 us
    ppermute x18, starting transfers between devices, exchange(): return lax.ppermute(x, axis, [(i, i ^ mask) for i in range(size)])  23.5 us
    dot_general x3, matrix products, project(): jnp.dot(scaled, query_key_value_weight[:, j, :], preferred_element_type=f32)  3.6 us
    dot_general x1, matrix products, shards(): jnp.einsum('rnc,rpc->rnp', q_block, cached_key_rows, preferred_element_ty...  3.17 us
    dot_general x1, matrix products, shards(): jnp.einsum('rnp,rpc->rnc', expo.astype(bf16), cached_value_rows, preferre...  2.68 us
  transfers between devices with their start and end apart: 18, of which 11 were waited for; matrix products, arithmetic and copies ran while one was open for 6% of the time, Pallas kernels for 0%

profile of v8, /device:TPU:1, one launch (start us, length us, event | category | flops | bytes accessed | tf_op | source)
XLA Modules:
  0.0 88.8 jit_solution(15404545744029468680)
XLA Ops:
  0.6 0.9 fusion.53
  1.6 1.0 %fusion.86 = f32[16,128]{1,0:T(8,128)S(1)} fusion(bf16[224,128]{1,0:T(8,128)(2,1)} %param.14, bf16[16,224]{1,0:T(8,128)(2,1)} %param.11, f32[224]{0:T(256)} %param.12), kind=kOutput, calls=%fused_computation.147 | convolution fusion | flops 928256 | bytes 73600 | tf_op jit(solution)/shard_map/dot_general | solution.py:107
  2.6 1.2 %fusion.6 = f32[16,896]{1,0:T(8,128)S(1)} fusion(bf16[224,3,896]{2,0,1:T(8,128)(2,1)} %param.13, bf16[16,224]{1,0:T(8,128)(2,1)} %param.11, f32[224]{0:T(256)} %param.12), kind=kOutput, calls=%fused_computation.9 | convolution fusion | flops 6433280 | bytes 467968 | tf_op jit(solution)/shard_map/dot_general | solution.py:105
  3.9 5.2 %collective-permute-start.2 = (f32[16,1152]{1,0:T(8,128)S(1)}, f32[16,1152]{1,0:T(8,128)S(1)}, u32[]{:S(2)}, u32[]{:S(2)}) collective-permute-start(f32[16,1152]{1,0:T(8,128)S(1)} %concatenate.16), channel_id=1, source_target_pairs={{0,24},{8,16},{16,8},{24,0},{32,56},{40,48},{48,40},{56,32},{64,88... | collective-permute-start | bytes 221192 | tf_op jit(solution)/shard_map/ppermute | solution.py:28
  9.1 0.4 collective-permute-start
  9.5 1.2 %fusion.2 = f32[16,896]{1,0:T(8,128)S(1)} fusion(bf16[224,3,896]{2,0,1:T(8,128)(2,1)} %param.13, bf16[16,224]{1,0:T(8,128)(2,1)} %param.11, f32[224]{0:T(256)} %param.12), kind=kOutput, calls=%fused_computation.5 | convolution fusion | flops 6433280 | bytes 467968 | tf_op jit(solution)/shard_map/dot_general | solution.py:105
  10.6 1.2 %fusion.4 = f32[16,896]{1,0:T(8,128)S(1)} fusion(bf16[224,3,896]{2,0,1:T(8,128)(2,1)} %param.13, bf16[16,224]{1,0:T(8,128)(2,1)} %param.11, f32[224]{0:T(256)} %param.12), kind=kOutput, calls=%fused_computation.7 | convolution fusion | flops 6433280 | bytes 467968 | tf_op jit(solution)/shard_map/dot_general | solution.py:105
  11.9 0.7 iota_add_fusion
  12.6 0.7 broadcast_compare_fusion.1
  13.3 0.7 fusion.49
  14.1 1.2 %collective-permute-done.1 = f32[16,1152]{1,0:T(8,128)S(1)} collective-permute-done((f32[16,1152]{1,0:T(8,128)S(1)}, f32[16,1152]{1,0:T(8,128)S(1)}, u32[]{:S(2)}, u32[]{:S(2)}) %collective-permute-start.1) | collective-permute-done | bytes 73760 | tf_op jit(solution)/shard_map/ppermute | solution.py:28
  15.3 3.0 %collective-permute-start.3 = (f32[16,1152]{1,0:T(8,128)S(1)}, f32[16,1152]{1,0:T(8,128)S(1)}, u32[]{:S(2)}, u32[]{:S(2)}) collective-permute-start(f32[16,1152]{1,0:T(8,128)S(1)} %add_add_fusion.1), channel_id=1, source_target_pairs={{0,48},{8,56},{16,32},{24,40},{32,16},{40,24},{48,0},{56,8},{64,11... | collective-permute-start | bytes 221192 | tf_op jit(solution)/shard_map/ppermute | solution.py:28
  18.4 2.3 %collective-permute-done.3 = f32[16,1152]{1,0:T(8,128)S(1)} collective-permute-done((f32[16,1152]{1,0:T(8,128)S(1)}, f32[16,1152]{1,0:T(8,128)S(1)}, u32[]{:S(2)}, u32[]{:S(2)}) %collective-permute-start.3) | collective-permute-done | bytes 73760 | tf_op jit(solution)/shard_map/ppermute | solution.py:28
  20.7 2.8 %collective-permute-start.6 = (f32[16,1152]{1,0:T(8,128)S(1)}, f32[16,1152]{1,0:T(8,128)S(1)}, u32[]{:S(2)}, u32[]{:S(2)}) collective-permute-start(f32[16,1152]{1,0:T(8,128)S(1)} %add.148), channel_id=1, source_target_pairs={{0,128},{8,136},{16,144},{24,152},{32,160},{40,168},{48,176},{56,1... | collective-permute-start | bytes 221192 | tf_op jit(solution)/shard_map/ppermute | solution.py:28
  23.6 0.9 collective-permute-start.5
  24.5 1.0 %collective-permute-done.6 = f32[16,1152]{1,0:T(8,128)S(1)} collective-permute-done((f32[16,1152]{1,0:T(8,128)S(1)}, f32[16,1152]{1,0:T(8,128)S(1)}, u32[]{:S(2)}, u32[]{:S(2)}) %collective-permute-start.6) | collective-permute-done | bytes 73760 | tf_op jit(solution)/shard_map/ppermute | solution.py:28
  25.5 3.2 %collective-permute-done.5 = f32[16,1152]{1,0:T(8,128)S(1)} collective-permute-done((f32[16,1152]{1,0:T(8,128)S(1)}, f32[16,1152]{1,0:T(8,128)S(1)}, u32[]{:S(2)}, u32[]{:S(2)}) %collective-permute-start.5) | collective-permute-done | bytes 73760 | tf_op jit(solution)/shard_map/ppermute | solution.py:28
  28.8 0.1 fusion.73
  28.9 0.2 fusion.37
  29.2 3.2 %fusion.99 = (f32[4,16]{1,0:T(4,128)S(1)}, f32[4,16,512]{2,1,0:T(8,128)S(1)}) fusion(pred[4,16,512]{2,1,0:T(8,128)(4,1)S(1)} %reshape.227, bf16[4,512,896]{2,1,0:T(8,128)(2,1)} %param.17, bf16[4,16,896]{2,1,0:T(8,128)(2,1)S(1)} %broadcast_in_dim.148, pred[16,896]{1,0:T(8,128)(4,1)S(1)} %broadcast_in_dim.142), kind=kOutput, calls=%fused_computation.159 | convolution fusion | flops 58875840 | bytes 3963136 | tf_op jit(solution)/shard_map/rnc,rpc->rnp/dot_general | solution.py:126
  32.5 0.2 fusion.15
  32.8 0.1 copy.73
  32.9 0.1 copy.71
  33.0 2.7 %fusion.17 = f32[4,16,896]{2,1,0:T(8,128)S(1)} fusion(bf16[4,512,896]{2,1,0:T(8,128)(2,1)} %param.18, f32[4,16,512]{2,1,0:T(8,128)S(1)} %get-tuple-element.32, f32[4,16]{1,0:T(4,128)S(1)} %get-tuple-element.31, u8[16,512]{1,0:T(8,128)(4,1)S(1)} %fusion.44), kind=kOutput, calls=%fused_computation.32 | convolution fusion | flops 58949632 | bytes 4038912 | tf_op jit(solution)/shard_map/rnp,rpc->rnc/dot_general | solution.py:142
  35.9 1.6 %collective-permute-start.9 = (f32[16,2816]{1,0:T(8,128)S(1)}, f32[16,2816]{1,0:T(8,128)S(1)}, u32[]{:S(2)}, u32[]{:S(2)}) collective-permute-start(f32[16,2816]{1,0:T(8,128)S(1)} %concatenate.17), channel_id=1, source_target_pairs={{0,24},{8,16},{16,8},{24,0},{32,56},{40,48},{48,40},{56,32},{64,88... | collective-permute-start | bytes 540680 | tf_op jit(solution)/shard_map/ppermute | solution.py:28
  37.5 2.2 %collective-permute-start.8 = (f32[16,2816]{1,0:T(8,128)S(1)}, f32[16,2816]{1,0:T(8,128)S(1)}, u32[]{:S(2)}, u32[]{:S(2)}) collective-permute-start(f32[16,2816]{1,0:T(8,128)S(1)} %concatenate.17), channel_id=1, source_target_pairs={{0,16},{8,24},{16,0},{24,8},{32,48},{40,56},{48,32},{56,40},{64,80... | collective-permute-start | bytes 540680 | tf_op jit(solution)/shard_map/ppermute | solution.py:28
  39.8 2.4 %collective-permute-done.9 = f32[16,2816]{1,0:T(8,128)S(1)} collective-permute-done((f32[16,2816]{1,0:T(8,128)S(1)}, f32[16,2816]{1,0:T(8,128)S(1)}, u32[]{:S(2)}, u32[]{:S(2)}) %collective-permute-start.9) | collective-permute-done | bytes 180256 | tf_op jit(solution)/shard_map/ppermute | solution.py:28
  42.2 13.4 %collective-permute-done.8 = f32[16,2816]{1,0:T(8,128)S(1)} collective-permute-done((f32[16,2816]{1,0:T(8,128)S(1)}, f32[16,2816]{1,0:T(8,128)S(1)}, u32[]{:S(2)}, u32[]{:S(2)}) %collective-permute-start.8) | collective-permute-done | bytes 180256 | tf_op jit(solution)/shard_map/ppermute | solution.py:28
  55.8 0.1 reshape.234
  56.0 0.1 reshape.235
  56.2 0.1 reshape.236
  56.4 0.1 reshape.237
  56.6 0.1 reshape.238
  56.8 0.1 reshape.239
  57.1 7.6 %collective-permute-done.10 = f32[16,2816]{1,0:T(8,128)S(1)} collective-permute-done((f32[16,2816]{1,0:T(8,128)S(1)}, f32[16,2816]{1,0:T(8,128)S(1)}, u32[]{:S(2)}, u32[]{:S(2)}) %collective-permute-start.10) | collective-permute-done | bytes 180256 | tf_op jit(solution)/shard_map/ppermute | solution.py:28
  64.9 0.1 reshape.240
  65.0 0.1 reshape.241
  65.3 0.3 collective-permute-start.13
  65.6 2.4 %collective-permute-start.11 = (f32[16,2816]{1,0:T(8,128)S(1)}, f32[16,2816]{1,0:T(8,128)S(1)}, u32[]{:S(2)}, u32[]{:S(2)}) collective-permute-start(f32[16,2816]{1,0:T(8,128)S(1)} %concatenate.20), channel_id=1, source_target_pairs={{0,64},{8,72},{16,80},{24,88},{32,96},{40,104},{48,112},{56,120},{... | collective-permute-start | bytes 540680 | tf_op jit(solution)/shard_map/ppermute | solution.py:28
  68.1 3.2 %collective-permute-done.13 = f32[16,2816]{1,0:T(8,128)S(1)} collective-permute-done((f32[16,2816]{1,0:T(8,128)S(1)}, f32[16,2816]{1,0:T(8,128)S(1)}, u32[]{:S(2)}, u32[]{:S(2)}) %collective-permute-start.13) | collective-permute-done | bytes 180256 | tf_op jit(solution)/shard_map/ppermute | solution.py:28
  71.3 5.4 %collective-permute-done.12 = f32[16,2816]{1,0:T(8,128)S(1)} collective-permute-done((f32[16,2816]{1,0:T(8,128)S(1)}, f32[16,2816]{1,0:T(8,128)S(1)}, u32[]{:S(2)}, u32[]{:S(2)}) %collective-permute-start.12) | collective-permute-done | bytes 180256 | tf_op jit(solution)/shard_map/ppermute | solution.py:28
  76.8 0.1 reshape.252
  77.0 0.2 fusion.100
  77.2 0.1 copy.67
  77.4 0.1 copy.60
  77.5 0.2 convolution_bitcast_fusion
  77.8 0.1 reshape.254
  77.9 0.1 copy.70
  78.2 0.1 reshape.256
  78.4 0.1 reshape.242
  78.6 0.1 reshape.243
  78.7 0.1 reshape.244
  78.9 0.1 reshape.245
  79.1 0.1 reshape.246
  79.3 0.1 reshape.247
  79.5 0.1 reshape.251
  79.6 0.2 fusion.50
  79.8 1.0 %collective-permute-start.14 = (f32[16,112]{1,0:T(8,128)S(1)}, f32[16,112]{1,0:T(8,128)S(1)}, u32[]{:S(2)}, u32[]{:S(2)}) collective-permute-start(f32[16,112]{1,0:T(8,128)S(1)} %fusion.50), channel_id=1, source_target_pairs={{0,1},{1,0},{2,3},{3,2},{4,5},{5,4},{6,7},{7,6},{8,9},{9,8},{10,11... | collective-permute-start | bytes 21512 | tf_op jit(solution)/shard_map/ppermute | solution.py:28
  80.8 0.8 collective-permute-done.14
  81.6 2.8 %collective-permute-start.17 = (f32[16,112]{1,0:T(8,128)S(1)}, f32[16,112]{1,0:T(8,128)S(1)}, u32[]{:S(2)}, u32[]{:S(2)}) collective-permute-start(f32[16,112]{1,0:T(8,128)S(1)} %add.177), channel_id=1, source_target_pairs={{0,4},{1,5},{2,6},{3,7},{4,0},{5,1},{6,2},{7,3},{8,12},{9,13},{10,... | collective-permute-start | bytes 21512 | tf_op jit(solution)/shard_map/ppermute | solution.py:28
  84.4 0.8 collective-permute-start.16
  85.2 0.7 pad_maximum_fusion
  85.9 2.3 %collective-permute-done.16 = f32[16,112]{1,0:T(8,128)S(1)} collective-permute-done((f32[16,112]{1,0:T(8,128)S(1)}, f32[16,112]{1,0:T(8,128)S(1)}, u32[]{:S(2)}, u32[]{:S(2)}) %collective-permute-start.16) | collective-permute-done | bytes 7200 | tf_op jit(solution)/shard_map/ppermute | solution.py:28
  88.1 0.6 add_add_fusion.2
  (76 shorter events, 3.3 us)
Async XLA Ops:
  0.6 28.3 %copy-start = (bf16[128,896]{1,0:T(8,128)(2,1)S(1)}, bf16[128,896]{1,0:T(8,128)(2,1)}, u32[]{:S(2)}) copy-start(bf16[128,896]{1,0:T(8,128)(2,1)} %param.15) | copy-start | bytes 688132
  3.9 10.2 %collective-permute-start.2 = (f32[16,1152]{1,0:T(8,128)S(1)}, f32[16,1152]{1,0:T(8,128)S(1)}, u32[]{:S(2)}, u32[]{:S(2)}) collective-permute-start(f32[16,1152]{1,0:T(8,128)S(1)} %concatenate.16), channel_id=1, source_target_pairs={{0,24},{8,16},{16,8},{24,0},{32,56},{40,48},{48,40},{56,32},{64,88... | collective-permute-start | bytes 221192 | tf_op jit(solution)/shard_map/ppermute | solution.py:28
  9.1 6.2 %collective-permute-start.1 = (f32[16,1152]{1,0:T(8,128)S(1)}, f32[16,1152]{1,0:T(8,128)S(1)}, u32[]{:S(2)}, u32[]{:S(2)}) collective-permute-start(f32[16,1152]{1,0:T(8,128)S(1)} %concatenate.16), channel_id=1, source_target_pairs={{0,16},{8,24},{16,0},{24,8},{32,48},{40,56},{48,32},{56,40},{64,80... | collective-permute-start | bytes 221192 | tf_op jit(solution)/shard_map/ppermute | solution.py:28
  9.1 6.2 %collective-permute-start = (f32[16,1152]{1,0:T(8,128)S(1)}, f32[16,1152]{1,0:T(8,128)S(1)}, u32[]{:S(2)}, u32[]{:S(2)}) collective-permute-start(f32[16,1152]{1,0:T(8,128)S(1)} %concatenate.16), channel_id=1, source_target_pairs={{0,8},{8,0},{16,24},{24,16},{32,40},{40,32},{48,56},{56,48},{64,72... | collective-permute-start | bytes 221192 | tf_op jit(solution)/shard_map/ppermute | solution.py:28
  15.3 5.4 %collective-permute-start.3 = (f32[16,1152]{1,0:T(8,128)S(1)}, f32[16,1152]{1,0:T(8,128)S(1)}, u32[]{:S(2)}, u32[]{:S(2)}) collective-permute-start(f32[16,1152]{1,0:T(8,128)S(1)} %add_add_fusion.1), channel_id=1, source_target_pairs={{0,48},{8,56},{16,32},{24,40},{32,16},{40,24},{48,0},{56,8},{64,11... | collective-permute-start | bytes 221192 | tf_op jit(solution)/shard_map/ppermute | solution.py:28
  20.7 4.8 %collective-permute-start.6 = (f32[16,1152]{1,0:T(8,128)S(1)}, f32[16,1152]{1,0:T(8,128)S(1)}, u32[]{:S(2)}, u32[]{:S(2)}) collective-permute-start(f32[16,1152]{1,0:T(8,128)S(1)} %add.148), channel_id=1, source_target_pairs={{0,128},{8,136},{16,144},{24,152},{32,160},{40,168},{48,176},{56,1... | collective-permute-start | bytes 221192 | tf_op jit(solution)/shard_map/ppermute | solution.py:28
  23.6 5.2 %collective-permute-start.5 = (f32[16,1152]{1,0:T(8,128)S(1)}, f32[16,1152]{1,0:T(8,128)S(1)}, u32[]{:S(2)}, u32[]{:S(2)}) collective-permute-start(f32[16,1152]{1,0:T(8,128)S(1)} %add.148), channel_id=1, source_target_pairs={{0,192},{8,200},{16,208},{24,216},{32,224},{40,232},{48,240},{56,2... | collective-permute-start | bytes 221192 | tf_op jit(solution)/shard_map/ppermute | solution.py:28
  24.4 4.3 %collective-permute-start.4 = (f32[16,1152]{1,0:T(8,128)S(1)}, f32[16,1152]{1,0:T(8,128)S(1)}, u32[]{:S(2)}, u32[]{:S(2)}) collective-permute-start(f32[16,1152]{1,0:T(8,128)S(1)} %add.148), channel_id=1, source_target_pairs={{0,64},{8,72},{16,80},{24,88},{32,96},{40,104},{48,112},{56,120},{... | collective-permute-start | bytes 221192 | tf_op jit(solution)/shard_map/ppermute | solution.py:28
  35.9 6.3 %collective-permute-start.9 = (f32[16,2816]{1,0:T(8,128)S(1)}, f32[16,2816]{1,0:T(8,128)S(1)}, u32[]{:S(2)}, u32[]{:S(2)}) collective-permute-start(f32[16,2816]{1,0:T(8,128)S(1)} %concatenate.17), channel_id=1, source_target_pairs={{0,24},{8,16},{16,8},{24,0},{32,56},{40,48},{48,40},{56,32},{64,88... | collective-permute-start | bytes 540680 | tf_op jit(solution)/shard_map/ppermute | solution.py:28
  37.5 18.1 %collective-permute-start.8 = (f32[16,2816]{1,0:T(8,128)S(1)}, f32[16,2816]{1,0:T(8,128)S(1)}, u32[]{:S(2)}, u32[]{:S(2)}) collective-permute-start(f32[16,2816]{1,0:T(8,128)S(1)} %concatenate.17), channel_id=1, source_target_pairs={{0,16},{8,24},{16,0},{24,8},{32,48},{40,56},{48,32},{56,40},{64,80... | collective-permute-start | bytes 540680 | tf_op jit(solution)/shard_map/ppermute | solution.py:28
  39.8 15.9 %collective-permute-start.7 = (f32[16,2816]{1,0:T(8,128)S(1)}, f32[16,2816]{1,0:T(8,128)S(1)}, u32[]{:S(2)}, u32[]{:S(2)}) collective-permute-start(f32[16,2816]{1,0:T(8,128)S(1)} %concatenate.17), channel_id=1, source_target_pairs={{0,8},{8,0},{16,24},{24,16},{32,40},{40,32},{48,56},{56,48},{64,72... | collective-permute-start | bytes 540680 | tf_op jit(solution)/shard_map/ppermute | solution.py:28
  56.4 23.2 %copy-start.1 = (bf16[896,112]{0,1:T(8,128)(2,1)S(1)}, bf16[896,112]{0,1:T(8,128)(2,1)}, u32[]{:S(2)}) copy-start(bf16[896,112]{0,1:T(8,128)(2,1)} %param.16) | copy-start | bytes 602116
  57.0 7.6 %collective-permute-start.10 = (f32[16,2816]{1,0:T(8,128)S(1)}, f32[16,2816]{1,0:T(8,128)S(1)}, u32[]{:S(2)}, u32[]{:S(2)}) collective-permute-start(f32[16,2816]{1,0:T(8,128)S(1)} %concatenate.19), channel_id=1, source_target_pairs={{0,48},{8,56},{16,32},{24,40},{32,16},{40,24},{48,0},{56,8},{64,11... | collective-permute-start | bytes 540680 | tf_op jit(solution)/shard_map/ppermute | solution.py:28
  65.3 6.0 %collective-permute-start.13 = (f32[16,2816]{1,0:T(8,128)S(1)}, f32[16,2816]{1,0:T(8,128)S(1)}, u32[]{:S(2)}, u32[]{:S(2)}) collective-permute-start(f32[16,2816]{1,0:T(8,128)S(1)} %concatenate.20), channel_id=1, source_target_pairs={{0,128},{8,136},{16,144},{24,152},{32,160},{40,168},{48,176},{56,1... | collective-permute-start | bytes 540680 | tf_op jit(solution)/shard_map/ppermute | solution.py:28
  65.6 11.1 %collective-permute-start.12 = (f32[16,2816]{1,0:T(8,128)S(1)}, f32[16,2816]{1,0:T(8,128)S(1)}, u32[]{:S(2)}, u32[]{:S(2)}) collective-permute-start(f32[16,2816]{1,0:T(8,128)S(1)} %concatenate.20), channel_id=1, source_target_pairs={{0,192},{8,200},{16,208},{24,216},{32,224},{40,232},{48,240},{56,2... | collective-permute-start | bytes 540680 | tf_op jit(solution)/shard_map/ppermute | solution.py:28
  65.6 11.1 %collective-permute-start.11 = (f32[16,2816]{1,0:T(8,128)S(1)}, f32[16,2816]{1,0:T(8,128)S(1)}, u32[]{:S(2)}, u32[]{:S(2)}) collective-permute-start(f32[16,2816]{1,0:T(8,128)S(1)} %concatenate.20), channel_id=1, source_target_pairs={{0,64},{8,72},{16,80},{24,88},{32,96},{40,104},{48,112},{56,120},{... | collective-permute-start | bytes 540680 | tf_op jit(solution)/shard_map/ppermute | solution.py:28
  79.8 1.8 %collective-permute-start.14 = (f32[16,112]{1,0:T(8,128)S(1)}, f32[16,112]{1,0:T(8,128)S(1)}, u32[]{:S(2)}, u32[]{:S(2)}) collective-permute-start(f32[16,112]{1,0:T(8,128)S(1)} %fusion.50), channel_id=1, source_target_pairs={{0,1},{1,0},{2,3},{3,2},{4,5},{5,4},{6,7},{7,6},{8,9},{9,8},{10,11... | collective-permute-start | bytes 21512 | tf_op jit(solution)/shard_map/ppermute | solution.py:28
  81.6 4.3 %collective-permute-start.17 = (f32[16,112]{1,0:T(8,128)S(1)}, f32[16,112]{1,0:T(8,128)S(1)}, u32[]{:S(2)}, u32[]{:S(2)}) collective-permute-start(f32[16,112]{1,0:T(8,128)S(1)} %add.177), channel_id=1, source_target_pairs={{0,4},{1,5},{2,6},{3,7},{4,0},{5,1},{6,2},{7,3},{8,12},{9,13},{10,... | collective-permute-start | bytes 21512 | tf_op jit(solution)/shard_map/ppermute | solution.py:28
  84.4 3.7 %collective-permute-start.16 = (f32[16,112]{1,0:T(8,128)S(1)}, f32[16,112]{1,0:T(8,128)S(1)}, u32[]{:S(2)}, u32[]{:S(2)}) collective-permute-start(f32[16,112]{1,0:T(8,128)S(1)} %add.177), channel_id=1, source_target_pairs={{0,6},{1,7},{2,4},{3,5},{4,2},{5,3},{6,0},{7,1},{8,14},{9,15},{10,... | collective-permute-start | bytes 21512 | tf_op jit(solution)/shard_map/ppermute | solution.py:28
  85.2 2.9 %collective-permute-start.15 = (f32[16,112]{1,0:T(8,128)S(1)}, f32[16,112]{1,0:T(8,128)S(1)}, u32[]{:S(2)}, u32[]{:S(2)}) collective-permute-start(f32[16,112]{1,0:T(8,128)S(1)} %add.177), channel_id=1, source_target_pairs={{0,2},{1,3},{2,0},{3,1},{4,6},{5,7},{6,4},{7,5},{8,10},{9,11},{10,... | collective-permute-start | bytes 21512 | tf_op jit(solution)/shard_map/ppermute | solution.py:28

commit v9 on v4

--- a/solution.py
+++ b/solution.py
@@ -67,7 +67,7 @@
 
 def axis_masks(axis, size):
     rings = RINGS[axis].get(size, (size,))
-    return butterfly_rounds(rings)
+    return sorted(butterfly_rounds(rings), key=len)
 
 
 def shards(

time: 83.1 us -> 80.4 us (0.968)
  waiting for transfers between devices: 22.6 us -> 13.4 us
  starting transfers between devices: 37.6 us -> 44.2 us
    ppermute x25, waiting for transfers between devices: 22.6 us -> 13.4 us  [exchange(): return lax.ppermute(x, axis, [(i, i ^ mask) for i in range(size)])]
    ppermute x25, starting transfers between devices: 37.6 us -> 44.2 us  [exchange(): return lax.ppermute(x, axis, [(i, i ^ mask) for i in range(size)])]
  transfers between devices with their start and end apart: 25 -> 25, of which waited for: 12 -> 10; matrix products, arithmetic and copies ran while one was open for 18% -> 17% of each run, Pallas kernels for 0% -> 0%
where the time goes in v9:
time: 80.4 us; the launch traced here: 80.1 us
  starting transfers between devices  44.2 us (55%)
  waiting for transfers between devices  13.4 us (17%)
  matrix products  11.2 us (14%)
  other arithmetic  5.72 us (7%)
  local copies, waits for them, and re-layouts  4.55 us (6%)
  between operations  1.01 us (1%)
    ppermute x25, starting transfers between devices, exchange(): return lax.ppermute(x, axis, [(i, i ^ mask) for i in range(size)])  44.2 us
    ppermute x25, waiting for transfers between devices, exchange(): return lax.ppermute(x, axis, [(i, i ^ mask) for i in range(size)])  13.4 us
    dot_general x3, matrix products, project(): jnp.dot(scaled, query_key_value_weight[:, j, :], preferred_element_type=f32)  3.6 us
    dot_general x1, matrix products, shards(): jnp.einsum('rnc,rpc->rnp', q_block, cached_key_rows, preferred_element_ty...  3.17 us
    dot_general x1, matrix products, shards(): jnp.einsum('rnp,rpc->rnc', expo.astype(bf16), cached_value_rows, preferre...  2.68 us
  transfers between devices with their start and end apart: 25, of which 10 were waited for; matrix products, arithmetic and copies ran while one was open for 17% of the time, Pallas kernels for 0%

profile of v9, /device:TPU:1, one launch (start us, length us, event | category | flops | bytes accessed | tf_op | source)
XLA Modules:
  0.0 80.1 jit_solution(3002969161413760178)
XLA Ops:
  0.6 0.9 %fusion.51 = f32[16]{0:T(128)S(1)} fusion(bf16[16,224]{1,0:T(8,128)(2,1)} %param.11), kind=kLoop, calls=%fused_computation.81 | loop fusion | flops 10736 | bytes 7232 | tf_op jit(solution)/shard_map/reduce_sum | solution.py:102
  1.6 1.0 %fusion.84 = f32[16,128]{1,0:T(8,128)S(1)} fusion(bf16[224,128]{1,0:T(8,128)(2,1)} %param.14, bf16[16,224]{1,0:T(8,128)(2,1)} %param.11, f32[224]{0:T(256)} %param.12), kind=kOutput, calls=%fused_computation.146 | convolution fusion | flops 928256 | bytes 73600 | tf_op jit(solution)/shard_map/dot_general | solution.py:101
  2.6 1.2 %fusion.6 = f32[16,896]{1,0:T(8,128)S(1)} fusion(bf16[224,3,896]{2,0,1:T(8,128)(2,1)} %param.13, bf16[16,224]{1,0:T(8,128)(2,1)} %param.11, f32[224]{0:T(256)} %param.12), kind=kOutput, calls=%fused_computation.9 | convolution fusion | flops 6433280 | bytes 467968 | tf_op jit(solution)/shard_map/dot_general | solution.py:99
  3.9 6.9 %collective-permute-start = (f32[16,1152]{1,0:T(8,128)S(1)}, f32[16,1152]{1,0:T(8,128)S(1)}, u32[]{:S(2)}, u32[]{:S(2)}) collective-permute-start(f32[16,1152]{1,0:T(8,128)S(1)} %concatenate.15), channel_id=1, source_target_pairs={{0,48},{8,56},{16,32},{24,40},{32,16},{40,24},{48,0},{56,8},{64,11... | collective-permute-start | bytes 221192 | tf_op jit(solution)/shard_map/ppermute | solution.py:28
  10.7 1.2 %fusion.2 = f32[16,896]{1,0:T(8,128)S(1)} fusion(bf16[224,3,896]{2,0,1:T(8,128)(2,1)} %param.13, bf16[16,224]{1,0:T(8,128)(2,1)} %param.11, f32[224]{0:T(256)} %param.12), kind=kOutput, calls=%fused_computation.5 | convolution fusion | flops 6433280 | bytes 467968 | tf_op jit(solution)/shard_map/dot_general | solution.py:99
  11.9 1.2 %fusion.4 = f32[16,896]{1,0:T(8,128)S(1)} fusion(bf16[224,3,896]{2,0,1:T(8,128)(2,1)} %param.13, bf16[16,224]{1,0:T(8,128)(2,1)} %param.11, f32[224]{0:T(256)} %param.12), kind=kOutput, calls=%fused_computation.7 | convolution fusion | flops 6433280 | bytes 467968 | tf_op jit(solution)/shard_map/dot_general | solution.py:99
  13.2 0.1 collective-permute-start.14
  13.3 0.7 iota_add_fusion
  14.0 0.7 broadcast_compare_fusion.1
  14.8 0.7 fusion.47
  15.8 2.0 %collective-permute-start.3 = (f32[16,1152]{1,0:T(8,128)S(1)}, f32[16,1152]{1,0:T(8,128)S(1)}, u32[]{:S(2)}, u32[]{:S(2)}) collective-permute-start(f32[16,1152]{1,0:T(8,128)S(1)} %add.145), channel_id=1, source_target_pairs={{0,24},{8,16},{16,8},{24,0},{32,56},{40,48},{48,40},{56,32},{64,88... | collective-permute-start | bytes 221192 | tf_op jit(solution)/shard_map/ppermute | solution.py:28
  17.8 1.6 %collective-permute-start.1 = (f32[16,1152]{1,0:T(8,128)S(1)}, f32[16,1152]{1,0:T(8,128)S(1)}, u32[]{:S(2)}, u32[]{:S(2)}) collective-permute-start(f32[16,1152]{1,0:T(8,128)S(1)} %add.145), channel_id=1, source_target_pairs={{0,8},{8,0},{16,24},{24,16},{32,40},{40,32},{48,56},{56,48},{64,72... | collective-permute-start | bytes 221192 | tf_op jit(solution)/shard_map/ppermute | solution.py:28
  19.4 1.6 %collective-permute-done.3 = f32[16,1152]{1,0:T(8,128)S(1)} collective-permute-done((f32[16,1152]{1,0:T(8,128)S(1)}, f32[16,1152]{1,0:T(8,128)S(1)}, u32[]{:S(2)}, u32[]{:S(2)}) %collective-permute-start.3) | collective-permute-done | bytes 73760 | tf_op jit(solution)/shard_map/ppermute | solution.py:28
  21.0 2.5 %collective-permute-done.2 = f32[16,1152]{1,0:T(8,128)S(1)} collective-permute-done((f32[16,1152]{1,0:T(8,128)S(1)}, f32[16,1152]{1,0:T(8,128)S(1)}, u32[]{:S(2)}, u32[]{:S(2)}) %collective-permute-start.2) | collective-permute-done | bytes 73760 | tf_op jit(solution)/shard_map/ppermute | solution.py:28
  23.6 2.8 %collective-permute-start.6 = (f32[16,1152]{1,0:T(8,128)S(1)}, f32[16,1152]{1,0:T(8,128)S(1)}, u32[]{:S(2)}, u32[]{:S(2)}) collective-permute-start(f32[16,1152]{1,0:T(8,128)S(1)} %add_add_fusion.3), channel_id=1, source_target_pairs={{0,128},{8,136},{16,144},{24,152},{32,160},{40,168},{48,176},{56,1... | collective-permute-start | bytes 221192 | tf_op jit(solution)/shard_map/ppermute | solution.py:28
  26.4 0.9 %collective-permute-start.5 = (f32[16,1152]{1,0:T(8,128)S(1)}, f32[16,1152]{1,0:T(8,128)S(1)}, u32[]{:S(2)}, u32[]{:S(2)}) collective-permute-start(f32[16,1152]{1,0:T(8,128)S(1)} %add_add_fusion.3), channel_id=1, source_target_pairs={{0,192},{8,200},{16,208},{24,216},{32,224},{40,232},{48,240},{56,2... | collective-permute-start | bytes 221192 | tf_op jit(solution)/shard_map/ppermute | solution.py:28
  27.3 1.5 %collective-permute-start.17 = (f32[16,1792]{1,0:T(8,128)S(1)}, f32[16,1792]{1,0:T(8,128)S(1)}, u32[]{:S(2)}, u32[]{:S(2)}) collective-permute-start(f32[16,1792]{1,0:T(8,128)S(1)} %fusion.94), channel_id=1, source_target_pairs={{0,24},{8,16},{16,8},{24,0},{32,56},{40,48},{48,40},{56,32},{64,88... | collective-permute-start | bytes 344072 | tf_op jit(solution)/shard_map/ppermute | solution.py:28
  28.8 1.5 %collective-permute-start.16 = (f32[16,1792]{1,0:T(8,128)S(1)}, f32[16,1792]{1,0:T(8,128)S(1)}, u32[]{:S(2)}, u32[]{:S(2)}) collective-permute-start(f32[16,1792]{1,0:T(8,128)S(1)} %fusion.94), channel_id=1, source_target_pairs={{0,16},{8,24},{16,0},{24,8},{32,48},{40,56},{48,32},{56,40},{64,80... | collective-permute-start | bytes 344072 | tf_op jit(solution)/shard_map/ppermute | solution.py:28
  30.2 0.7 collective-permute-start.15
  30.9 0.2 collective-permute-done.5
  31.2 0.1 fusion.71
  31.3 0.2 fusion.35
  31.7 3.2 %fusion.99 = (f32[4,16]{1,0:T(4,128)S(1)}, f32[4,16,512]{2,1,0:T(8,128)S(1)}) fusion(pred[4,16,512]{2,1,0:T(8,128)(4,1)S(1)} %reshape.227, bf16[4,512,896]{2,1,0:T(8,128)(2,1)} %param.17, bf16[4,16,896]{2,1,0:T(8,128)(2,1)S(1)} %broadcast_in_dim.148, pred[16,896]{1,0:T(8,128)(4,1)S(1)} %broadcast_in_dim.142), kind=kOutput, calls=%fused_computation.160 | convolution fusion | flops 58875840 | bytes 3963136 | tf_op jit(solution)/shard_map/rnc,rpc->rnp/dot_general | solution.py:124
  35.0 0.2 fusion.13
  35.2 0.1 copy.64
  35.4 0.1 copy.62
  35.5 2.7 %fusion.15 = f32[4,16,896]{2,1,0:T(8,128)S(1)} fusion(bf16[4,512,896]{2,1,0:T(8,128)(2,1)} %param.18, f32[4,16,512]{2,1,0:T(8,128)S(1)} %get-tuple-element.34, f32[4,16]{1,0:T(4,128)S(1)} %get-tuple-element.33, u8[16,512]{1,0:T(8,128)(4,1)S(1)} %fusion.42), kind=kOutput, calls=%fused_computation.28 | convolution fusion | flops 58949632 | bytes 4038912 | tf_op jit(solution)/shard_map/rnp,rpc->rnc/dot_general | solution.py:140
  38.4 4.5 %collective-permute-start.7 = (f32[16,1024]{1,0:T(8,128)S(1)}, f32[16,1024]{1,0:T(8,128)S(1)}, u32[]{:S(2)}, u32[]{:S(2)}) collective-permute-start(f32[16,1024]{1,0:T(8,128)S(1)} %maximum_maximum_fusion), channel_id=1, source_target_pairs={{0,48},{8,56},{16,32},{24,40},{32,16},{40,24},{48,0},{56,8},{64,11... | collective-permute-start | bytes 196616 | tf_op jit(solution)/shard_map/ppermute | solution.py:28
  42.9 3.1 %collective-permute-start.20 = (f32[16,1792]{1,0:T(8,128)S(1)}, f32[16,1792]{1,0:T(8,128)S(1)}, u32[]{:S(2)}, u32[]{:S(2)}) collective-permute-start(f32[16,1792]{1,0:T(8,128)S(1)} %add_add_fusion.1), channel_id=1, source_target_pairs={{0,128},{8,136},{16,144},{24,152},{32,160},{40,168},{48,176},{56,1... | collective-permute-start | bytes 344072 | tf_op jit(solution)/shard_map/ppermute | solution.py:28
  46.0 0.9 %collective-permute-start.19 = (f32[16,1792]{1,0:T(8,128)S(1)}, f32[16,1792]{1,0:T(8,128)S(1)}, u32[]{:S(2)}, u32[]{:S(2)}) collective-permute-start(f32[16,1792]{1,0:T(8,128)S(1)} %add_add_fusion.1), channel_id=1, source_target_pairs={{0,192},{8,200},{16,208},{24,216},{32,224},{40,232},{48,240},{56,2... | collective-permute-start | bytes 344072 | tf_op jit(solution)/shard_map/ppermute | solution.py:28
  47.0 0.1 reshape.234
  47.2 0.1 reshape.235
  47.4 1.7 %collective-permute-start.10 = (f32[16,1024]{1,0:T(8,128)S(1)}, f32[16,1024]{1,0:T(8,128)S(1)}, u32[]{:S(2)}, u32[]{:S(2)}) collective-permute-start(f32[16,1024]{1,0:T(8,128)S(1)} %maximum_maximum_fusion.1), channel_id=1, source_target_pairs={{0,24},{8,16},{16,8},{24,0},{32,56},{40,48},{48,40},{56,32},{64,88... | collective-permute-start | bytes 196616 | tf_op jit(solution)/shard_map/ppermute | solution.py:28
  49.1 1.0 %collective-permute-start.9 = (f32[16,1024]{1,0:T(8,128)S(1)}, f32[16,1024]{1,0:T(8,128)S(1)}, u32[]{:S(2)}, u32[]{:S(2)}) collective-permute-start(f32[16,1024]{1,0:T(8,128)S(1)} %maximum_maximum_fusion.1), channel_id=1, source_target_pairs={{0,16},{8,24},{16,0},{24,8},{32,48},{40,56},{48,32},{56,40},{64,80... | collective-permute-start | bytes 196616 | tf_op jit(solution)/shard_map/ppermute | solution.py:28
  50.1 0.9 %collective-permute-start.8 = (f32[16,1024]{1,0:T(8,128)S(1)}, f32[16,1024]{1,0:T(8,128)S(1)}, u32[]{:S(2)}, u32[]{:S(2)}) collective-permute-start(f32[16,1024]{1,0:T(8,128)S(1)} %maximum_maximum_fusion.1), channel_id=1, source_target_pairs={{0,8},{8,0},{16,24},{24,16},{32,40},{40,32},{48,56},{56,48},{64,72... | collective-permute-start | bytes 196616 | tf_op jit(solution)/shard_map/ppermute | solution.py:28
  51.0 0.9 %collective-permute-done.19 = f32[16,1792]{1,0:T(8,128)S(1)} collective-permute-done((f32[16,1792]{1,0:T(8,128)S(1)}, f32[16,1792]{1,0:T(8,128)S(1)}, u32[]{:S(2)}, u32[]{:S(2)}) %collective-permute-start.19) | collective-permute-done | bytes 114720 | tf_op jit(solution)/shard_map/ppermute | solution.py:28
  52.2 0.2 fusion.98
  52.4 0.1 copy.58
  52.5 0.1 collective-permute-done.10
  52.7 1.5 %collective-permute-done.9 = f32[16,1024]{1,0:T(8,128)S(1)} collective-permute-done((f32[16,1024]{1,0:T(8,128)S(1)}, f32[16,1024]{1,0:T(8,128)S(1)}, u32[]{:S(2)}, u32[]{:S(2)}) %collective-permute-start.9) | collective-permute-done | bytes 65568 | tf_op jit(solution)/shard_map/ppermute | solution.py:28
  54.3 0.1 reshape.236
  54.5 0.1 reshape.237
  54.7 0.1 reshape.238
  54.9 0.1 reshape.239
  55.1 0.1 reshape.240
  55.3 0.1 reshape.241
  55.5 2.7 %collective-permute-start.13 = (f32[16,1024]{1,0:T(8,128)S(1)}, f32[16,1024]{1,0:T(8,128)S(1)}, u32[]{:S(2)}, u32[]{:S(2)}) collective-permute-start(f32[16,1024]{1,0:T(8,128)S(1)} %maximum_maximum_fusion.2), channel_id=1, source_target_pairs={{0,128},{8,136},{16,144},{24,152},{32,160},{40,168},{48,176},{56,1... | collective-permute-start | bytes 196616 | tf_op jit(solution)/shard_map/ppermute | solution.py:28
  58.2 0.9 %collective-permute-start.12 = (f32[16,1024]{1,0:T(8,128)S(1)}, f32[16,1024]{1,0:T(8,128)S(1)}, u32[]{:S(2)}, u32[]{:S(2)}) collective-permute-start(f32[16,1024]{1,0:T(8,128)S(1)} %maximum_maximum_fusion.2), channel_id=1, source_target_pairs={{0,192},{8,200},{16,208},{24,216},{32,224},{40,232},{48,240},{56,2... | collective-permute-start | bytes 196616 | tf_op jit(solution)/shard_map/ppermute | solution.py:28
  59.1 1.0 %collective-permute-done.13 = f32[16,1024]{1,0:T(8,128)S(1)} collective-permute-done((f32[16,1024]{1,0:T(8,128)S(1)}, f32[16,1024]{1,0:T(8,128)S(1)}, u32[]{:S(2)}, u32[]{:S(2)}) %collective-permute-start.13) | collective-permute-done | bytes 65568 | tf_op jit(solution)/shard_map/ppermute | solution.py:28
  60.2 2.4 %collective-permute-done.12 = f32[16,1024]{1,0:T(8,128)S(1)} collective-permute-done((f32[16,1024]{1,0:T(8,128)S(1)}, f32[16,1024]{1,0:T(8,128)S(1)}, u32[]{:S(2)}, u32[]{:S(2)}) %collective-permute-start.12) | collective-permute-done | bytes 65568 | tf_op jit(solution)/shard_map/ppermute | solution.py:28
  62.6 0.1 copy.51
  62.8 0.2 convolution_bitcast_fusion
  63.1 0.1 reshape.254
  63.2 0.1 copy.61
  63.5 0.1 reshape.256
  63.6 0.1 reshape.242
  64.9 0.2 fusion.48
  65.1 7.0 %collective-permute-start.21 = (f32[16,112]{1,0:T(8,128)S(1)}, f32[16,112]{1,0:T(8,128)S(1)}, u32[]{:S(2)}, u32[]{:S(2)}) collective-permute-start(f32[16,112]{1,0:T(8,128)S(1)} %fusion.48), channel_id=1, source_target_pairs={{0,1},{1,0},{2,3},{3,2},{4,5},{5,4},{6,7},{7,6},{8,9},{9,8},{10,11... | collective-permute-start | bytes 21512 | tf_op jit(solution)/shard_map/ppermute | solution.py:28
  72.1 0.8 %collective-permute-done.21 = f32[16,112]{1,0:T(8,128)S(1)} collective-permute-done((f32[16,112]{1,0:T(8,128)S(1)}, f32[16,112]{1,0:T(8,128)S(1)}, u32[]{:S(2)}, u32[]{:S(2)}) %collective-permute-start.21) | collective-permute-done | bytes 7200 | tf_op jit(solution)/shard_map/ppermute | solution.py:28
  72.9 2.9 %collective-permute-start.24 = (f32[16,112]{1,0:T(8,128)S(1)}, f32[16,112]{1,0:T(8,128)S(1)}, u32[]{:S(2)}, u32[]{:S(2)}) collective-permute-start(f32[16,112]{1,0:T(8,128)S(1)} %add.177), channel_id=1, source_target_pairs={{0,4},{1,5},{2,6},{3,7},{4,0},{5,1},{6,2},{7,3},{8,12},{9,13},{10,... | collective-permute-start | bytes 21512 | tf_op jit(solution)/shard_map/ppermute | solution.py:28
  75.8 0.8 collective-permute-start.23
  76.6 0.7 pad_maximum_fusion.1
  77.2 2.3 %collective-permute-done.23 = f32[16,112]{1,0:T(8,128)S(1)} collective-permute-done((f32[16,112]{1,0:T(8,128)S(1)}, f32[16,112]{1,0:T(8,128)S(1)}, u32[]{:S(2)}, u32[]{:S(2)}) %collective-permute-start.23) | collective-permute-done | bytes 7200 | tf_op jit(solution)/shard_map/ppermute | solution.py:28
  79.5 0.6 add_add_fusion.4
  (92 shorter events, 4.1 us)
Async XLA Ops:
  0.6 30.6 %copy-start = (bf16[128,896]{1,0:T(8,128)(2,1)S(1)}, bf16[128,896]{1,0:T(8,128)(2,1)}, u32[]{:S(2)}) copy-start(bf16[128,896]{1,0:T(8,128)(2,1)} %param.15) | copy-start | bytes 688132
  3.9 11.9 %collective-permute-start = (f32[16,1152]{1,0:T(8,128)S(1)}, f32[16,1152]{1,0:T(8,128)S(1)}, u32[]{:S(2)}, u32[]{:S(2)}) collective-permute-start(f32[16,1152]{1,0:T(8,128)S(1)} %concatenate.15), channel_id=1, source_target_pairs={{0,48},{8,56},{16,32},{24,40},{32,16},{40,24},{48,0},{56,8},{64,11... | collective-permute-start | bytes 221192 | tf_op jit(solution)/shard_map/ppermute | solution.py:28
  13.2 14.1 %collective-permute-start.14 = (f32[16,1792]{1,0:T(8,128)S(1)}, f32[16,1792]{1,0:T(8,128)S(1)}, u32[]{:S(2)}, u32[]{:S(2)}) collective-permute-start(f32[16,1792]{1,0:T(8,128)S(1)} %pad_maximum_fusion), channel_id=1, source_target_pairs={{0,48},{8,56},{16,32},{24,40},{32,16},{40,24},{48,0},{56,8},{64,11... | collective-permute-start | bytes 344072 | tf_op jit(solution)/shard_map/ppermute | solution.py:28
  15.8 5.2 %collective-permute-start.3 = (f32[16,1152]{1,0:T(8,128)S(1)}, f32[16,1152]{1,0:T(8,128)S(1)}, u32[]{:S(2)}, u32[]{:S(2)}) collective-permute-start(f32[16,1152]{1,0:T(8,128)S(1)} %add.145), channel_id=1, source_target_pairs={{0,24},{8,16},{16,8},{24,0},{32,56},{40,48},{48,40},{56,32},{64,88... | collective-permute-start | bytes 221192 | tf_op jit(solution)/shard_map/ppermute | solution.py:28
  17.7 5.8 %collective-permute-start.2 = (f32[16,1152]{1,0:T(8,128)S(1)}, f32[16,1152]{1,0:T(8,128)S(1)}, u32[]{:S(2)}, u32[]{:S(2)}) collective-permute-start(f32[16,1152]{1,0:T(8,128)S(1)} %add.145), channel_id=1, source_target_pairs={{0,16},{8,24},{16,0},{24,8},{32,48},{40,56},{48,32},{56,40},{64,80... | collective-permute-start | bytes 221192 | tf_op jit(solution)/shard_map/ppermute | solution.py:28
  17.8 5.8 %collective-permute-start.1 = (f32[16,1152]{1,0:T(8,128)S(1)}, f32[16,1152]{1,0:T(8,128)S(1)}, u32[]{:S(2)}, u32[]{:S(2)}) collective-permute-start(f32[16,1152]{1,0:T(8,128)S(1)} %add.145), channel_id=1, source_target_pairs={{0,8},{8,0},{16,24},{24,16},{32,40},{40,32},{48,56},{56,48},{64,72... | collective-permute-start | bytes 221192 | tf_op jit(solution)/shard_map/ppermute | solution.py:28
  23.6 6.7 %collective-permute-start.6 = (f32[16,1152]{1,0:T(8,128)S(1)}, f32[16,1152]{1,0:T(8,128)S(1)}, u32[]{:S(2)}, u32[]{:S(2)}) collective-permute-start(f32[16,1152]{1,0:T(8,128)S(1)} %add_add_fusion.3), channel_id=1, source_target_pairs={{0,128},{8,136},{16,144},{24,152},{32,160},{40,168},{48,176},{56,1... | collective-permute-start | bytes 221192 | tf_op jit(solution)/shard_map/ppermute | solution.py:28
  26.4 4.7 %collective-permute-start.5 = (f32[16,1152]{1,0:T(8,128)S(1)}, f32[16,1152]{1,0:T(8,128)S(1)}, u32[]{:S(2)}, u32[]{:S(2)}) collective-permute-start(f32[16,1152]{1,0:T(8,128)S(1)} %add_add_fusion.3), channel_id=1, source_target_pairs={{0,192},{8,200},{16,208},{24,216},{32,224},{40,232},{48,240},{56,2... | collective-permute-start | bytes 221192 | tf_op jit(solution)/shard_map/ppermute | solution.py:28
  27.3 3.9 %collective-permute-start.4 = (f32[16,1152]{1,0:T(8,128)S(1)}, f32[16,1152]{1,0:T(8,128)S(1)}, u32[]{:S(2)}, u32[]{:S(2)}) collective-permute-start(f32[16,1152]{1,0:T(8,128)S(1)} %add_add_fusion.3), channel_id=1, source_target_pairs={{0,64},{8,72},{16,80},{24,88},{32,96},{40,104},{48,112},{56,120},{... | collective-permute-start | bytes 221192 | tf_op jit(solution)/shard_map/ppermute | solution.py:28
  27.3 15.6 %collective-permute-start.17 = (f32[16,1792]{1,0:T(8,128)S(1)}, f32[16,1792]{1,0:T(8,128)S(1)}, u32[]{:S(2)}, u32[]{:S(2)}) collective-permute-start(f32[16,1792]{1,0:T(8,128)S(1)} %fusion.94), channel_id=1, source_target_pairs={{0,24},{8,16},{16,8},{24,0},{32,56},{40,48},{48,40},{56,32},{64,88... | collective-permute-start | bytes 344072 | tf_op jit(solution)/shard_map/ppermute | solution.py:28
  28.8 14.1 %collective-permute-start.16 = (f32[16,1792]{1,0:T(8,128)S(1)}, f32[16,1792]{1,0:T(8,128)S(1)}, u32[]{:S(2)}, u32[]{:S(2)}) collective-permute-start(f32[16,1792]{1,0:T(8,128)S(1)} %fusion.94), channel_id=1, source_target_pairs={{0,16},{8,24},{16,0},{24,8},{32,48},{40,56},{48,32},{56,40},{64,80... | collective-permute-start | bytes 344072 | tf_op jit(solution)/shard_map/ppermute | solution.py:28
  30.2 12.6 %collective-permute-start.15 = (f32[16,1792]{1,0:T(8,128)S(1)}, f32[16,1792]{1,0:T(8,128)S(1)}, u32[]{:S(2)}, u32[]{:S(2)}) collective-permute-start(f32[16,1792]{1,0:T(8,128)S(1)} %fusion.94), channel_id=1, source_target_pairs={{0,8},{8,0},{16,24},{24,16},{32,40},{40,32},{48,56},{56,48},{64,72... | collective-permute-start | bytes 344072 | tf_op jit(solution)/shard_map/ppermute | solution.py:28
  38.4 26.5 %copy-start.1 = (bf16[896,112]{0,1:T(8,128)(2,1)S(1)}, bf16[896,112]{0,1:T(8,128)(2,1)}, u32[]{:S(2)}) copy-start(bf16[896,112]{0,1:T(8,128)(2,1)} %param.16) | copy-start | bytes 602116
  38.4 8.5 %collective-permute-start.7 = (f32[16,1024]{1,0:T(8,128)S(1)}, f32[16,1024]{1,0:T(8,128)S(1)}, u32[]{:S(2)}, u32[]{:S(2)}) collective-permute-start(f32[16,1024]{1,0:T(8,128)S(1)} %maximum_maximum_fusion), channel_id=1, source_target_pairs={{0,48},{8,56},{16,32},{24,40},{32,16},{40,24},{48,0},{56,8},{64,11... | collective-permute-start | bytes 196616 | tf_op jit(solution)/shard_map/ppermute | solution.py:28
  42.9 7.2 %collective-permute-start.20 = (f32[16,1792]{1,0:T(8,128)S(1)}, f32[16,1792]{1,0:T(8,128)S(1)}, u32[]{:S(2)}, u32[]{:S(2)}) collective-permute-start(f32[16,1792]{1,0:T(8,128)S(1)} %add_add_fusion.1), channel_id=1, source_target_pairs={{0,128},{8,136},{16,144},{24,152},{32,160},{40,168},{48,176},{56,1... | collective-permute-start | bytes 344072 | tf_op jit(solution)/shard_map/ppermute | solution.py:28
  46.0 5.9 %collective-permute-start.19 = (f32[16,1792]{1,0:T(8,128)S(1)}, f32[16,1792]{1,0:T(8,128)S(1)}, u32[]{:S(2)}, u32[]{:S(2)}) collective-permute-start(f32[16,1792]{1,0:T(8,128)S(1)} %add_add_fusion.1), channel_id=1, source_target_pairs={{0,192},{8,200},{16,208},{24,216},{32,224},{40,232},{48,240},{56,2... | collective-permute-start | bytes 344072 | tf_op jit(solution)/shard_map/ppermute | solution.py:28
  46.9 5.1 %collective-permute-start.18 = (f32[16,1792]{1,0:T(8,128)S(1)}, f32[16,1792]{1,0:T(8,128)S(1)}, u32[]{:S(2)}, u32[]{:S(2)}) collective-permute-start(f32[16,1792]{1,0:T(8,128)S(1)} %add_add_fusion.1), channel_id=1, source_target_pairs={{0,64},{8,72},{16,80},{24,88},{32,96},{40,104},{48,112},{56,120},{... | collective-permute-start | bytes 344072 | tf_op jit(solution)/shard_map/ppermute | solution.py:28
  47.4 5.2 %collective-permute-start.10 = (f32[16,1024]{1,0:T(8,128)S(1)}, f32[16,1024]{1,0:T(8,128)S(1)}, u32[]{:S(2)}, u32[]{:S(2)}) collective-permute-start(f32[16,1024]{1,0:T(8,128)S(1)} %maximum_maximum_fusion.1), channel_id=1, source_target_pairs={{0,24},{8,16},{16,8},{24,0},{32,56},{40,48},{48,40},{56,32},{64,88... | collective-permute-start | bytes 196616 | tf_op jit(solution)/shard_map/ppermute | solution.py:28
  49.1 5.0 %collective-permute-start.9 = (f32[16,1024]{1,0:T(8,128)S(1)}, f32[16,1024]{1,0:T(8,128)S(1)}, u32[]{:S(2)}, u32[]{:S(2)}) collective-permute-start(f32[16,1024]{1,0:T(8,128)S(1)} %maximum_maximum_fusion.1), channel_id=1, source_target_pairs={{0,16},{8,24},{16,0},{24,8},{32,48},{40,56},{48,32},{56,40},{64,80... | collective-permute-start | bytes 196616 | tf_op jit(solution)/shard_map/ppermute | solution.py:28
  50.1 4.1 %collective-permute-start.8 = (f32[16,1024]{1,0:T(8,128)S(1)}, f32[16,1024]{1,0:T(8,128)S(1)}, u32[]{:S(2)}, u32[]{:S(2)}) collective-permute-start(f32[16,1024]{1,0:T(8,128)S(1)} %maximum_maximum_fusion.1), channel_id=1, source_target_pairs={{0,8},{8,0},{16,24},{24,16},{32,40},{40,32},{48,56},{56,48},{64,72... | collective-permute-start | bytes 196616 | tf_op jit(solution)/shard_map/ppermute | solution.py:28
  55.5 4.6 %collective-permute-start.13 = (f32[16,1024]{1,0:T(8,128)S(1)}, f32[16,1024]{1,0:T(8,128)S(1)}, u32[]{:S(2)}, u32[]{:S(2)}) collective-permute-start(f32[16,1024]{1,0:T(8,128)S(1)} %maximum_maximum_fusion.2), channel_id=1, source_target_pairs={{0,128},{8,136},{16,144},{24,152},{32,160},{40,168},{48,176},{56,1... | collective-permute-start | bytes 196616 | tf_op jit(solution)/shard_map/ppermute | solution.py:28
  58.2 4.3 %collective-permute-start.12 = (f32[16,1024]{1,0:T(8,128)S(1)}, f32[16,1024]{1,0:T(8,128)S(1)}, u32[]{:S(2)}, u32[]{:S(2)}) collective-permute-start(f32[16,1024]{1,0:T(8,128)S(1)} %maximum_maximum_fusion.2), channel_id=1, source_target_pairs={{0,192},{8,200},{16,208},{24,216},{32,224},{40,232},{48,240},{56,2... | collective-permute-start | bytes 196616 | tf_op jit(solution)/shard_map/ppermute | solution.py:28
  59.1 3.5 %collective-permute-start.11 = (f32[16,1024]{1,0:T(8,128)S(1)}, f32[16,1024]{1,0:T(8,128)S(1)}, u32[]{:S(2)}, u32[]{:S(2)}) collective-permute-start(f32[16,1024]{1,0:T(8,128)S(1)} %maximum_maximum_fusion.2), channel_id=1, source_target_pairs={{0,64},{8,72},{16,80},{24,88},{32,96},{40,104},{48,112},{56,120},{... | collective-permute-start | bytes 196616 | tf_op jit(solution)/shard_map/ppermute | solution.py:28
  65.1 7.8 %collective-permute-start.21 = (f32[16,112]{1,0:T(8,128)S(1)}, f32[16,112]{1,0:T(8,128)S(1)}, u32[]{:S(2)}, u32[]{:S(2)}) collective-permute-start(f32[16,112]{1,0:T(8,128)S(1)} %fusion.48), channel_id=1, source_target_pairs={{0,1},{1,0},{2,3},{3,2},{4,5},{5,4},{6,7},{7,6},{8,9},{9,8},{10,11... | collective-permute-start | bytes 21512 | tf_op jit(solution)/shard_map/ppermute | solution.py:28
  72.9 4.4 %collective-permute-start.24 = (f32[16,112]{1,0:T(8,128)S(1)}, f32[16,112]{1,0:T(8,128)S(1)}, u32[]{:S(2)}, u32[]{:S(2)}) collective-permute-start(f32[16,112]{1,0:T(8,128)S(1)} %add.177), channel_id=1, source_target_pairs={{0,4},{1,5},{2,6},{3,7},{4,0},{5,1},{6,2},{7,3},{8,12},{9,13},{10,... | collective-permute-start | bytes 21512 | tf_op jit(solution)/shard_map/ppermute | solution.py:28
  75.8 3.7 %collective-permute-start.23 = (f32[16,112]{1,0:T(8,128)S(1)}, f32[16,112]{1,0:T(8,128)S(1)}, u32[]{:S(2)}, u32[]{:S(2)}) collective-permute-start(f32[16,112]{1,0:T(8,128)S(1)} %add.177), channel_id=1, source_target_pairs={{0,6},{1,7},{2,4},{3,5},{4,2},{5,3},{6,0},{7,1},{8,14},{9,15},{10,... | collective-permute-start | bytes 21512 | tf_op jit(solution)/shard_map/ppermute | solution.py:28
  76.6 2.9 %collective-permute-start.22 = (f32[16,112]{1,0:T(8,128)S(1)}, f32[16,112]{1,0:T(8,128)S(1)}, u32[]{:S(2)}, u32[]{:S(2)}) collective-permute-start(f32[16,112]{1,0:T(8,128)S(1)} %add.177), channel_id=1, source_target_pairs={{0,2},{1,3},{2,0},{3,1},{4,6},{5,7},{6,4},{7,5},{8,10},{9,11},{10,... | collective-permute-start | bytes 21512 | tf_op jit(solution)/shard_map/ppermute | solution.py:28

commit v10 on v9

--- a/solution.py
+++ b/solution.py
@@ -104,7 +104,9 @@
         [project(0), partial_low, partial_sq, jnp.zeros((rows, 127), f32)], axis=1
     )
     summed = butterfly_sum(packed, "seq", seq_masks)
-    kv_summed = butterfly_sum(jnp.concatenate([project(1), project(2)], axis=1), "seq", seq_masks)
+    kv_summed = butterfly_sum(
+        jnp.concatenate([project(1), project(2)], axis=1), "seq", [(m,) for r in seq_masks for m in r]
+    )
     low = summed[:, local : local + rank]
     total_sq = summed[:, local + rank]
     scale_rows = lax.rsqrt(total_sq / INPUT_WIDTH + 1e-05)[:, None]

time: 80.4 us -> 79.9 us (level)
  starting transfers between devices: 44.2 us -> 40.2 us
  waiting for transfers between devices: 13.4 us -> 16.8 us
    ppermute x25 -> x23, starting transfers between devices: 44.2 us -> 40.2 us  [exchange(): return lax.ppermute(x, axis, [(i, i ^ mask) for i in range(size)])]
    ppermute x25 -> x23, waiting for transfers between devices: 13.4 us -> 16.8 us  [exchange(): return lax.ppermute(x, axis, [(i, i ^ mask) for i in range(size)])]
  transfers between devices with their start and end apart: 25 -> 23, of which waited for: 10 -> 11; matrix products, arithmetic and copies ran while one was open for 17% -> 19% of each run, Pallas kernels for 0% -> 0%
where the time goes in v10:
time: 79.9 us; the launch traced here: 79.6 us
  starting transfers between devices  40.2 us (50%)
  waiting for transfers between devices  16.8 us (21%)
  matrix products  11.2 us (14%)
  other arithmetic  5.72 us (7%)
  local copies, waits for them, and re-layouts  4.56 us (6%)
  between operations  1.04 us (1%)
    ppermute x23, starting transfers between devices, exchange(): return lax.ppermute(x, axis, [(i, i ^ mask) for i in range(size)])  40.2 us
    ppermute x23, waiting for transfers between devices, exchange(): return lax.ppermute(x, axis, [(i, i ^ mask) for i in range(size)])  16.8 us
    dot_general x3, matrix products, project(): jnp.dot(scaled, query_key_value_weight[:, j, :], preferred_element_type=f32)  3.6 us
    dot_general x1, matrix products, shards(): jnp.einsum('rnc,rpc->rnp', q_block, cached_key_rows, preferred_element_ty...  3.17 us
    dot_general x1, matrix products, shards(): jnp.einsum('rnp,rpc->rnc', expo.astype(bf16), cached_value_rows, preferre...  2.68 us
  transfers between devices with their start and end apart: 23, of which 11 were waited for; matrix products, arithmetic and copies ran while one was open for 19% of the time, Pallas kernels for 0%

profile of v10, /device:TPU:1, one launch (start us, length us, event | category | flops | bytes accessed | tf_op | source)
XLA Modules:
  0.0 79.6 jit_solution(10786936873653143903)
XLA Ops:
  0.6 0.9 %fusion.51 = f32[16]{0:T(128)S(1)} fusion(bf16[16,224]{1,0:T(8,128)(2,1)} %param.11), kind=kLoop, calls=%fused_computation.79 | loop fusion | flops 10736 | bytes 7232 | tf_op jit(solution)/shard_map/reduce_sum | solution.py:102
  1.6 1.0 %fusion.84 = f32[16,128]{1,0:T(8,128)S(1)} fusion(bf16[224,128]{1,0:T(8,128)(2,1)} %param.14, bf16[16,224]{1,0:T(8,128)(2,1)} %param.11, f32[224]{0:T(256)} %param.12), kind=kOutput, calls=%fused_computation.144 | convolution fusion | flops 928256 | bytes 73600 | tf_op jit(solution)/shard_map/dot_general | solution.py:101
  2.6 1.2 %fusion.6 = f32[16,896]{1,0:T(8,128)S(1)} fusion(bf16[224,3,896]{2,0,1:T(8,128)(2,1)} %param.13, bf16[16,224]{1,0:T(8,128)(2,1)} %param.11, f32[224]{0:T(256)} %param.12), kind=kOutput, calls=%fused_computation.9 | convolution fusion | flops 6433280 | bytes 467968 | tf_op jit(solution)/shard_map/dot_general | solution.py:99
  3.9 6.9 %collective-permute-start = (f32[16,1152]{1,0:T(8,128)S(1)}, f32[16,1152]{1,0:T(8,128)S(1)}, u32[]{:S(2)}, u32[]{:S(2)}) collective-permute-start(f32[16,1152]{1,0:T(8,128)S(1)} %concatenate.15), channel_id=1, source_target_pairs={{0,48},{8,56},{16,32},{24,40},{32,16},{40,24},{48,0},{56,8},{64,11... | collective-permute-start | bytes 221192 | tf_op jit(solution)/shard_map/ppermute | solution.py:28
  10.7 1.2 %fusion.2 = f32[16,896]{1,0:T(8,128)S(1)} fusion(bf16[224,3,896]{2,0,1:T(8,128)(2,1)} %param.13, bf16[16,224]{1,0:T(8,128)(2,1)} %param.11, f32[224]{0:T(256)} %param.12), kind=kOutput, calls=%fused_computation.5 | convolution fusion | flops 6433280 | bytes 467968 | tf_op jit(solution)/shard_map/dot_general | solution.py:99
  11.9 1.2 %fusion.4 = f32[16,896]{1,0:T(8,128)S(1)} fusion(bf16[224,3,896]{2,0,1:T(8,128)(2,1)} %param.13, bf16[16,224]{1,0:T(8,128)(2,1)} %param.11, f32[224]{0:T(256)} %param.12), kind=kOutput, calls=%fused_computation.7 | convolution fusion | flops 6433280 | bytes 467968 | tf_op jit(solution)/shard_map/dot_general | solution.py:99
  13.2 0.1 collective-permute-start.14
  13.3 0.7 iota_add_fusion
  14.0 0.7 broadcast_compare_fusion.1
  14.8 0.7 fusion.47
  15.6 2.0 %collective-permute-start.3 = (f32[16,1152]{1,0:T(8,128)S(1)}, f32[16,1152]{1,0:T(8,128)S(1)}, u32[]{:S(2)}, u32[]{:S(2)}) collective-permute-start(f32[16,1152]{1,0:T(8,128)S(1)} %add.139), channel_id=1, source_target_pairs={{0,24},{8,16},{16,8},{24,0},{32,56},{40,48},{48,40},{56,32},{64,88... | collective-permute-start | bytes 221192 | tf_op jit(solution)/shard_map/ppermute | solution.py:28
  17.6 1.6 %collective-permute-start.1 = (f32[16,1152]{1,0:T(8,128)S(1)}, f32[16,1152]{1,0:T(8,128)S(1)}, u32[]{:S(2)}, u32[]{:S(2)}) collective-permute-start(f32[16,1152]{1,0:T(8,128)S(1)} %add.139), channel_id=1, source_target_pairs={{0,8},{8,0},{16,24},{24,16},{32,40},{40,32},{48,56},{56,48},{64,72... | collective-permute-start | bytes 221192 | tf_op jit(solution)/shard_map/ppermute | solution.py:28
  19.4 1.4 %collective-permute-done.3 = f32[16,1152]{1,0:T(8,128)S(1)} collective-permute-done((f32[16,1152]{1,0:T(8,128)S(1)}, f32[16,1152]{1,0:T(8,128)S(1)}, u32[]{:S(2)}, u32[]{:S(2)}) %collective-permute-start.3) | collective-permute-done | bytes 73760 | tf_op jit(solution)/shard_map/ppermute | solution.py:28
  20.8 2.6 %collective-permute-done.2 = f32[16,1152]{1,0:T(8,128)S(1)} collective-permute-done((f32[16,1152]{1,0:T(8,128)S(1)}, f32[16,1152]{1,0:T(8,128)S(1)}, u32[]{:S(2)}, u32[]{:S(2)}) %collective-permute-start.2) | collective-permute-done | bytes 73760 | tf_op jit(solution)/shard_map/ppermute | solution.py:28
  23.4 2.8 %collective-permute-start.6 = (f32[16,1152]{1,0:T(8,128)S(1)}, f32[16,1152]{1,0:T(8,128)S(1)}, u32[]{:S(2)}, u32[]{:S(2)}) collective-permute-start(f32[16,1152]{1,0:T(8,128)S(1)} %add_add_fusion.1), channel_id=1, source_target_pairs={{0,128},{8,136},{16,144},{24,152},{32,160},{40,168},{48,176},{56,1... | collective-permute-start | bytes 221192 | tf_op jit(solution)/shard_map/ppermute | solution.py:28
  26.2 0.9 %collective-permute-start.5 = (f32[16,1152]{1,0:T(8,128)S(1)}, f32[16,1152]{1,0:T(8,128)S(1)}, u32[]{:S(2)}, u32[]{:S(2)}) collective-permute-start(f32[16,1152]{1,0:T(8,128)S(1)} %add_add_fusion.1), channel_id=1, source_target_pairs={{0,192},{8,200},{16,208},{24,216},{32,224},{40,232},{48,240},{56,2... | collective-permute-start | bytes 221192 | tf_op jit(solution)/shard_map/ppermute | solution.py:28
  27.1 1.6 %collective-permute-start.15 = (f32[16,1792]{1,0:T(8,128)S(1)}, f32[16,1792]{1,0:T(8,128)S(1)}, u32[]{:S(2)}, u32[]{:S(2)}) collective-permute-start(f32[16,1792]{1,0:T(8,128)S(1)} %fusion.94), channel_id=1, source_target_pairs={{0,8},{8,0},{16,24},{24,16},{32,40},{40,32},{48,56},{56,48},{64,72... | collective-permute-start | bytes 344072 | tf_op jit(solution)/shard_map/ppermute | solution.py:28
  28.7 2.2 %collective-permute-done.5 = f32[16,1152]{1,0:T(8,128)S(1)} collective-permute-done((f32[16,1152]{1,0:T(8,128)S(1)}, f32[16,1152]{1,0:T(8,128)S(1)}, u32[]{:S(2)}, u32[]{:S(2)}) %collective-permute-start.5) | collective-permute-done | bytes 73760 | tf_op jit(solution)/shard_map/ppermute | solution.py:28
  30.9 0.1 fusion.71
  31.1 0.2 fusion.35
  31.4 3.2 %fusion.99 = (f32[4,16]{1,0:T(4,128)S(1)}, f32[4,16,512]{2,1,0:T(8,128)S(1)}) fusion(pred[4,16,512]{2,1,0:T(8,128)(4,1)S(1)} %reshape.227, bf16[4,512,896]{2,1,0:T(8,128)(2,1)} %param.17, bf16[4,16,896]{2,1,0:T(8,128)(2,1)S(1)} %broadcast_in_dim.148, pred[16,896]{1,0:T(8,128)(4,1)S(1)} %broadcast_in_dim.142), kind=kOutput, calls=%fused_computation.158 | convolution fusion | flops 58875840 | bytes 3963136 | tf_op jit(solution)/shard_map/rnc,rpc->rnp/dot_general | solution.py:126
  34.7 0.2 fusion.13
  34.9 0.1 copy.64
  35.0 0.1 copy.62
  35.2 2.7 %fusion.15 = f32[4,16,896]{2,1,0:T(8,128)S(1)} fusion(bf16[4,512,896]{2,1,0:T(8,128)(2,1)} %param.18, f32[4,16,512]{2,1,0:T(8,128)S(1)} %get-tuple-element.34, f32[4,16]{1,0:T(4,128)S(1)} %get-tuple-element.33, u8[16,512]{1,0:T(8,128)(4,1)S(1)} %fusion.42), kind=kOutput, calls=%fused_computation.26 | convolution fusion | flops 58949632 | bytes 4038912 | tf_op jit(solution)/shard_map/rnp,rpc->rnc/dot_general | solution.py:142
  38.1 4.1 %collective-permute-start.7 = (f32[16,1024]{1,0:T(8,128)S(1)}, f32[16,1024]{1,0:T(8,128)S(1)}, u32[]{:S(2)}, u32[]{:S(2)}) collective-permute-start(f32[16,1024]{1,0:T(8,128)S(1)} %maximum_maximum_fusion), channel_id=1, source_target_pairs={{0,48},{8,56},{16,32},{24,40},{32,16},{40,24},{48,0},{56,8},{64,11... | collective-permute-start | bytes 196616 | tf_op jit(solution)/shard_map/ppermute | solution.py:28
  42.2 2.7 %collective-permute-start.16 = (f32[16,1792]{1,0:T(8,128)S(1)}, f32[16,1792]{1,0:T(8,128)S(1)}, u32[]{:S(2)}, u32[]{:S(2)}) collective-permute-start(f32[16,1792]{1,0:T(8,128)S(1)} %add.160), channel_id=1, source_target_pairs={{0,16},{8,24},{16,0},{24,8},{32,48},{40,56},{48,32},{56,40},{64,80... | collective-permute-start | bytes 344072 | tf_op jit(solution)/shard_map/ppermute | solution.py:28
  45.1 0.1 reshape.234
  45.3 0.1 reshape.235
  45.5 1.6 %collective-permute-start.10 = (f32[16,1024]{1,0:T(8,128)S(1)}, f32[16,1024]{1,0:T(8,128)S(1)}, u32[]{:S(2)}, u32[]{:S(2)}) collective-permute-start(f32[16,1024]{1,0:T(8,128)S(1)} %maximum_maximum_fusion.1), channel_id=1, source_target_pairs={{0,24},{8,16},{16,8},{24,0},{32,56},{40,48},{48,40},{56,32},{64,88... | collective-permute-start | bytes 196616 | tf_op jit(solution)/shard_map/ppermute | solution.py:28
  47.1 0.6 collective-permute-start.9
  47.8 1.3 %collective-permute-start.8 = (f32[16,1024]{1,0:T(8,128)S(1)}, f32[16,1024]{1,0:T(8,128)S(1)}, u32[]{:S(2)}, u32[]{:S(2)}) collective-permute-start(f32[16,1024]{1,0:T(8,128)S(1)} %maximum_maximum_fusion.1), channel_id=1, source_target_pairs={{0,8},{8,0},{16,24},{24,16},{32,40},{40,32},{48,56},{56,48},{64,72... | collective-permute-start | bytes 196616 | tf_op jit(solution)/shard_map/ppermute | solution.py:28
  49.3 1.2 %collective-permute-done.10 = f32[16,1024]{1,0:T(8,128)S(1)} collective-permute-done((f32[16,1024]{1,0:T(8,128)S(1)}, f32[16,1024]{1,0:T(8,128)S(1)}, u32[]{:S(2)}, u32[]{:S(2)}) %collective-permute-start.10) | collective-permute-done | bytes 65568 | tf_op jit(solution)/shard_map/ppermute | solution.py:28
  50.5 3.9 %collective-permute-done.9 = f32[16,1024]{1,0:T(8,128)S(1)} collective-permute-done((f32[16,1024]{1,0:T(8,128)S(1)}, f32[16,1024]{1,0:T(8,128)S(1)}, u32[]{:S(2)}, u32[]{:S(2)}) %collective-permute-start.9) | collective-permute-done | bytes 65568 | tf_op jit(solution)/shard_map/ppermute | solution.py:28
  54.5 0.1 reshape.236
  54.7 0.1 reshape.237
  54.9 0.1 reshape.238
  55.1 0.1 reshape.239
  55.7 1.1 %collective-permute-start.18 = (f32[16,1792]{1,0:T(8,128)S(1)}, f32[16,1792]{1,0:T(8,128)S(1)}, u32[]{:S(2)}, u32[]{:S(2)}) collective-permute-start(f32[16,1792]{1,0:T(8,128)S(1)} %add.162), channel_id=1, source_target_pairs={{0,192},{8,200},{16,208},{24,216},{32,224},{40,232},{48,240},{56,2... | collective-permute-start | bytes 344072 | tf_op jit(solution)/shard_map/ppermute | solution.py:28
  56.9 0.8 %collective-permute-start.13 = (f32[16,1024]{1,0:T(8,128)S(1)}, f32[16,1024]{1,0:T(8,128)S(1)}, u32[]{:S(2)}, u32[]{:S(2)}) collective-permute-start(f32[16,1024]{1,0:T(8,128)S(1)} %maximum_maximum_fusion.2), channel_id=1, source_target_pairs={{0,128},{8,136},{16,144},{24,152},{32,160},{40,168},{48,176},{56,1... | collective-permute-start | bytes 196616 | tf_op jit(solution)/shard_map/ppermute | solution.py:28
  57.7 2.1 %collective-permute-start.12 = (f32[16,1024]{1,0:T(8,128)S(1)}, f32[16,1024]{1,0:T(8,128)S(1)}, u32[]{:S(2)}, u32[]{:S(2)}) collective-permute-start(f32[16,1024]{1,0:T(8,128)S(1)} %maximum_maximum_fusion.2), channel_id=1, source_target_pairs={{0,192},{8,200},{16,208},{24,216},{32,224},{40,232},{48,240},{56,2... | collective-permute-start | bytes 196616 | tf_op jit(solution)/shard_map/ppermute | solution.py:28
  59.8 0.8 %collective-permute-done.18 = f32[16,1792]{1,0:T(8,128)S(1)} collective-permute-done((f32[16,1792]{1,0:T(8,128)S(1)}, f32[16,1792]{1,0:T(8,128)S(1)}, u32[]{:S(2)}, u32[]{:S(2)}) %collective-permute-start.18) | collective-permute-done | bytes 114720 | tf_op jit(solution)/shard_map/ppermute | solution.py:28
  60.9 0.2 fusion.98
  61.1 0.1 copy.58
  61.2 0.5 collective-permute-done.13
  61.7 0.7 collective-permute-done.12
  62.4 0.5 collective-permute-done.11
  63.0 0.1 copy.51
  63.1 0.2 convolution_bitcast_fusion
  63.4 0.1 reshape.254
  63.5 0.1 copy.61
  63.8 0.1 reshape.256
  64.0 0.1 reshape.242
  64.1 0.1 reshape.243
  64.3 0.1 reshape.244
  64.5 0.1 reshape.245
  65.2 0.2 fusion.48
  65.4 6.1 %collective-permute-start.19 = (f32[16,112]{1,0:T(8,128)S(1)}, f32[16,112]{1,0:T(8,128)S(1)}, u32[]{:S(2)}, u32[]{:S(2)}) collective-permute-start(f32[16,112]{1,0:T(8,128)S(1)} %fusion.48), channel_id=1, source_target_pairs={{0,1},{1,0},{2,3},{3,2},{4,5},{5,4},{6,7},{7,6},{8,9},{9,8},{10,11... | collective-permute-start | bytes 21512 | tf_op jit(solution)/shard_map/ppermute | solution.py:28
  71.5 0.8 %collective-permute-done.19 = f32[16,112]{1,0:T(8,128)S(1)} collective-permute-done((f32[16,112]{1,0:T(8,128)S(1)}, f32[16,112]{1,0:T(8,128)S(1)}, u32[]{:S(2)}, u32[]{:S(2)}) %collective-permute-start.19) | collective-permute-done | bytes 7200 | tf_op jit(solution)/shard_map/ppermute | solution.py:28
  72.3 2.9 %collective-permute-start.22 = (f32[16,112]{1,0:T(8,128)S(1)}, f32[16,112]{1,0:T(8,128)S(1)}, u32[]{:S(2)}, u32[]{:S(2)}) collective-permute-start(f32[16,112]{1,0:T(8,128)S(1)} %add.169), channel_id=1, source_target_pairs={{0,4},{1,5},{2,6},{3,7},{4,0},{5,1},{6,2},{7,3},{8,12},{9,13},{10,... | collective-permute-start | bytes 21512 | tf_op jit(solution)/shard_map/ppermute | solution.py:28
  75.3 0.8 collective-permute-start.21
  76.0 0.7 pad_maximum_fusion.1
  76.7 2.3 %collective-permute-done.21 = f32[16,112]{1,0:T(8,128)S(1)} collective-permute-done((f32[16,112]{1,0:T(8,128)S(1)}, f32[16,112]{1,0:T(8,128)S(1)}, u32[]{:S(2)}, u32[]{:S(2)}) %collective-permute-start.21) | collective-permute-done | bytes 7200 | tf_op jit(solution)/shard_map/ppermute | solution.py:28
  79.0 0.6 add_add_fusion.2
  (90 shorter events, 4.1 us)
Async XLA Ops:
  0.6 30.4 %copy-start = (bf16[128,896]{1,0:T(8,128)(2,1)S(1)}, bf16[128,896]{1,0:T(8,128)(2,1)}, u32[]{:S(2)}) copy-start(bf16[128,896]{1,0:T(8,128)(2,1)} %param.15) | copy-start | bytes 688132
  3.9 11.7 %collective-permute-start = (f32[16,1152]{1,0:T(8,128)S(1)}, f32[16,1152]{1,0:T(8,128)S(1)}, u32[]{:S(2)}, u32[]{:S(2)}) collective-permute-start(f32[16,1152]{1,0:T(8,128)S(1)} %concatenate.15), channel_id=1, source_target_pairs={{0,48},{8,56},{16,32},{24,40},{32,16},{40,24},{48,0},{56,8},{64,11... | collective-permute-start | bytes 221192 | tf_op jit(solution)/shard_map/ppermute | solution.py:28
  13.2 13.9 %collective-permute-start.14 = (f32[16,1792]{1,0:T(8,128)S(1)}, f32[16,1792]{1,0:T(8,128)S(1)}, u32[]{:S(2)}, u32[]{:S(2)}) collective-permute-start(f32[16,1792]{1,0:T(8,128)S(1)} %pad_maximum_fusion), channel_id=1, source_target_pairs={{0,48},{8,56},{16,32},{24,40},{32,16},{40,24},{48,0},{56,8},{64,11... | collective-permute-start | bytes 344072 | tf_op jit(solution)/shard_map/ppermute | solution.py:28
  15.6 5.2 %collective-permute-start.3 = (f32[16,1152]{1,0:T(8,128)S(1)}, f32[16,1152]{1,0:T(8,128)S(1)}, u32[]{:S(2)}, u32[]{:S(2)}) collective-permute-start(f32[16,1152]{1,0:T(8,128)S(1)} %add.139), channel_id=1, source_target_pairs={{0,24},{8,16},{16,8},{24,0},{32,56},{40,48},{48,40},{56,32},{64,88... | collective-permute-start | bytes 221192 | tf_op jit(solution)/shard_map/ppermute | solution.py:28
  17.5 5.8 %collective-permute-start.2 = (f32[16,1152]{1,0:T(8,128)S(1)}, f32[16,1152]{1,0:T(8,128)S(1)}, u32[]{:S(2)}, u32[]{:S(2)}) collective-permute-start(f32[16,1152]{1,0:T(8,128)S(1)} %add.139), channel_id=1, source_target_pairs={{0,16},{8,24},{16,0},{24,8},{32,48},{40,56},{48,32},{56,40},{64,80... | collective-permute-start | bytes 221192 | tf_op jit(solution)/shard_map/ppermute | solution.py:28
  17.6 5.8 %collective-permute-start.1 = (f32[16,1152]{1,0:T(8,128)S(1)}, f32[16,1152]{1,0:T(8,128)S(1)}, u32[]{:S(2)}, u32[]{:S(2)}) collective-permute-start(f32[16,1152]{1,0:T(8,128)S(1)} %add.139), channel_id=1, source_target_pairs={{0,8},{8,0},{16,24},{24,16},{32,40},{40,32},{48,56},{56,48},{64,72... | collective-permute-start | bytes 221192 | tf_op jit(solution)/shard_map/ppermute | solution.py:28
  23.4 5.4 %collective-permute-start.6 = (f32[16,1152]{1,0:T(8,128)S(1)}, f32[16,1152]{1,0:T(8,128)S(1)}, u32[]{:S(2)}, u32[]{:S(2)}) collective-permute-start(f32[16,1152]{1,0:T(8,128)S(1)} %add_add_fusion.1), channel_id=1, source_target_pairs={{0,128},{8,136},{16,144},{24,152},{32,160},{40,168},{48,176},{56,1... | collective-permute-start | bytes 221192 | tf_op jit(solution)/shard_map/ppermute | solution.py:28
  26.2 4.7 %collective-permute-start.5 = (f32[16,1152]{1,0:T(8,128)S(1)}, f32[16,1152]{1,0:T(8,128)S(1)}, u32[]{:S(2)}, u32[]{:S(2)}) collective-permute-start(f32[16,1152]{1,0:T(8,128)S(1)} %add_add_fusion.1), channel_id=1, source_target_pairs={{0,192},{8,200},{16,208},{24,216},{32,224},{40,232},{48,240},{56,2... | collective-permute-start | bytes 221192 | tf_op jit(solution)/shard_map/ppermute | solution.py:28
  27.1 3.9 %collective-permute-start.4 = (f32[16,1152]{1,0:T(8,128)S(1)}, f32[16,1152]{1,0:T(8,128)S(1)}, u32[]{:S(2)}, u32[]{:S(2)}) collective-permute-start(f32[16,1152]{1,0:T(8,128)S(1)} %add_add_fusion.1), channel_id=1, source_target_pairs={{0,64},{8,72},{16,80},{24,88},{32,96},{40,104},{48,112},{56,120},{... | collective-permute-start | bytes 221192 | tf_op jit(solution)/shard_map/ppermute | solution.py:28
  27.1 15.1 %collective-permute-start.15 = (f32[16,1792]{1,0:T(8,128)S(1)}, f32[16,1792]{1,0:T(8,128)S(1)}, u32[]{:S(2)}, u32[]{:S(2)}) collective-permute-start(f32[16,1792]{1,0:T(8,128)S(1)} %fusion.94), channel_id=1, source_target_pairs={{0,8},{8,0},{16,24},{24,16},{32,40},{40,32},{48,56},{56,48},{64,72... | collective-permute-start | bytes 344072 | tf_op jit(solution)/shard_map/ppermute | solution.py:28
  38.1 6.8 %collective-permute-start.7 = (f32[16,1024]{1,0:T(8,128)S(1)}, f32[16,1024]{1,0:T(8,128)S(1)}, u32[]{:S(2)}, u32[]{:S(2)}) collective-permute-start(f32[16,1024]{1,0:T(8,128)S(1)} %maximum_maximum_fusion), channel_id=1, source_target_pairs={{0,48},{8,56},{16,32},{24,40},{32,16},{40,24},{48,0},{56,8},{64,11... | collective-permute-start | bytes 196616 | tf_op jit(solution)/shard_map/ppermute | solution.py:28
  42.2 23.0 %copy-start.1 = (bf16[896,112]{0,1:T(8,128)(2,1)S(1)}, bf16[896,112]{0,1:T(8,128)(2,1)}, u32[]{:S(2)}) copy-start(bf16[896,112]{0,1:T(8,128)(2,1)} %param.16) | copy-start | bytes 602116
  42.2 7.0 %collective-permute-start.16 = (f32[16,1792]{1,0:T(8,128)S(1)}, f32[16,1792]{1,0:T(8,128)S(1)}, u32[]{:S(2)}, u32[]{:S(2)}) collective-permute-start(f32[16,1792]{1,0:T(8,128)S(1)} %add.160), channel_id=1, source_target_pairs={{0,16},{8,24},{16,0},{24,8},{32,48},{40,56},{48,32},{56,40},{64,80... | collective-permute-start | bytes 344072 | tf_op jit(solution)/shard_map/ppermute | solution.py:28
  45.5 5.0 %collective-permute-start.10 = (f32[16,1024]{1,0:T(8,128)S(1)}, f32[16,1024]{1,0:T(8,128)S(1)}, u32[]{:S(2)}, u32[]{:S(2)}) collective-permute-start(f32[16,1024]{1,0:T(8,128)S(1)} %maximum_maximum_fusion.1), channel_id=1, source_target_pairs={{0,24},{8,16},{16,8},{24,0},{32,56},{40,48},{48,40},{56,32},{64,88... | collective-permute-start | bytes 196616 | tf_op jit(solution)/shard_map/ppermute | solution.py:28
  47.1 7.2 %collective-permute-start.9 = (f32[16,1024]{1,0:T(8,128)S(1)}, f32[16,1024]{1,0:T(8,128)S(1)}, u32[]{:S(2)}, u32[]{:S(2)}) collective-permute-start(f32[16,1024]{1,0:T(8,128)S(1)} %maximum_maximum_fusion.1), channel_id=1, source_target_pairs={{0,16},{8,24},{16,0},{24,8},{32,48},{40,56},{48,32},{56,40},{64,80... | collective-permute-start | bytes 196616 | tf_op jit(solution)/shard_map/ppermute | solution.py:28
  47.8 6.6 %collective-permute-start.8 = (f32[16,1024]{1,0:T(8,128)S(1)}, f32[16,1024]{1,0:T(8,128)S(1)}, u32[]{:S(2)}, u32[]{:S(2)}) collective-permute-start(f32[16,1024]{1,0:T(8,128)S(1)} %maximum_maximum_fusion.1), channel_id=1, source_target_pairs={{0,8},{8,0},{16,24},{24,16},{32,40},{40,32},{48,56},{56,48},{64,72... | collective-permute-start | bytes 196616 | tf_op jit(solution)/shard_map/ppermute | solution.py:28
  49.2 6.4 %collective-permute-start.17 = (f32[16,1792]{1,0:T(8,128)S(1)}, f32[16,1792]{1,0:T(8,128)S(1)}, u32[]{:S(2)}, u32[]{:S(2)}) collective-permute-start(f32[16,1792]{1,0:T(8,128)S(1)} %add.161), channel_id=1, source_target_pairs={{0,64},{8,72},{16,80},{24,88},{32,96},{40,104},{48,112},{56,120},{... | collective-permute-start | bytes 344072 | tf_op jit(solution)/shard_map/ppermute | solution.py:28
  55.7 4.9 %collective-permute-start.18 = (f32[16,1792]{1,0:T(8,128)S(1)}, f32[16,1792]{1,0:T(8,128)S(1)}, u32[]{:S(2)}, u32[]{:S(2)}) collective-permute-start(f32[16,1792]{1,0:T(8,128)S(1)} %add.162), channel_id=1, source_target_pairs={{0,192},{8,200},{16,208},{24,216},{32,224},{40,232},{48,240},{56,2... | collective-permute-start | bytes 344072 | tf_op jit(solution)/shard_map/ppermute | solution.py:28
  56.9 4.9 %collective-permute-start.13 = (f32[16,1024]{1,0:T(8,128)S(1)}, f32[16,1024]{1,0:T(8,128)S(1)}, u32[]{:S(2)}, u32[]{:S(2)}) collective-permute-start(f32[16,1024]{1,0:T(8,128)S(1)} %maximum_maximum_fusion.2), channel_id=1, source_target_pairs={{0,128},{8,136},{16,144},{24,152},{32,160},{40,168},{48,176},{56,1... | collective-permute-start | bytes 196616 | tf_op jit(solution)/shard_map/ppermute | solution.py:28
  57.7 4.7 %collective-permute-start.12 = (f32[16,1024]{1,0:T(8,128)S(1)}, f32[16,1024]{1,0:T(8,128)S(1)}, u32[]{:S(2)}, u32[]{:S(2)}) collective-permute-start(f32[16,1024]{1,0:T(8,128)S(1)} %maximum_maximum_fusion.2), channel_id=1, source_target_pairs={{0,192},{8,200},{16,208},{24,216},{32,224},{40,232},{48,240},{56,2... | collective-permute-start | bytes 196616 | tf_op jit(solution)/shard_map/ppermute | solution.py:28
  59.8 3.1 %collective-permute-start.11 = (f32[16,1024]{1,0:T(8,128)S(1)}, f32[16,1024]{1,0:T(8,128)S(1)}, u32[]{:S(2)}, u32[]{:S(2)}) collective-permute-start(f32[16,1024]{1,0:T(8,128)S(1)} %maximum_maximum_fusion.2), channel_id=1, source_target_pairs={{0,64},{8,72},{16,80},{24,88},{32,96},{40,104},{48,112},{56,120},{... | collective-permute-start | bytes 196616 | tf_op jit(solution)/shard_map/ppermute | solution.py:28
  65.4 7.0 %collective-permute-start.19 = (f32[16,112]{1,0:T(8,128)S(1)}, f32[16,112]{1,0:T(8,128)S(1)}, u32[]{:S(2)}, u32[]{:S(2)}) collective-permute-start(f32[16,112]{1,0:T(8,128)S(1)} %fusion.48), channel_id=1, source_target_pairs={{0,1},{1,0},{2,3},{3,2},{4,5},{5,4},{6,7},{7,6},{8,9},{9,8},{10,11... | collective-permute-start | bytes 21512 | tf_op jit(solution)/shard_map/ppermute | solution.py:28
  72.3 4.3 %collective-permute-start.22 = (f32[16,112]{1,0:T(8,128)S(1)}, f32[16,112]{1,0:T(8,128)S(1)}, u32[]{:S(2)}, u32[]{:S(2)}) collective-permute-start(f32[16,112]{1,0:T(8,128)S(1)} %add.169), channel_id=1, source_target_pairs={{0,4},{1,5},{2,6},{3,7},{4,0},{5,1},{6,2},{7,3},{8,12},{9,13},{10,... | collective-permute-start | bytes 21512 | tf_op jit(solution)/shard_map/ppermute | solution.py:28
  75.3 3.7 %collective-permute-start.21 = (f32[16,112]{1,0:T(8,128)S(1)}, f32[16,112]{1,0:T(8,128)S(1)}, u32[]{:S(2)}, u32[]{:S(2)}) collective-permute-start(f32[16,112]{1,0:T(8,128)S(1)} %add.169), channel_id=1, source_target_pairs={{0,6},{1,7},{2,4},{3,5},{4,2},{5,3},{6,0},{7,1},{8,14},{9,15},{10,... | collective-permute-start | bytes 21512 | tf_op jit(solution)/shard_map/ppermute | solution.py:28
  76.0 2.9 %collective-permute-start.20 = (f32[16,112]{1,0:T(8,128)S(1)}, f32[16,112]{1,0:T(8,128)S(1)}, u32[]{:S(2)}, u32[]{:S(2)}) collective-permute-start(f32[16,112]{1,0:T(8,128)S(1)} %add.169), channel_id=1, source_target_pairs={{0,2},{1,3},{2,0},{3,1},{4,6},{5,7},{6,4},{7,5},{8,10},{9,11},{10,... | collective-permute-start | bytes 21512 | tf_op jit(solution)/shard_map/ppermute | solution.py:28

commit v11 on v10

--- a/solution.py
+++ b/solution.py
@@ -172,17 +172,18 @@
     ) * HD ** (-0.5)
     causal = order[:, None] >= order[None, :]
     fresh = jnp.where(causal[None, None], fresh, NEG)
-    own_top = by_row(jnp.max(fresh, axis=-1))
-    top = jnp.maximum(cache_top, own_top)
-    top_rht = top.reshape(count, NEW, heads).transpose(0, 2, 1)
-    own_e = jnp.where(fresh > CUT, jnp.exp(fresh - top_rht[..., None]), 0.0)
+    own_top_rht = jnp.max(fresh, axis=-1)
+    own_e = jnp.where(fresh > CUT, jnp.exp(fresh - own_top_rht[..., None]), 0.0)
     own_total = by_row(jnp.sum(own_e, axis=-1))
     own_out = jnp.einsum(
         "rhtu,ruhd->rthd", own_e.astype(bf16), value_all, preferred_element_type=f32
     ).reshape(rows, local)
+    own_top = by_row(own_top_rht)
+    top = jnp.maximum(cache_top, own_top)
     cache_scale = jnp.exp(cache_top - top)
-    output = cache_out * jnp.repeat(cache_scale, HD, axis=1) + own_out
-    total = cache_total * cache_scale + own_total
+    own_scale = jnp.exp(own_top - top)
+    output = cache_out * jnp.repeat(cache_scale, HD, axis=1) + own_out * jnp.repeat(own_scale, HD, axis=1)
+    total = cache_total * cache_scale + own_total * own_scale
     attn = (output / jnp.repeat(total, HD, axis=1)).astype(bf16)
     partial_out = jnp.dot(attn, output_weight, preferred_element_type=f32)
     mixed = butterfly_sum(partial_out, "tensor", tensor_masks)

time: 79.9 us -> 79.4 us (level)
  transfers between devices with their start and end apart: 23 -> 23, of which waited for: 11 -> 10; matrix products, arithmetic and copies ran while one was open for 19% -> 20% of each run, Pallas kernels for 0% -> 0%
where the time goes in v11:
time: 79.4 us; the launch traced here: 79.1 us
  starting transfers between devices  40.2 us (51%)
  waiting for transfers between devices  16.3 us (21%)
  matrix products  11.2 us (14%)
  other arithmetic  5.65 us (7%)
  local copies, waits for them, and re-layouts  4.63 us (6%)
  between operations  1.05 us (1%)
    ppermute x23, starting transfers between devices, exchange(): return lax.ppermute(x, axis, [(i, i ^ mask) for i in range(size)])  40.2 us
    ppermute x23, waiting for transfers between devices, exchange(): return lax.ppermute(x, axis, [(i, i ^ mask) for i in range(size)])  16.3 us
    dot_general x3, matrix products, project(): jnp.dot(scaled, query_key_value_weight[:, j, :], preferred_element_type=f32)  3.6 us
    dot_general x1, matrix products, shards(): jnp.einsum('rnc,rpc->rnp', q_block, cached_key_rows, preferred_element_ty...  3.17 us
    dot_general x1, matrix products, shards(): jnp.einsum('rnp,rpc->rnc', expo.astype(bf16), cached_value_rows, preferre...  2.68 us
  transfers between devices with their start and end apart: 23, of which 10 were waited for; matrix products, arithmetic and copies ran while one was open for 20% of the time, Pallas kernels for 0%

profile of v11, /device:TPU:1, one launch (start us, length us, event | category | flops | bytes accessed | tf_op | source)
XLA Modules:
  0.0 79.1 jit_solution(18405665107361304177)
XLA Ops:
  0.6 0.9 %fusion.51 = f32[16]{0:T(128)S(1)} fusion(bf16[16,224]{1,0:T(8,128)(2,1)} %param.11), kind=kLoop, calls=%fused_computation.79 | loop fusion | flops 10736 | bytes 7232 | tf_op jit(solution)/shard_map/reduce_sum | solution.py:102
  1.6 1.0 %fusion.86 = f32[16,128]{1,0:T(8,128)S(1)} fusion(bf16[224,128]{1,0:T(8,128)(2,1)} %param.14, bf16[16,224]{1,0:T(8,128)(2,1)} %param.11, f32[224]{0:T(256)} %param.12), kind=kOutput, calls=%fused_computation.147 | convolution fusion | flops 928256 | bytes 73600 | tf_op jit(solution)/shard_map/dot_general | solution.py:101
  2.6 1.2 %fusion.6 = f32[16,896]{1,0:T(8,128)S(1)} fusion(bf16[224,3,896]{2,0,1:T(8,128)(2,1)} %param.13, bf16[16,224]{1,0:T(8,128)(2,1)} %param.11, f32[224]{0:T(256)} %param.12), kind=kOutput, calls=%fused_computation.9 | convolution fusion | flops 6433280 | bytes 467968 | tf_op jit(solution)/shard_map/dot_general | solution.py:99
  3.9 6.9 %collective-permute-start = (f32[16,1152]{1,0:T(8,128)S(1)}, f32[16,1152]{1,0:T(8,128)S(1)}, u32[]{:S(2)}, u32[]{:S(2)}) collective-permute-start(f32[16,1152]{1,0:T(8,128)S(1)} %concatenate.15), channel_id=1, source_target_pairs={{0,48},{8,56},{16,32},{24,40},{32,16},{40,24},{48,0},{56,8},{64,11... | collective-permute-start | bytes 221192 | tf_op jit(solution)/shard_map/ppermute | solution.py:28
  10.7 1.2 %fusion.2 = f32[16,896]{1,0:T(8,128)S(1)} fusion(bf16[224,3,896]{2,0,1:T(8,128)(2,1)} %param.13, bf16[16,224]{1,0:T(8,128)(2,1)} %param.11, f32[224]{0:T(256)} %param.12), kind=kOutput, calls=%fused_computation.5 | convolution fusion | flops 6433280 | bytes 467968 | tf_op jit(solution)/shard_map/dot_general | solution.py:99
  11.9 1.2 %fusion.4 = f32[16,896]{1,0:T(8,128)S(1)} fusion(bf16[224,3,896]{2,0,1:T(8,128)(2,1)} %param.13, bf16[16,224]{1,0:T(8,128)(2,1)} %param.11, f32[224]{0:T(256)} %param.12), kind=kOutput, calls=%fused_computation.7 | convolution fusion | flops 6433280 | bytes 467968 | tf_op jit(solution)/shard_map/dot_general | solution.py:99
  13.2 0.1 collective-permute-start.14
  13.3 0.7 iota_add_fusion
  14.0 0.7 broadcast_compare_fusion.1
  14.8 0.7 fusion.47
  15.6 2.0 %collective-permute-start.3 = (f32[16,1152]{1,0:T(8,128)S(1)}, f32[16,1152]{1,0:T(8,128)S(1)}, u32[]{:S(2)}, u32[]{:S(2)}) collective-permute-start(f32[16,1152]{1,0:T(8,128)S(1)} %add.139), channel_id=1, source_target_pairs={{0,24},{8,16},{16,8},{24,0},{32,56},{40,48},{48,40},{56,32},{64,88... | collective-permute-start | bytes 221192 | tf_op jit(solution)/shard_map/ppermute | solution.py:28
  17.6 1.6 %collective-permute-start.1 = (f32[16,1152]{1,0:T(8,128)S(1)}, f32[16,1152]{1,0:T(8,128)S(1)}, u32[]{:S(2)}, u32[]{:S(2)}) collective-permute-start(f32[16,1152]{1,0:T(8,128)S(1)} %add.139), channel_id=1, source_target_pairs={{0,8},{8,0},{16,24},{24,16},{32,40},{40,32},{48,56},{56,48},{64,72... | collective-permute-start | bytes 221192 | tf_op jit(solution)/shard_map/ppermute | solution.py:28
  19.4 1.4 %collective-permute-done.3 = f32[16,1152]{1,0:T(8,128)S(1)} collective-permute-done((f32[16,1152]{1,0:T(8,128)S(1)}, f32[16,1152]{1,0:T(8,128)S(1)}, u32[]{:S(2)}, u32[]{:S(2)}) %collective-permute-start.3) | collective-permute-done | bytes 73760 | tf_op jit(solution)/shard_map/ppermute | solution.py:28
  20.8 2.6 %collective-permute-done.2 = f32[16,1152]{1,0:T(8,128)S(1)} collective-permute-done((f32[16,1152]{1,0:T(8,128)S(1)}, f32[16,1152]{1,0:T(8,128)S(1)}, u32[]{:S(2)}, u32[]{:S(2)}) %collective-permute-start.2) | collective-permute-done | bytes 73760 | tf_op jit(solution)/shard_map/ppermute | solution.py:28
  23.4 2.8 %collective-permute-start.6 = (f32[16,1152]{1,0:T(8,128)S(1)}, f32[16,1152]{1,0:T(8,128)S(1)}, u32[]{:S(2)}, u32[]{:S(2)}) collective-permute-start(f32[16,1152]{1,0:T(8,128)S(1)} %add_add_fusion.1), channel_id=1, source_target_pairs={{0,128},{8,136},{16,144},{24,152},{32,160},{40,168},{48,176},{56,1... | collective-permute-start | bytes 221192 | tf_op jit(solution)/shard_map/ppermute | solution.py:28
  26.2 0.9 %collective-permute-start.5 = (f32[16,1152]{1,0:T(8,128)S(1)}, f32[16,1152]{1,0:T(8,128)S(1)}, u32[]{:S(2)}, u32[]{:S(2)}) collective-permute-start(f32[16,1152]{1,0:T(8,128)S(1)} %add_add_fusion.1), channel_id=1, source_target_pairs={{0,192},{8,200},{16,208},{24,216},{32,224},{40,232},{48,240},{56,2... | collective-permute-start | bytes 221192 | tf_op jit(solution)/shard_map/ppermute | solution.py:28
  27.1 1.6 %collective-permute-start.15 = (f32[16,1792]{1,0:T(8,128)S(1)}, f32[16,1792]{1,0:T(8,128)S(1)}, u32[]{:S(2)}, u32[]{:S(2)}) collective-permute-start(f32[16,1792]{1,0:T(8,128)S(1)} %fusion.95), channel_id=1, source_target_pairs={{0,8},{8,0},{16,24},{24,16},{32,40},{40,32},{48,56},{56,48},{64,72... | collective-permute-start | bytes 344072 | tf_op jit(solution)/shard_map/ppermute | solution.py:28
  28.7 2.2 %collective-permute-done.5 = f32[16,1152]{1,0:T(8,128)S(1)} collective-permute-done((f32[16,1152]{1,0:T(8,128)S(1)}, f32[16,1152]{1,0:T(8,128)S(1)}, u32[]{:S(2)}, u32[]{:S(2)}) %collective-permute-start.5) | collective-permute-done | bytes 73760 | tf_op jit(solution)/shard_map/ppermute | solution.py:28
  30.9 0.1 fusion.73
  31.1 0.2 fusion.35
  31.4 3.2 %fusion.99 = (f32[4,16]{1,0:T(4,128)S(1)}, f32[4,16,512]{2,1,0:T(8,128)S(1)}) fusion(pred[4,16,512]{2,1,0:T(8,128)(4,1)S(1)} %reshape.227, bf16[4,512,896]{2,1,0:T(8,128)(2,1)} %param.17, bf16[4,16,896]{2,1,0:T(8,128)(2,1)S(1)} %broadcast_in_dim.151, pred[16,896]{1,0:T(8,128)(4,1)S(1)} %broadcast_in_dim.145), kind=kOutput, calls=%fused_computation.158 | convolution fusion | flops 58875840 | bytes 3963136 | tf_op jit(solution)/shard_map/rnc,rpc->rnp/dot_general | solution.py:126
  34.7 0.2 fusion.13
  34.9 0.1 copy.60
  35.0 0.1 copy.58
  35.2 2.7 %fusion.15 = f32[4,16,896]{2,1,0:T(8,128)S(1)} fusion(bf16[4,512,896]{2,1,0:T(8,128)(2,1)} %param.18, f32[4,16,512]{2,1,0:T(8,128)S(1)} %get-tuple-element.30, f32[4,16]{1,0:T(4,128)S(1)} %get-tuple-element.29, u8[16,512]{1,0:T(8,128)(4,1)S(1)} %fusion.42), kind=kOutput, calls=%fused_computation.26 | convolution fusion | flops 58949632 | bytes 4038912 | tf_op jit(solution)/shard_map/rnp,rpc->rnc/dot_general | solution.py:142
  38.1 4.1 %collective-permute-start.7 = (f32[16,1024]{1,0:T(8,128)S(1)}, f32[16,1024]{1,0:T(8,128)S(1)}, u32[]{:S(2)}, u32[]{:S(2)}) collective-permute-start(f32[16,1024]{1,0:T(8,128)S(1)} %maximum_maximum_fusion), channel_id=1, source_target_pairs={{0,48},{8,56},{16,32},{24,40},{32,16},{40,24},{48,0},{56,8},{64,11... | collective-permute-start | bytes 196616 | tf_op jit(solution)/shard_map/ppermute | solution.py:28
  42.2 2.7 %collective-permute-start.16 = (f32[16,1792]{1,0:T(8,128)S(1)}, f32[16,1792]{1,0:T(8,128)S(1)}, u32[]{:S(2)}, u32[]{:S(2)}) collective-permute-start(f32[16,1792]{1,0:T(8,128)S(1)} %add.160), channel_id=1, source_target_pairs={{0,16},{8,24},{16,0},{24,8},{32,48},{40,56},{48,32},{56,40},{64,80... | collective-permute-start | bytes 344072 | tf_op jit(solution)/shard_map/ppermute | solution.py:28
  45.1 0.1 reshape.234
  45.3 0.1 reshape.235
  45.5 1.6 %collective-permute-start.10 = (f32[16,1024]{1,0:T(8,128)S(1)}, f32[16,1024]{1,0:T(8,128)S(1)}, u32[]{:S(2)}, u32[]{:S(2)}) collective-permute-start(f32[16,1024]{1,0:T(8,128)S(1)} %maximum_maximum_fusion.1), channel_id=1, source_target_pairs={{0,24},{8,16},{16,8},{24,0},{32,56},{40,48},{48,40},{56,32},{64,88... | collective-permute-start | bytes 196616 | tf_op jit(solution)/shard_map/ppermute | solution.py:28
  47.1 0.6 collective-permute-start.9
  47.8 1.3 %collective-permute-start.8 = (f32[16,1024]{1,0:T(8,128)S(1)}, f32[16,1024]{1,0:T(8,128)S(1)}, u32[]{:S(2)}, u32[]{:S(2)}) collective-permute-start(f32[16,1024]{1,0:T(8,128)S(1)} %maximum_maximum_fusion.1), channel_id=1, source_target_pairs={{0,8},{8,0},{16,24},{24,16},{32,40},{40,32},{48,56},{56,48},{64,72... | collective-permute-start | bytes 196616 | tf_op jit(solution)/shard_map/ppermute | solution.py:28
  49.3 1.2 %collective-permute-done.10 = f32[16,1024]{1,0:T(8,128)S(1)} collective-permute-done((f32[16,1024]{1,0:T(8,128)S(1)}, f32[16,1024]{1,0:T(8,128)S(1)}, u32[]{:S(2)}, u32[]{:S(2)}) %collective-permute-start.10) | collective-permute-done | bytes 65568 | tf_op jit(solution)/shard_map/ppermute | solution.py:28
  50.5 3.9 %collective-permute-done.9 = f32[16,1024]{1,0:T(8,128)S(1)} collective-permute-done((f32[16,1024]{1,0:T(8,128)S(1)}, f32[16,1024]{1,0:T(8,128)S(1)}, u32[]{:S(2)}, u32[]{:S(2)}) %collective-permute-start.9) | collective-permute-done | bytes 65568 | tf_op jit(solution)/shard_map/ppermute | solution.py:28
  54.5 0.1 reshape.236
  54.7 0.1 reshape.237
  54.9 0.1 reshape.238
  55.1 0.1 reshape.239
  55.3 0.1 reshape.240
  55.5 0.1 reshape.241
  55.7 1.1 %collective-permute-start.18 = (f32[16,1792]{1,0:T(8,128)S(1)}, f32[16,1792]{1,0:T(8,128)S(1)}, u32[]{:S(2)}, u32[]{:S(2)}) collective-permute-start(f32[16,1792]{1,0:T(8,128)S(1)} %add.162), channel_id=1, source_target_pairs={{0,192},{8,200},{16,208},{24,216},{32,224},{40,232},{48,240},{56,2... | collective-permute-start | bytes 344072 | tf_op jit(solution)/shard_map/ppermute | solution.py:28
  56.9 0.8 %collective-permute-start.13 = (f32[16,1024]{1,0:T(8,128)S(1)}, f32[16,1024]{1,0:T(8,128)S(1)}, u32[]{:S(2)}, u32[]{:S(2)}) collective-permute-start(f32[16,1024]{1,0:T(8,128)S(1)} %maximum_maximum_fusion.2), channel_id=1, source_target_pairs={{0,128},{8,136},{16,144},{24,152},{32,160},{40,168},{48,176},{56,1... | collective-permute-start | bytes 196616 | tf_op jit(solution)/shard_map/ppermute | solution.py:28
  57.7 2.1 %collective-permute-start.12 = (f32[16,1024]{1,0:T(8,128)S(1)}, f32[16,1024]{1,0:T(8,128)S(1)}, u32[]{:S(2)}, u32[]{:S(2)}) collective-permute-start(f32[16,1024]{1,0:T(8,128)S(1)} %maximum_maximum_fusion.2), channel_id=1, source_target_pairs={{0,192},{8,200},{16,208},{24,216},{32,224},{40,232},{48,240},{56,2... | collective-permute-start | bytes 196616 | tf_op jit(solution)/shard_map/ppermute | solution.py:28
  59.8 0.8 %collective-permute-done.18 = f32[16,1792]{1,0:T(8,128)S(1)} collective-permute-done((f32[16,1792]{1,0:T(8,128)S(1)}, f32[16,1792]{1,0:T(8,128)S(1)}, u32[]{:S(2)}, u32[]{:S(2)}) %collective-permute-start.18) | collective-permute-done | bytes 114720 | tf_op jit(solution)/shard_map/ppermute | solution.py:28
  60.9 0.2 fusion.100
  61.1 0.2 convolution_bitcast_fusion
  61.5 0.1 copy.57
  61.6 0.1 copy.62
  61.7 0.7 collective-permute-done.12
  62.4 0.5 collective-permute-done.11
  63.3 0.1 reshape.242
  63.4 0.1 reshape.254
  63.6 0.1 reshape.243
  63.8 0.1 reshape.244
  64.0 0.1 reshape.245
  64.2 0.1 reshape.246
  64.7 0.2 fusion.48
  64.9 6.1 %collective-permute-start.19 = (f32[16,112]{1,0:T(8,128)S(1)}, f32[16,112]{1,0:T(8,128)S(1)}, u32[]{:S(2)}, u32[]{:S(2)}) collective-permute-start(f32[16,112]{1,0:T(8,128)S(1)} %fusion.48), channel_id=1, source_target_pairs={{0,1},{1,0},{2,3},{3,2},{4,5},{5,4},{6,7},{7,6},{8,9},{9,8},{10,11... | collective-permute-start | bytes 21512 | tf_op jit(solution)/shard_map/ppermute | solution.py:28
  71.0 0.8 %collective-permute-done.19 = f32[16,112]{1,0:T(8,128)S(1)} collective-permute-done((f32[16,112]{1,0:T(8,128)S(1)}, f32[16,112]{1,0:T(8,128)S(1)}, u32[]{:S(2)}, u32[]{:S(2)}) %collective-permute-start.19) | collective-permute-done | bytes 7200 | tf_op jit(solution)/shard_map/ppermute | solution.py:28
  71.8 2.9 %collective-permute-start.22 = (f32[16,112]{1,0:T(8,128)S(1)}, f32[16,112]{1,0:T(8,128)S(1)}, u32[]{:S(2)}, u32[]{:S(2)}) collective-permute-start(f32[16,112]{1,0:T(8,128)S(1)} %add.169), channel_id=1, source_target_pairs={{0,4},{1,5},{2,6},{3,7},{4,0},{5,1},{6,2},{7,3},{8,12},{9,13},{10,... | collective-permute-start | bytes 21512 | tf_op jit(solution)/shard_map/ppermute | solution.py:28
  74.7 0.8 collective-permute-start.21
  75.5 0.7 pad_maximum_fusion.1
  76.2 2.3 %collective-permute-done.21 = f32[16,112]{1,0:T(8,128)S(1)} collective-permute-done((f32[16,112]{1,0:T(8,128)S(1)}, f32[16,112]{1,0:T(8,128)S(1)}, u32[]{:S(2)}, u32[]{:S(2)}) %collective-permute-start.21) | collective-permute-done | bytes 7200 | tf_op jit(solution)/shard_map/ppermute | solution.py:28
  78.5 0.6 add_add_fusion.2
  (90 shorter events, 4.0 us)
Async XLA Ops:
  0.6 30.4 %copy-start = (bf16[128,896]{1,0:T(8,128)(2,1)S(1)}, bf16[128,896]{1,0:T(8,128)(2,1)}, u32[]{:S(2)}) copy-start(bf16[128,896]{1,0:T(8,128)(2,1)} %param.15) | copy-start | bytes 688132
  3.9 11.7 %collective-permute-start = (f32[16,1152]{1,0:T(8,128)S(1)}, f32[16,1152]{1,0:T(8,128)S(1)}, u32[]{:S(2)}, u32[]{:S(2)}) collective-permute-start(f32[16,1152]{1,0:T(8,128)S(1)} %concatenate.15), channel_id=1, source_target_pairs={{0,48},{8,56},{16,32},{24,40},{32,16},{40,24},{48,0},{56,8},{64,11... | collective-permute-start | bytes 221192 | tf_op jit(solution)/shard_map/ppermute | solution.py:28
  13.2 13.9 %collective-permute-start.14 = (f32[16,1792]{1,0:T(8,128)S(1)}, f32[16,1792]{1,0:T(8,128)S(1)}, u32[]{:S(2)}, u32[]{:S(2)}) collective-permute-start(f32[16,1792]{1,0:T(8,128)S(1)} %pad_maximum_fusion), channel_id=1, source_target_pairs={{0,48},{8,56},{16,32},{24,40},{32,16},{40,24},{48,0},{56,8},{64,11... | collective-permute-start | bytes 344072 | tf_op jit(solution)/shard_map/ppermute | solution.py:28
  15.6 5.2 %collective-permute-start.3 = (f32[16,1152]{1,0:T(8,128)S(1)}, f32[16,1152]{1,0:T(8,128)S(1)}, u32[]{:S(2)}, u32[]{:S(2)}) collective-permute-start(f32[16,1152]{1,0:T(8,128)S(1)} %add.139), channel_id=1, source_target_pairs={{0,24},{8,16},{16,8},{24,0},{32,56},{40,48},{48,40},{56,32},{64,88... | collective-permute-start | bytes 221192 | tf_op jit(solution)/shard_map/ppermute | solution.py:28
  17.5 5.8 %collective-permute-start.2 = (f32[16,1152]{1,0:T(8,128)S(1)}, f32[16,1152]{1,0:T(8,128)S(1)}, u32[]{:S(2)}, u32[]{:S(2)}) collective-permute-start(f32[16,1152]{1,0:T(8,128)S(1)} %add.139), channel_id=1, source_target_pairs={{0,16},{8,24},{16,0},{24,8},{32,48},{40,56},{48,32},{56,40},{64,80... | collective-permute-start | bytes 221192 | tf_op jit(solution)/shard_map/ppermute | solution.py:28
  17.6 5.8 %collective-permute-start.1 = (f32[16,1152]{1,0:T(8,128)S(1)}, f32[16,1152]{1,0:T(8,128)S(1)}, u32[]{:S(2)}, u32[]{:S(2)}) collective-permute-start(f32[16,1152]{1,0:T(8,128)S(1)} %add.139), channel_id=1, source_target_pairs={{0,8},{8,0},{16,24},{24,16},{32,40},{40,32},{48,56},{56,48},{64,72... | collective-permute-start | bytes 221192 | tf_op jit(solution)/shard_map/ppermute | solution.py:28
  23.4 5.4 %collective-permute-start.6 = (f32[16,1152]{1,0:T(8,128)S(1)}, f32[16,1152]{1,0:T(8,128)S(1)}, u32[]{:S(2)}, u32[]{:S(2)}) collective-permute-start(f32[16,1152]{1,0:T(8,128)S(1)} %add_add_fusion.1), channel_id=1, source_target_pairs={{0,128},{8,136},{16,144},{24,152},{32,160},{40,168},{48,176},{56,1... | collective-permute-start | bytes 221192 | tf_op jit(solution)/shard_map/ppermute | solution.py:28
  26.2 4.7 %collective-permute-start.5 = (f32[16,1152]{1,0:T(8,128)S(1)}, f32[16,1152]{1,0:T(8,128)S(1)}, u32[]{:S(2)}, u32[]{:S(2)}) collective-permute-start(f32[16,1152]{1,0:T(8,128)S(1)} %add_add_fusion.1), channel_id=1, source_target_pairs={{0,192},{8,200},{16,208},{24,216},{32,224},{40,232},{48,240},{56,2... | collective-permute-start | bytes 221192 | tf_op jit(solution)/shard_map/ppermute | solution.py:28
  27.1 3.9 %collective-permute-start.4 = (f32[16,1152]{1,0:T(8,128)S(1)}, f32[16,1152]{1,0:T(8,128)S(1)}, u32[]{:S(2)}, u32[]{:S(2)}) collective-permute-start(f32[16,1152]{1,0:T(8,128)S(1)} %add_add_fusion.1), channel_id=1, source_target_pairs={{0,64},{8,72},{16,80},{24,88},{32,96},{40,104},{48,112},{56,120},{... | collective-permute-start | bytes 221192 | tf_op jit(solution)/shard_map/ppermute | solution.py:28
  27.1 15.1 %collective-permute-start.15 = (f32[16,1792]{1,0:T(8,128)S(1)}, f32[16,1792]{1,0:T(8,128)S(1)}, u32[]{:S(2)}, u32[]{:S(2)}) collective-permute-start(f32[16,1792]{1,0:T(8,128)S(1)} %fusion.95), channel_id=1, source_target_pairs={{0,8},{8,0},{16,24},{24,16},{32,40},{40,32},{48,56},{56,48},{64,72... | collective-permute-start | bytes 344072 | tf_op jit(solution)/shard_map/ppermute | solution.py:28
  38.1 6.8 %collective-permute-start.7 = (f32[16,1024]{1,0:T(8,128)S(1)}, f32[16,1024]{1,0:T(8,128)S(1)}, u32[]{:S(2)}, u32[]{:S(2)}) collective-permute-start(f32[16,1024]{1,0:T(8,128)S(1)} %maximum_maximum_fusion), channel_id=1, source_target_pairs={{0,48},{8,56},{16,32},{24,40},{32,16},{40,24},{48,0},{56,8},{64,11... | collective-permute-start | bytes 196616 | tf_op jit(solution)/shard_map/ppermute | solution.py:28
  42.2 22.5 %copy-start.1 = (bf16[896,112]{0,1:T(8,128)(2,1)S(1)}, bf16[896,112]{0,1:T(8,128)(2,1)}, u32[]{:S(2)}) copy-start(bf16[896,112]{0,1:T(8,128)(2,1)} %param.16) | copy-start | bytes 602116
  42.2 7.0 %collective-permute-start.16 = (f32[16,1792]{1,0:T(8,128)S(1)}, f32[16,1792]{1,0:T(8,128)S(1)}, u32[]{:S(2)}, u32[]{:S(2)}) collective-permute-start(f32[16,1792]{1,0:T(8,128)S(1)} %add.160), channel_id=1, source_target_pairs={{0,16},{8,24},{16,0},{24,8},{32,48},{40,56},{48,32},{56,40},{64,80... | collective-permute-start | bytes 344072 | tf_op jit(solution)/shard_map/ppermute | solution.py:28
  45.5 5.0 %collective-permute-start.10 = (f32[16,1024]{1,0:T(8,128)S(1)}, f32[16,1024]{1,0:T(8,128)S(1)}, u32[]{:S(2)}, u32[]{:S(2)}) collective-permute-start(f32[16,1024]{1,0:T(8,128)S(1)} %maximum_maximum_fusion.1), channel_id=1, source_target_pairs={{0,24},{8,16},{16,8},{24,0},{32,56},{40,48},{48,40},{56,32},{64,88... | collective-permute-start | bytes 196616 | tf_op jit(solution)/shard_map/ppermute | solution.py:28
  47.1 7.2 %collective-permute-start.9 = (f32[16,1024]{1,0:T(8,128)S(1)}, f32[16,1024]{1,0:T(8,128)S(1)}, u32[]{:S(2)}, u32[]{:S(2)}) collective-permute-start(f32[16,1024]{1,0:T(8,128)S(1)} %maximum_maximum_fusion.1), channel_id=1, source_target_pairs={{0,16},{8,24},{16,0},{24,8},{32,48},{40,56},{48,32},{56,40},{64,80... | collective-permute-start | bytes 196616 | tf_op jit(solution)/shard_map/ppermute | solution.py:28
  47.8 6.6 %collective-permute-start.8 = (f32[16,1024]{1,0:T(8,128)S(1)}, f32[16,1024]{1,0:T(8,128)S(1)}, u32[]{:S(2)}, u32[]{:S(2)}) collective-permute-start(f32[16,1024]{1,0:T(8,128)S(1)} %maximum_maximum_fusion.1), channel_id=1, source_target_pairs={{0,8},{8,0},{16,24},{24,16},{32,40},{40,32},{48,56},{56,48},{64,72... | collective-permute-start | bytes 196616 | tf_op jit(solution)/shard_map/ppermute | solution.py:28
  49.2 6.4 %collective-permute-start.17 = (f32[16,1792]{1,0:T(8,128)S(1)}, f32[16,1792]{1,0:T(8,128)S(1)}, u32[]{:S(2)}, u32[]{:S(2)}) collective-permute-start(f32[16,1792]{1,0:T(8,128)S(1)} %add.161), channel_id=1, source_target_pairs={{0,64},{8,72},{16,80},{24,88},{32,96},{40,104},{48,112},{56,120},{... | collective-permute-start | bytes 344072 | tf_op jit(solution)/shard_map/ppermute | solution.py:28
  55.7 4.9 %collective-permute-start.18 = (f32[16,1792]{1,0:T(8,128)S(1)}, f32[16,1792]{1,0:T(8,128)S(1)}, u32[]{:S(2)}, u32[]{:S(2)}) collective-permute-start(f32[16,1792]{1,0:T(8,128)S(1)} %add.162), channel_id=1, source_target_pairs={{0,192},{8,200},{16,208},{24,216},{32,224},{40,232},{48,240},{56,2... | collective-permute-start | bytes 344072 | tf_op jit(solution)/shard_map/ppermute | solution.py:28
  56.9 4.9 %collective-permute-start.13 = (f32[16,1024]{1,0:T(8,128)S(1)}, f32[16,1024]{1,0:T(8,128)S(1)}, u32[]{:S(2)}, u32[]{:S(2)}) collective-permute-start(f32[16,1024]{1,0:T(8,128)S(1)} %maximum_maximum_fusion.2), channel_id=1, source_target_pairs={{0,128},{8,136},{16,144},{24,152},{32,160},{40,168},{48,176},{56,1... | collective-permute-start | bytes 196616 | tf_op jit(solution)/shard_map/ppermute | solution.py:28
  57.7 4.7 %collective-permute-start.12 = (f32[16,1024]{1,0:T(8,128)S(1)}, f32[16,1024]{1,0:T(8,128)S(1)}, u32[]{:S(2)}, u32[]{:S(2)}) collective-permute-start(f32[16,1024]{1,0:T(8,128)S(1)} %maximum_maximum_fusion.2), channel_id=1, source_target_pairs={{0,192},{8,200},{16,208},{24,216},{32,224},{40,232},{48,240},{56,2... | collective-permute-start | bytes 196616 | tf_op jit(solution)/shard_map/ppermute | solution.py:28
  59.8 3.1 %collective-permute-start.11 = (f32[16,1024]{1,0:T(8,128)S(1)}, f32[16,1024]{1,0:T(8,128)S(1)}, u32[]{:S(2)}, u32[]{:S(2)}) collective-permute-start(f32[16,1024]{1,0:T(8,128)S(1)} %maximum_maximum_fusion.2), channel_id=1, source_target_pairs={{0,64},{8,72},{16,80},{24,88},{32,96},{40,104},{48,112},{56,120},{... | collective-permute-start | bytes 196616 | tf_op jit(solution)/shard_map/ppermute | solution.py:28
  64.9 6.9 %collective-permute-start.19 = (f32[16,112]{1,0:T(8,128)S(1)}, f32[16,112]{1,0:T(8,128)S(1)}, u32[]{:S(2)}, u32[]{:S(2)}) collective-permute-start(f32[16,112]{1,0:T(8,128)S(1)} %fusion.48), channel_id=1, source_target_pairs={{0,1},{1,0},{2,3},{3,2},{4,5},{5,4},{6,7},{7,6},{8,9},{9,8},{10,11... | collective-permute-start | bytes 21512 | tf_op jit(solution)/shard_map/ppermute | solution.py:28
  71.8 4.4 %collective-permute-start.22 = (f32[16,112]{1,0:T(8,128)S(1)}, f32[16,112]{1,0:T(8,128)S(1)}, u32[]{:S(2)}, u32[]{:S(2)}) collective-permute-start(f32[16,112]{1,0:T(8,128)S(1)} %add.169), channel_id=1, source_target_pairs={{0,4},{1,5},{2,6},{3,7},{4,0},{5,1},{6,2},{7,3},{8,12},{9,13},{10,... | collective-permute-start | bytes 21512 | tf_op jit(solution)/shard_map/ppermute | solution.py:28
  74.7 3.7 %collective-permute-start.21 = (f32[16,112]{1,0:T(8,128)S(1)}, f32[16,112]{1,0:T(8,128)S(1)}, u32[]{:S(2)}, u32[]{:S(2)}) collective-permute-start(f32[16,112]{1,0:T(8,128)S(1)} %add.169), channel_id=1, source_target_pairs={{0,6},{1,7},{2,4},{3,5},{4,2},{5,3},{6,0},{7,1},{8,14},{9,15},{10,... | collective-permute-start | bytes 21512 | tf_op jit(solution)/shard_map/ppermute | solution.py:28
  75.5 2.9 %collective-permute-start.20 = (f32[16,112]{1,0:T(8,128)S(1)}, f32[16,112]{1,0:T(8,128)S(1)}, u32[]{:S(2)}, u32[]{:S(2)}) collective-permute-start(f32[16,112]{1,0:T(8,128)S(1)} %add.169), channel_id=1, source_target_pairs={{0,2},{1,3},{2,0},{3,1},{4,6},{5,7},{6,4},{7,5},{8,10},{9,11},{10,... | collective-permute-start | bytes 21512 | tf_op jit(solution)/shard_map/ppermute | solution.py:28

commit v12 on v11

--- a/solution.py
+++ b/solution.py
@@ -40,11 +40,19 @@
     return x
 
 
+def per_column(s, width):
+    col = lax.broadcasted_iota(jnp.int32, (s.shape[0], width), 1) // HD
+    out = jnp.broadcast_to(s[:, 0:1], (s.shape[0], width))
+    for h in range(1, s.shape[1]):
+        out = jnp.where(col == h, s[:, h : h + 1], out)
+    return out
+
+
 def merge_softmax(a, b, width, heads):
     top = jnp.maximum(a[:, width + heads : width + 2 * heads], b[:, width + heads : width + 2 * heads])
     sa = jnp.exp(a[:, width + heads : width + 2 * heads] - top)
     sb = jnp.exp(b[:, width + heads : width + 2 * heads] - top)
-    values = a[:, :width] * jnp.repeat(sa, HD, axis=1) + b[:, :width] * jnp.repeat(sb, HD, axis=1)
+    values = a[:, :width] * per_column(sa, width) + b[:, :width] * per_column(sb, width)
     totals = a[:, width : width + heads] * sa + b[:, width : width + heads] * sb
     pad = a.shape[1] - width - 2 * heads
     return jnp.concatenate([values, totals, top, jnp.zeros((a.shape[0], pad), jnp.float32)], axis=1)
@@ -182,9 +190,9 @@
     top = jnp.maximum(cache_top, own_top)
     cache_scale = jnp.exp(cache_top - top)
     own_scale = jnp.exp(own_top - top)
-    output = cache_out * jnp.repeat(cache_scale, HD, axis=1) + own_out * jnp.repeat(own_scale, HD, axis=1)
+    output = cache_out * per_column(cache_scale, local) + own_out * per_column(own_scale, local)
     total = cache_total * cache_scale + own_total * own_scale
-    attn = (output / jnp.repeat(total, HD, axis=1)).astype(bf16)
+    attn = (output / per_column(total, local)).astype(bf16)
     partial_out = jnp.dot(attn, output_weight, preferred_element_type=f32)
     mixed = butterfly_sum(partial_out, "tensor", tensor_masks)
     return (mixed, jnp.stack([keys_full, values_full]))

time: 79.4 us -> 80.3 us (1.011)
    slice x0 -> x16, local copies, waits for them, and re-layouts: none -> 3.62 us  [per_column(): out = jnp.where(col == h, s[:, h:h + 1], out)]
    reshape x17 -> x0, local copies, waits for them, and re-layouts: 1.71 us -> none  [the longest x7 0.7 us: merge_softmax(): jnp.repeat(sa, HD, axis=1)]
    broadcast_in_dim x17 -> x0, local copies, waits for them, and re-layouts: 1.35 us -> none  [the longest x7 0.56 us: merge_softmax(): jnp.repeat(sb, HD, axis=1)]
  transfers between devices with their start and end apart: 23 -> 23, of which waited for: 10 -> 9; matrix products, arithmetic and copies ran while one was open for 20% -> 20% of each run, Pallas kernels for 0% -> 0%
where the time goes in v12:
time: 80.3 us; the launch traced here: 80 us
  starting transfers between devices  39.9 us (50%)
  waiting for transfers between devices  16.8 us (21%)
  matrix products  11.3 us (14%)
  other arithmetic  5.84 us (7%)
  local copies, waits for them, and re-layouts  5.18 us (6%)
  between operations  0.93 us (1%)
    ppermute x23, starting transfers between devices, exchange(): return lax.ppermute(x, axis, [(i, i ^ mask) for i in range(size)])  39.9 us
    ppermute x23, waiting for transfers between devices, exchange(): return lax.ppermute(x, axis, [(i, i ^ mask) for i in range(size)])  16.8 us
    slice x16, local copies, waits for them, and re-layouts, per_column(): out = jnp.where(col == h, s[:, h:h + 1], out)  3.62 us
    dot_general x3, matrix products, project(): jnp.dot(scaled, query_key_value_weight[:, j, :], preferred_element_type=f32)  3.6 us
    dot_general x1, matrix products, shards(): jnp.einsum('rnc,rpc->rnp', q_block, cached_key_rows, preferred_element_ty...  3.17 us
    dot_general x1, matrix products, shards(): jnp.einsum('rnp,rpc->rnc', expo.astype(bf16), cached_value_rows, preferre...  2.68 us
  transfers between devices with their start and end apart: 23, of which 9 were waited for; matrix products, arithmetic and copies ran while one was open for 20% of the time, Pallas kernels for 0%

profile of v12, /device:TPU:1, one launch (start us, length us, event | category | flops | bytes accessed | tf_op | source)
XLA Modules:
  0.0 80.0 jit_solution(15240801418607192778)
XLA Ops:
  0.6 0.9 %fusion.113 = f32[16]{0:T(128)S(1)} fusion(bf16[16,224]{1,0:T(8,128)(2,1)} %param.11), kind=kLoop, calls=%fused_computation.137 | loop fusion | flops 10736 | bytes 7232 | tf_op jit(solution)/shard_map/reduce_sum | solution.py:110
  1.6 1.0 %fusion.148 = f32[16,128]{1,0:T(8,128)S(1)} fusion(bf16[224,128]{1,0:T(8,128)(2,1)} %param.14, bf16[16,224]{1,0:T(8,128)(2,1)} %param.11, f32[224]{0:T(256)} %param.12), kind=kOutput, calls=%fused_computation.272 | convolution fusion | flops 928256 | bytes 73600 | tf_op jit(solution)/shard_map/dot_general | solution.py:109
  2.6 1.2 %fusion.6 = f32[16,896]{1,0:T(8,128)S(1)} fusion(bf16[224,3,896]{2,0,1:T(8,128)(2,1)} %param.13, bf16[16,224]{1,0:T(8,128)(2,1)} %param.11, f32[224]{0:T(256)} %param.12), kind=kOutput, calls=%fused_computation.9 | convolution fusion | flops 6433280 | bytes 467968 | tf_op jit(solution)/shard_map/dot_general | solution.py:107
  3.9 6.9 %collective-permute-start = (f32[16,1152]{1,0:T(8,128)S(1)}, f32[16,1152]{1,0:T(8,128)S(1)}, u32[]{:S(2)}, u32[]{:S(2)}) collective-permute-start(f32[16,1152]{1,0:T(8,128)S(1)} %concatenate.15), channel_id=1, source_target_pairs={{0,48},{8,56},{16,32},{24,40},{32,16},{40,24},{48,0},{56,8},{64,11... | collective-permute-start | bytes 221192 | tf_op jit(solution)/shard_map/ppermute | solution.py:28
  10.7 1.2 %fusion.2 = f32[16,896]{1,0:T(8,128)S(1)} fusion(bf16[224,3,896]{2,0,1:T(8,128)(2,1)} %param.13, bf16[16,224]{1,0:T(8,128)(2,1)} %param.11, f32[224]{0:T(256)} %param.12), kind=kOutput, calls=%fused_computation.5 | convolution fusion | flops 6433280 | bytes 467968 | tf_op jit(solution)/shard_map/dot_general | solution.py:107
  11.9 1.2 %fusion.4 = f32[16,896]{1,0:T(8,128)S(1)} fusion(bf16[224,3,896]{2,0,1:T(8,128)(2,1)} %param.13, bf16[16,224]{1,0:T(8,128)(2,1)} %param.11, f32[224]{0:T(256)} %param.12), kind=kOutput, calls=%fused_computation.7 | convolution fusion | flops 6433280 | bytes 467968 | tf_op jit(solution)/shard_map/dot_general | solution.py:107
  13.3 0.7 iota_add_fusion
  14.0 0.7 broadcast_compare_fusion.1
  14.8 0.7 fusion.109
  15.8 2.0 %collective-permute-start.3 = (f32[16,1152]{1,0:T(8,128)S(1)}, f32[16,1152]{1,0:T(8,128)S(1)}, u32[]{:S(2)}, u32[]{:S(2)}) collective-permute-start(f32[16,1152]{1,0:T(8,128)S(1)} %add.141), channel_id=1, source_target_pairs={{0,24},{8,16},{16,8},{24,0},{32,56},{40,48},{48,40},{56,32},{64,88... | collective-permute-start | bytes 221192 | tf_op jit(solution)/shard_map/ppermute | solution.py:28
  17.8 1.6 %collective-permute-start.1 = (f32[16,1152]{1,0:T(8,128)S(1)}, f32[16,1152]{1,0:T(8,128)S(1)}, u32[]{:S(2)}, u32[]{:S(2)}) collective-permute-start(f32[16,1152]{1,0:T(8,128)S(1)} %add.141), channel_id=1, source_target_pairs={{0,8},{8,0},{16,24},{24,16},{32,40},{40,32},{48,56},{56,48},{64,72... | collective-permute-start | bytes 221192 | tf_op jit(solution)/shard_map/ppermute | solution.py:28
  19.4 1.6 %collective-permute-done.3 = f32[16,1152]{1,0:T(8,128)S(1)} collective-permute-done((f32[16,1152]{1,0:T(8,128)S(1)}, f32[16,1152]{1,0:T(8,128)S(1)}, u32[]{:S(2)}, u32[]{:S(2)}) %collective-permute-start.3) | collective-permute-done | bytes 73760 | tf_op jit(solution)/shard_map/ppermute | solution.py:28
  21.0 2.5 %collective-permute-done.2 = f32[16,1152]{1,0:T(8,128)S(1)} collective-permute-done((f32[16,1152]{1,0:T(8,128)S(1)}, f32[16,1152]{1,0:T(8,128)S(1)}, u32[]{:S(2)}, u32[]{:S(2)}) %collective-permute-start.2) | collective-permute-done | bytes 73760 | tf_op jit(solution)/shard_map/ppermute | solution.py:28
  23.6 2.8 %collective-permute-start.6 = (f32[16,1152]{1,0:T(8,128)S(1)}, f32[16,1152]{1,0:T(8,128)S(1)}, u32[]{:S(2)}, u32[]{:S(2)}) collective-permute-start(f32[16,1152]{1,0:T(8,128)S(1)} %add_add_fusion.1), channel_id=1, source_target_pairs={{0,128},{8,136},{16,144},{24,152},{32,160},{40,168},{48,176},{56,1... | collective-permute-start | bytes 221192 | tf_op jit(solution)/shard_map/ppermute | solution.py:28
  26.4 0.9 %collective-permute-start.5 = (f32[16,1152]{1,0:T(8,128)S(1)}, f32[16,1152]{1,0:T(8,128)S(1)}, u32[]{:S(2)}, u32[]{:S(2)}) collective-permute-start(f32[16,1152]{1,0:T(8,128)S(1)} %add_add_fusion.1), channel_id=1, source_target_pairs={{0,192},{8,200},{16,208},{24,216},{32,224},{40,232},{48,240},{56,2... | collective-permute-start | bytes 221192 | tf_op jit(solution)/shard_map/ppermute | solution.py:28
  27.3 1.8 %collective-permute-start.15 = (f32[16,1792]{1,0:T(8,128)S(1)}, f32[16,1792]{1,0:T(8,128)S(1)}, u32[]{:S(2)}, u32[]{:S(2)}) collective-permute-start(f32[16,1792]{1,0:T(8,128)S(1)} %fusion.161), channel_id=1, source_target_pairs={{0,8},{8,0},{16,24},{24,16},{32,40},{40,32},{48,56},{56,48},{64,72... | collective-permute-start | bytes 344072 | tf_op jit(solution)/shard_map/ppermute | solution.py:28
  29.1 2.1 %collective-permute-done.5 = f32[16,1152]{1,0:T(8,128)S(1)} collective-permute-done((f32[16,1152]{1,0:T(8,128)S(1)}, f32[16,1152]{1,0:T(8,128)S(1)}, u32[]{:S(2)}, u32[]{:S(2)}) %collective-permute-start.5) | collective-permute-done | bytes 73760 | tf_op jit(solution)/shard_map/ppermute | solution.py:28
  31.2 0.1 fusion.135
  31.3 0.2 fusion.97
  31.6 3.2 %fusion.166 = (f32[4,16]{1,0:T(4,128)S(1)}, f32[4,16,512]{2,1,0:T(8,128)S(1)}) fusion(pred[4,16,512]{2,1,0:T(8,128)(4,1)S(1)} %reshape.176, bf16[4,512,896]{2,1,0:T(8,128)(2,1)} %param.17, bf16[4,16,896]{2,1,0:T(8,128)(2,1)S(1)} %broadcast_in_dim.579, pred[16,896]{1,0:T(8,128)(4,1)S(1)} %broadcast_in_dim.573), kind=kOutput, calls=%fused_computation.289 | convolution fusion | flops 58875840 | bytes 3963136 | tf_op jit(solution)/shard_map/rnc,rpc->rnp/dot_general | solution.py:134
  34.9 0.2 fusion.13
  35.1 0.1 copy.77
  35.3 0.1 copy.75
  35.4 2.7 %fusion.66 = f32[4,16,896]{2,1,0:T(8,128)S(1)} fusion(bf16[4,512,896]{2,1,0:T(8,128)(2,1)} %param.18, f32[4,16,512]{2,1,0:T(8,128)S(1)} %get-tuple-element.100, f32[4,16]{1,0:T(4,128)S(1)} %get-tuple-element.99, u8[16,512]{1,0:T(8,128)(4,1)S(1)} %fusion.104), kind=kOutput, calls=%fused_computation.80 | convolution fusion | flops 58949632 | bytes 4038912 | tf_op jit(solution)/shard_map/rnp,rpc->rnc/dot_general | solution.py:150
  38.3 4.1 %collective-permute-start.7 = (f32[16,1024]{1,0:T(8,128)S(1)}, f32[16,1024]{1,0:T(8,128)S(1)}, u32[]{:S(2)}, u32[]{:S(2)}) collective-permute-start(f32[16,1024]{1,0:T(8,128)S(1)} %maximum_maximum_fusion), channel_id=1, source_target_pairs={{0,48},{8,56},{16,32},{24,40},{32,16},{40,24},{48,0},{56,8},{64,11... | collective-permute-start | bytes 196616 | tf_op jit(solution)/shard_map/ppermute | solution.py:28
  42.4 2.7 %collective-permute-start.16 = (f32[16,1792]{1,0:T(8,128)S(1)}, f32[16,1792]{1,0:T(8,128)S(1)}, u32[]{:S(2)}, u32[]{:S(2)}) collective-permute-start(f32[16,1792]{1,0:T(8,128)S(1)} %add.162), channel_id=1, source_target_pairs={{0,16},{8,24},{16,0},{24,8},{32,48},{40,56},{48,32},{56,40},{64,80... | collective-permute-start | bytes 344072 | tf_op jit(solution)/shard_map/ppermute | solution.py:28
  45.2 0.3 slice_reduce_fusion.63
  45.7 1.6 %collective-permute-start.10 = (f32[16,1024]{1,0:T(8,128)S(1)}, f32[16,1024]{1,0:T(8,128)S(1)}, u32[]{:S(2)}, u32[]{:S(2)}) collective-permute-start(f32[16,1024]{1,0:T(8,128)S(1)} %maximum_maximum_fusion.1), channel_id=1, source_target_pairs={{0,24},{8,16},{16,8},{24,0},{32,56},{40,48},{48,40},{56,32},{64,88... | collective-permute-start | bytes 196616 | tf_op jit(solution)/shard_map/ppermute | solution.py:28
  47.3 0.6 collective-permute-start.9
  47.9 1.3 %collective-permute-start.8 = (f32[16,1024]{1,0:T(8,128)S(1)}, f32[16,1024]{1,0:T(8,128)S(1)}, u32[]{:S(2)}, u32[]{:S(2)}) collective-permute-start(f32[16,1024]{1,0:T(8,128)S(1)} %maximum_maximum_fusion.1), channel_id=1, source_target_pairs={{0,8},{8,0},{16,24},{24,16},{32,40},{40,32},{48,56},{56,48},{64,72... | collective-permute-start | bytes 196616 | tf_op jit(solution)/shard_map/ppermute | solution.py:28
  49.5 1.2 %collective-permute-done.10 = f32[16,1024]{1,0:T(8,128)S(1)} collective-permute-done((f32[16,1024]{1,0:T(8,128)S(1)}, f32[16,1024]{1,0:T(8,128)S(1)}, u32[]{:S(2)}, u32[]{:S(2)}) %collective-permute-start.10) | collective-permute-done | bytes 65568 | tf_op jit(solution)/shard_map/ppermute | solution.py:28
  50.7 4.0 %collective-permute-done.9 = f32[16,1024]{1,0:T(8,128)S(1)} collective-permute-done((f32[16,1024]{1,0:T(8,128)S(1)}, f32[16,1024]{1,0:T(8,128)S(1)}, u32[]{:S(2)}, u32[]{:S(2)}) %collective-permute-start.9) | collective-permute-done | bytes 65568 | tf_op jit(solution)/shard_map/ppermute | solution.py:28
  54.8 0.2 slice_reduce_fusion.59
  55.0 0.2 slice_reduce_fusion.55
  55.2 0.2 slice_reduce_fusion.51
  55.4 0.2 slice_reduce_fusion.47
  55.7 0.2 slice_reduce_fusion.43
  55.9 0.2 slice_reduce_fusion.39
  56.1 0.2 fusion.77
  56.3 1.2 %collective-permute-start.18 = (f32[16,1792]{1,0:T(8,128)S(1)}, f32[16,1792]{1,0:T(8,128)S(1)}, u32[]{:S(2)}, u32[]{:S(2)}) collective-permute-start(f32[16,1792]{1,0:T(8,128)S(1)} %add.164), channel_id=1, source_target_pairs={{0,192},{8,200},{16,208},{24,216},{32,224},{40,232},{48,240},{56,2... | collective-permute-start | bytes 344072 | tf_op jit(solution)/shard_map/ppermute | solution.py:28
  57.6 2.4 %collective-permute-start.13 = (f32[16,1024]{1,0:T(8,128)S(1)}, f32[16,1024]{1,0:T(8,128)S(1)}, u32[]{:S(2)}, u32[]{:S(2)}) collective-permute-start(f32[16,1024]{1,0:T(8,128)S(1)} %maximum_maximum_fusion.2), channel_id=1, source_target_pairs={{0,128},{8,136},{16,144},{24,152},{32,160},{40,168},{48,176},{56,1... | collective-permute-start | bytes 196616 | tf_op jit(solution)/shard_map/ppermute | solution.py:28
  60.0 2.1 %collective-permute-start.12 = (f32[16,1024]{1,0:T(8,128)S(1)}, f32[16,1024]{1,0:T(8,128)S(1)}, u32[]{:S(2)}, u32[]{:S(2)}) collective-permute-start(f32[16,1024]{1,0:T(8,128)S(1)} %maximum_maximum_fusion.2), channel_id=1, source_target_pairs={{0,192},{8,200},{16,208},{24,216},{32,224},{40,232},{48,240},{56,2... | collective-permute-start | bytes 196616 | tf_op jit(solution)/shard_map/ppermute | solution.py:28
  62.4 0.2 fusion.165
  62.6 0.2 convolution_bitcast_fusion
  63.0 0.1 copy.74
  63.2 1.5 %collective-permute-done.12 = f32[16,1024]{1,0:T(8,128)S(1)} collective-permute-done((f32[16,1024]{1,0:T(8,128)S(1)}, f32[16,1024]{1,0:T(8,128)S(1)}, u32[]{:S(2)}, u32[]{:S(2)}) %collective-permute-start.12) | collective-permute-done | bytes 65568 | tf_op jit(solution)/shard_map/ppermute | solution.py:28
  64.7 0.8 collective-permute-done.11
  65.6 0.2 slice_reduce_fusion.3
  65.8 0.2 slice_reduce_fusion.35
  66.0 0.2 slice_reduce_fusion.7
  66.2 0.2 slice_reduce_fusion.31
  66.5 0.2 slice_reduce_fusion.27
  66.7 0.2 slice_reduce_fusion.23
  66.9 0.2 slice_reduce_fusion.19
  67.1 0.2 slice_reduce_fusion.15
  67.3 0.2 slice_reduce_fusion.11
  67.6 0.3 fusion.110
  67.9 4.0 %collective-permute-start.19 = (f32[16,112]{1,0:T(8,128)S(1)}, f32[16,112]{1,0:T(8,128)S(1)}, u32[]{:S(2)}, u32[]{:S(2)}) collective-permute-start(f32[16,112]{1,0:T(8,128)S(1)} %fusion.110), channel_id=1, source_target_pairs={{0,1},{1,0},{2,3},{3,2},{4,5},{5,4},{6,7},{7,6},{8,9},{9,8},{10,11... | collective-permute-start | bytes 21512 | tf_op jit(solution)/shard_map/ppermute | solution.py:28
  71.9 0.8 %collective-permute-done.19 = f32[16,112]{1,0:T(8,128)S(1)} collective-permute-done((f32[16,112]{1,0:T(8,128)S(1)}, f32[16,112]{1,0:T(8,128)S(1)}, u32[]{:S(2)}, u32[]{:S(2)}) %collective-permute-start.19) | collective-permute-done | bytes 7200 | tf_op jit(solution)/shard_map/ppermute | solution.py:28
  72.7 2.9 %collective-permute-start.22 = (f32[16,112]{1,0:T(8,128)S(1)}, f32[16,112]{1,0:T(8,128)S(1)}, u32[]{:S(2)}, u32[]{:S(2)}) collective-permute-start(f32[16,112]{1,0:T(8,128)S(1)} %add.171), channel_id=1, source_target_pairs={{0,4},{1,5},{2,6},{3,7},{4,0},{5,1},{6,2},{7,3},{8,12},{9,13},{10,... | collective-permute-start | bytes 21512 | tf_op jit(solution)/shard_map/ppermute | solution.py:28
  75.6 0.8 collective-permute-start.21
  76.4 0.7 pad_maximum_fusion.1
  77.1 2.3 %collective-permute-done.21 = f32[16,112]{1,0:T(8,128)S(1)} collective-permute-done((f32[16,112]{1,0:T(8,128)S(1)}, f32[16,112]{1,0:T(8,128)S(1)}, u32[]{:S(2)}, u32[]{:S(2)}) %collective-permute-start.21) | collective-permute-done | bytes 7200 | tf_op jit(solution)/shard_map/ppermute | solution.py:28
  79.3 0.6 add_add_fusion.2
  (74 shorter events, 2.6 us)
Async XLA Ops:
  0.6 30.6 %copy-start = (bf16[128,896]{1,0:T(8,128)(2,1)S(1)}, bf16[128,896]{1,0:T(8,128)(2,1)}, u32[]{:S(2)}) copy-start(bf16[128,896]{1,0:T(8,128)(2,1)} %param.15) | copy-start | bytes 688132
  3.9 11.9 %collective-permute-start = (f32[16,1152]{1,0:T(8,128)S(1)}, f32[16,1152]{1,0:T(8,128)S(1)}, u32[]{:S(2)}, u32[]{:S(2)}) collective-permute-start(f32[16,1152]{1,0:T(8,128)S(1)} %concatenate.15), channel_id=1, source_target_pairs={{0,48},{8,56},{16,32},{24,40},{32,16},{40,24},{48,0},{56,8},{64,11... | collective-permute-start | bytes 221192 | tf_op jit(solution)/shard_map/ppermute | solution.py:28
  13.2 14.1 %collective-permute-start.14 = (f32[16,1792]{1,0:T(8,128)S(1)}, f32[16,1792]{1,0:T(8,128)S(1)}, u32[]{:S(2)}, u32[]{:S(2)}) collective-permute-start(f32[16,1792]{1,0:T(8,128)S(1)} %pad_maximum_fusion), channel_id=1, source_target_pairs={{0,48},{8,56},{16,32},{24,40},{32,16},{40,24},{48,0},{56,8},{64,11... | collective-permute-start | bytes 344072 | tf_op jit(solution)/shard_map/ppermute | solution.py:28
  15.8 5.2 %collective-permute-start.3 = (f32[16,1152]{1,0:T(8,128)S(1)}, f32[16,1152]{1,0:T(8,128)S(1)}, u32[]{:S(2)}, u32[]{:S(2)}) collective-permute-start(f32[16,1152]{1,0:T(8,128)S(1)} %add.141), channel_id=1, source_target_pairs={{0,24},{8,16},{16,8},{24,0},{32,56},{40,48},{48,40},{56,32},{64,88... | collective-permute-start | bytes 221192 | tf_op jit(solution)/shard_map/ppermute | solution.py:28
  17.7 5.8 %collective-permute-start.2 = (f32[16,1152]{1,0:T(8,128)S(1)}, f32[16,1152]{1,0:T(8,128)S(1)}, u32[]{:S(2)}, u32[]{:S(2)}) collective-permute-start(f32[16,1152]{1,0:T(8,128)S(1)} %add.141), channel_id=1, source_target_pairs={{0,16},{8,24},{16,0},{24,8},{32,48},{40,56},{48,32},{56,40},{64,80... | collective-permute-start | bytes 221192 | tf_op jit(solution)/shard_map/ppermute | solution.py:28
  17.8 5.8 %collective-permute-start.1 = (f32[16,1152]{1,0:T(8,128)S(1)}, f32[16,1152]{1,0:T(8,128)S(1)}, u32[]{:S(2)}, u32[]{:S(2)}) collective-permute-start(f32[16,1152]{1,0:T(8,128)S(1)} %add.141), channel_id=1, source_target_pairs={{0,8},{8,0},{16,24},{24,16},{32,40},{40,32},{48,56},{56,48},{64,72... | collective-permute-start | bytes 221192 | tf_op jit(solution)/shard_map/ppermute | solution.py:28
  23.6 5.5 %collective-permute-start.6 = (f32[16,1152]{1,0:T(8,128)S(1)}, f32[16,1152]{1,0:T(8,128)S(1)}, u32[]{:S(2)}, u32[]{:S(2)}) collective-permute-start(f32[16,1152]{1,0:T(8,128)S(1)} %add_add_fusion.1), channel_id=1, source_target_pairs={{0,128},{8,136},{16,144},{24,152},{32,160},{40,168},{48,176},{56,1... | collective-permute-start | bytes 221192 | tf_op jit(solution)/shard_map/ppermute | solution.py:28
  26.4 4.7 %collective-permute-start.5 = (f32[16,1152]{1,0:T(8,128)S(1)}, f32[16,1152]{1,0:T(8,128)S(1)}, u32[]{:S(2)}, u32[]{:S(2)}) collective-permute-start(f32[16,1152]{1,0:T(8,128)S(1)} %add_add_fusion.1), channel_id=1, source_target_pairs={{0,192},{8,200},{16,208},{24,216},{32,224},{40,232},{48,240},{56,2... | collective-permute-start | bytes 221192 | tf_op jit(solution)/shard_map/ppermute | solution.py:28
  27.3 3.9 %collective-permute-start.4 = (f32[16,1152]{1,0:T(8,128)S(1)}, f32[16,1152]{1,0:T(8,128)S(1)}, u32[]{:S(2)}, u32[]{:S(2)}) collective-permute-start(f32[16,1152]{1,0:T(8,128)S(1)} %add_add_fusion.1), channel_id=1, source_target_pairs={{0,64},{8,72},{16,80},{24,88},{32,96},{40,104},{48,112},{56,120},{... | collective-permute-start | bytes 221192 | tf_op jit(solution)/shard_map/ppermute | solution.py:28
  27.3 15.1 %collective-permute-start.15 = (f32[16,1792]{1,0:T(8,128)S(1)}, f32[16,1792]{1,0:T(8,128)S(1)}, u32[]{:S(2)}, u32[]{:S(2)}) collective-permute-start(f32[16,1792]{1,0:T(8,128)S(1)} %fusion.161), channel_id=1, source_target_pairs={{0,8},{8,0},{16,24},{24,16},{32,40},{40,32},{48,56},{56,48},{64,72... | collective-permute-start | bytes 344072 | tf_op jit(solution)/shard_map/ppermute | solution.py:28
  38.1 29.5 %copy-start.1 = (bf16[896,112]{0,1:T(8,128)(2,1)S(1)}, bf16[896,112]{0,1:T(8,128)(2,1)}, u32[]{:S(2)}) copy-start(bf16[896,112]{0,1:T(8,128)(2,1)} %param.16) | copy-start | bytes 602116
  38.3 6.8 %collective-permute-start.7 = (f32[16,1024]{1,0:T(8,128)S(1)}, f32[16,1024]{1,0:T(8,128)S(1)}, u32[]{:S(2)}, u32[]{:S(2)}) collective-permute-start(f32[16,1024]{1,0:T(8,128)S(1)} %maximum_maximum_fusion), channel_id=1, source_target_pairs={{0,48},{8,56},{16,32},{24,40},{32,16},{40,24},{48,0},{56,8},{64,11... | collective-permute-start | bytes 196616 | tf_op jit(solution)/shard_map/ppermute | solution.py:28
  42.4 6.9 %collective-permute-start.16 = (f32[16,1792]{1,0:T(8,128)S(1)}, f32[16,1792]{1,0:T(8,128)S(1)}, u32[]{:S(2)}, u32[]{:S(2)}) collective-permute-start(f32[16,1792]{1,0:T(8,128)S(1)} %add.162), channel_id=1, source_target_pairs={{0,16},{8,24},{16,0},{24,8},{32,48},{40,56},{48,32},{56,40},{64,80... | collective-permute-start | bytes 344072 | tf_op jit(solution)/shard_map/ppermute | solution.py:28
  45.7 5.0 %collective-permute-start.10 = (f32[16,1024]{1,0:T(8,128)S(1)}, f32[16,1024]{1,0:T(8,128)S(1)}, u32[]{:S(2)}, u32[]{:S(2)}) collective-permute-start(f32[16,1024]{1,0:T(8,128)S(1)} %maximum_maximum_fusion.1), channel_id=1, source_target_pairs={{0,24},{8,16},{16,8},{24,0},{32,56},{40,48},{48,40},{56,32},{64,88... | collective-permute-start | bytes 196616 | tf_op jit(solution)/shard_map/ppermute | solution.py:28
  47.3 7.3 %collective-permute-start.9 = (f32[16,1024]{1,0:T(8,128)S(1)}, f32[16,1024]{1,0:T(8,128)S(1)}, u32[]{:S(2)}, u32[]{:S(2)}) collective-permute-start(f32[16,1024]{1,0:T(8,128)S(1)} %maximum_maximum_fusion.1), channel_id=1, source_target_pairs={{0,16},{8,24},{16,0},{24,8},{32,48},{40,56},{48,32},{56,40},{64,80... | collective-permute-start | bytes 196616 | tf_op jit(solution)/shard_map/ppermute | solution.py:28
  47.9 6.7 %collective-permute-start.8 = (f32[16,1024]{1,0:T(8,128)S(1)}, f32[16,1024]{1,0:T(8,128)S(1)}, u32[]{:S(2)}, u32[]{:S(2)}) collective-permute-start(f32[16,1024]{1,0:T(8,128)S(1)} %maximum_maximum_fusion.1), channel_id=1, source_target_pairs={{0,8},{8,0},{16,24},{24,16},{32,40},{40,32},{48,56},{56,48},{64,72... | collective-permute-start | bytes 196616 | tf_op jit(solution)/shard_map/ppermute | solution.py:28
  49.4 6.9 %collective-permute-start.17 = (f32[16,1792]{1,0:T(8,128)S(1)}, f32[16,1792]{1,0:T(8,128)S(1)}, u32[]{:S(2)}, u32[]{:S(2)}) collective-permute-start(f32[16,1792]{1,0:T(8,128)S(1)} %add.163), channel_id=1, source_target_pairs={{0,64},{8,72},{16,80},{24,88},{32,96},{40,104},{48,112},{56,120},{... | collective-permute-start | bytes 344072 | tf_op jit(solution)/shard_map/ppermute | solution.py:28
  56.3 5.8 %collective-permute-start.18 = (f32[16,1792]{1,0:T(8,128)S(1)}, f32[16,1792]{1,0:T(8,128)S(1)}, u32[]{:S(2)}, u32[]{:S(2)}) collective-permute-start(f32[16,1792]{1,0:T(8,128)S(1)} %add.164), channel_id=1, source_target_pairs={{0,192},{8,200},{16,208},{24,216},{32,224},{40,232},{48,240},{56,2... | collective-permute-start | bytes 344072 | tf_op jit(solution)/shard_map/ppermute | solution.py:28
  57.6 5.6 %collective-permute-start.13 = (f32[16,1024]{1,0:T(8,128)S(1)}, f32[16,1024]{1,0:T(8,128)S(1)}, u32[]{:S(2)}, u32[]{:S(2)}) collective-permute-start(f32[16,1024]{1,0:T(8,128)S(1)} %maximum_maximum_fusion.2), channel_id=1, source_target_pairs={{0,128},{8,136},{16,144},{24,152},{32,160},{40,168},{48,176},{56,1... | collective-permute-start | bytes 196616 | tf_op jit(solution)/shard_map/ppermute | solution.py:28
  60.0 4.7 %collective-permute-start.12 = (f32[16,1024]{1,0:T(8,128)S(1)}, f32[16,1024]{1,0:T(8,128)S(1)}, u32[]{:S(2)}, u32[]{:S(2)}) collective-permute-start(f32[16,1024]{1,0:T(8,128)S(1)} %maximum_maximum_fusion.2), channel_id=1, source_target_pairs={{0,192},{8,200},{16,208},{24,216},{32,224},{40,232},{48,240},{56,2... | collective-permute-start | bytes 196616 | tf_op jit(solution)/shard_map/ppermute | solution.py:28
  62.1 3.4 %collective-permute-start.11 = (f32[16,1024]{1,0:T(8,128)S(1)}, f32[16,1024]{1,0:T(8,128)S(1)}, u32[]{:S(2)}, u32[]{:S(2)}) collective-permute-start(f32[16,1024]{1,0:T(8,128)S(1)} %maximum_maximum_fusion.2), channel_id=1, source_target_pairs={{0,64},{8,72},{16,80},{24,88},{32,96},{40,104},{48,112},{56,120},{... | collective-permute-start | bytes 196616 | tf_op jit(solution)/shard_map/ppermute | solution.py:28
  67.9 4.8 %collective-permute-start.19 = (f32[16,112]{1,0:T(8,128)S(1)}, f32[16,112]{1,0:T(8,128)S(1)}, u32[]{:S(2)}, u32[]{:S(2)}) collective-permute-start(f32[16,112]{1,0:T(8,128)S(1)} %fusion.110), channel_id=1, source_target_pairs={{0,1},{1,0},{2,3},{3,2},{4,5},{5,4},{6,7},{7,6},{8,9},{9,8},{10,11... | collective-permute-start | bytes 21512 | tf_op jit(solution)/shard_map/ppermute | solution.py:28
  72.7 4.4 %collective-permute-start.22 = (f32[16,112]{1,0:T(8,128)S(1)}, f32[16,112]{1,0:T(8,128)S(1)}, u32[]{:S(2)}, u32[]{:S(2)}) collective-permute-start(f32[16,112]{1,0:T(8,128)S(1)} %add.171), channel_id=1, source_target_pairs={{0,4},{1,5},{2,6},{3,7},{4,0},{5,1},{6,2},{7,3},{8,12},{9,13},{10,... | collective-permute-start | bytes 21512 | tf_op jit(solution)/shard_map/ppermute | solution.py:28
  75.6 3.7 %collective-permute-start.21 = (f32[16,112]{1,0:T(8,128)S(1)}, f32[16,112]{1,0:T(8,128)S(1)}, u32[]{:S(2)}, u32[]{:S(2)}) collective-permute-start(f32[16,112]{1,0:T(8,128)S(1)} %add.171), channel_id=1, source_target_pairs={{0,6},{1,7},{2,4},{3,5},{4,2},{5,3},{6,0},{7,1},{8,14},{9,15},{10,... | collective-permute-start | bytes 21512 | tf_op jit(solution)/shard_map/ppermute | solution.py:28
  76.4 2.9 %collective-permute-start.20 = (f32[16,112]{1,0:T(8,128)S(1)}, f32[16,112]{1,0:T(8,128)S(1)}, u32[]{:S(2)}, u32[]{:S(2)}) collective-permute-start(f32[16,112]{1,0:T(8,128)S(1)} %add.171), channel_id=1, source_target_pairs={{0,2},{1,3},{2,0},{3,1},{4,6},{5,7},{6,4},{7,5},{8,10},{9,11},{10,... | collective-permute-start | bytes 21512 | tf_op jit(solution)/shard_map/ppermute | solution.py:28

commit v13 on v11

--- a/solution.py
+++ b/solution.py
@@ -105,7 +105,7 @@
     )
     summed = butterfly_sum(packed, "seq", seq_masks)
     kv_summed = butterfly_sum(
-        jnp.concatenate([project(1), project(2)], axis=1), "seq", [(m,) for r in seq_masks for m in r]
+        jnp.concatenate([project(1), project(2)], axis=1), "seq", [(m,) for r in seq_masks[:-1] for m in r] + seq_masks[-1:]
     )
     low = summed[:, local : local + rank]
     total_sq = summed[:, local + rank]

time: 79.4 us -> 78.9 us (level)
  waiting for transfers between devices: 16.3 us -> 15.2 us
    ppermute x23 -> x24, waiting for transfers between devices: 16.3 us -> 15.2 us  [exchange(): return lax.ppermute(x, axis, [(i, i ^ mask) for i in range(size)])]
    ppermute x23 -> x24, starting transfers between devices: 40.2 us -> 40.9 us  [exchange(): return lax.ppermute(x, axis, [(i, i ^ mask) for i in range(size)])]
  transfers between devices with their start and end apart: 23 -> 24, of which waited for: 10 -> 8; matrix products, arithmetic and copies ran while one was open for 20% -> 20% of each run, Pallas kernels for 0% -> 0%
where the time goes in v13:
time: 78.9 us; the launch traced here: 78.6 us
  starting transfers between devices  40.9 us (52%)
  waiting for transfers between devices  15.2 us (19%)
  matrix products  11.2 us (14%)
  other arithmetic  5.65 us (7%)
  local copies, waits for them, and re-layouts  4.63 us (6%)
  between operations  1.03 us (1%)
    ppermute x24, starting transfers between devices, exchange(): return lax.ppermute(x, axis, [(i, i ^ mask) for i in range(size)])  40.9 us
    ppermute x24, waiting for transfers between devices, exchange(): return lax.ppermute(x, axis, [(i, i ^ mask) for i in range(size)])  15.2 us
    dot_general x3, matrix products, project(): jnp.dot(scaled, query_key_value_weight[:, j, :], preferred_element_type=f32)  3.6 us
    dot_general x1, matrix products, shards(): jnp.einsum('rnc,rpc->rnp', q_block, cached_key_rows, preferred_element_ty...  3.17 us
    dot_general x1, matrix products, shards(): jnp.einsum('rnp,rpc->rnc', expo.astype(bf16), cached_value_rows, preferre...  2.68 us
  transfers between devices with their start and end apart: 24, of which 8 were waited for; matrix products, arithmetic and copies ran while one was open for 20% of the time, Pallas kernels for 0%

profile of v13, /device:TPU:1, one launch (start us, length us, event | category | flops | bytes accessed | tf_op | source)
XLA Modules:
  0.0 78.6 jit_solution(1389374719069087196)
XLA Ops:
  0.6 0.9 %fusion.51 = f32[16]{0:T(128)S(1)} fusion(bf16[16,224]{1,0:T(8,128)(2,1)} %param.11), kind=kLoop, calls=%fused_computation.80 | loop fusion | flops 10736 | bytes 7232 | tf_op jit(solution)/shard_map/reduce_sum | solution.py:102
  1.6 1.0 %fusion.86 = f32[16,128]{1,0:T(8,128)S(1)} fusion(bf16[224,128]{1,0:T(8,128)(2,1)} %param.14, bf16[16,224]{1,0:T(8,128)(2,1)} %param.11, f32[224]{0:T(256)} %param.12), kind=kOutput, calls=%fused_computation.148 | convolution fusion | flops 928256 | bytes 73600 | tf_op jit(solution)/shard_map/dot_general | solution.py:101
  2.6 1.2 %fusion.6 = f32[16,896]{1,0:T(8,128)S(1)} fusion(bf16[224,3,896]{2,0,1:T(8,128)(2,1)} %param.13, bf16[16,224]{1,0:T(8,128)(2,1)} %param.11, f32[224]{0:T(256)} %param.12), kind=kOutput, calls=%fused_computation.9 | convolution fusion | flops 6433280 | bytes 467968 | tf_op jit(solution)/shard_map/dot_general | solution.py:99
  3.9 6.9 %collective-permute-start = (f32[16,1152]{1,0:T(8,128)S(1)}, f32[16,1152]{1,0:T(8,128)S(1)}, u32[]{:S(2)}, u32[]{:S(2)}) collective-permute-start(f32[16,1152]{1,0:T(8,128)S(1)} %concatenate.15), channel_id=1, source_target_pairs={{0,48},{8,56},{16,32},{24,40},{32,16},{40,24},{48,0},{56,8},{64,11... | collective-permute-start | bytes 221192 | tf_op jit(solution)/shard_map/ppermute | solution.py:28
  10.7 1.2 %fusion.2 = f32[16,896]{1,0:T(8,128)S(1)} fusion(bf16[224,3,896]{2,0,1:T(8,128)(2,1)} %param.13, bf16[16,224]{1,0:T(8,128)(2,1)} %param.11, f32[224]{0:T(256)} %param.12), kind=kOutput, calls=%fused_computation.5 | convolution fusion | flops 6433280 | bytes 467968 | tf_op jit(solution)/shard_map/dot_general | solution.py:99
  11.9 1.2 %fusion.4 = f32[16,896]{1,0:T(8,128)S(1)} fusion(bf16[224,3,896]{2,0,1:T(8,128)(2,1)} %param.13, bf16[16,224]{1,0:T(8,128)(2,1)} %param.11, f32[224]{0:T(256)} %param.12), kind=kOutput, calls=%fused_computation.7 | convolution fusion | flops 6433280 | bytes 467968 | tf_op jit(solution)/shard_map/dot_general | solution.py:99
  13.2 0.1 collective-permute-start.14
  13.3 0.7 iota_add_fusion
  14.0 0.7 broadcast_compare_fusion.1
  14.8 0.7 fusion.47
  15.6 2.0 %collective-permute-start.3 = (f32[16,1152]{1,0:T(8,128)S(1)}, f32[16,1152]{1,0:T(8,128)S(1)}, u32[]{:S(2)}, u32[]{:S(2)}) collective-permute-start(f32[16,1152]{1,0:T(8,128)S(1)} %add.142), channel_id=1, source_target_pairs={{0,24},{8,16},{16,8},{24,0},{32,56},{40,48},{48,40},{56,32},{64,88... | collective-permute-start | bytes 221192 | tf_op jit(solution)/shard_map/ppermute | solution.py:28
  17.6 1.6 %collective-permute-start.1 = (f32[16,1152]{1,0:T(8,128)S(1)}, f32[16,1152]{1,0:T(8,128)S(1)}, u32[]{:S(2)}, u32[]{:S(2)}) collective-permute-start(f32[16,1152]{1,0:T(8,128)S(1)} %add.142), channel_id=1, source_target_pairs={{0,8},{8,0},{16,24},{24,16},{32,40},{40,32},{48,56},{56,48},{64,72... | collective-permute-start | bytes 221192 | tf_op jit(solution)/shard_map/ppermute | solution.py:28
  19.4 1.4 %collective-permute-done.3 = f32[16,1152]{1,0:T(8,128)S(1)} collective-permute-done((f32[16,1152]{1,0:T(8,128)S(1)}, f32[16,1152]{1,0:T(8,128)S(1)}, u32[]{:S(2)}, u32[]{:S(2)}) %collective-permute-start.3) | collective-permute-done | bytes 73760 | tf_op jit(solution)/shard_map/ppermute | solution.py:28
  20.8 2.6 %collective-permute-done.2 = f32[16,1152]{1,0:T(8,128)S(1)} collective-permute-done((f32[16,1152]{1,0:T(8,128)S(1)}, f32[16,1152]{1,0:T(8,128)S(1)}, u32[]{:S(2)}, u32[]{:S(2)}) %collective-permute-start.2) | collective-permute-done | bytes 73760 | tf_op jit(solution)/shard_map/ppermute | solution.py:28
  23.4 2.8 %collective-permute-start.6 = (f32[16,1152]{1,0:T(8,128)S(1)}, f32[16,1152]{1,0:T(8,128)S(1)}, u32[]{:S(2)}, u32[]{:S(2)}) collective-permute-start(f32[16,1152]{1,0:T(8,128)S(1)} %add_add_fusion.2), channel_id=1, source_target_pairs={{0,128},{8,136},{16,144},{24,152},{32,160},{40,168},{48,176},{56,1... | collective-permute-start | bytes 221192 | tf_op jit(solution)/shard_map/ppermute | solution.py:28
  26.2 0.9 %collective-permute-start.5 = (f32[16,1152]{1,0:T(8,128)S(1)}, f32[16,1152]{1,0:T(8,128)S(1)}, u32[]{:S(2)}, u32[]{:S(2)}) collective-permute-start(f32[16,1152]{1,0:T(8,128)S(1)} %add_add_fusion.2), channel_id=1, source_target_pairs={{0,192},{8,200},{16,208},{24,216},{32,224},{40,232},{48,240},{56,2... | collective-permute-start | bytes 221192 | tf_op jit(solution)/shard_map/ppermute | solution.py:28
  27.1 1.6 %collective-permute-start.15 = (f32[16,1792]{1,0:T(8,128)S(1)}, f32[16,1792]{1,0:T(8,128)S(1)}, u32[]{:S(2)}, u32[]{:S(2)}) collective-permute-start(f32[16,1792]{1,0:T(8,128)S(1)} %fusion.95), channel_id=1, source_target_pairs={{0,8},{8,0},{16,24},{24,16},{32,40},{40,32},{48,56},{56,48},{64,72... | collective-permute-start | bytes 344072 | tf_op jit(solution)/shard_map/ppermute | solution.py:28
  28.7 2.2 %collective-permute-done.5 = f32[16,1152]{1,0:T(8,128)S(1)} collective-permute-done((f32[16,1152]{1,0:T(8,128)S(1)}, f32[16,1152]{1,0:T(8,128)S(1)}, u32[]{:S(2)}, u32[]{:S(2)}) %collective-permute-start.5) | collective-permute-done | bytes 73760 | tf_op jit(solution)/shard_map/ppermute | solution.py:28
  30.9 0.1 fusion.73
  31.1 0.2 fusion.35
  31.4 3.2 %fusion.99 = (f32[4,16]{1,0:T(4,128)S(1)}, f32[4,16,512]{2,1,0:T(8,128)S(1)}) fusion(pred[4,16,512]{2,1,0:T(8,128)(4,1)S(1)} %reshape.227, bf16[4,512,896]{2,1,0:T(8,128)(2,1)} %param.17, bf16[4,16,896]{2,1,0:T(8,128)(2,1)S(1)} %broadcast_in_dim.151, pred[16,896]{1,0:T(8,128)(4,1)S(1)} %broadcast_in_dim.145), kind=kOutput, calls=%fused_computation.159 | convolution fusion | flops 58875840 | bytes 3963136 | tf_op jit(solution)/shard_map/rnc,rpc->rnp/dot_general | solution.py:126
  34.7 0.2 fusion.13
  34.9 0.1 copy.60
  35.0 0.1 copy.58
  35.2 2.7 %fusion.15 = f32[4,16,896]{2,1,0:T(8,128)S(1)} fusion(bf16[4,512,896]{2,1,0:T(8,128)(2,1)} %param.18, f32[4,16,512]{2,1,0:T(8,128)S(1)} %get-tuple-element.30, f32[4,16]{1,0:T(4,128)S(1)} %get-tuple-element.29, u8[16,512]{1,0:T(8,128)(4,1)S(1)} %fusion.42), kind=kOutput, calls=%fused_computation.27 | convolution fusion | flops 58949632 | bytes 4038912 | tf_op jit(solution)/shard_map/rnp,rpc->rnc/dot_general | solution.py:142
  38.1 4.1 %collective-permute-start.7 = (f32[16,1024]{1,0:T(8,128)S(1)}, f32[16,1024]{1,0:T(8,128)S(1)}, u32[]{:S(2)}, u32[]{:S(2)}) collective-permute-start(f32[16,1024]{1,0:T(8,128)S(1)} %maximum_maximum_fusion), channel_id=1, source_target_pairs={{0,48},{8,56},{16,32},{24,40},{32,16},{40,24},{48,0},{56,8},{64,11... | collective-permute-start | bytes 196616 | tf_op jit(solution)/shard_map/ppermute | solution.py:28
  42.2 2.7 %collective-permute-start.16 = (f32[16,1792]{1,0:T(8,128)S(1)}, f32[16,1792]{1,0:T(8,128)S(1)}, u32[]{:S(2)}, u32[]{:S(2)}) collective-permute-start(f32[16,1792]{1,0:T(8,128)S(1)} %add.163), channel_id=1, source_target_pairs={{0,16},{8,24},{16,0},{24,8},{32,48},{40,56},{48,32},{56,40},{64,80... | collective-permute-start | bytes 344072 | tf_op jit(solution)/shard_map/ppermute | solution.py:28
  45.1 0.1 reshape.234
  45.3 0.1 reshape.235
  45.5 1.6 %collective-permute-start.10 = (f32[16,1024]{1,0:T(8,128)S(1)}, f32[16,1024]{1,0:T(8,128)S(1)}, u32[]{:S(2)}, u32[]{:S(2)}) collective-permute-start(f32[16,1024]{1,0:T(8,128)S(1)} %maximum_maximum_fusion.1), channel_id=1, source_target_pairs={{0,24},{8,16},{16,8},{24,0},{32,56},{40,48},{48,40},{56,32},{64,88... | collective-permute-start | bytes 196616 | tf_op jit(solution)/shard_map/ppermute | solution.py:28
  47.1 0.6 collective-permute-start.9
  47.8 1.3 %collective-permute-start.8 = (f32[16,1024]{1,0:T(8,128)S(1)}, f32[16,1024]{1,0:T(8,128)S(1)}, u32[]{:S(2)}, u32[]{:S(2)}) collective-permute-start(f32[16,1024]{1,0:T(8,128)S(1)} %maximum_maximum_fusion.1), channel_id=1, source_target_pairs={{0,8},{8,0},{16,24},{24,16},{32,40},{40,32},{48,56},{56,48},{64,72... | collective-permute-start | bytes 196616 | tf_op jit(solution)/shard_map/ppermute | solution.py:28
  49.2 1.5 %collective-permute-start.19 = (f32[16,1792]{1,0:T(8,128)S(1)}, f32[16,1792]{1,0:T(8,128)S(1)}, u32[]{:S(2)}, u32[]{:S(2)}) collective-permute-start(f32[16,1792]{1,0:T(8,128)S(1)} %add.164), channel_id=1, source_target_pairs={{0,128},{8,136},{16,144},{24,152},{32,160},{40,168},{48,176},{56,1... | collective-permute-start | bytes 344072 | tf_op jit(solution)/shard_map/ppermute | solution.py:28
  50.7 0.2 collective-permute-start.18
  50.9 1.0 %collective-permute-start.17 = (f32[16,1792]{1,0:T(8,128)S(1)}, f32[16,1792]{1,0:T(8,128)S(1)}, u32[]{:S(2)}, u32[]{:S(2)}) collective-permute-start(f32[16,1792]{1,0:T(8,128)S(1)} %add.164), channel_id=1, source_target_pairs={{0,64},{8,72},{16,80},{24,88},{32,96},{40,104},{48,112},{56,120},{... | collective-permute-start | bytes 344072 | tf_op jit(solution)/shard_map/ppermute | solution.py:28
  51.9 2.4 %collective-permute-done.9 = f32[16,1024]{1,0:T(8,128)S(1)} collective-permute-done((f32[16,1024]{1,0:T(8,128)S(1)}, f32[16,1024]{1,0:T(8,128)S(1)}, u32[]{:S(2)}, u32[]{:S(2)}) %collective-permute-start.9) | collective-permute-done | bytes 65568 | tf_op jit(solution)/shard_map/ppermute | solution.py:28
  54.5 0.1 reshape.236
  54.7 0.1 reshape.237
  54.9 0.1 reshape.238
  55.1 0.1 reshape.239
  55.3 0.1 reshape.240
  55.5 0.1 reshape.241
  55.7 1.7 %collective-permute-start.13 = (f32[16,1024]{1,0:T(8,128)S(1)}, f32[16,1024]{1,0:T(8,128)S(1)}, u32[]{:S(2)}, u32[]{:S(2)}) collective-permute-start(f32[16,1024]{1,0:T(8,128)S(1)} %maximum_maximum_fusion.2), channel_id=1, source_target_pairs={{0,128},{8,136},{16,144},{24,152},{32,160},{40,168},{48,176},{56,1... | collective-permute-start | bytes 196616 | tf_op jit(solution)/shard_map/ppermute | solution.py:28
  57.4 1.0 %collective-permute-start.11 = (f32[16,1024]{1,0:T(8,128)S(1)}, f32[16,1024]{1,0:T(8,128)S(1)}, u32[]{:S(2)}, u32[]{:S(2)}) collective-permute-start(f32[16,1024]{1,0:T(8,128)S(1)} %maximum_maximum_fusion.2), channel_id=1, source_target_pairs={{0,64},{8,72},{16,80},{24,88},{32,96},{40,104},{48,112},{56,120},{... | collective-permute-start | bytes 196616 | tf_op jit(solution)/shard_map/ppermute | solution.py:28
  58.7 0.2 fusion.100
  58.9 0.2 convolution_bitcast_fusion
  59.2 0.1 reshape.253
  59.3 0.1 copy.57
  59.4 0.1 copy.62
  59.5 1.8 %collective-permute-done.13 = f32[16,1024]{1,0:T(8,128)S(1)} collective-permute-done((f32[16,1024]{1,0:T(8,128)S(1)}, f32[16,1024]{1,0:T(8,128)S(1)}, u32[]{:S(2)}, u32[]{:S(2)}) %collective-permute-start.13) | collective-permute-done | bytes 65568 | tf_op jit(solution)/shard_map/ppermute | solution.py:28
  61.4 1.7 %collective-permute-done.12 = f32[16,1024]{1,0:T(8,128)S(1)} collective-permute-done((f32[16,1024]{1,0:T(8,128)S(1)}, f32[16,1024]{1,0:T(8,128)S(1)}, u32[]{:S(2)}, u32[]{:S(2)}) %collective-permute-start.12) | collective-permute-done | bytes 65568 | tf_op jit(solution)/shard_map/ppermute | solution.py:28
  63.3 0.1 reshape.256
  63.4 0.1 reshape.242
  63.6 0.1 reshape.254
  64.6 0.1 reshape.247
  64.8 0.1 reshape.251
  64.9 0.2 fusion.48
  65.1 5.4 %collective-permute-start.20 = (f32[16,112]{1,0:T(8,128)S(1)}, f32[16,112]{1,0:T(8,128)S(1)}, u32[]{:S(2)}, u32[]{:S(2)}) collective-permute-start(f32[16,112]{1,0:T(8,128)S(1)} %fusion.48), channel_id=1, source_target_pairs={{0,1},{1,0},{2,3},{3,2},{4,5},{5,4},{6,7},{7,6},{8,9},{9,8},{10,11... | collective-permute-start | bytes 21512 | tf_op jit(solution)/shard_map/ppermute | solution.py:28
  70.5 0.8 %collective-permute-done.20 = f32[16,112]{1,0:T(8,128)S(1)} collective-permute-done((f32[16,112]{1,0:T(8,128)S(1)}, f32[16,112]{1,0:T(8,128)S(1)}, u32[]{:S(2)}, u32[]{:S(2)}) %collective-permute-start.20) | collective-permute-done | bytes 7200 | tf_op jit(solution)/shard_map/ppermute | solution.py:28
  71.3 2.9 %collective-permute-start.23 = (f32[16,112]{1,0:T(8,128)S(1)}, f32[16,112]{1,0:T(8,128)S(1)}, u32[]{:S(2)}, u32[]{:S(2)}) collective-permute-start(f32[16,112]{1,0:T(8,128)S(1)} %add.173), channel_id=1, source_target_pairs={{0,4},{1,5},{2,6},{3,7},{4,0},{5,1},{6,2},{7,3},{8,12},{9,13},{10,... | collective-permute-start | bytes 21512 | tf_op jit(solution)/shard_map/ppermute | solution.py:28
  74.3 0.8 collective-permute-start.22
  75.0 0.7 pad_maximum_fusion.1
  75.7 2.3 %collective-permute-done.22 = f32[16,112]{1,0:T(8,128)S(1)} collective-permute-done((f32[16,112]{1,0:T(8,128)S(1)}, f32[16,112]{1,0:T(8,128)S(1)}, u32[]{:S(2)}, u32[]{:S(2)}) %collective-permute-start.22) | collective-permute-done | bytes 7200 | tf_op jit(solution)/shard_map/ppermute | solution.py:28
  78.0 0.6 add_add_fusion.3
  (91 shorter events, 3.9 us)
Async XLA Ops:
  0.6 30.4 %copy-start = (bf16[128,896]{1,0:T(8,128)(2,1)S(1)}, bf16[128,896]{1,0:T(8,128)(2,1)}, u32[]{:S(2)}) copy-start(bf16[128,896]{1,0:T(8,128)(2,1)} %param.15) | copy-start | bytes 688132
  3.9 11.7 %collective-permute-start = (f32[16,1152]{1,0:T(8,128)S(1)}, f32[16,1152]{1,0:T(8,128)S(1)}, u32[]{:S(2)}, u32[]{:S(2)}) collective-permute-start(f32[16,1152]{1,0:T(8,128)S(1)} %concatenate.15), channel_id=1, source_target_pairs={{0,48},{8,56},{16,32},{24,40},{32,16},{40,24},{48,0},{56,8},{64,11... | collective-permute-start | bytes 221192 | tf_op jit(solution)/shard_map/ppermute | solution.py:28
  13.2 13.9 %collective-permute-start.14 = (f32[16,1792]{1,0:T(8,128)S(1)}, f32[16,1792]{1,0:T(8,128)S(1)}, u32[]{:S(2)}, u32[]{:S(2)}) collective-permute-start(f32[16,1792]{1,0:T(8,128)S(1)} %pad_maximum_fusion), channel_id=1, source_target_pairs={{0,48},{8,56},{16,32},{24,40},{32,16},{40,24},{48,0},{56,8},{64,11... | collective-permute-start | bytes 344072 | tf_op jit(solution)/shard_map/ppermute | solution.py:28
  15.6 5.2 %collective-permute-start.3 = (f32[16,1152]{1,0:T(8,128)S(1)}, f32[16,1152]{1,0:T(8,128)S(1)}, u32[]{:S(2)}, u32[]{:S(2)}) collective-permute-start(f32[16,1152]{1,0:T(8,128)S(1)} %add.142), channel_id=1, source_target_pairs={{0,24},{8,16},{16,8},{24,0},{32,56},{40,48},{48,40},{56,32},{64,88... | collective-permute-start | bytes 221192 | tf_op jit(solution)/shard_map/ppermute | solution.py:28
  17.5 5.8 %collective-permute-start.2 = (f32[16,1152]{1,0:T(8,128)S(1)}, f32[16,1152]{1,0:T(8,128)S(1)}, u32[]{:S(2)}, u32[]{:S(2)}) collective-permute-start(f32[16,1152]{1,0:T(8,128)S(1)} %add.142), channel_id=1, source_target_pairs={{0,16},{8,24},{16,0},{24,8},{32,48},{40,56},{48,32},{56,40},{64,80... | collective-permute-start | bytes 221192 | tf_op jit(solution)/shard_map/ppermute | solution.py:28
  17.6 5.8 %collective-permute-start.1 = (f32[16,1152]{1,0:T(8,128)S(1)}, f32[16,1152]{1,0:T(8,128)S(1)}, u32[]{:S(2)}, u32[]{:S(2)}) collective-permute-start(f32[16,1152]{1,0:T(8,128)S(1)} %add.142), channel_id=1, source_target_pairs={{0,8},{8,0},{16,24},{24,16},{32,40},{40,32},{48,56},{56,48},{64,72... | collective-permute-start | bytes 221192 | tf_op jit(solution)/shard_map/ppermute | solution.py:28
  23.4 5.4 %collective-permute-start.6 = (f32[16,1152]{1,0:T(8,128)S(1)}, f32[16,1152]{1,0:T(8,128)S(1)}, u32[]{:S(2)}, u32[]{:S(2)}) collective-permute-start(f32[16,1152]{1,0:T(8,128)S(1)} %add_add_fusion.2), channel_id=1, source_target_pairs={{0,128},{8,136},{16,144},{24,152},{32,160},{40,168},{48,176},{56,1... | collective-permute-start | bytes 221192 | tf_op jit(solution)/shard_map/ppermute | solution.py:28
  26.2 4.7 %collective-permute-start.5 = (f32[16,1152]{1,0:T(8,128)S(1)}, f32[16,1152]{1,0:T(8,128)S(1)}, u32[]{:S(2)}, u32[]{:S(2)}) collective-permute-start(f32[16,1152]{1,0:T(8,128)S(1)} %add_add_fusion.2), channel_id=1, source_target_pairs={{0,192},{8,200},{16,208},{24,216},{32,224},{40,232},{48,240},{56,2... | collective-permute-start | bytes 221192 | tf_op jit(solution)/shard_map/ppermute | solution.py:28
  27.1 3.9 %collective-permute-start.4 = (f32[16,1152]{1,0:T(8,128)S(1)}, f32[16,1152]{1,0:T(8,128)S(1)}, u32[]{:S(2)}, u32[]{:S(2)}) collective-permute-start(f32[16,1152]{1,0:T(8,128)S(1)} %add_add_fusion.2), channel_id=1, source_target_pairs={{0,64},{8,72},{16,80},{24,88},{32,96},{40,104},{48,112},{56,120},{... | collective-permute-start | bytes 221192 | tf_op jit(solution)/shard_map/ppermute | solution.py:28
  27.1 15.1 %collective-permute-start.15 = (f32[16,1792]{1,0:T(8,128)S(1)}, f32[16,1792]{1,0:T(8,128)S(1)}, u32[]{:S(2)}, u32[]{:S(2)}) collective-permute-start(f32[16,1792]{1,0:T(8,128)S(1)} %fusion.95), channel_id=1, source_target_pairs={{0,8},{8,0},{16,24},{24,16},{32,40},{40,32},{48,56},{56,48},{64,72... | collective-permute-start | bytes 344072 | tf_op jit(solution)/shard_map/ppermute | solution.py:28
  38.1 6.8 %collective-permute-start.7 = (f32[16,1024]{1,0:T(8,128)S(1)}, f32[16,1024]{1,0:T(8,128)S(1)}, u32[]{:S(2)}, u32[]{:S(2)}) collective-permute-start(f32[16,1024]{1,0:T(8,128)S(1)} %maximum_maximum_fusion), channel_id=1, source_target_pairs={{0,48},{8,56},{16,32},{24,40},{32,16},{40,24},{48,0},{56,8},{64,11... | collective-permute-start | bytes 196616 | tf_op jit(solution)/shard_map/ppermute | solution.py:28
  42.2 22.7 %copy-start.1 = (bf16[896,112]{0,1:T(8,128)(2,1)S(1)}, bf16[896,112]{0,1:T(8,128)(2,1)}, u32[]{:S(2)}) copy-start(bf16[896,112]{0,1:T(8,128)(2,1)} %param.16) | copy-start | bytes 602116
  42.2 7.0 %collective-permute-start.16 = (f32[16,1792]{1,0:T(8,128)S(1)}, f32[16,1792]{1,0:T(8,128)S(1)}, u32[]{:S(2)}, u32[]{:S(2)}) collective-permute-start(f32[16,1792]{1,0:T(8,128)S(1)} %add.163), channel_id=1, source_target_pairs={{0,16},{8,24},{16,0},{24,8},{32,48},{40,56},{48,32},{56,40},{64,80... | collective-permute-start | bytes 344072 | tf_op jit(solution)/shard_map/ppermute | solution.py:28
  45.5 5.4 %collective-permute-start.10 = (f32[16,1024]{1,0:T(8,128)S(1)}, f32[16,1024]{1,0:T(8,128)S(1)}, u32[]{:S(2)}, u32[]{:S(2)}) collective-permute-start(f32[16,1024]{1,0:T(8,128)S(1)} %maximum_maximum_fusion.1), channel_id=1, source_target_pairs={{0,24},{8,16},{16,8},{24,0},{32,56},{40,48},{48,40},{56,32},{64,88... | collective-permute-start | bytes 196616 | tf_op jit(solution)/shard_map/ppermute | solution.py:28
  47.1 7.2 %collective-permute-start.9 = (f32[16,1024]{1,0:T(8,128)S(1)}, f32[16,1024]{1,0:T(8,128)S(1)}, u32[]{:S(2)}, u32[]{:S(2)}) collective-permute-start(f32[16,1024]{1,0:T(8,128)S(1)} %maximum_maximum_fusion.1), channel_id=1, source_target_pairs={{0,16},{8,24},{16,0},{24,8},{32,48},{40,56},{48,32},{56,40},{64,80... | collective-permute-start | bytes 196616 | tf_op jit(solution)/shard_map/ppermute | solution.py:28
  47.8 6.6 %collective-permute-start.8 = (f32[16,1024]{1,0:T(8,128)S(1)}, f32[16,1024]{1,0:T(8,128)S(1)}, u32[]{:S(2)}, u32[]{:S(2)}) collective-permute-start(f32[16,1024]{1,0:T(8,128)S(1)} %maximum_maximum_fusion.1), channel_id=1, source_target_pairs={{0,8},{8,0},{16,24},{24,16},{32,40},{40,32},{48,56},{56,48},{64,72... | collective-permute-start | bytes 196616 | tf_op jit(solution)/shard_map/ppermute | solution.py:28
  49.2 8.2 %collective-permute-start.19 = (f32[16,1792]{1,0:T(8,128)S(1)}, f32[16,1792]{1,0:T(8,128)S(1)}, u32[]{:S(2)}, u32[]{:S(2)}) collective-permute-start(f32[16,1792]{1,0:T(8,128)S(1)} %add.164), channel_id=1, source_target_pairs={{0,128},{8,136},{16,144},{24,152},{32,160},{40,168},{48,176},{56,1... | collective-permute-start | bytes 344072 | tf_op jit(solution)/shard_map/ppermute | solution.py:28
  50.7 7.7 %collective-permute-start.18 = (f32[16,1792]{1,0:T(8,128)S(1)}, f32[16,1792]{1,0:T(8,128)S(1)}, u32[]{:S(2)}, u32[]{:S(2)}) collective-permute-start(f32[16,1792]{1,0:T(8,128)S(1)} %add.164), channel_id=1, source_target_pairs={{0,192},{8,200},{16,208},{24,216},{32,224},{40,232},{48,240},{56,2... | collective-permute-start | bytes 344072 | tf_op jit(solution)/shard_map/ppermute | solution.py:28
  50.9 7.5 %collective-permute-start.17 = (f32[16,1792]{1,0:T(8,128)S(1)}, f32[16,1792]{1,0:T(8,128)S(1)}, u32[]{:S(2)}, u32[]{:S(2)}) collective-permute-start(f32[16,1792]{1,0:T(8,128)S(1)} %add.164), channel_id=1, source_target_pairs={{0,64},{8,72},{16,80},{24,88},{32,96},{40,104},{48,112},{56,120},{... | collective-permute-start | bytes 344072 | tf_op jit(solution)/shard_map/ppermute | solution.py:28
  55.7 5.6 %collective-permute-start.13 = (f32[16,1024]{1,0:T(8,128)S(1)}, f32[16,1024]{1,0:T(8,128)S(1)}, u32[]{:S(2)}, u32[]{:S(2)}) collective-permute-start(f32[16,1024]{1,0:T(8,128)S(1)} %maximum_maximum_fusion.2), channel_id=1, source_target_pairs={{0,128},{8,136},{16,144},{24,152},{32,160},{40,168},{48,176},{56,1... | collective-permute-start | bytes 196616 | tf_op jit(solution)/shard_map/ppermute | solution.py:28
  57.4 5.7 %collective-permute-start.12 = (f32[16,1024]{1,0:T(8,128)S(1)}, f32[16,1024]{1,0:T(8,128)S(1)}, u32[]{:S(2)}, u32[]{:S(2)}) collective-permute-start(f32[16,1024]{1,0:T(8,128)S(1)} %maximum_maximum_fusion.2), channel_id=1, source_target_pairs={{0,192},{8,200},{16,208},{24,216},{32,224},{40,232},{48,240},{56,2... | collective-permute-start | bytes 196616 | tf_op jit(solution)/shard_map/ppermute | solution.py:28
  57.4 5.7 %collective-permute-start.11 = (f32[16,1024]{1,0:T(8,128)S(1)}, f32[16,1024]{1,0:T(8,128)S(1)}, u32[]{:S(2)}, u32[]{:S(2)}) collective-permute-start(f32[16,1024]{1,0:T(8,128)S(1)} %maximum_maximum_fusion.2), channel_id=1, source_target_pairs={{0,64},{8,72},{16,80},{24,88},{32,96},{40,104},{48,112},{56,120},{... | collective-permute-start | bytes 196616 | tf_op jit(solution)/shard_map/ppermute | solution.py:28
  65.1 6.3 %collective-permute-start.20 = (f32[16,112]{1,0:T(8,128)S(1)}, f32[16,112]{1,0:T(8,128)S(1)}, u32[]{:S(2)}, u32[]{:S(2)}) collective-permute-start(f32[16,112]{1,0:T(8,128)S(1)} %fusion.48), channel_id=1, source_target_pairs={{0,1},{1,0},{2,3},{3,2},{4,5},{5,4},{6,7},{7,6},{8,9},{9,8},{10,11... | collective-permute-start | bytes 21512 | tf_op jit(solution)/shard_map/ppermute | solution.py:28
  71.3 4.4 %collective-permute-start.23 = (f32[16,112]{1,0:T(8,128)S(1)}, f32[16,112]{1,0:T(8,128)S(1)}, u32[]{:S(2)}, u32[]{:S(2)}) collective-permute-start(f32[16,112]{1,0:T(8,128)S(1)} %add.173), channel_id=1, source_target_pairs={{0,4},{1,5},{2,6},{3,7},{4,0},{5,1},{6,2},{7,3},{8,12},{9,13},{10,... | collective-permute-start | bytes 21512 | tf_op jit(solution)/shard_map/ppermute | solution.py:28
  74.3 3.7 %collective-permute-start.22 = (f32[16,112]{1,0:T(8,128)S(1)}, f32[16,112]{1,0:T(8,128)S(1)}, u32[]{:S(2)}, u32[]{:S(2)}) collective-permute-start(f32[16,112]{1,0:T(8,128)S(1)} %add.173), channel_id=1, source_target_pairs={{0,6},{1,7},{2,4},{3,5},{4,2},{5,3},{6,0},{7,1},{8,14},{9,15},{10,... | collective-permute-start | bytes 21512 | tf_op jit(solution)/shard_map/ppermute | solution.py:28
  75.0 2.9 %collective-permute-start.21 = (f32[16,112]{1,0:T(8,128)S(1)}, f32[16,112]{1,0:T(8,128)S(1)}, u32[]{:S(2)}, u32[]{:S(2)}) collective-permute-start(f32[16,112]{1,0:T(8,128)S(1)} %add.173), channel_id=1, source_target_pairs={{0,2},{1,3},{2,0},{3,1},{4,6},{5,7},{6,4},{7,5},{8,10},{9,11},{10,... | collective-permute-start | bytes 21512 | tf_op jit(solution)/shard_map/ppermute | solution.py:28
